TPU v7x, 32 devices: a whole 2x2x4 slice. The times are simulated.
32 devices in a mesh: dp: 2 (over core), expert: 16 (over z, y, x).
Axes of the slice: x: 2, y: 2, z: 4, core: 2. Of those that a mesh axis runs over, the one named last changes fastest.
Arguments:
- tokens: bfloat16 [1024, 3584], P(('dp', 'expert')), may hold values from -6 to 6
- out_grad: bfloat16 [1024, 3584], P(('dp', 'expert')), may hold values from -6 to 6
- expert_ids: int32 [1024, 8], P(('dp', 'expert')), may hold values from 0 to 15, all different within a row; in each aligned block of 32 rows (0 to 31, 32 to 63, ...) at most 20 rows name the same one
- gate_probs: float32 [1024, 8], P(('dp', 'expert')), may hold values from 0.2 to 1.5
- weights: bfloat16 [16, 3584, 3, 128], P('expert', 'dp'), may hold values from -0.09375 to 0.09375
- first_moment: bfloat16 [16, 3584, 3, 128], P('expert', 'dp'), may hold values from -6 to 6
- second_moment: bfloat16 [16, 3584, 3, 128], P('expert', 'dp'), may hold values from 0.5 to 5
- moving_pairs: int32 [8], replicated, may hold values from 0 to 1, as said below
Outputs:
- token_grad: bfloat16 [1024, 3584], P(('dp', 'expert'))
- prob_grad: bfloat16 [1024, 8], P(('dp', 'expert'))
- moved_weights: bfloat16 [16, 3584, 3, 128], P('expert', 'dp')
- weight_grad: float32 [16, 3584, 3, 128], P('expert', 'dp')
- new_first: bfloat16 [16, 3584, 3, 128], P('expert', 'dp')
- new_second: bfloat16 [16, 3584, 3, 128], P('expert', 'dp')
Inputs may be any that keep to these rules, and one draw needn't show every extreme that they name: `expert_ids`: each row names 8 different experts. Among the entries of the 32 rows of one device, no expert is named more than 20 times, a bound that some block reaches. `moving_pairs`: entry p is 1 where devices p and p + 8 of the expert axis exchange their experts. The last entry is always 1.
All inputs are finite; a program needn't handle non-finite values.
Results may differ from a plain program's by a relative error of at most 0.018.
Values may be sent and summed in bfloat16 or wider, within the bound.
No kernel may reach another device: no remote copies, remote signals or barrier semaphores. Data moves between devices by JAX's collectives and lax.ppermute only.
A program may use at most 64 MiB of HBM per device.

v0:
```python
import jax
import jax.numpy as jnp
from jax import lax
from jax.sharding import PartitionSpec as P


def from_partner(value, axis, bit):
    return lax.ppermute(value, axis, [(i, i ^ 1 << bit) for i in range(lax.axis_size(axis))])


def silu_parts(pre_gate):
    sig = jax.nn.sigmoid(pre_gate)
    return (pre_gate * sig, sig * (1.0 + pre_gate * (1.0 - sig)))


def on_device(
    tokens, out_grad, expert_ids, gate_probs, weights, first_moment, second_moment, moving_pairs
):
    axis_width = lax.axis_size("expert")
    half_axis = axis_width // 2
    swap_bit = half_axis.bit_length() - 1
    groups = lax.axis_size("dp")
    my_index = lax.axis_index("expert")
    tok_rows, route_count = expert_ids.shape
    model_width = tokens.shape[1]
    entry_count = tok_rows * route_count
    slot_cap = 5 * entry_count // (4 * axis_width)
    slot_count = axis_width * slot_cap
    pair_lanes = jnp.arange(half_axis, dtype=jnp.int32)
    my_move = jnp.sum(jnp.where(pair_lanes == my_index % half_axis, moving_pairs, 0))
    swapped = my_move == 1
    flat_ids = expert_ids.reshape(-1)
    theirs = from_partner((weights, first_moment, second_moment), "expert", swap_bit)
    weights = jnp.where(swapped, theirs[0], weights)
    first_moment = jnp.where(swapped, theirs[1], first_moment)
    second_moment = jnp.where(swapped, theirs[2], second_moment)
    lane_hit = (flat_ids % half_axis)[:, None] == pair_lanes[None, :]
    moves = jnp.sum(jnp.where(lane_hit, moving_pairs[None, :], 0), axis=1)
    target_dev = jnp.where(moves == 1, (flat_ids + half_axis) % axis_width, flat_ids)
    id_onehot = (flat_ids[:, None] == jnp.arange(axis_width, dtype=jnp.int32)[None, :]).astype(
        jnp.int32
    )
    id_rank = jnp.sum((jnp.cumsum(id_onehot, axis=0) - id_onehot) * id_onehot, axis=1)
    slot_of = target_dev * slot_cap + id_rank
    slot_hit = jnp.arange(slot_count, dtype=jnp.int32)[:, None] == slot_of[None, :]
    filled = jnp.any(slot_hit, axis=1)
    entry_lanes = jnp.arange(entry_count, dtype=jnp.int32)
    slot_entry = jnp.sum(jnp.where(slot_hit, entry_lanes[None, :], 0), axis=1)
    token_of = slot_entry // route_count
    flat_gate = gate_probs.reshape(-1)
    zero_row = jnp.zeros((), jnp.bfloat16)
    send_rows = jnp.where(filled[:, None], tokens[token_of], zero_row).reshape(
        axis_width, slot_cap, model_width
    )
    send_grads = jnp.where(filled[:, None], out_grad[token_of], zero_row).reshape(
        axis_width, slot_cap, model_width
    )
    send_gate = (
        jnp.where(filled, flat_gate[slot_entry], 0.0)
        .astype(jnp.bfloat16)
        .reshape(axis_width, slot_cap)
    )
    recv_rows, recv_grads, recv_gate = (
        lax.all_to_all(send_rows, "expert", split_axis=0, concat_axis=0, tiled=True),
        lax.all_to_all(send_grads, "expert", split_axis=0, concat_axis=0, tiled=True),
        lax.all_to_all(send_gate, "expert", split_axis=0, concat_axis=0, tiled=True),
    )
    whole = lax.all_gather(weights, "dp", axis=1, tiled=True)[0]
    w_gate = whole[:, 0, :]
    w_up = whole[:, 1, :]
    w_down = whole[:, 2, :]
    w_both = jnp.concatenate([w_gate, w_up], axis=1)
    rows = recv_rows.reshape(slot_count, model_width)
    pre_gate = jnp.dot(rows, w_gate, preferred_element_type=jnp.float32)
    pre_up = jnp.dot(rows, w_up, preferred_element_type=jnp.float32)
    activated, act_slope = silu_parts(pre_gate)
    hidden = (activated * pre_up).astype(jnp.bfloat16)
    contract_hidden = (((1,), (1,)), ((), ()))
    grads_in = recv_grads.reshape(slot_count, model_width)
    gates = recv_gate.reshape(slot_count).astype(jnp.float32)
    projected = jnp.dot(grads_in, w_down, preferred_element_type=jnp.float32)
    gate_rows = jnp.sum(hidden.astype(jnp.float32) * projected, axis=1).astype(jnp.bfloat16)
    scaled_grad = (gates[:, None] * grads_in.astype(jnp.float32)).astype(jnp.bfloat16)
    hidden_grad = jnp.dot(scaled_grad, w_down, preferred_element_type=jnp.float32)
    gate_delta = (hidden_grad * pre_up * act_slope).astype(jnp.bfloat16)
    up_delta = (hidden_grad * activated).astype(jnp.bfloat16)
    both_delta = jnp.concatenate([gate_delta, up_delta], axis=1)
    row_grad = lax.dot_general(
        both_delta, w_both, contract_hidden, preferred_element_type=jnp.float32
    )
    row_grad = row_grad.astype(jnp.bfloat16)
    back_rows, back_gate = (
        lax.all_to_all(
            row_grad.reshape(axis_width, slot_cap, model_width),
            "expert",
            split_axis=0,
            concat_axis=0,
            tiled=True,
        ),
        lax.all_to_all(
            gate_rows.reshape(axis_width, slot_cap),
            "expert",
            split_axis=0,
            concat_axis=0,
            tiled=True,
        ),
    )
    contract_rows = (((0,), (0,)), ((), ()))
    grad_gate = lax.dot_general(rows, gate_delta, contract_rows, preferred_element_type=jnp.float32)
    grad_up = lax.dot_general(rows, up_delta, contract_rows, preferred_element_type=jnp.float32)
    grad_down = lax.dot_general(
        scaled_grad, hidden, contract_rows, preferred_element_type=jnp.float32
    )
    grad = lax.psum_scatter(
        jnp.stack([grad_gate, grad_up, grad_down], axis=1).astype(jnp.bfloat16),
        "dp",
        scatter_dimension=0,
        tiled=True,
    ).astype(jnp.float32) * (1.0 / groups)
    grad = grad[None]
    new_first = (0.9 * first_moment.astype(jnp.float32) + 0.1 * grad).astype(jnp.bfloat16)
    new_second = (0.95 * second_moment.astype(jnp.float32) + 0.05 * grad * grad).astype(
        jnp.bfloat16
    )
    gathered = back_rows.reshape(slot_count, model_width)[slot_of].astype(jnp.float32)
    token_grad = (
        (gathered * flat_gate[:, None])
        .reshape(tok_rows, route_count, model_width)
        .sum(axis=1)
        .astype(jnp.bfloat16)
    )
    prob_grad = back_gate.reshape(slot_count)[slot_of].reshape(tok_rows, route_count)
    return (token_grad, prob_grad, weights, grad, new_first, new_second)


def solution(mesh):
    in_specs = (
        P(("dp", "expert"), None),
        P(("dp", "expert"), None),
        P(("dp", "expert"), None),
        P(("dp", "expert"), None),
        P("expert", "dp", None, None),
        P("expert", "dp", None, None),
        P("expert", "dp", None, None),
        P(),
    )
    out_specs = (
        P(("dp", "expert"), None),
        P(("dp", "expert"), None),
        P("expert", "dp", None, None),
        P("expert", "dp", None, None),
        P("expert", "dp", None, None),
        P("expert", "dp", None, None),
    )
    return jax.shard_map(
        on_device, mesh=mesh, in_specs=in_specs, out_specs=out_specs, check_vma=False
    )
```

profile of v0, /device:TPU:6, one launch (start us, length us, event | category | flops | bytes accessed | tf_op | source)
XLA Modules:
  0.0 455.4 jit_solution(9229121527226329171)
XLA Ops:
  7.2 0.8 copy.39
  9.1 0.7 select_reduce_fusion.1
  10.2 0.8 copy.42
  11.1 2.4 gather_fusion
  13.4 0.7 convert_element_type.137
  14.1 7.3 %all-to-all-start = ((bf16[16,1,20]{2,1,0:T(2,128)(2,1)}), bf16[16,1,20]{2,1,0:T(2,128)(2,1)S(1)}, u32[]{:S(2)}, u32[]{:S(2)}) async-start(bf16[16,1,20]{2,1,0:T(2,128)(2,1)} %convert_element_type.137), calls=%async_computation | async-start | bytes 16384 | tf_op jit(solution)/shard_map/all_to_all | solution.py:66
  21.5 3.7 gather_fusion.1
  25.2 2.6 gather.21
  27.9 3.7 gather_fusion.2
  31.6 4.1 gather.23
  35.7 4.7 %broadcast_select_fusion = (bf16[16,20,3584]{2,1,0:T(8,128)(2,1)}, bf16[16,20,3584]{2,1,0:T(8,128)(2,1)}) fusion(bf16[16,20,3584]{2,1,0:T(8,128)(2,1)} %gather.23, pred[16,20]{1,0:T(8,128)(4,1)S(1)} %broadcast_in_dim.73, bf16[16,20,3584]{2,1,0:T(8,128)(2,1)S(1)} %gather.21), kind=kLoop, calls=%fused_computation.28 | loop fusion | flops 2293760 | bytes 9175360 | tf_op jit(solution)/shard_map/jit(_where)/select_n | solution.py:52
  40.3 6.9 %all-to-all-start.1 = ((bf16[16,20,3584]{2,1,0:T(8,128)(2,1)}), bf16[16,20,3584]{2,1,0:T(8,128)(2,1)S(1)}, u32[]{:S(2)}, u32[]{:S(2)}) async-start(bf16[16,20,3584]{2,1,0:T(8,128)(2,1)} %get-tuple-element.42), calls=%async_computation.1 | async-start | bytes 5505024 | tf_op jit(solution)/shard_map/all_to_all | solution.py:65
  47.3 2.4 collective-permute-start
  49.6 83.1 %all-to-all-done.1 = bf16[16,20,3584]{2,1,0:T(8,128)(2,1)S(1)} async-done(((bf16[16,20,3584]{2,1,0:T(8,128)(2,1)}), bf16[16,20,3584]{2,1,0:T(8,128)(2,1)S(1)}, u32[]{:S(2)}, u32[]{:S(2)}) %all-to-all-start.1) | async-done | bytes 2293792 | tf_op jit(solution)/shard_map/all_to_all | solution.py:65
  132.7 12.5 %all-to-all-start.2 = ((bf16[16,20,3584]{2,1,0:T(8,128)(2,1)}), bf16[16,20,3584]{2,1,0:T(8,128)(2,1)}, u32[]{:S(2)}, u32[]{:S(2)}) async-start(bf16[16,20,3584]{2,1,0:T(8,128)(2,1)} %get-tuple-element.41), calls=%async_computation.2 | async-start | bytes 5505024 | tf_op jit(solution)/shard_map/all_to_all | solution.py:64
  146.6 51.8 %collective-permute-done = bf16[1,1792,3,128]{3,1,2,0:T(8,128)(2,1)} collective-permute-done((bf16[1,1792,3,128]{3,1,2,0:T(8,128)(2,1)}, bf16[1,1792,3,128]{3,1,2,0:T(8,128)(2,1)}, u32[]{:S(2)}, u32[]{:S(2)}) %collective-permute-start) | collective-permute-done | bytes 1376288 | tf_op jit(solution)/shard_map/ppermute | solution.py:8
  198.3 2.6 broadcast_select_fusion.2
  201.3 2.4 multiply_convert_fusion
  203.7 2.7 convert_element_type.114
  206.4 6.2 %all-gather.2.cloned.1.call-done = bf16[1,3584,3,128]{3,1,2,0:T(8,128)(2,1)} async-done(((bf16[1,1792,3,128]{3,1,2,0:T(8,128)(2,1)}), bf16[1,3584,3,128]{3,1,2,0:T(8,128)(2,1)}) %all-gather.2.cloned.1.call-update) | async-done | bytes 2752528 | tf_op jit(solution)/shard_map/all_gather | solution.py:68
  212.6 1.9 fusion.17
  214.6 6.8 %all-to-all-done.2 = bf16[16,20,3584]{2,1,0:T(8,128)(2,1)} async-done(((bf16[16,20,3584]{2,1,0:T(8,128)(2,1)}), bf16[16,20,3584]{2,1,0:T(8,128)(2,1)}, u32[]{:S(2)}, u32[]{:S(2)}) %all-to-all-start.2) | async-done | bytes 2293792 | tf_op jit(solution)/shard_map/all_to_all | solution.py:64
  221.3 2.7 reshape.344
  224.0 1.9 fusion.36
  226.0 2.6 multiply_convert_fusion.3
  228.6 0.9 fusion
  229.5 1.9 fusion.1
  231.4 2.7 reshape.348
  234.1 2.1 fusion.2
  236.2 1.9 pad_maximum_fusion
  238.1 2.5 slice_bitcast_fusion
  240.6 2.0 fusion.16
  242.6 0.7 convert_element_type.138
  243.4 10.5 %all-to-all-start.4 = ((bf16[16,1,20]{2,1,0:T(2,128)(2,1)}), bf16[16,1,20]{2,1,0:T(2,128)(2,1)S(1)}, u32[]{:S(2)}, u32[]{:S(2)}) async-start(bf16[16,1,20]{2,1,0:T(2,128)(2,1)} %convert_element_type.138), calls=%async_computation.4 | async-start | bytes 16384 | tf_op jit(solution)/shard_map/all_to_all | solution.py:100
  253.9 2.0 convolution_convert_fusion
  255.9 2.2 reshape.345
  258.0 0.8 all-to-all-done.4
  258.8 6.6 %all-to-all-start.3 = ((bf16[16,20,3584]{2,1,0:T(8,128)(2,1)}), bf16[16,20,3584]{2,1,0:T(8,128)(2,1)}, u32[]{:S(2)}, u32[]{:S(2)}) async-start(bf16[16,20,3584]{2,1,0:T(8,128)(2,1)} %reshape.345), calls=%async_computation.3 | async-start | bytes 5505024 | tf_op jit(solution)/shard_map/all_to_all | solution.py:93
  265.4 2.5 collective-permute-start.1
  268.6 1.9 gather_fusion.4
  271.3 107.9 %all-to-all-done.3 = bf16[16,20,3584]{2,1,0:T(8,128)(2,1)} async-done(((bf16[16,20,3584]{2,1,0:T(8,128)(2,1)}), bf16[16,20,3584]{2,1,0:T(8,128)(2,1)}, u32[]{:S(2)}, u32[]{:S(2)}) %all-to-all-start.3) | async-done | bytes 2293792 | tf_op jit(solution)/shard_map/all_to_all | solution.py:93
  379.3 2.7 reshape.346
  382.0 2.9 gather_fusion.3
  384.9 3.6 fusion.3
  388.6 3.2 fusion.5
  391.7 23.5 %collective-permute-done.1 = bf16[1,1792,3,128]{3,1,2,0:T(8,128)(2,1)} collective-permute-done((bf16[1,1792,3,128]{3,1,2,0:T(8,128)(2,1)}, bf16[1,1792,3,128]{3,1,2,0:T(8,128)(2,1)}, u32[]{:S(2)}, u32[]{:S(2)}) %collective-permute-start.1) | collective-permute-done | bytes 1376288 | tf_op jit(solution)/shard_map/ppermute | solution.py:8
  415.2 28.4 %collective-permute-done.2 = bf16[1,1792,3,128]{3,1,2,0:T(8,128)(2,1)} collective-permute-done((bf16[1,1792,3,128]{3,1,2,0:T(8,128)(2,1)}, bf16[1,1792,3,128]{3,1,2,0:T(8,128)(2,1)}, u32[]{:S(2)}, u32[]{:S(2)}) %collective-permute-start.2) | collective-permute-done | bytes 1376288 | tf_op jit(solution)/shard_map/ppermute | solution.py:8
  443.7 4.8 %fusion.8 = (bf16[1,1792,3,128]{3,1,2,0:T(8,128)(2,1)}, bf16[1,1792,3,128]{3,1,2,0:T(8,128)(2,1)}) fusion(bf16[1792,3,128]{2,0,1:T(8,128)(2,1)S(1)} %copy-done.4, bf16[1,1792,3,128]{3,1,2,0:T(8,128)(2,1)} %collective-permute-done.2, bf16[1,1792,3,128]{3,1,2,0:T(8,128)(2,1)} %param.14, pred[]{:T(512)S(6)} %eq.100, ...), kind=kLoop, calls=%fused_computation.23 | loop fusion | flops 10321920 | bytes 9633793 | tf_op jit(solution)/shard_map/convert_element_type | solution.py:122
  (51 shorter events, 4.2 us)
Async XLA Ops:
  7.2 14.3 %copy-start = (bf16[32,3584]{1,0:T(8,128)(2,1)S(1)}, bf16[32,3584]{1,0:T(8,128)(2,1)}, u32[]{:S(2)}) copy-start(bf16[32,3584]{1,0:T(8,128)(2,1)} %param.9) | copy-start | bytes 688132
  14.1 26.2 %all-to-all-start = ((bf16[16,1,20]{2,1,0:T(2,128)(2,1)}), bf16[16,1,20]{2,1,0:T(2,128)(2,1)S(1)}, u32[]{:S(2)}, u32[]{:S(2)}) async-start(bf16[16,1,20]{2,1,0:T(2,128)(2,1)} %convert_element_type.137), calls=%async_computation | async-start | bytes 16384 | tf_op jit(solution)/shard_map/all_to_all | solution.py:66
  25.2 2.6 copy-start.2
  40.3 92.4 %all-to-all-start.1 = ((bf16[16,20,3584]{2,1,0:T(8,128)(2,1)}), bf16[16,20,3584]{2,1,0:T(8,128)(2,1)S(1)}, u32[]{:S(2)}, u32[]{:S(2)}) async-start(bf16[16,20,3584]{2,1,0:T(8,128)(2,1)} %get-tuple-element.42), calls=%async_computation.1 | async-start | bytes 5505024 | tf_op jit(solution)/shard_map/all_to_all | solution.py:65
  47.3 151.1 %collective-permute-start = (bf16[1,1792,3,128]{3,1,2,0:T(8,128)(2,1)}, bf16[1,1792,3,128]{3,1,2,0:T(8,128)(2,1)}, u32[]{:S(2)}, u32[]{:S(2)}) collective-permute-start(bf16[1,1792,3,128]{3,1,2,0:T(8,128)(2,1)} %param.12), channel_id=1, source_target_pairs={{0,8},{1,9},{2,10},{3,11},{4,12},{5,13},{6,14},{7,15},{8,0},{9,1},... | collective-permute-start | bytes 4128776 | tf_op jit(solution)/shard_map/ppermute | solution.py:8
  132.7 68.6 %copy-start.3 = (bf16[16,20,3584]{2,1,0:T(8,128)(2,1)}, bf16[16,20,3584]{2,1,0:T(8,128)(2,1)S(1)}, u32[]{:S(2)}) copy-start(bf16[16,20,3584]{2,1,0:T(8,128)(2,1)S(1)} %all-to-all-done.1) | copy-start | bytes 6881284
  132.7 12.6 %copy-start.6 = (s32[8]{0:T(128)S(1)}, s32[8]{0:T(128)}, u32[]{:S(2)}) copy-start(s32[8]{0:T(128)} %param.15) | copy-start | bytes 100
  132.7 88.6 %all-to-all-start.2 = ((bf16[16,20,3584]{2,1,0:T(8,128)(2,1)}), bf16[16,20,3584]{2,1,0:T(8,128)(2,1)}, u32[]{:S(2)}, u32[]{:S(2)}) async-start(bf16[16,20,3584]{2,1,0:T(8,128)(2,1)} %get-tuple-element.41), calls=%async_computation.2 | async-start | bytes 5505024 | tf_op jit(solution)/shard_map/all_to_all | solution.py:64
  145.2 67.4 %all-gather.2.cloned.1.call-start = ((), (), s32[]{:S(2)}) async-start(), calls=%async_computation.6 | async-start | bytes 4128768 | tf_op jit(solution)/shard_map/all_gather | solution.py:68
  200.9 187.7 %reduce-scatter.2.cloned.1.call-start = ((), (), s32[]{:S(2)}) async-start(), calls=%async_computation.7 | async-start | bytes 4128768 | tf_op jit(solution)/shard_map/reduce_scatter | solution.py:114
  234.1 2.1 copy-start.5
  238.1 2.5 copy-start.7
  243.4 15.5 %all-to-all-start.4 = ((bf16[16,1,20]{2,1,0:T(2,128)(2,1)}), bf16[16,1,20]{2,1,0:T(2,128)(2,1)S(1)}, u32[]{:S(2)}, u32[]{:S(2)}) async-start(bf16[16,1,20]{2,1,0:T(2,128)(2,1)} %convert_element_type.138), calls=%async_computation.4 | async-start | bytes 16384 | tf_op jit(solution)/shard_map/all_to_all | solution.py:100
  258.8 120.5 %all-to-all-start.3 = ((bf16[16,20,3584]{2,1,0:T(8,128)(2,1)}), bf16[16,20,3584]{2,1,0:T(8,128)(2,1)}, u32[]{:S(2)}, u32[]{:S(2)}) async-start(bf16[16,20,3584]{2,1,0:T(8,128)(2,1)} %reshape.345), calls=%async_computation.3 | async-start | bytes 5505024 | tf_op jit(solution)/shard_map/all_to_all | solution.py:93
  265.4 149.9 %collective-permute-start.1 = (bf16[1,1792,3,128]{3,1,2,0:T(8,128)(2,1)}, bf16[1,1792,3,128]{3,1,2,0:T(8,128)(2,1)}, u32[]{:S(2)}, u32[]{:S(2)}) collective-permute-start(bf16[1,1792,3,128]{3,1,2,0:T(8,128)(2,1)} %param.13), channel_id=1, source_target_pairs={{0,8},{1,9},{2,10},{3,11},{4,12},{5,13},{6,14},{7,15},{8,0},{9,1},... | collective-permute-start | bytes 4128776 | tf_op jit(solution)/shard_map/ppermute | solution.py:8
  267.9 175.8 %collective-permute-start.2 = (bf16[1,1792,3,128]{3,1,2,0:T(8,128)(2,1)}, bf16[1,1792,3,128]{3,1,2,0:T(8,128)(2,1)}, u32[]{:S(2)}, u32[]{:S(2)}) collective-permute-start(bf16[1,1792,3,128]{3,1,2,0:T(8,128)(2,1)} %param.14), channel_id=1, source_target_pairs={{0,8},{1,9},{2,10},{3,11},{4,12},{5,13},{6,14},{7,15},{8,0},{9,1},... | collective-permute-start | bytes 4128776 | tf_op jit(solution)/shard_map/ppermute | solution.py:8
  388.6 55.1 %copy-start.4 = (bf16[1792,3,128]{2,0,1:T(8,128)(2,1)S(1)}, bf16[1792,3,128]{2,0,1:T(8,128)(2,1)}, u32[]{:S(2)}) copy-start(bf16[1792,3,128]{2,0,1:T(8,128)(2,1)} %reduce-scatter.2.cloned.1.call-done) | copy-start | bytes 4128772
  443.7 4.8 %copy-start.1 = (bf16[32,3584]{1,0:T(8,128)(2,1)S(1)}, bf16[32,3584]{1,0:T(8,128)(2,1)}, u32[]{:S(2)}) copy-start(bf16[32,3584]{1,0:T(8,128)(2,1)} %param.9) | copy-start | bytes 688132
Sparse Core Ops, SparseCore 0:
  201.0 11.5 all-gather.1
  238.2 15.0 reduce-scatter.1
where the time goes:
time: 458 us; the launch traced here: 455 us
  waiting for transfers between devices  308 us (67%)
  starting transfers between devices  49.4 us (11%)
  local copies, waits for them, and re-layouts  41.5 us (9%)
  other arithmetic  25.7 us (6%)
  matrix products  15.3 us (3%)
  between operations  15 us (3%)
    all_to_all x1, waiting for transfers between devices, on_device(): lax.all_to_all(row_grad.reshape(axis_width, slot_cap, model_width), 'expe...  108 us
    ppermute x3, waiting for transfers between devices, from_partner(): lax.ppermute(value, axis, [(i, i ^ 1 << bit) for i in range(lax.axis_size...  104 us
    all_to_all x1, waiting for transfers between devices, on_device(): lax.all_to_all(send_grads, 'expert', split_axis=0, concat_axis=0, tiled=T...  83.1 us
    all_to_all x1, starting transfers between devices, on_device(): lax.all_to_all(send_rows, 'expert', split_axis=0, concat_axis=0, tiled=True)  12.5 us
    all_to_all x1, starting transfers between devices, on_device(): lax.all_to_all(gate_rows.reshape(axis_width, slot_cap), 'expert', split_a...  10.5 us
  transfers between devices with their start and end apart: 10, of which 8 were waited for; matrix products, arithmetic and copies ran while one was open for 12% of the time, Pallas kernels for 0%

commit v1 on v0

--- a/solution.py
+++ b/solution.py
@@ -29,55 +29,43 @@
     pair_lanes = jnp.arange(half_axis, dtype=jnp.int32)
     my_move = jnp.sum(jnp.where(pair_lanes == my_index % half_axis, moving_pairs, 0))
     swapped = my_move == 1
-    flat_ids = expert_ids.reshape(-1)
+    held = jnp.where(swapped, (my_index + half_axis) % axis_width, my_index)
     theirs = from_partner((weights, first_moment, second_moment), "expert", swap_bit)
     weights = jnp.where(swapped, theirs[0], weights)
     first_moment = jnp.where(swapped, theirs[1], first_moment)
     second_moment = jnp.where(swapped, theirs[2], second_moment)
-    lane_hit = (flat_ids % half_axis)[:, None] == pair_lanes[None, :]
-    moves = jnp.sum(jnp.where(lane_hit, moving_pairs[None, :], 0), axis=1)
-    target_dev = jnp.where(moves == 1, (flat_ids + half_axis) % axis_width, flat_ids)
-    id_onehot = (flat_ids[:, None] == jnp.arange(axis_width, dtype=jnp.int32)[None, :]).astype(
-        jnp.int32
-    )
-    id_rank = jnp.sum((jnp.cumsum(id_onehot, axis=0) - id_onehot) * id_onehot, axis=1)
-    slot_of = target_dev * slot_cap + id_rank
-    slot_hit = jnp.arange(slot_count, dtype=jnp.int32)[:, None] == slot_of[None, :]
-    filled = jnp.any(slot_hit, axis=1)
+
+    flat_gate = gate_probs.reshape(-1)
+    all_rows = lax.all_gather(tokens, "expert", axis=0, tiled=True)
+    all_grads = lax.all_gather(out_grad, "expert", axis=0, tiled=True)
+    all_ids = lax.all_gather(expert_ids, "expert", axis=0, tiled=True)
+    all_gate = lax.all_gather(flat_gate.astype(jnp.bfloat16), "expert", axis=0, tiled=True)
+
+    src_ids = all_ids.reshape(axis_width, entry_count)
+    hit = (src_ids == held).astype(jnp.int32)
+    pos = jnp.cumsum(hit, axis=1) - hit
+    ranks = jnp.arange(slot_cap, dtype=jnp.int32)
+    sel = (hit[:, None, :] == 1) & (pos[:, None, :] == ranks[None, :, None])
+    filled = jnp.any(sel, axis=2).reshape(slot_count)
     entry_lanes = jnp.arange(entry_count, dtype=jnp.int32)
-    slot_entry = jnp.sum(jnp.where(slot_hit, entry_lanes[None, :], 0), axis=1)
-    token_of = slot_entry // route_count
-    flat_gate = gate_probs.reshape(-1)
-    zero_row = jnp.zeros((), jnp.bfloat16)
-    send_rows = jnp.where(filled[:, None], tokens[token_of], zero_row).reshape(
-        axis_width, slot_cap, model_width
-    )
-    send_grads = jnp.where(filled[:, None], out_grad[token_of], zero_row).reshape(
-        axis_width, slot_cap, model_width
-    )
-    send_gate = (
-        jnp.where(filled, flat_gate[slot_entry], 0.0)
-        .astype(jnp.bfloat16)
-        .reshape(axis_width, slot_cap)
-    )
-    recv_rows, recv_grads, recv_gate = (
-        lax.all_to_all(send_rows, "expert", split_axis=0, concat_axis=0, tiled=True),
-        lax.all_to_all(send_grads, "expert", split_axis=0, concat_axis=0, tiled=True),
-        lax.all_to_all(send_gate, "expert", split_axis=0, concat_axis=0, tiled=True),
-    )
+    slot_entry = jnp.sum(jnp.where(sel, entry_lanes[None, None, :], 0), axis=2)
+    src_base = (jnp.arange(axis_width, dtype=jnp.int32) * entry_count)[:, None]
+    flat_entry = (slot_entry + src_base).reshape(slot_count)
+    token_of = flat_entry // route_count
+    rows = all_rows[token_of]
+    grads_in = all_grads[token_of]
+    gates = jnp.where(filled, all_gate[flat_entry].astype(jnp.float32), 0.0)
+
     whole = lax.all_gather(weights, "dp", axis=1, tiled=True)[0]
     w_gate = whole[:, 0, :]
     w_up = whole[:, 1, :]
     w_down = whole[:, 2, :]
     w_both = jnp.concatenate([w_gate, w_up], axis=1)
-    rows = recv_rows.reshape(slot_count, model_width)
     pre_gate = jnp.dot(rows, w_gate, preferred_element_type=jnp.float32)
     pre_up = jnp.dot(rows, w_up, preferred_element_type=jnp.float32)
     activated, act_slope = silu_parts(pre_gate)
     hidden = (activated * pre_up).astype(jnp.bfloat16)
     contract_hidden = (((1,), (1,)), ((), ()))
-    grads_in = recv_grads.reshape(slot_count, model_width)
-    gates = recv_gate.reshape(slot_count).astype(jnp.float32)
     projected = jnp.dot(grads_in, w_down, preferred_element_type=jnp.float32)
     gate_rows = jnp.sum(hidden.astype(jnp.float32) * projected, axis=1).astype(jnp.bfloat16)
     scaled_grad = (gates[:, None] * grads_in.astype(jnp.float32)).astype(jnp.bfloat16)
@@ -122,6 +110,16 @@
     new_second = (0.95 * second_moment.astype(jnp.float32) + 0.05 * grad * grad).astype(
         jnp.bfloat16
     )
+
+    flat_ids = expert_ids.reshape(-1)
+    lane_hit = (flat_ids % half_axis)[:, None] == pair_lanes[None, :]
+    moves = jnp.sum(jnp.where(lane_hit, moving_pairs[None, :], 0), axis=1)
+    target_dev = jnp.where(moves == 1, (flat_ids + half_axis) % axis_width, flat_ids)
+    id_onehot = (flat_ids[:, None] == jnp.arange(axis_width, dtype=jnp.int32)[None, :]).astype(
+        jnp.int32
+    )
+    id_rank = jnp.sum((jnp.cumsum(id_onehot, axis=0) - id_onehot) * id_onehot, axis=1)
+    slot_of = target_dev * slot_cap + id_rank
     gathered = back_rows.reshape(slot_count, model_width)[slot_of].astype(jnp.float32)
     token_grad = (
         (gathered * flat_gate[:, None])

time: 458 us -> 452 us (0.987)
  blocking collectives: 0 us -> 73.9 us
  waiting for transfers between devices: 308 us -> 273 us
  starting transfers between devices: 49.4 us -> 17.9 us
  other arithmetic: 25.7 us -> 18.6 us
    all_to_all x3 -> x0, waiting for transfers between devices: 89.8 us -> none  [the longest x1 83.1 us: on_device(): lax.all_to_all(send_grads, 'expert', split_axis=0, concat_axis=0, tiled=T...]
    all_gather x0 -> x2, blocking collectives: none -> 73.9 us  [the longest x1 39.8 us: on_device(): all_ids = lax.all_gather(expert_ids, 'expert', axis=0, tiled=True)]
    all_gather x0 -> x2, waiting for transfers between devices: none -> 48.5 us  [the longest x1 48.5 us: on_device(): all_grads = lax.all_gather(out_grad, 'expert', axis=0, tiled=True)]
    all_to_all x3 -> x0, starting transfers between devices: 26.7 us -> none  [the longest x1 12.5 us: on_device(): lax.all_to_all(send_rows, 'expert', split_axis=0, concat_axis=0, tiled=True)]
    ppermute x3, waiting for transfers between devices: 104 us -> 115 us  [from_partner(): lax.ppermute(value, axis, [(i, i ^ 1 << bit) for i in range(lax.axis_size...]
    all_gather x1, waiting for transfers between devices: 6.2 us -> 0.02 us  [on_device(): whole = lax.all_gather(weights, 'dp', axis=1, tiled=True)[0]]
    reshape x3 -> x1, local copies, waits for them, and re-layouts: 5.5 us -> 0.1 us  [on_device(): filled = jnp.any(sel, axis=2).reshape(slot_count)]
    gather x5 -> x3, local copies, waits for them, and re-layouts: 16.5 us -> 21.8 us  [the longest x1 9.94 us: on_device(): grads_in = all_grads[token_of]]
  transfers between devices with their start and end apart: 10 -> 9, of which waited for: 8 -> 6; matrix products, arithmetic and copies ran while one was open for 12% -> 10% of each run, Pallas kernels for 0% -> 0%
where the time goes in v1:
time: 452 us; the launch traced here: 450 us
  waiting for transfers between devices  273 us (60%)
  blocking collectives  73.9 us (16%)
  local copies, waits for them, and re-layouts  38.9 us (9%)
  other arithmetic  18.6 us (4%)
  starting transfers between devices  17.9 us (4%)
  between operations  14.7 us (3%)
  matrix products  12.8 us (3%)
    ppermute x3, waiting for transfers between devices, from_partner(): lax.ppermute(value, axis, [(i, i ^ 1 << bit) for i in range(lax.axis_size...  115 us
    all_to_all x1, waiting for transfers between devices, on_device(): lax.all_to_all(row_grad.reshape(axis_width, slot_cap, model_width), 'expe...  108 us
    all_gather x1, waiting for transfers between devices, on_device(): all_grads = lax.all_gather(out_grad, 'expert', axis=0, tiled=True)  48.5 us
    all_gather x1, blocking collectives, on_device(): all_ids = lax.all_gather(expert_ids, 'expert', axis=0, tiled=True)  39.8 us
    all_gather x1, blocking collectives, on_device(): lax.all_gather(flat_gate.astype(jnp.bfloat16), 'expert', axis=0, tiled=True)  34 us
    gather x1, local copies, waits for them, and re-layouts, on_device(): grads_in = all_grads[token_of]  9.94 us
    gather x1, local copies, waits for them, and re-layouts, on_device(): rows = all_rows[token_of]  9.37 us
  transfers between devices with their start and end apart: 9, of which 6 were waited for; matrix products, arithmetic and copies ran while one was open for 10% of the time, Pallas kernels for 0%

profile of v1, /device:TPU:6, one launch (start us, length us, event | category | flops | bytes accessed | tf_op | source)
XLA Modules:
  0.0 449.7 jit_solution(1303724513147508749)
XLA Ops:
  7.2 0.7 all-gather.10.cloned.1.call-update
  7.9 2.7 collective-permute-start
  10.6 1.3 fusion.31
  12.6 62.9 %collective-permute-done = bf16[1,1792,3,128]{3,1,2,0:T(8,128)(2,1)S(1)} collective-permute-done((bf16[1,1792,3,128]{3,1,2,0:T(8,128)(2,1)}, bf16[1,1792,3,128]{3,1,2,0:T(8,128)(2,1)S(1)}, u32[]{:S(2)}, u32[]{:S(2)}) %collective-permute-start) | collective-permute-done | bytes 1376288 | tf_op jit(solution)/shard_map/ppermute | solution.py:8
  75.5 1.2 broadcast_select_fusion
  76.8 0.7 all-gather.6.cloned.1.call-update
  77.7 34.0 %all-gather.1 = bf16[16,1,256]{2,1,0:T(2,128)(2,1)S(1)} all-gather(bf16[1,1,256]{2,1,0:T(2,128)(2,1)S(1)} %reshape.377), channel_id=1, replica_groups=mesh['dp'=2,'expert'=16] {'expert'}, dimensions={0}, use_global_device_ids=true | all-gather | bytes 8704 | tf_op jit(solution)/shard_map/all_gather | solution.py:42
  111.9 39.8 %all-gather = s32[16,32,8]{1,2,0:T(8,128)S(1)} all-gather(s32[1,32,8]{1,2,0:T(8,128)S(1)} %bitcast.85), channel_id=1, replica_groups=mesh['dp'=2,'expert'=16] {'expert'}, dimensions={0}, use_global_device_ids=true | all-gather | bytes 17408 | tf_op jit(solution)/shard_map/all_gather | solution.py:41
  151.7 0.1 copy.76
  151.9 0.6 reduce-window.14
  152.5 0.2 slice_reduce_fusion.1
  152.9 0.4 select_reduce_fusion
  153.5 0.4 fusion.18
  154.3 2.5 gather_fusion
  156.8 9.4 %gather_fusion.2 = bf16[320,3584]{1,0:T(8,128)(2,1)S(1)} fusion(bf16[512,3584]{1,0:T(8,128)(2,1)} %all-gather.10.cloned.1.call-done, s32[1024]{0:T(1024)S(1)} %pad_clamp_fusion.1), kind=kCustom, calls=%fused_computation.2 | custom fusion | bytes 4588800 | tf_op jit(solution)/shard_map/gather | solution.py:55
  166.2 1.9 fusion.34
  168.2 48.5 %all-gather.6.cloned.1.call-done = bf16[512,3584]{1,0:T(8,128)(2,1)} async-done(((bf16[32,3584]{1,0:T(8,128)(2,1)}), bf16[512,3584]{1,0:T(8,128)(2,1)}) %all-gather.6.cloned.1.call-update) | async-done | bytes 3670032 | tf_op jit(solution)/shard_map/all_gather | solution.py:40
  216.7 9.9 %gather_fusion.1 = bf16[320,3584]{1,0:T(8,128)(2,1)} fusion(bf16[512,3584]{1,0:T(8,128)(2,1)} %all-gather.6.cloned.1.call-done, s32[1024]{0:T(1024)S(1)} %pad_clamp_fusion.1), kind=kCustom, calls=%fused_computation.1 | custom fusion | bytes 4588800 | tf_op jit(solution)/shard_map/gather | solution.py:56
  226.6 2.7 fusion.16
  229.3 2.1 multiply_convert_fusion.3
  231.4 1.1 fusion.2
  232.5 1.0 fusion
  233.5 1.0 fusion.1
  234.4 1.9 pad_maximum_fusion
  236.3 1.8 copy-done.3
  238.1 1.3 slice_bitcast_fusion
  239.4 1.0 copy-done.2
  240.4 0.9 fusion.15
  241.2 0.7 convert_element_type.130
  241.9 5.5 %all-to-all-start.1 = ((bf16[16,1,20]{2,1,0:T(2,128)(2,1)}), bf16[16,1,20]{2,1,0:T(2,128)(2,1)S(1)}, u32[]{:S(2)}, u32[]{:S(2)}) async-start(bf16[16,1,20]{2,1,0:T(2,128)(2,1)} %convert_element_type.130), calls=%async_computation.1 | async-start | bytes 16384 | tf_op jit(solution)/shard_map/all_to_all | solution.py:88
  247.5 2.2 convolution_convert_fusion
  249.7 2.2 reshape.325
  251.9 0.5 all-to-all-done.1
  252.4 6.6 %all-to-all-start = ((bf16[16,20,3584]{2,1,0:T(8,128)(2,1)}), bf16[16,20,3584]{2,1,0:T(8,128)(2,1)}, u32[]{:S(2)}, u32[]{:S(2)}) async-start(bf16[16,20,3584]{2,1,0:T(8,128)(2,1)} %reshape.325), calls=%async_computation | async-start | bytes 5505024 | tf_op jit(solution)/shard_map/all_to_all | solution.py:81
  259.0 2.5 collective-permute-start.1
  261.5 0.5 collective-permute-start.2
  262.2 0.6 reduce-window.16
  262.8 0.2 slice_reduce_fusion
  263.6 1.9 gather_fusion.4
  265.6 0.7 copy.91
  266.3 107.7 %all-to-all-done = bf16[16,20,3584]{2,1,0:T(8,128)(2,1)} async-done(((bf16[16,20,3584]{2,1,0:T(8,128)(2,1)}), bf16[16,20,3584]{2,1,0:T(8,128)(2,1)}, u32[]{:S(2)}, u32[]{:S(2)}) %all-to-all-start) | async-done | bytes 2293792 | tf_op jit(solution)/shard_map/all_to_all | solution.py:81
  374.0 2.7 reshape.326
  376.7 2.9 gather_fusion.3
  379.6 3.6 fusion.3
  383.3 3.2 fusion.5
  386.4 23.5 %collective-permute-done.1 = bf16[1,1792,3,128]{3,1,2,0:T(8,128)(2,1)} collective-permute-done((bf16[1,1792,3,128]{3,1,2,0:T(8,128)(2,1)}, bf16[1,1792,3,128]{3,1,2,0:T(8,128)(2,1)}, u32[]{:S(2)}, u32[]{:S(2)}) %collective-permute-start.1) | collective-permute-done | bytes 1376288 | tf_op jit(solution)/shard_map/ppermute | solution.py:8
  409.9 28.4 %collective-permute-done.2 = bf16[1,1792,3,128]{3,1,2,0:T(8,128)(2,1)} collective-permute-done((bf16[1,1792,3,128]{3,1,2,0:T(8,128)(2,1)}, bf16[1,1792,3,128]{3,1,2,0:T(8,128)(2,1)}, u32[]{:S(2)}, u32[]{:S(2)}) %collective-permute-start.2) | collective-permute-done | bytes 1376288 | tf_op jit(solution)/shard_map/ppermute | solution.py:8
  438.4 4.8 %fusion.8 = (bf16[1,1792,3,128]{3,1,2,0:T(8,128)(2,1)}, bf16[1,1792,3,128]{3,1,2,0:T(8,128)(2,1)}) fusion(bf16[1792,3,128]{2,0,1:T(8,128)(2,1)S(1)} %copy-done, bf16[1,1792,3,128]{3,1,2,0:T(8,128)(2,1)} %collective-permute-done.2, bf16[1,1792,3,128]{3,1,2,0:T(8,128)(2,1)} %param.14, pred[]{:T(512)S(6)} %eq.109, ...), kind=kLoop, calls=%fused_computation.22 | loop fusion | flops 10321920 | bytes 9633793 | tf_op jit(solution)/shard_map/convert_element_type | solution.py:110
  (61 shorter events, 2.3 us)
Async XLA Ops:
  7.2 149.7 %all-gather.10.cloned.1.call-start = ((), (), s32[]{:S(2)}) async-start(), calls=%async_computation.5 | async-start | bytes 3899392 | tf_op jit(solution)/shard_map/all_gather | solution.py:39
  7.9 158.3 %all-gather.8.cloned.1.call-start = ((), (), s32[]{:S(2)}) async-start(), calls=%async_computation.4 | async-start | bytes 4128768 | tf_op jit(solution)/shard_map/all_gather | solution.py:59
  7.9 67.5 %collective-permute-start = (bf16[1,1792,3,128]{3,1,2,0:T(8,128)(2,1)}, bf16[1,1792,3,128]{3,1,2,0:T(8,128)(2,1)S(1)}, u32[]{:S(2)}, u32[]{:S(2)}) collective-permute-start(bf16[1,1792,3,128]{3,1,2,0:T(8,128)(2,1)} %param.12), channel_id=1, source_target_pairs={{0,8},{1,9},{2,10},{3,11},{4,12},{5,13},{6,14},{7,15},{8,0},{9,1},... | collective-permute-start | bytes 4128776 | tf_op jit(solution)/shard_map/ppermute | solution.py:8
  12.5 65.0 %copy-start.5 = (f32[32,8]{0,1:T(8,128)S(1)}, f32[32,8]{0,1:T(8,128)}, u32[]{:S(2)}) copy-start(f32[32,8]{0,1:T(8,128)} %param.11) | copy-start | bytes 3076
  12.6 99.3 %copy-start.4 = (s32[32,8]{0,1:T(8,128)S(1)}, s32[32,8]{0,1:T(8,128)}, u32[]{:S(2)}) copy-start(s32[32,8]{0,1:T(8,128)} %param.10) | copy-start | bytes 3076
  76.7 139.9 %all-gather.6.cloned.1.call-start = ((), (), s32[]{:S(2)}) async-start(), calls=%async_computation.3 | async-start | bytes 3899392 | tf_op jit(solution)/shard_map/all_gather | solution.py:40
  77.5 305.8 %reduce-scatter.2.cloned.1.call-start = ((), (), s32[]{:S(2)}) async-start(), calls=%async_computation.6 | async-start | bytes 4128768 | tf_op jit(solution)/shard_map/reduce_scatter | solution.py:102
  229.3 2.1 copy-start.1
  236.3 1.8 copy-start.3
  238.1 2.3 copy-start.2
  241.9 10.5 %all-to-all-start.1 = ((bf16[16,1,20]{2,1,0:T(2,128)(2,1)}), bf16[16,1,20]{2,1,0:T(2,128)(2,1)S(1)}, u32[]{:S(2)}, u32[]{:S(2)}) async-start(bf16[16,1,20]{2,1,0:T(2,128)(2,1)} %convert_element_type.130), calls=%async_computation.1 | async-start | bytes 16384 | tf_op jit(solution)/shard_map/all_to_all | solution.py:88
  251.9 11.3 %copy-start.6 = (s32[8]{0:T(128)S(1)}, s32[8]{0:T(128)}, u32[]{:S(2)}) copy-start(s32[8]{0:T(128)} %param.15) | copy-start | bytes 100
  252.4 121.5 %all-to-all-start = ((bf16[16,20,3584]{2,1,0:T(8,128)(2,1)}), bf16[16,20,3584]{2,1,0:T(8,128)(2,1)}, u32[]{:S(2)}, u32[]{:S(2)}) async-start(bf16[16,20,3584]{2,1,0:T(8,128)(2,1)} %reshape.325), calls=%async_computation | async-start | bytes 5505024 | tf_op jit(solution)/shard_map/all_to_all | solution.py:81
  259.0 150.9 %collective-permute-start.1 = (bf16[1,1792,3,128]{3,1,2,0:T(8,128)(2,1)}, bf16[1,1792,3,128]{3,1,2,0:T(8,128)(2,1)}, u32[]{:S(2)}, u32[]{:S(2)}) collective-permute-start(bf16[1,1792,3,128]{3,1,2,0:T(8,128)(2,1)} %param.13), channel_id=1, source_target_pairs={{0,8},{1,9},{2,10},{3,11},{4,12},{5,13},{6,14},{7,15},{8,0},{9,1},... | collective-permute-start | bytes 4128776 | tf_op jit(solution)/shard_map/ppermute | solution.py:8
  261.5 176.9 %collective-permute-start.2 = (bf16[1,1792,3,128]{3,1,2,0:T(8,128)(2,1)}, bf16[1,1792,3,128]{3,1,2,0:T(8,128)(2,1)}, u32[]{:S(2)}, u32[]{:S(2)}) collective-permute-start(bf16[1,1792,3,128]{3,1,2,0:T(8,128)(2,1)} %param.14), channel_id=1, source_target_pairs={{0,8},{1,9},{2,10},{3,11},{4,12},{5,13},{6,14},{7,15},{8,0},{9,1},... | collective-permute-start | bytes 4128776 | tf_op jit(solution)/shard_map/ppermute | solution.py:8
  383.3 55.1 %copy-start = (bf16[1792,3,128]{2,0,1:T(8,128)(2,1)S(1)}, bf16[1792,3,128]{2,0,1:T(8,128)(2,1)}, u32[]{:S(2)}) copy-start(bf16[1792,3,128]{2,0,1:T(8,128)(2,1)} %reduce-scatter.2.cloned.1.call-done) | copy-start | bytes 4128772
Sparse Core Ops, SparseCore 0:
  10.8 117.5 all-gather.9
  130.5 11.1 all-gather.7
  144.5 72.1 all-gather.5
  236.4 10.1 reduce-scatter.1

commit v2 on v0

--- a/solution.py
+++ b/solution.py
@@ -11,6 +11,74 @@
 def silu_parts(pre_gate):
     sig = jax.nn.sigmoid(pre_gate)
     return (pre_gate * sig, sig * (1.0 + pre_gate * (1.0 - sig)))
+
+
+def gather_slots(tokens, out_grad, expert_ids, gate_probs, held, slot_cap):
+    axis_width = lax.axis_size("expert")
+    tok_rows, route_count = expert_ids.shape
+    model_width = tokens.shape[1]
+    entry_count = tok_rows * route_count
+    slot_count = axis_width * slot_cap
+    side = jnp.concatenate(
+        [
+            expert_ids.astype(jnp.bfloat16),
+            gate_probs.astype(jnp.bfloat16),
+            jnp.zeros((tok_rows, 128 - 2 * route_count), jnp.bfloat16),
+        ],
+        axis=1,
+    )
+    packed = jnp.concatenate([tokens, out_grad, side], axis=1)
+    all_packed = lax.all_gather(packed, "expert", axis=0, tiled=True)
+    side_at = 2 * model_width
+    all_ids = all_packed[:, side_at : side_at + route_count].astype(jnp.int32)
+    all_gate = all_packed[:, side_at + route_count : side_at + 2 * route_count].reshape(-1)
+    src_ids = all_ids.reshape(axis_width, entry_count)
+    hit = (src_ids == held).astype(jnp.int32)
+    pos = jnp.cumsum(hit, axis=1) - hit
+    ranks = jnp.arange(slot_cap, dtype=jnp.int32)
+    sel = (hit[:, None, :] == 1) & (pos[:, None, :] == ranks[None, :, None])
+    filled = jnp.any(sel, axis=2).reshape(slot_count)
+    entry_lanes = jnp.arange(entry_count, dtype=jnp.int32)
+    slot_entry = jnp.sum(jnp.where(sel, entry_lanes[None, None, :], 0), axis=2)
+    src_base = (jnp.arange(axis_width, dtype=jnp.int32) * entry_count)[:, None]
+    flat_entry = (slot_entry + src_base).reshape(slot_count)
+    token_of = flat_entry // route_count
+    picked = all_packed[token_of]
+    rows = picked[:, :model_width]
+    grads_in = picked[:, model_width:side_at]
+    gates = jnp.where(filled, all_gate[flat_entry].astype(jnp.float32), 0.0)
+    return rows, grads_in, gates
+
+
+def send_slots(tokens, out_grad, flat_gate, slot_of, slot_cap):
+    axis_width = lax.axis_size("expert")
+    model_width = tokens.shape[1]
+    entry_count = flat_gate.shape[0]
+    route_count = entry_count // tokens.shape[0]
+    slot_count = axis_width * slot_cap
+    slot_hit = jnp.arange(slot_count, dtype=jnp.int32)[:, None] == slot_of[None, :]
+    filled = jnp.any(slot_hit, axis=1)
+    entry_lanes = jnp.arange(entry_count, dtype=jnp.int32)
+    slot_entry = jnp.sum(jnp.where(slot_hit, entry_lanes[None, :], 0), axis=1)
+    token_of = slot_entry // route_count
+    zero_row = jnp.zeros((), jnp.bfloat16)
+    send_rows = jnp.where(filled[:, None], tokens[token_of], zero_row)
+    send_grads = jnp.where(filled[:, None], out_grad[token_of], zero_row)
+    send_gate = jnp.where(filled, flat_gate[slot_entry], 0.0).astype(jnp.bfloat16)
+    moved = [
+        lax.all_to_all(
+            part.reshape((axis_width, slot_cap) + part.shape[1:]),
+            "expert",
+            split_axis=0,
+            concat_axis=0,
+            tiled=True,
+        )
+        for part in (send_rows, send_grads, send_gate)
+    ]
+    rows = moved[0].reshape(slot_count, model_width)
+    grads_in = moved[1].reshape(slot_count, model_width)
+    gates = moved[2].reshape(slot_count).astype(jnp.float32)
+    return rows, grads_in, gates
 
 
 def on_device(
@@ -29,11 +97,13 @@
     pair_lanes = jnp.arange(half_axis, dtype=jnp.int32)
     my_move = jnp.sum(jnp.where(pair_lanes == my_index % half_axis, moving_pairs, 0))
     swapped = my_move == 1
+    held = jnp.where(swapped, (my_index + half_axis) % axis_width, my_index)
+    their_weights = from_partner(weights, "expert", swap_bit)
+    their_moments = from_partner((first_moment, second_moment), "expert", swap_bit)
+    weights = jnp.where(swapped, their_weights, weights)
+
+    flat_gate = gate_probs.reshape(-1)
     flat_ids = expert_ids.reshape(-1)
-    theirs = from_partner((weights, first_moment, second_moment), "expert", swap_bit)
-    weights = jnp.where(swapped, theirs[0], weights)
-    first_moment = jnp.where(swapped, theirs[1], first_moment)
-    second_moment = jnp.where(swapped, theirs[2], second_moment)
     lane_hit = (flat_ids % half_axis)[:, None] == pair_lanes[None, :]
     moves = jnp.sum(jnp.where(lane_hit, moving_pairs[None, :], 0), axis=1)
     target_dev = jnp.where(moves == 1, (flat_ids + half_axis) % axis_width, flat_ids)
@@ -42,42 +112,25 @@
     )
     id_rank = jnp.sum((jnp.cumsum(id_onehot, axis=0) - id_onehot) * id_onehot, axis=1)
     slot_of = target_dev * slot_cap + id_rank
-    slot_hit = jnp.arange(slot_count, dtype=jnp.int32)[:, None] == slot_of[None, :]
-    filled = jnp.any(slot_hit, axis=1)
-    entry_lanes = jnp.arange(entry_count, dtype=jnp.int32)
-    slot_entry = jnp.sum(jnp.where(slot_hit, entry_lanes[None, :], 0), axis=1)
-    token_of = slot_entry // route_count
-    flat_gate = gate_probs.reshape(-1)
-    zero_row = jnp.zeros((), jnp.bfloat16)
-    send_rows = jnp.where(filled[:, None], tokens[token_of], zero_row).reshape(
-        axis_width, slot_cap, model_width
-    )
-    send_grads = jnp.where(filled[:, None], out_grad[token_of], zero_row).reshape(
-        axis_width, slot_cap, model_width
-    )
-    send_gate = (
-        jnp.where(filled, flat_gate[slot_entry], 0.0)
-        .astype(jnp.bfloat16)
-        .reshape(axis_width, slot_cap)
-    )
-    recv_rows, recv_grads, recv_gate = (
-        lax.all_to_all(send_rows, "expert", split_axis=0, concat_axis=0, tiled=True),
-        lax.all_to_all(send_grads, "expert", split_axis=0, concat_axis=0, tiled=True),
-        lax.all_to_all(send_gate, "expert", split_axis=0, concat_axis=0, tiled=True),
-    )
+    packed_width = 2 * model_width + 128
+    if axis_width * tok_rows * packed_width * 2 <= 16 * 2**20:
+        rows, grads_in, gates = gather_slots(
+            tokens, out_grad, expert_ids, gate_probs, held, slot_cap
+        )
+    else:
+        rows, grads_in, gates = send_slots(
+            tokens, out_grad, flat_gate, slot_of, slot_cap
+        )
     whole = lax.all_gather(weights, "dp", axis=1, tiled=True)[0]
     w_gate = whole[:, 0, :]
     w_up = whole[:, 1, :]
     w_down = whole[:, 2, :]
     w_both = jnp.concatenate([w_gate, w_up], axis=1)
-    rows = recv_rows.reshape(slot_count, model_width)
     pre_gate = jnp.dot(rows, w_gate, preferred_element_type=jnp.float32)
     pre_up = jnp.dot(rows, w_up, preferred_element_type=jnp.float32)
     activated, act_slope = silu_parts(pre_gate)
     hidden = (activated * pre_up).astype(jnp.bfloat16)
     contract_hidden = (((1,), (1,)), ((), ()))
-    grads_in = recv_grads.reshape(slot_count, model_width)
-    gates = recv_gate.reshape(slot_count).astype(jnp.float32)
     projected = jnp.dot(grads_in, w_down, preferred_element_type=jnp.float32)
     gate_rows = jnp.sum(hidden.astype(jnp.float32) * projected, axis=1).astype(jnp.bfloat16)
     scaled_grad = (gates[:, None] * grads_in.astype(jnp.float32)).astype(jnp.bfloat16)
@@ -89,6 +142,9 @@
         both_delta, w_both, contract_hidden, preferred_element_type=jnp.float32
     )
     row_grad = row_grad.astype(jnp.bfloat16)
+    row_grad, their_moments = lax.optimization_barrier((row_grad, their_moments))
+    first_moment = jnp.where(swapped, their_moments[0], first_moment)
+    second_moment = jnp.where(swapped, their_moments[1], second_moment)
     back_rows, back_gate = (
         lax.all_to_all(
             row_grad.reshape(axis_width, slot_cap, model_width),
@@ -122,6 +178,7 @@
     new_second = (0.95 * second_moment.astype(jnp.float32) + 0.05 * grad * grad).astype(
         jnp.bfloat16
     )
+
     gathered = back_rows.reshape(slot_count, model_width)[slot_of].astype(jnp.float32)
     token_grad = (
         (gathered * flat_gate[:, None])

time: 458 us -> 369 us (0.81)
  waiting for transfers between devices: 308 us -> 257 us
  starting transfers between devices: 49.4 us -> 16.8 us
    all_gather x0 -> x1, waiting for transfers between devices: none -> 117 us  [gather_slots(): all_packed = lax.all_gather(packed, 'expert', axis=0, tiled=True)]
    all_to_all x3 -> x0, waiting for transfers between devices: 89.8 us -> none  [the longest x1 83.1 us: on_device(): lax.all_to_all(send_grads, 'expert', split_axis=0, concat_axis=0, tiled=T...]
    all_to_all x1, waiting for transfers between devices: 108 us -> 51.8 us  [on_device(): lax.all_to_all(row_grad.reshape(axis_width, slot_cap, model_width), 'expe...]
    all_to_all x3 -> x0, starting transfers between devices: 26.7 us -> none  [the longest x1 12.5 us: on_device(): lax.all_to_all(send_rows, 'expert', split_axis=0, concat_axis=0, tiled=True)]
    ppermute x3, waiting for transfers between devices: 104 us -> 88.1 us  [from_partner(): lax.ppermute(value, axis, [(i, i ^ 1 << bit) for i in range(lax.axis_size...]
    all_gather x1, waiting for transfers between devices: 6.2 us -> 0.01 us  [on_device(): whole = lax.all_gather(weights, 'dp', axis=1, tiled=True)[0]]
    all_to_all x1, starting transfers between devices: 10.5 us -> 4.41 us  [on_device(): lax.all_to_all(gate_rows.reshape(axis_width, slot_cap), 'expert', split_a...]
    reshape x3 -> x2, local copies, waits for them, and re-layouts: 5.5 us -> 0.26 us  [the longest x1 0.16 us: gather_slots(): all_packed[:, side_at + route_count:side_at + 2 * route_count].reshape(-1)]
  transfers between devices with their start and end apart: 10 -> 8, of which waited for: 8 -> 4; matrix products, arithmetic and copies ran while one was open for 12% -> 17% of each run, Pallas kernels for 0% -> 0%
where the time goes in v2:
time: 369 us; the launch traced here: 363 us
  waiting for transfers between devices  257 us (70%)
  local copies, waits for them, and re-layouts  38.5 us (10%)
  other arithmetic  22.4 us (6%)
  starting transfers between devices  16.8 us (5%)
  between operations  14.6 us (4%)
  matrix products  13.5 us (4%)
    all_gather x1, waiting for transfers between devices, gather_slots(): all_packed = lax.all_gather(packed, 'expert', axis=0, tiled=True)  117 us
    ppermute x3, waiting for transfers between devices, from_partner(): lax.ppermute(value, axis, [(i, i ^ 1 << bit) for i in range(lax.axis_size...  88.1 us
    all_to_all x1, waiting for transfers between devices, on_device(): lax.all_to_all(row_grad.reshape(axis_width, slot_cap, model_width), 'expe...  51.8 us
    gather x1, local copies, waits for them, and re-layouts, gather_slots(): picked = all_packed[token_of]  18.1 us
  transfers between devices with their start and end apart: 8, of which 4 were waited for; matrix products, arithmetic and copies ran while one was open for 17% of the time, Pallas kernels for 0%

profile of v2, /device:TPU:6, one launch (start us, length us, event | category | flops | bytes accessed | tf_op | source)
XLA Modules:
  0.0 362.9 jit_solution(379791067339326496)
XLA Ops:
  7.2 0.7 convert_element_type.103
  7.9 0.7 convert_element_type.104
  8.8 1.9 concatenate.9
  10.8 2.7 collective-permute-start
  13.4 1.3 fusion.45
  15.4 88.1 %collective-permute-done = bf16[1,1792,3,128]{3,1,2,0:T(8,128)(2,1)S(1)} collective-permute-done((bf16[1,1792,3,128]{3,1,2,0:T(8,128)(2,1)}, bf16[1,1792,3,128]{3,1,2,0:T(8,128)(2,1)S(1)}, u32[]{:S(2)}, u32[]{:S(2)}) %collective-permute-start) | collective-permute-done | bytes 1376288 | tf_op jit(solution)/shard_map/ppermute | solution.py:8
  103.5 2.7 broadcast_select_fusion
  106.4 2.9 collective-permute-start.2
  109.3 116.6 %all-gather.3.cloned.1.call-done = bf16[512,7296]{1,0:T(8,128)(2,1)} async-done(((bf16[32,7296]{1,0:T(8,128)(2,1)}), bf16[512,7296]{1,0:T(8,128)(2,1)}) %all-gather.3.cloned.1.call-update) | async-done | bytes 7471120 | tf_op jit(solution)/shard_map/all_gather | solution.py:31
  225.9 0.9 fusion.32
  226.9 0.2 reshape.334
  227.0 0.2 reshape.335
  227.2 1.0 slice.54
  228.2 0.2 reshape.326
  228.4 0.6 reduce-window.14
  229.0 0.2 slice_reduce_fusion.1
  229.3 0.4 select_reduce_fusion
  229.8 0.4 fusion.31
  230.3 0.1 reshape.325
  230.6 2.5 gather_fusion
  233.1 18.1 %gather_fusion.1 = bf16[320,7296]{1,0:T(8,128)(2,1)} fusion(bf16[512,7296]{1,0:T(8,128)(2,1)} %all-gather.3.cloned.1.call-done, s32[1024]{0:T(1024)S(1)} %pad_clamp_fusion.1), kind=kCustom, calls=%fused_computation.1 | custom fusion | bytes 9340160 | tf_op jit(solution)/shard_map/gather | solution.py:46
  251.2 2.8 fusion.19
  254.0 0.5 copy-done.1
  254.5 2.1 fusion.29
  256.6 0.8 multiply_convert_fusion.3
  257.4 1.1 fusion.2
  258.5 1.0 fusion
  259.5 1.0 fusion.1
  260.5 1.9 pad_maximum_fusion
  262.3 1.3 slice_bitcast_fusion
  263.7 2.5 fusion.26
  266.2 0.7 convert_element_type.133
  266.9 4.4 %all-to-all-start.1 = ((bf16[16,1,20]{2,1,0:T(2,128)(2,1)}), bf16[16,1,20]{2,1,0:T(2,128)(2,1)S(1)}, u32[]{:S(2)}, u32[]{:S(2)}) async-start(bf16[16,1,20]{2,1,0:T(2,128)(2,1)} %convert_element_type.133), calls=%async_computation.1 | async-start | bytes 16384 | tf_op jit(solution)/shard_map/all_to_all | solution.py:156
  271.3 2.3 convolution_convert_fusion
  273.6 2.2 reshape.327
  275.8 0.5 all-to-all-done.1
  276.3 6.6 %all-to-all-start = ((bf16[16,20,3584]{2,1,0:T(8,128)(2,1)}), bf16[16,20,3584]{2,1,0:T(8,128)(2,1)}, u32[]{:S(2)}, u32[]{:S(2)}) async-start(bf16[16,20,3584]{2,1,0:T(8,128)(2,1)} %reshape.327), calls=%async_computation | async-start | bytes 5505024 | tf_op jit(solution)/shard_map/all_to_all | solution.py:149
  283.4 0.6 reduce-window.16
  284.0 0.2 slice_reduce_fusion
  284.5 0.1 reshape.332
  284.6 1.9 gather_fusion.3
  286.6 0.7 copy.75
  287.3 51.8 %all-to-all-done = bf16[16,20,3584]{2,1,0:T(8,128)(2,1)} async-done(((bf16[16,20,3584]{2,1,0:T(8,128)(2,1)}), bf16[16,20,3584]{2,1,0:T(8,128)(2,1)}, u32[]{:S(2)}, u32[]{:S(2)}) %all-to-all-start) | async-done | bytes 2293792 | tf_op jit(solution)/shard_map/all_to_all | solution.py:149
  339.1 2.7 reshape.328
  341.8 3.0 gather_fusion.2
  344.8 3.6 %fusion.3 = bf16[32,3584]{1,0:T(8,128)(2,1)} fusion(bf16[256,3584]{1,0:T(8,128)(2,1)} %gather_fusion.2, f32[32,8]{1,0:T(8,128)S(1)} %copy.73), kind=kLoop, calls=%fused_computation.16 | loop fusion | flops 2637824 | bytes 2065408 | tf_op jit(solution)/shard_map/reduce_sum | solution.py:186
  348.4 3.2 fusion.5
  351.6 4.8 %fusion.8 = (bf16[1,1792,3,128]{3,1,2,0:T(8,128)(2,1)}, bf16[1,1792,3,128]{3,1,2,0:T(8,128)(2,1)}) fusion(bf16[1792,3,128]{2,0,1:T(8,128)(2,1)S(1)} %copy-done, bf16[1,1792,3,128]{3,1,2,0:T(8,128)(2,1)} %collective-permute-done.2, bf16[1,1792,3,128]{3,1,2,0:T(8,128)(2,1)} %param.14, pred[]{:T(512)S(6)} %eq.109, ...), kind=kLoop, calls=%fused_computation.21 | loop fusion | flops 10321920 | bytes 9633793 | tf_op jit(solution)/shard_map/convert_element_type | solution.py:178
  (55 shorter events, 1.8 us)
Async XLA Ops:
  7.2 218.8 %all-gather.3.cloned.1.call-start = ((), (), s32[]{:S(2)}) async-start(), calls=%async_computation.3 | async-start | bytes 7938048 | tf_op jit(solution)/shard_map/all_gather | solution.py:31
  10.7 240.5 %all-gather.5.cloned.1.call-start = ((), (), s32[]{:S(2)}) async-start(), calls=%async_computation.4 | async-start | bytes 4128768 | tf_op jit(solution)/shard_map/all_gather | solution.py:124
  10.8 92.7 %collective-permute-start = (bf16[1,1792,3,128]{3,1,2,0:T(8,128)(2,1)}, bf16[1,1792,3,128]{3,1,2,0:T(8,128)(2,1)S(1)}, u32[]{:S(2)}, u32[]{:S(2)}) collective-permute-start(bf16[1,1792,3,128]{3,1,2,0:T(8,128)(2,1)} %param.12), channel_id=1, source_target_pairs={{0,8},{1,9},{2,10},{3,11},{4,12},{5,13},{6,14},{7,15},{8,0},{9,1},... | collective-permute-start | bytes 4128776 | tf_op jit(solution)/shard_map/ppermute | solution.py:8
  106.3 242.2 %reduce-scatter.2.cloned.1.call-start = ((), (), s32[]{:S(2)}) async-start(), calls=%async_computation.5 | async-start | bytes 4128768 | tf_op jit(solution)/shard_map/reduce_scatter | solution.py:170
  106.3 167.3 %collective-permute-start.1 = (bf16[1,1792,3,128]{3,1,2,0:T(8,128)(2,1)}, bf16[1,1792,3,128]{3,1,2,0:T(8,128)(2,1)}, u32[]{:S(2)}, u32[]{:S(2)}) collective-permute-start(bf16[1,1792,3,128]{3,1,2,0:T(8,128)(2,1)} %param.13), channel_id=1, source_target_pairs={{0,8},{1,9},{2,10},{3,11},{4,12},{5,13},{6,14},{7,15},{8,0},{9,1},... | collective-permute-start | bytes 4128776 | tf_op jit(solution)/shard_map/ppermute | solution.py:8
  106.4 167.2 %collective-permute-start.2 = (bf16[1,1792,3,128]{3,1,2,0:T(8,128)(2,1)}, bf16[1,1792,3,128]{3,1,2,0:T(8,128)(2,1)}, u32[]{:S(2)}, u32[]{:S(2)}) collective-permute-start(bf16[1,1792,3,128]{3,1,2,0:T(8,128)(2,1)} %param.14), channel_id=1, source_target_pairs={{0,8},{1,9},{2,10},{3,11},{4,12},{5,13},{6,14},{7,15},{8,0},{9,1},... | collective-permute-start | bytes 4128776 | tf_op jit(solution)/shard_map/ppermute | solution.py:8
  251.2 3.3 copy-start.1
  254.5 2.2 copy-start.2
  266.9 9.4 %all-to-all-start.1 = ((bf16[16,1,20]{2,1,0:T(2,128)(2,1)}), bf16[16,1,20]{2,1,0:T(2,128)(2,1)S(1)}, u32[]{:S(2)}, u32[]{:S(2)}) async-start(bf16[16,1,20]{2,1,0:T(2,128)(2,1)} %convert_element_type.133), calls=%async_computation.1 | async-start | bytes 16384 | tf_op jit(solution)/shard_map/all_to_all | solution.py:156
  275.8 7.2 %copy-start.3 = (s32[32,8]{0,1:T(8,128)S(1)}, s32[32,8]{0,1:T(8,128)}, u32[]{:S(2)}) copy-start(s32[32,8]{0,1:T(8,128)} %param.10) | copy-start | bytes 3076
  275.8 7.5 %copy-start.4 = (f32[32,8]{0,1:T(8,128)S(1)}, f32[32,8]{0,1:T(8,128)}, u32[]{:S(2)}) copy-start(f32[32,8]{0,1:T(8,128)} %param.11) | copy-start | bytes 3076
  275.8 8.4 %copy-start.5 = (s32[8]{0:T(128)S(1)}, s32[8]{0:T(128)}, u32[]{:S(2)}) copy-start(s32[8]{0:T(128)} %param.15) | copy-start | bytes 100
  276.3 62.8 %all-to-all-start = ((bf16[16,20,3584]{2,1,0:T(8,128)(2,1)}), bf16[16,20,3584]{2,1,0:T(8,128)(2,1)}, u32[]{:S(2)}, u32[]{:S(2)}) async-start(bf16[16,20,3584]{2,1,0:T(8,128)(2,1)} %reshape.327), calls=%async_computation | async-start | bytes 5505024 | tf_op jit(solution)/shard_map/all_to_all | solution.py:149
  348.4 3.2 copy-start
Sparse Core Ops, SparseCore 0:
  11.4 214.4 all-gather.2
  228.0 10.4 all-gather.4
  262.5 8.8 reduce-scatter.1

commit v3 on v2

--- a/solution.py
+++ b/solution.py
@@ -11,43 +11,6 @@
 def silu_parts(pre_gate):
     sig = jax.nn.sigmoid(pre_gate)
     return (pre_gate * sig, sig * (1.0 + pre_gate * (1.0 - sig)))
-
-
-def gather_slots(tokens, out_grad, expert_ids, gate_probs, held, slot_cap):
-    axis_width = lax.axis_size("expert")
-    tok_rows, route_count = expert_ids.shape
-    model_width = tokens.shape[1]
-    entry_count = tok_rows * route_count
-    slot_count = axis_width * slot_cap
-    side = jnp.concatenate(
-        [
-            expert_ids.astype(jnp.bfloat16),
-            gate_probs.astype(jnp.bfloat16),
-            jnp.zeros((tok_rows, 128 - 2 * route_count), jnp.bfloat16),
-        ],
-        axis=1,
-    )
-    packed = jnp.concatenate([tokens, out_grad, side], axis=1)
-    all_packed = lax.all_gather(packed, "expert", axis=0, tiled=True)
-    side_at = 2 * model_width
-    all_ids = all_packed[:, side_at : side_at + route_count].astype(jnp.int32)
-    all_gate = all_packed[:, side_at + route_count : side_at + 2 * route_count].reshape(-1)
-    src_ids = all_ids.reshape(axis_width, entry_count)
-    hit = (src_ids == held).astype(jnp.int32)
-    pos = jnp.cumsum(hit, axis=1) - hit
-    ranks = jnp.arange(slot_cap, dtype=jnp.int32)
-    sel = (hit[:, None, :] == 1) & (pos[:, None, :] == ranks[None, :, None])
-    filled = jnp.any(sel, axis=2).reshape(slot_count)
-    entry_lanes = jnp.arange(entry_count, dtype=jnp.int32)
-    slot_entry = jnp.sum(jnp.where(sel, entry_lanes[None, None, :], 0), axis=2)
-    src_base = (jnp.arange(axis_width, dtype=jnp.int32) * entry_count)[:, None]
-    flat_entry = (slot_entry + src_base).reshape(slot_count)
-    token_of = flat_entry // route_count
-    picked = all_packed[token_of]
-    rows = picked[:, :model_width]
-    grads_in = picked[:, model_width:side_at]
-    gates = jnp.where(filled, all_gate[flat_entry].astype(jnp.float32), 0.0)
-    return rows, grads_in, gates
 
 
 def send_slots(tokens, out_grad, flat_gate, slot_of, slot_cap):
@@ -81,6 +44,17 @@
     return rows, grads_in, gates
 
 
+def xor_permute(value, mask):
+    return lax.ppermute(value, "expert", [(i, i ^ mask) for i in range(lax.axis_size("expert"))])
+
+
+def entry_ranks(flat_ids, axis_width):
+    id_onehot = (flat_ids[:, None] == jnp.arange(axis_width, dtype=jnp.int32)[None, :]).astype(
+        jnp.int32
+    )
+    return jnp.sum((jnp.cumsum(id_onehot, axis=0) - id_onehot) * id_onehot, axis=1)
+
+
 def on_device(
     tokens, out_grad, expert_ids, gate_probs, weights, first_moment, second_moment, moving_pairs
 ):
@@ -104,23 +78,53 @@
 
     flat_gate = gate_probs.reshape(-1)
     flat_ids = expert_ids.reshape(-1)
-    lane_hit = (flat_ids % half_axis)[:, None] == pair_lanes[None, :]
-    moves = jnp.sum(jnp.where(lane_hit, moving_pairs[None, :], 0), axis=1)
-    target_dev = jnp.where(moves == 1, (flat_ids + half_axis) % axis_width, flat_ids)
-    id_onehot = (flat_ids[:, None] == jnp.arange(axis_width, dtype=jnp.int32)[None, :]).astype(
-        jnp.int32
-    )
-    id_rank = jnp.sum((jnp.cumsum(id_onehot, axis=0) - id_onehot) * id_onehot, axis=1)
-    slot_of = target_dev * slot_cap + id_rank
-    packed_width = 2 * model_width + 128
-    if axis_width * tok_rows * packed_width * 2 <= 16 * 2**20:
-        rows, grads_in, gates = gather_slots(
-            tokens, out_grad, expert_ids, gate_probs, held, slot_cap
-        )
+
+    def holder_of(ids):
+        lane_hit = (ids % half_axis)[:, None] == pair_lanes[None, :]
+        moves = jnp.sum(jnp.where(lane_hit, moving_pairs[None, :], 0), axis=1)
+        return jnp.where(moves == 1, (ids + half_axis) % axis_width, ids)
+
+    two_stage = half_axis <= 8
+    if two_stage:
+        p_tokens, p_grads, p_ids, p_gate = from_partner(
+            (tokens, out_grad, expert_ids, gate_probs), "expert", swap_bit
+        )
+        toks2 = jnp.concatenate([tokens, p_tokens], axis=0)
+        grads2 = jnp.concatenate([out_grad, p_grads], axis=0)
+        ids2 = jnp.concatenate([flat_ids, p_ids.reshape(-1)])
+        gate2 = jnp.concatenate([flat_gate, p_gate.reshape(-1)])
+        holder2 = holder_of(ids2)
+        rank2 = jnp.concatenate(
+            [entry_ranks(flat_ids, axis_width), entry_ranks(p_ids.reshape(-1), axis_width)]
+        )
+        src2 = jnp.arange(2 * entry_count, dtype=jnp.int32) // entry_count
+        in_half = holder2 // half_axis == my_index // half_axis
+        lane2 = (holder2 ^ my_index) % half_axis
+        chunk = 2 * slot_cap
+        slot2 = lane2 * chunk + src2 * slot_cap + rank2
+        slot_hit = (
+            jnp.arange(half_axis * chunk, dtype=jnp.int32)[:, None] == slot2[None, :]
+        ) & in_half[None, :]
+        tok_hit = jnp.any(slot_hit.reshape(half_axis * chunk, 2 * tok_rows, route_count), axis=2)
+        tok_pick = tok_hit.astype(jnp.bfloat16)
+        send_rows = jnp.dot(tok_pick, toks2, preferred_element_type=jnp.float32).astype(
+            jnp.bfloat16
+        )
+        send_grads = jnp.dot(tok_pick, grads2, preferred_element_type=jnp.float32).astype(
+            jnp.bfloat16
+        )
+        wire2 = gate2.astype(jnp.bfloat16).astype(jnp.float32)
+        send_gate = jnp.sum(jnp.where(slot_hit, wire2[None, :], 0.0), axis=1)
+
+        def spread(value):
+            parts = value.reshape((half_axis, chunk) + value.shape[1:])
+            moved = [parts[0]] + [xor_permute(parts[m], m) for m in range(1, half_axis)]
+            return jnp.stack(moved).reshape(value.shape)
+
+        rows, grads_in, gates = spread(send_rows), spread(send_grads), spread(send_gate)
     else:
-        rows, grads_in, gates = send_slots(
-            tokens, out_grad, flat_gate, slot_of, slot_cap
-        )
+        slot_of = holder_of(flat_ids) * slot_cap + entry_ranks(flat_ids, axis_width)
+        rows, grads_in, gates = send_slots(tokens, out_grad, flat_gate, slot_of, slot_cap)
     whole = lax.all_gather(weights, "dp", axis=1, tiled=True)[0]
     w_gate = whole[:, 0, :]
     w_up = whole[:, 1, :]
@@ -145,22 +149,6 @@
     row_grad, their_moments = lax.optimization_barrier((row_grad, their_moments))
     first_moment = jnp.where(swapped, their_moments[0], first_moment)
     second_moment = jnp.where(swapped, their_moments[1], second_moment)
-    back_rows, back_gate = (
-        lax.all_to_all(
-            row_grad.reshape(axis_width, slot_cap, model_width),
-            "expert",
-            split_axis=0,
-            concat_axis=0,
-            tiled=True,
-        ),
-        lax.all_to_all(
-            gate_rows.reshape(axis_width, slot_cap),
-            "expert",
-            split_axis=0,
-            concat_axis=0,
-            tiled=True,
-        ),
-    )
     contract_rows = (((0,), (0,)), ((), ()))
     grad_gate = lax.dot_general(rows, gate_delta, contract_rows, preferred_element_type=jnp.float32)
     grad_up = lax.dot_general(rows, up_delta, contract_rows, preferred_element_type=jnp.float32)
@@ -179,14 +167,46 @@
         jnp.bfloat16
     )
 
-    gathered = back_rows.reshape(slot_count, model_width)[slot_of].astype(jnp.float32)
-    token_grad = (
-        (gathered * flat_gate[:, None])
-        .reshape(tok_rows, route_count, model_width)
-        .sum(axis=1)
-        .astype(jnp.bfloat16)
-    )
-    prob_grad = back_gate.reshape(slot_count)[slot_of].reshape(tok_rows, route_count)
+    if two_stage:
+        back_rows = spread(row_grad)
+        back_gate = spread(gate_rows).astype(jnp.float32)
+        weight_of = jnp.where(slot_hit, gate2[None, :], 0.0)
+        weight_of = jnp.sum(weight_of.reshape(half_axis * chunk, 2 * tok_rows, route_count), axis=2)
+        partial = lax.dot_general(
+            weight_of,
+            back_rows.astype(jnp.float32),
+            (((0,), (0,)), ((), ())),
+            precision=lax.Precision.HIGHEST,
+            preferred_element_type=jnp.float32,
+        )
+        prob2 = jnp.sum(jnp.where(slot_hit, back_gate[:, None], 0.0), axis=0)
+        p_partial, p_prob = from_partner(
+            (partial[tok_rows:], prob2[entry_count:].astype(jnp.bfloat16)), "expert", swap_bit
+        )
+        token_grad = (partial[:tok_rows] + p_partial).astype(jnp.bfloat16)
+        prob_grad = jnp.where(
+            in_half[:entry_count], prob2[:entry_count], p_prob.astype(jnp.float32)
+        )
+        prob_grad = prob_grad.astype(jnp.bfloat16).reshape(tok_rows, route_count)
+    else:
+        back_rows, back_gate = [
+            lax.all_to_all(
+                part.reshape((axis_width, slot_cap) + part.shape[1:]),
+                "expert",
+                split_axis=0,
+                concat_axis=0,
+                tiled=True,
+            )
+            for part in (row_grad, gate_rows)
+        ]
+        gathered = back_rows.reshape(slot_count, model_width)[slot_of].astype(jnp.float32)
+        token_grad = (
+            (gathered * flat_gate[:, None])
+            .reshape(tok_rows, route_count, model_width)
+            .sum(axis=1)
+            .astype(jnp.bfloat16)
+        )
+        prob_grad = back_gate.reshape(slot_count)[slot_of].reshape(tok_rows, route_count)
     return (token_grad, prob_grad, weights, grad, new_first, new_second)
 
 

time: 369 us -> 374 us (1.014)
  starting transfers between devices: 16.8 us -> 52.9 us
  local copies, waits for them, and re-layouts: 38.5 us -> 12.3 us
    all_gather x1 -> x0, waiting for transfers between devices: 117 us -> none  [gather_slots(): all_packed = lax.all_gather(packed, 'expert', axis=0, tiled=True)]
    ppermute x0 -> x35, waiting for transfers between devices: none -> 93.3 us  [xor_permute(): lax.ppermute(value, 'expert', [(i, i ^ mask) for i in range(lax.axis_size...]
    ppermute x3 -> x9, waiting for transfers between devices: 88.1 us -> 163 us  [from_partner(): lax.ppermute(value, axis, [(i, i ^ 1 << bit) for i in range(lax.axis_size...]
    all_to_all x2 -> x0, waiting for transfers between devices: 52.4 us -> none  [the longest x1 51.8 us: on_device(): lax.all_to_all(row_grad.reshape(axis_width, slot_cap, model_width), 'expe...]
    ppermute x0 -> x35, starting transfers between devices: none -> 39.8 us  [xor_permute(): lax.ppermute(value, 'expert', [(i, i ^ mask) for i in range(lax.axis_size...]
    gather x4 -> x0, local copies, waits for them, and re-layouts: 25.4 us -> none  [the longest x1 18.1 us: gather_slots(): picked = all_packed[token_of]]
    all_to_all x2 -> x0, starting transfers between devices: 11 us -> none  [the longest x1 6.63 us: on_device(): lax.all_to_all(row_grad.reshape(axis_width, slot_cap, model_width), 'expe...]
    ppermute x3 -> x9, starting transfers between devices: 5.64 us -> 12.8 us  [from_partner(): lax.ppermute(value, axis, [(i, i ^ 1 << bit) for i in range(lax.axis_size...]
  transfers between devices with their start and end apart: 8 -> 46, of which waited for: 4 -> 23; matrix products, arithmetic and copies ran while one was open for 17% -> 10% of each run, Pallas kernels for 0% -> 0%
where the time goes in v3:
time: 374 us; the launch traced here: 370 us
  waiting for transfers between devices  256 us (68%)
  starting transfers between devices  52.9 us (14%)
  other arithmetic  19.9 us (5%)
  between operations  15.3 us (4%)
  matrix products  13.6 us (4%)
  local copies, waits for them, and re-layouts  12.3 us (3%)
    ppermute x9, waiting for transfers between devices, from_partner(): lax.ppermute(value, axis, [(i, i ^ 1 << bit) for i in range(lax.axis_size...  163 us
    ppermute x35, waiting for transfers between devices, xor_permute(): lax.ppermute(value, 'expert', [(i, i ^ mask) for i in range(lax.axis_size...  93.3 us
    ppermute x35, starting transfers between devices, xor_permute(): lax.ppermute(value, 'expert', [(i, i ^ mask) for i in range(lax.axis_size...  39.8 us
    ppermute x9, starting transfers between devices, from_partner(): lax.ppermute(value, axis, [(i, i ^ 1 << bit) for i in range(lax.axis_size...  12.8 us
  transfers between devices with their start and end apart: 46, of which 23 were waited for; matrix products, arithmetic and copies ran while one was open for 10% of the time, Pallas kernels for 0%

profile of v3, /device:TPU:6, one launch (start us, length us, event | category | flops | bytes accessed | tf_op | source)
XLA Modules:
  0.0 370.0 jit_solution(7142508768346597887)
XLA Ops:
  7.2 2.7 collective-permute-start
  10.2 2.6 collective-permute-start.18
  13.1 2.6 collective-permute-start.1
  23.4 99.2 %collective-permute-done.1 = f32[32,8]{0,1:T(8,128)S(1)} collective-permute-done((f32[32,8]{0,1:T(8,128)}, f32[32,8]{0,1:T(8,128)S(1)}, u32[]{:S(2)}, u32[]{:S(2)}) %collective-permute-start.1) | collective-permute-done | bytes 1056 | tf_op jit(solution)/shard_map/ppermute | solution.py:8
  124.5 1.7 convolution_convert_fusion.2
  129.6 2.3 collective-permute-start.12
  131.9 3.6 collective-permute-done.10
  135.6 6.3 %collective-permute-done.11 = bf16[40,3584]{1,0:T(8,128)(2,1)S(1)} collective-permute-done((bf16[40,3584]{1,0:T(8,128)(2,1)S(1)}, bf16[40,3584]{1,0:T(8,128)(2,1)S(1)}, u32[]{:S(2)}, u32[]{:S(2)}) %collective-permute-start.11) | collective-permute-done | bytes 286752 | tf_op jit(solution)/shard_map/ppermute | solution.py:48
  142.0 2.5 collective-permute-start.15
  144.5 12.7 %collective-permute-done.13 = bf16[40,3584]{1,0:T(8,128)(2,1)S(1)} collective-permute-done((bf16[40,3584]{1,0:T(8,128)(2,1)S(1)}, bf16[40,3584]{1,0:T(8,128)(2,1)S(1)}, u32[]{:S(2)}, u32[]{:S(2)}) %collective-permute-start.13) | collective-permute-done | bytes 286752 | tf_op jit(solution)/shard_map/ppermute | solution.py:48
  157.2 6.1 %collective-permute-done.14 = bf16[40,3584]{1,0:T(8,128)(2,1)S(1)} collective-permute-done((bf16[40,3584]{1,0:T(8,128)(2,1)S(1)}, bf16[40,3584]{1,0:T(8,128)(2,1)S(1)}, u32[]{:S(2)}, u32[]{:S(2)}) %collective-permute-start.14) | collective-permute-done | bytes 286752 | tf_op jit(solution)/shard_map/ppermute | solution.py:48
  163.3 1.5 collective-permute-start.19
  164.8 4.6 %collective-permute-done.15 = bf16[40,3584]{1,0:T(8,128)(2,1)S(1)} collective-permute-done((bf16[40,3584]{1,0:T(8,128)(2,1)S(1)}, bf16[40,3584]{1,0:T(8,128)(2,1)S(1)}, u32[]{:S(2)}, u32[]{:S(2)}) %collective-permute-start.15) | collective-permute-done | bytes 286752 | tf_op jit(solution)/shard_map/ppermute | solution.py:48
  169.4 1.5 collective-permute-start.20
  171.0 4.7 %collective-permute-done.16 = bf16[40,3584]{1,0:T(8,128)(2,1)S(1)} collective-permute-done((bf16[40,3584]{1,0:T(8,128)(2,1)S(1)}, bf16[40,3584]{1,0:T(8,128)(2,1)S(1)}, u32[]{:S(2)}, u32[]{:S(2)}) %collective-permute-start.16) | collective-permute-done | bytes 286752 | tf_op jit(solution)/shard_map/ppermute | solution.py:48
  175.6 2.4 collective-permute-start.21
  178.2 9.6 %collective-permute-done.20 = bf16[40,3584]{1,0:T(8,128)(2,1)S(1)} collective-permute-done((bf16[40,3584]{1,0:T(8,128)(2,1)S(1)}, bf16[40,3584]{1,0:T(8,128)(2,1)S(1)}, u32[]{:S(2)}, u32[]{:S(2)}) %collective-permute-start.20) | collective-permute-done | bytes 286752 | tf_op jit(solution)/shard_map/ppermute | solution.py:48
  187.9 4.0 %collective-permute-start.24 = (bf16[40,3584]{1,0:T(8,128)(2,1)}, bf16[40,3584]{1,0:T(8,128)(2,1)S(1)}, u32[]{:S(2)}, u32[]{:S(2)}) collective-permute-start(bf16[40,3584]{1,0:T(8,128)(2,1)} %get-tuple-element.38), channel_id=1, source_target_pairs={{0,6},{1,7},{2,4},{3,5},{4,2},{5,3},{6,0},{7,1},{8,14},{9,15},{10,... | collective-permute-start | bytes 860168 | tf_op jit(solution)/shard_map/ppermute | solution.py:48
  193.5 5.1 %collective-permute-done.23 = bf16[40,3584]{1,0:T(8,128)(2,1)S(1)} collective-permute-done((bf16[40,3584]{1,0:T(8,128)(2,1)}, bf16[40,3584]{1,0:T(8,128)(2,1)S(1)}, u32[]{:S(2)}, u32[]{:S(2)}) %collective-permute-start.23) | collective-permute-done | bytes 286752 | tf_op jit(solution)/shard_map/ppermute | solution.py:48
  198.6 7.1 %collective-permute-done.24 = bf16[40,3584]{1,0:T(8,128)(2,1)S(1)} collective-permute-done((bf16[40,3584]{1,0:T(8,128)(2,1)}, bf16[40,3584]{1,0:T(8,128)(2,1)S(1)}, u32[]{:S(2)}, u32[]{:S(2)}) %collective-permute-start.24) | collective-permute-done | bytes 286752 | tf_op jit(solution)/shard_map/ppermute | solution.py:48
  205.8 5.3 %collective-permute-done.25 = bf16[40,3584]{1,0:T(8,128)(2,1)} collective-permute-done((bf16[40,3584]{1,0:T(8,128)(2,1)}, bf16[40,3584]{1,0:T(8,128)(2,1)}, u32[]{:S(2)}, u32[]{:S(2)}) %collective-permute-start.25) | collective-permute-done | bytes 286752 | tf_op jit(solution)/shard_map/ppermute | solution.py:48
  212.1 2.6 slice_bitcast_fusion
  215.5 1.4 multiply_convert_fusion.3
  218.1 1.5 collective-permute-start.36
  220.1 1.5 collective-permute-start.38
  221.9 2.6 collective-permute-start.40
  224.5 2.9 collective-permute-start.42
  227.5 1.5 collective-permute-done.41
  230.4 2.9 collective-permute-start.7
  234.8 1.4 collective-permute-start.3
  237.0 1.6 collective-permute-done.8
  238.8 1.9 collective-permute-start.6
  243.2 3.6 multiply_convert_fusion.1
  246.9 2.8 multiply_convert_fusion.5
  252.5 45.3 %collective-permute-done.27 = bf16[1,1792,3,128]{3,1,2,0:T(8,128)(2,1)} collective-permute-done((bf16[1,1792,3,128]{3,1,2,0:T(8,128)(2,1)}, bf16[1,1792,3,128]{3,1,2,0:T(8,128)(2,1)}, u32[]{:S(2)}, u32[]{:S(2)}) %collective-permute-start.27) | collective-permute-done | bytes 1376288 | tf_op jit(solution)/shard_map/ppermute | solution.py:8
  301.6 1.8 pad_maximum_fusion
  304.3 1.5 collective-permute-start.30
  305.8 2.7 collective-permute-start.32
  308.4 1.9 collective-permute-done.28
  312.1 7.8 %collective-permute-done.29 = bf16[40,3584]{1,0:T(8,128)(2,1)S(1)} collective-permute-done((bf16[40,3584]{1,0:T(8,128)(2,1)}, bf16[40,3584]{1,0:T(8,128)(2,1)S(1)}, u32[]{:S(2)}, u32[]{:S(2)}) %collective-permute-start.29) | collective-permute-done | bytes 286752 | tf_op jit(solution)/shard_map/ppermute | solution.py:48
  320.0 2.6 collective-permute-done.32
  322.6 5.8 %collective-permute-done.33 = bf16[40,3584]{1,0:T(8,128)(2,1)S(1)} collective-permute-done((bf16[40,3584]{1,0:T(8,128)(2,1)}, bf16[40,3584]{1,0:T(8,128)(2,1)S(1)}, u32[]{:S(2)}, u32[]{:S(2)}) %collective-permute-start.33) | collective-permute-done | bytes 286752 | tf_op jit(solution)/shard_map/ppermute | solution.py:48
  328.4 4.4 %collective-permute-done.34 = bf16[40,3584]{1,0:T(8,128)(2,1)S(1)} collective-permute-done((bf16[40,3584]{1,0:T(8,128)(2,1)}, bf16[40,3584]{1,0:T(8,128)(2,1)S(1)}, u32[]{:S(2)}, u32[]{:S(2)}) %collective-permute-start.34) | collective-permute-done | bytes 286752 | tf_op jit(solution)/shard_map/ppermute | solution.py:48
  332.8 1.4 fusion.79
  334.6 2.7 collective-permute-start.43
  337.3 18.1 %collective-permute-done.43 = bf16[256]{0:T(256)(128)(2,1)S(1)} collective-permute-done((bf16[256]{0:T(256)(128)(2,1)S(1)}, bf16[256]{0:T(256)(128)(2,1)S(1)}, u32[]{:S(2)}, u32[]{:S(2)}) %collective-permute-start.43) | collective-permute-done | bytes 544 | tf_op jit(solution)/shard_map/ppermute | solution.py:8
  356.9 3.2 fusion.4
  360.1 3.1 fusion.7
  (174 shorter events, 36.1 us)
Async XLA Ops:
  7.2 204.9 %all-gather.2.cloned.1.call-start = ((), (), s32[]{:S(2)}) async-start(), calls=%async_computation.1 | async-start | bytes 4128768 | tf_op jit(solution)/shard_map/all_gather | solution.py:128
  7.2 13.3 %collective-permute-start = (s32[32,8]{0,1:T(8,128)}, s32[32,8]{0,1:T(8,128)S(1)}, u32[]{:S(2)}, u32[]{:S(2)}) collective-permute-start(s32[32,8]{0,1:T(8,128)} %param.10), channel_id=1, source_target_pairs={{0,8},{1,9},{2,10},{3,11},{4,12},{5,13},{6,14},{7,15},{8,0},{9,1},... | collective-permute-start | bytes 3080 | tf_op jit(solution)/shard_map/ppermute | solution.py:8
  9.9 114.6 %collective-permute-start.9 = (bf16[32,3584]{1,0:T(8,128)(2,1)}, bf16[32,3584]{1,0:T(8,128)(2,1)S(1)}, u32[]{:S(2)}, u32[]{:S(2)}) collective-permute-start(bf16[32,3584]{1,0:T(8,128)(2,1)} %param.9), channel_id=1, source_target_pairs={{0,8},{1,9},{2,10},{3,11},{4,12},{5,13},{6,14},{7,15},{8,0},{9,1},... | collective-permute-start | bytes 688136 | tf_op jit(solution)/shard_map/ppermute | solution.py:8
  10.2 116.8 %collective-permute-start.18 = (bf16[32,3584]{1,0:T(8,128)(2,1)}, bf16[32,3584]{1,0:T(8,128)(2,1)S(1)}, u32[]{:S(2)}, u32[]{:S(2)}) collective-permute-start(bf16[32,3584]{1,0:T(8,128)(2,1)} %param.8), channel_id=1, source_target_pairs={{0,8},{1,9},{2,10},{3,11},{4,12},{5,13},{6,14},{7,15},{8,0},{9,1},... | collective-permute-start | bytes 688136 | tf_op jit(solution)/shard_map/ppermute | solution.py:8
  12.8 179.1 %collective-permute-start.17 = (bf16[1,1792,3,128]{3,1,2,0:T(8,128)(2,1)}, bf16[1,1792,3,128]{3,1,2,0:T(8,128)(2,1)}, u32[]{:S(2)}, u32[]{:S(2)}) collective-permute-start(bf16[1,1792,3,128]{3,1,2,0:T(8,128)(2,1)} %param.12), channel_id=1, source_target_pairs={{0,8},{1,9},{2,10},{3,11},{4,12},{5,13},{6,14},{7,15},{8,0},{9,1},... | collective-permute-start | bytes 4128776 | tf_op jit(solution)/shard_map/ppermute | solution.py:8
  13.1 109.5 %collective-permute-start.1 = (f32[32,8]{0,1:T(8,128)}, f32[32,8]{0,1:T(8,128)S(1)}, u32[]{:S(2)}, u32[]{:S(2)}) collective-permute-start(f32[32,8]{0,1:T(8,128)} %param.11), channel_id=1, source_target_pairs={{0,8},{1,9},{2,10},{3,11},{4,12},{5,13},{6,14},{7,15},{8,0},{9,1},... | collective-permute-start | bytes 3080 | tf_op jit(solution)/shard_map/ppermute | solution.py:8
  20.5 231.9 %collective-permute-start.26 = (bf16[1,1792,3,128]{3,1,2,0:T(8,128)(2,1)}, bf16[1,1792,3,128]{3,1,2,0:T(8,128)(2,1)}, u32[]{:S(2)}, u32[]{:S(2)}) collective-permute-start(bf16[1,1792,3,128]{3,1,2,0:T(8,128)(2,1)} %param.13), channel_id=1, source_target_pairs={{0,8},{1,9},{2,10},{3,11},{4,12},{5,13},{6,14},{7,15},{8,0},{9,1},... | collective-permute-start | bytes 4128776 | tf_op jit(solution)/shard_map/ppermute | solution.py:8
  126.4 9.1 %collective-permute-start.10 = (bf16[40,3584]{1,0:T(8,128)(2,1)S(1)}, bf16[40,3584]{1,0:T(8,128)(2,1)S(1)}, u32[]{:S(2)}, u32[]{:S(2)}) collective-permute-start(bf16[40,3584]{1,0:T(8,128)(2,1)S(1)} %get-tuple-element.50), channel_id=1, source_target_pairs={{0,1},{1,0},{2,3},{3,2},{4,5},{5,4},{6,7},{7,6},{8,9},{9,8},{10,11... | collective-permute-start | bytes 860168 | tf_op jit(solution)/shard_map/ppermute | solution.py:48
  129.0 12.8 %collective-permute-start.11 = (bf16[40,3584]{1,0:T(8,128)(2,1)S(1)}, bf16[40,3584]{1,0:T(8,128)(2,1)S(1)}, u32[]{:S(2)}, u32[]{:S(2)}) collective-permute-start(bf16[40,3584]{1,0:T(8,128)(2,1)S(1)} %get-tuple-element.49), channel_id=1, source_target_pairs={{0,2},{1,3},{2,0},{3,1},{4,6},{5,7},{6,4},{7,5},{8,10},{9,11},{10,... | collective-permute-start | bytes 860168 | tf_op jit(solution)/shard_map/ppermute | solution.py:48
  129.6 12.3 %collective-permute-start.12 = (bf16[40,3584]{1,0:T(8,128)(2,1)S(1)}, bf16[40,3584]{1,0:T(8,128)(2,1)S(1)}, u32[]{:S(2)}, u32[]{:S(2)}) collective-permute-start(bf16[40,3584]{1,0:T(8,128)(2,1)S(1)} %get-tuple-element.48), channel_id=1, source_target_pairs={{0,3},{1,2},{2,1},{3,0},{4,7},{5,6},{6,5},{7,4},{8,11},{9,10},{10,... | collective-permute-start | bytes 860168 | tf_op jit(solution)/shard_map/ppermute | solution.py:48
  135.5 21.6 %collective-permute-start.13 = (bf16[40,3584]{1,0:T(8,128)(2,1)S(1)}, bf16[40,3584]{1,0:T(8,128)(2,1)S(1)}, u32[]{:S(2)}, u32[]{:S(2)}) collective-permute-start(bf16[40,3584]{1,0:T(8,128)(2,1)S(1)} %get-tuple-element.47), channel_id=1, source_target_pairs={{0,4},{1,5},{2,6},{3,7},{4,0},{5,1},{6,2},{7,3},{8,12},{9,13},{10,... | collective-permute-start | bytes 860168 | tf_op jit(solution)/shard_map/ppermute | solution.py:48
  141.9 21.4 %collective-permute-start.14 = (bf16[40,3584]{1,0:T(8,128)(2,1)S(1)}, bf16[40,3584]{1,0:T(8,128)(2,1)S(1)}, u32[]{:S(2)}, u32[]{:S(2)}) collective-permute-start(bf16[40,3584]{1,0:T(8,128)(2,1)S(1)} %get-tuple-element.46), channel_id=1, source_target_pairs={{0,5},{1,4},{2,7},{3,6},{4,1},{5,0},{6,3},{7,2},{8,13},{9,12},{10,... | collective-permute-start | bytes 860168 | tf_op jit(solution)/shard_map/ppermute | solution.py:48
  141.9 50.0 %copy-start.6 = (bf16[1,1792,3,128]{3,1,2,0:T(8,128)(2,1)S(1)}, bf16[1,1792,3,128]{3,1,2,0:T(8,128)(2,1)}, u32[]{:S(2)}) copy-start(bf16[1,1792,3,128]{3,1,2,0:T(8,128)(2,1)} %param.12) | copy-start | bytes 4128772
  142.0 27.5 %collective-permute-start.15 = (bf16[40,3584]{1,0:T(8,128)(2,1)S(1)}, bf16[40,3584]{1,0:T(8,128)(2,1)S(1)}, u32[]{:S(2)}, u32[]{:S(2)}) collective-permute-start(bf16[40,3584]{1,0:T(8,128)(2,1)S(1)} %get-tuple-element.45), channel_id=1, source_target_pairs={{0,6},{1,7},{2,4},{3,5},{4,2},{5,3},{6,0},{7,1},{8,14},{9,15},{10,... | collective-permute-start | bytes 860168 | tf_op jit(solution)/shard_map/ppermute | solution.py:48
  157.2 18.5 %collective-permute-start.16 = (bf16[40,3584]{1,0:T(8,128)(2,1)S(1)}, bf16[40,3584]{1,0:T(8,128)(2,1)S(1)}, u32[]{:S(2)}, u32[]{:S(2)}) collective-permute-start(bf16[40,3584]{1,0:T(8,128)(2,1)S(1)} %get-tuple-element.44), channel_id=1, source_target_pairs={{0,7},{1,6},{2,5},{3,4},{4,3},{5,2},{6,1},{7,0},{8,15},{9,14},{10,... | collective-permute-start | bytes 860168 | tf_op jit(solution)/shard_map/ppermute | solution.py:48
  163.3 14.8 %collective-permute-start.19 = (bf16[40,3584]{1,0:T(8,128)(2,1)S(1)}, bf16[40,3584]{1,0:T(8,128)(2,1)S(1)}, u32[]{:S(2)}, u32[]{:S(2)}) collective-permute-start(bf16[40,3584]{1,0:T(8,128)(2,1)S(1)} %get-tuple-element.43), channel_id=1, source_target_pairs={{0,1},{1,0},{2,3},{3,2},{4,5},{5,4},{6,7},{7,6},{8,9},{9,8},{10,11... | collective-permute-start | bytes 860168 | tf_op jit(solution)/shard_map/ppermute | solution.py:48
  169.4 18.4 %collective-permute-start.20 = (bf16[40,3584]{1,0:T(8,128)(2,1)S(1)}, bf16[40,3584]{1,0:T(8,128)(2,1)S(1)}, u32[]{:S(2)}, u32[]{:S(2)}) collective-permute-start(bf16[40,3584]{1,0:T(8,128)(2,1)S(1)} %get-tuple-element.42), channel_id=1, source_target_pairs={{0,2},{1,3},{2,0},{3,1},{4,6},{5,7},{6,4},{7,5},{8,10},{9,11},{10,... | collective-permute-start | bytes 860168 | tf_op jit(solution)/shard_map/ppermute | solution.py:48
  175.6 12.2 %collective-permute-start.21 = (bf16[40,3584]{1,0:T(8,128)(2,1)S(1)}, bf16[40,3584]{1,0:T(8,128)(2,1)S(1)}, u32[]{:S(2)}, u32[]{:S(2)}) collective-permute-start(bf16[40,3584]{1,0:T(8,128)(2,1)S(1)} %get-tuple-element.41), channel_id=1, source_target_pairs={{0,3},{1,2},{2,1},{3,0},{4,7},{5,6},{6,5},{7,4},{8,11},{9,10},{10,... | collective-permute-start | bytes 860168 | tf_op jit(solution)/shard_map/ppermute | solution.py:48
  178.1 15.3 %collective-permute-start.22 = (bf16[40,3584]{1,0:T(8,128)(2,1)}, bf16[40,3584]{1,0:T(8,128)(2,1)S(1)}, u32[]{:S(2)}, u32[]{:S(2)}) collective-permute-start(bf16[40,3584]{1,0:T(8,128)(2,1)} %get-tuple-element.40), channel_id=1, source_target_pairs={{0,4},{1,5},{2,6},{3,7},{4,0},{5,1},{6,2},{7,3},{8,12},{9,13},{10,... | collective-permute-start | bytes 860168 | tf_op jit(solution)/shard_map/ppermute | solution.py:48
  187.8 10.8 %collective-permute-start.23 = (bf16[40,3584]{1,0:T(8,128)(2,1)}, bf16[40,3584]{1,0:T(8,128)(2,1)S(1)}, u32[]{:S(2)}, u32[]{:S(2)}) collective-permute-start(bf16[40,3584]{1,0:T(8,128)(2,1)} %get-tuple-element.39), channel_id=1, source_target_pairs={{0,5},{1,4},{2,7},{3,6},{4,1},{5,0},{6,3},{7,2},{8,13},{9,12},{10,... | collective-permute-start | bytes 860168 | tf_op jit(solution)/shard_map/ppermute | solution.py:48
  187.9 17.9 %collective-permute-start.24 = (bf16[40,3584]{1,0:T(8,128)(2,1)}, bf16[40,3584]{1,0:T(8,128)(2,1)S(1)}, u32[]{:S(2)}, u32[]{:S(2)}) collective-permute-start(bf16[40,3584]{1,0:T(8,128)(2,1)} %get-tuple-element.38), channel_id=1, source_target_pairs={{0,6},{1,7},{2,4},{3,5},{4,2},{5,3},{6,0},{7,1},{8,14},{9,15},{10,... | collective-permute-start | bytes 860168 | tf_op jit(solution)/shard_map/ppermute | solution.py:48
  191.9 19.2 %collective-permute-start.25 = (bf16[40,3584]{1,0:T(8,128)(2,1)}, bf16[40,3584]{1,0:T(8,128)(2,1)}, u32[]{:S(2)}, u32[]{:S(2)}) collective-permute-start(bf16[40,3584]{1,0:T(8,128)(2,1)} %get-tuple-element.37), channel_id=1, source_target_pairs={{0,7},{1,6},{2,5},{3,4},{4,3},{5,2},{6,1},{7,0},{8,15},{9,14},{10,... | collective-permute-start | bytes 860168 | tf_op jit(solution)/shard_map/ppermute | solution.py:48
  193.2 163.7 %reduce-scatter.2.cloned.1.call-start = ((), (), s32[]{:S(2)}) async-start(), calls=%async_computation.2 | async-start | bytes 4128768 | tf_op jit(solution)/shard_map/reduce_scatter | solution.py:158
  218.1 3.8 %collective-permute-start.36 = (bf16[40]{0:T(256)(128)(2,1)S(1)}, bf16[40]{0:T(256)(128)(2,1)S(1)}, u32[]{:S(2)}, u32[]{:S(2)}) collective-permute-start(bf16[40]{0:T(256)(128)(2,1)S(1)} %get-tuple-element.69), channel_id=1, source_target_pairs={{0,1},{1,0},{2,3},{3,2},{4,5},{5,4},{6,7},{7,6},{8,9},{9,8},{10,11... | collective-permute-start | bytes 248 | tf_op jit(solution)/shard_map/ppermute | solution.py:48
  219.6 5.0 %collective-permute-start.37 = (bf16[40]{0:T(256)(128)(2,1)S(1)}, bf16[40]{0:T(256)(128)(2,1)S(1)}, u32[]{:S(2)}, u32[]{:S(2)}) collective-permute-start(bf16[40]{0:T(256)(128)(2,1)S(1)} %get-tuple-element.68), channel_id=1, source_target_pairs={{0,2},{1,3},{2,0},{3,1},{4,6},{5,7},{6,4},{7,5},{8,10},{9,11},{10,... | collective-permute-start | bytes 248 | tf_op jit(solution)/shard_map/ppermute | solution.py:48
  220.1 4.5 %collective-permute-start.38 = (bf16[40]{0:T(256)(128)(2,1)S(1)}, bf16[40]{0:T(256)(128)(2,1)S(1)}, u32[]{:S(2)}, u32[]{:S(2)}) collective-permute-start(bf16[40]{0:T(256)(128)(2,1)S(1)} %get-tuple-element.67), channel_id=1, source_target_pairs={{0,3},{1,2},{2,1},{3,0},{4,7},{5,6},{6,5},{7,4},{8,11},{9,10},{10,... | collective-permute-start | bytes 248 | tf_op jit(solution)/shard_map/ppermute | solution.py:48
  221.6 5.9 %collective-permute-start.39 = (bf16[40]{0:T(256)(128)(2,1)S(1)}, bf16[40]{0:T(256)(128)(2,1)S(1)}, u32[]{:S(2)}, u32[]{:S(2)}) collective-permute-start(bf16[40]{0:T(256)(128)(2,1)S(1)} %get-tuple-element.66), channel_id=1, source_target_pairs={{0,4},{1,5},{2,6},{3,7},{4,0},{5,1},{6,2},{7,3},{8,12},{9,13},{10,... | collective-permute-start | bytes 248 | tf_op jit(solution)/shard_map/ppermute | solution.py:48
  221.9 5.6 %collective-permute-start.40 = (bf16[40]{0:T(256)(128)(2,1)S(1)}, bf16[40]{0:T(256)(128)(2,1)S(1)}, u32[]{:S(2)}, u32[]{:S(2)}) collective-permute-start(bf16[40]{0:T(256)(128)(2,1)S(1)} %get-tuple-element.65), channel_id=1, source_target_pairs={{0,5},{1,4},{2,7},{3,6},{4,1},{5,0},{6,3},{7,2},{8,13},{9,12},{10,... | collective-permute-start | bytes 248 | tf_op jit(solution)/shard_map/ppermute | solution.py:48
  224.5 4.4 %collective-permute-start.41 = (bf16[40]{0:T(256)(128)(2,1)S(1)}, bf16[40]{0:T(256)(128)(2,1)S(1)}, u32[]{:S(2)}, u32[]{:S(2)}) collective-permute-start(bf16[40]{0:T(256)(128)(2,1)S(1)} %get-tuple-element.64), channel_id=1, source_target_pairs={{0,6},{1,7},{2,4},{3,5},{4,2},{5,3},{6,0},{7,1},{8,14},{9,15},{10,... | collective-permute-start | bytes 248 | tf_op jit(solution)/shard_map/ppermute | solution.py:48
  224.5 5.4 %collective-permute-start.42 = (bf16[40]{0:T(256)(128)(2,1)S(1)}, bf16[40]{0:T(256)(128)(2,1)S(1)}, u32[]{:S(2)}, u32[]{:S(2)}) collective-permute-start(bf16[40]{0:T(256)(128)(2,1)S(1)} %get-tuple-element.63), channel_id=1, source_target_pairs={{0,7},{1,6},{2,5},{3,4},{4,3},{5,2},{6,1},{7,0},{8,15},{9,14},{10,... | collective-permute-start | bytes 248 | tf_op jit(solution)/shard_map/ppermute | solution.py:48
  230.4 5.8 %collective-permute-start.7 = (f32[40]{0:T(128)S(1)}, f32[40]{0:T(128)S(1)}, u32[]{:S(2)}, u32[]{:S(2)}) collective-permute-start(f32[40]{0:T(128)S(1)} %get-tuple-element.56), channel_id=1, source_target_pairs={{0,6},{1,7},{2,4},{3,5},{4,2},{5,3},{6,0},{7,1},{8,14},{9,15},{10,... | collective-permute-start | bytes 488 | tf_op jit(solution)/shard_map/ppermute | solution.py:48
  233.3 5.3 %collective-permute-start.8 = (f32[40]{0:T(128)S(1)}, f32[40]{0:T(128)S(1)}, u32[]{:S(2)}, u32[]{:S(2)}) collective-permute-start(f32[40]{0:T(128)S(1)} %get-tuple-element.55), channel_id=1, source_target_pairs={{0,7},{1,6},{2,5},{3,4},{4,3},{5,2},{6,1},{7,0},{8,15},{9,14},{10,... | collective-permute-start | bytes 488 | tf_op jit(solution)/shard_map/ppermute | solution.py:48
  233.5 5.2 %collective-permute-start.2 = (f32[40]{0:T(128)S(1)}, f32[40]{0:T(128)S(1)}, u32[]{:S(2)}, u32[]{:S(2)}) collective-permute-start(f32[40]{0:T(128)S(1)} %get-tuple-element.61), channel_id=1, source_target_pairs={{0,1},{1,0},{2,3},{3,2},{4,5},{5,4},{6,7},{7,6},{8,9},{9,8},{10,11... | collective-permute-start | bytes 488 | tf_op jit(solution)/shard_map/ppermute | solution.py:48
  234.8 5.8 %collective-permute-start.3 = (f32[40]{0:T(128)S(1)}, f32[40]{0:T(128)S(1)}, u32[]{:S(2)}, u32[]{:S(2)}) collective-permute-start(f32[40]{0:T(128)S(1)} %get-tuple-element.60), channel_id=1, source_target_pairs={{0,2},{1,3},{2,0},{3,1},{4,6},{5,7},{6,4},{7,5},{8,10},{9,11},{10,... | collective-permute-start | bytes 488 | tf_op jit(solution)/shard_map/ppermute | solution.py:48
  236.3 5.4 %collective-permute-start.4 = (f32[40]{0:T(128)S(1)}, f32[40]{0:T(128)S(1)}, u32[]{:S(2)}, u32[]{:S(2)}) collective-permute-start(f32[40]{0:T(128)S(1)} %get-tuple-element.59), channel_id=1, source_target_pairs={{0,3},{1,2},{2,1},{3,0},{4,7},{5,6},{6,5},{7,4},{8,11},{9,10},{10,... | collective-permute-start | bytes 488 | tf_op jit(solution)/shard_map/ppermute | solution.py:48
  238.6 3.5 collective-permute-start.5
  238.8 4.4 %collective-permute-start.6 = (f32[40]{0:T(128)S(1)}, f32[40]{0:T(128)S(1)}, u32[]{:S(2)}, u32[]{:S(2)}) collective-permute-start(f32[40]{0:T(128)S(1)} %get-tuple-element.57), channel_id=1, source_target_pairs={{0,5},{1,4},{2,7},{3,6},{4,1},{5,0},{6,3},{7,2},{8,13},{9,12},{10,... | collective-permute-start | bytes 488 | tf_op jit(solution)/shard_map/ppermute | solution.py:48
  240.7 57.1 %collective-permute-start.27 = (bf16[1,1792,3,128]{3,1,2,0:T(8,128)(2,1)}, bf16[1,1792,3,128]{3,1,2,0:T(8,128)(2,1)}, u32[]{:S(2)}, u32[]{:S(2)}) collective-permute-start(bf16[1,1792,3,128]{3,1,2,0:T(8,128)(2,1)} %param.14), channel_id=1, source_target_pairs={{0,8},{1,9},{2,10},{3,11},{4,12},{5,13},{6,14},{7,15},{8,0},{9,1},... | collective-permute-start | bytes 4128776 | tf_op jit(solution)/shard_map/ppermute | solution.py:8
  252.4 46.7 %copy-start.3 = (bf16[8,40,3584]{2,1,0:T(8,128)(2,1)S(1)}, bf16[8,40,3584]{2,1,0:T(8,128)(2,1)}, u32[]{:S(2)}) copy-start(bf16[8,40,3584]{2,1,0:T(8,128)(2,1)} %copy-done.1) | copy-start | bytes 6881284
  300.3 10.0 %collective-permute-start.28 = (bf16[40,3584]{1,0:T(8,128)(2,1)}, bf16[40,3584]{1,0:T(8,128)(2,1)S(1)}, u32[]{:S(2)}, u32[]{:S(2)}) collective-permute-start(bf16[40,3584]{1,0:T(8,128)(2,1)} %get-tuple-element.36), channel_id=1, source_target_pairs={{0,1},{1,0},{2,3},{3,2},{4,5},{5,4},{6,7},{7,6},{8,9},{9,8},{10,11... | collective-permute-start | bytes 860168 | tf_op jit(solution)/shard_map/ppermute | solution.py:48
  303.4 16.5 %collective-permute-start.29 = (bf16[40,3584]{1,0:T(8,128)(2,1)}, bf16[40,3584]{1,0:T(8,128)(2,1)S(1)}, u32[]{:S(2)}, u32[]{:S(2)}) collective-permute-start(bf16[40,3584]{1,0:T(8,128)(2,1)} %get-tuple-element.35), channel_id=1, source_target_pairs={{0,2},{1,3},{2,0},{3,1},{4,6},{5,7},{6,4},{7,5},{8,10},{9,11},{10,... | collective-permute-start | bytes 860168 | tf_op jit(solution)/shard_map/ppermute | solution.py:48
  304.3 15.6 %collective-permute-start.30 = (bf16[40,3584]{1,0:T(8,128)(2,1)}, bf16[40,3584]{1,0:T(8,128)(2,1)S(1)}, u32[]{:S(2)}, u32[]{:S(2)}) collective-permute-start(bf16[40,3584]{1,0:T(8,128)(2,1)} %get-tuple-element.34), channel_id=1, source_target_pairs={{0,3},{1,2},{2,1},{3,0},{4,7},{5,6},{6,5},{7,4},{8,11},{9,10},{10,... | collective-permute-start | bytes 860168 | tf_op jit(solution)/shard_map/ppermute | solution.py:48
  305.8 14.2 %collective-permute-start.31 = (bf16[40,3584]{1,0:T(8,128)(2,1)}, bf16[40,3584]{1,0:T(8,128)(2,1)S(1)}, u32[]{:S(2)}, u32[]{:S(2)}) collective-permute-start(bf16[40,3584]{1,0:T(8,128)(2,1)} %get-tuple-element.33), channel_id=1, source_target_pairs={{0,4},{1,5},{2,6},{3,7},{4,0},{5,1},{6,2},{7,3},{8,12},{9,13},{10,... | collective-permute-start | bytes 860168 | tf_op jit(solution)/shard_map/ppermute | solution.py:48
  305.8 16.8 %collective-permute-start.32 = (bf16[40,3584]{1,0:T(8,128)(2,1)}, bf16[40,3584]{1,0:T(8,128)(2,1)S(1)}, u32[]{:S(2)}, u32[]{:S(2)}) collective-permute-start(bf16[40,3584]{1,0:T(8,128)(2,1)} %get-tuple-element.32), channel_id=1, source_target_pairs={{0,5},{1,4},{2,7},{3,6},{4,1},{5,0},{6,3},{7,2},{8,13},{9,12},{10,... | collective-permute-start | bytes 860168 | tf_op jit(solution)/shard_map/ppermute | solution.py:48
  311.1 17.3 %collective-permute-start.33 = (bf16[40,3584]{1,0:T(8,128)(2,1)}, bf16[40,3584]{1,0:T(8,128)(2,1)S(1)}, u32[]{:S(2)}, u32[]{:S(2)}) collective-permute-start(bf16[40,3584]{1,0:T(8,128)(2,1)} %get-tuple-element.31), channel_id=1, source_target_pairs={{0,6},{1,7},{2,4},{3,5},{4,2},{5,3},{6,0},{7,1},{8,14},{9,15},{10,... | collective-permute-start | bytes 860168 | tf_op jit(solution)/shard_map/ppermute | solution.py:48
  319.9 12.9 %collective-permute-start.34 = (bf16[40,3584]{1,0:T(8,128)(2,1)}, bf16[40,3584]{1,0:T(8,128)(2,1)S(1)}, u32[]{:S(2)}, u32[]{:S(2)}) collective-permute-start(bf16[40,3584]{1,0:T(8,128)(2,1)} %get-tuple-element.30), channel_id=1, source_target_pairs={{0,7},{1,6},{2,5},{3,4},{4,3},{5,2},{6,1},{7,0},{8,15},{9,14},{10,... | collective-permute-start | bytes 860168 | tf_op jit(solution)/shard_map/ppermute | solution.py:48
  334.3 21.8 %collective-permute-start.35 = (f32[32,3584]{1,0:T(8,128)S(1)}, f32[32,3584]{1,0:T(8,128)S(1)}, u32[]{:S(2)}, u32[]{:S(2)}) collective-permute-start(f32[32,3584]{1,0:T(8,128)S(1)} %slice.286), channel_id=1, source_target_pairs={{0,8},{1,9},{2,10},{3,11},{4,12},{5,13},{6,14},{7,15},{8,0},{9,1},... | collective-permute-start | bytes 1376264 | tf_op jit(solution)/shard_map/ppermute | solution.py:8
  334.6 20.8 %collective-permute-start.43 = (bf16[256]{0:T(256)(128)(2,1)S(1)}, bf16[256]{0:T(256)(128)(2,1)S(1)}, u32[]{:S(2)}, u32[]{:S(2)}) collective-permute-start(bf16[256]{0:T(256)(128)(2,1)S(1)} %slice.263), channel_id=1, source_target_pairs={{0,8},{1,9},{2,10},{3,11},{4,12},{5,13},{6,14},{7,15},{8,0},{9,1},... | collective-permute-start | bytes 1544 | tf_op jit(solution)/shard_map/ppermute | solution.py:8
  (11 other events, 79.9 us)
Sparse Core Ops, SparseCore 0:
  193.3 12.7 all-gather.1
  303.5 9.6 reduce-scatter.1

commit v4 on v3

--- a/solution.py
+++ b/solution.py
@@ -48,6 +48,11 @@
     return lax.ppermute(value, "expert", [(i, i ^ mask) for i in range(lax.axis_size("expert"))])
 
 
+def with_tile(column):
+    lanes = jnp.arange(128, dtype=jnp.int32)[None, :] == 0
+    return jnp.where(lanes, column.astype(jnp.bfloat16)[:, None], jnp.zeros((), jnp.bfloat16))
+
+
 def entry_ranks(flat_ids, axis_width):
     id_onehot = (flat_ids[:, None] == jnp.arange(axis_width, dtype=jnp.int32)[None, :]).astype(
         jnp.int32
@@ -72,9 +77,6 @@
     my_move = jnp.sum(jnp.where(pair_lanes == my_index % half_axis, moving_pairs, 0))
     swapped = my_move == 1
     held = jnp.where(swapped, (my_index + half_axis) % axis_width, my_index)
-    their_weights = from_partner(weights, "expert", swap_bit)
-    their_moments = from_partner((first_moment, second_moment), "expert", swap_bit)
-    weights = jnp.where(swapped, their_weights, weights)
 
     flat_gate = gate_probs.reshape(-1)
     flat_ids = expert_ids.reshape(-1)
@@ -86,11 +88,12 @@
 
     two_stage = half_axis <= 8
     if two_stage:
-        p_tokens, p_grads, p_ids, p_gate = from_partner(
-            (tokens, out_grad, expert_ids, gate_probs), "expert", swap_bit
-        )
-        toks2 = jnp.concatenate([tokens, p_tokens], axis=0)
-        grads2 = jnp.concatenate([out_grad, p_grads], axis=0)
+        packed = jnp.concatenate([tokens, out_grad], axis=1)
+        p_packed, p_ids, p_gate = from_partner(
+            (packed, expert_ids, gate_probs), "expert", swap_bit
+        )
+        weights, p_packed = lax.optimization_barrier((weights, p_packed))
+        both = jnp.concatenate([packed, p_packed], axis=0)
         ids2 = jnp.concatenate([flat_ids, p_ids.reshape(-1)])
         gate2 = jnp.concatenate([flat_gate, p_gate.reshape(-1)])
         holder2 = holder_of(ids2)
@@ -107,24 +110,31 @@
         ) & in_half[None, :]
         tok_hit = jnp.any(slot_hit.reshape(half_axis * chunk, 2 * tok_rows, route_count), axis=2)
         tok_pick = tok_hit.astype(jnp.bfloat16)
-        send_rows = jnp.dot(tok_pick, toks2, preferred_element_type=jnp.float32).astype(
-            jnp.bfloat16
-        )
-        send_grads = jnp.dot(tok_pick, grads2, preferred_element_type=jnp.float32).astype(
+        send_both = jnp.dot(tok_pick, both, preferred_element_type=jnp.float32).astype(
             jnp.bfloat16
         )
         wire2 = gate2.astype(jnp.bfloat16).astype(jnp.float32)
         send_gate = jnp.sum(jnp.where(slot_hit, wire2[None, :], 0.0), axis=1)
+        send_all = jnp.concatenate([send_both, with_tile(send_gate)], axis=1)
 
         def spread(value):
             parts = value.reshape((half_axis, chunk) + value.shape[1:])
             moved = [parts[0]] + [xor_permute(parts[m], m) for m in range(1, half_axis)]
             return jnp.stack(moved).reshape(value.shape)
 
-        rows, grads_in, gates = spread(send_rows), spread(send_grads), spread(send_gate)
+        recv_all = spread(send_all)
+        rows = recv_all[:, :model_width]
+        grads_in = recv_all[:, model_width : 2 * model_width]
+        gates = recv_all[:, 2 * model_width].astype(jnp.float32)
     else:
         slot_of = holder_of(flat_ids) * slot_cap + entry_ranks(flat_ids, axis_width)
         rows, grads_in, gates = send_slots(tokens, out_grad, flat_gate, slot_of, slot_cap)
+    their_weights = from_partner(weights, "expert", swap_bit)
+    first_moment, second_moment, _ = lax.optimization_barrier(
+        (first_moment, second_moment, their_weights)
+    )
+    their_moments = from_partner((first_moment, second_moment), "expert", swap_bit)
+    weights = jnp.where(swapped, their_weights, weights)
     whole = lax.all_gather(weights, "dp", axis=1, tiled=True)[0]
     w_gate = whole[:, 0, :]
     w_up = whole[:, 1, :]
@@ -146,9 +156,6 @@
         both_delta, w_both, contract_hidden, preferred_element_type=jnp.float32
     )
     row_grad = row_grad.astype(jnp.bfloat16)
-    row_grad, their_moments = lax.optimization_barrier((row_grad, their_moments))
-    first_moment = jnp.where(swapped, their_moments[0], first_moment)
-    second_moment = jnp.where(swapped, their_moments[1], second_moment)
     contract_rows = (((0,), (0,)), ((), ()))
     grad_gate = lax.dot_general(rows, gate_delta, contract_rows, preferred_element_type=jnp.float32)
     grad_up = lax.dot_general(rows, up_delta, contract_rows, preferred_element_type=jnp.float32)
@@ -162,14 +169,17 @@
         tiled=True,
     ).astype(jnp.float32) * (1.0 / groups)
     grad = grad[None]
+    first_moment = jnp.where(swapped, their_moments[0], first_moment)
+    second_moment = jnp.where(swapped, their_moments[1], second_moment)
     new_first = (0.9 * first_moment.astype(jnp.float32) + 0.1 * grad).astype(jnp.bfloat16)
     new_second = (0.95 * second_moment.astype(jnp.float32) + 0.05 * grad * grad).astype(
         jnp.bfloat16
     )
 
     if two_stage:
-        back_rows = spread(row_grad)
-        back_gate = spread(gate_rows).astype(jnp.float32)
+        back_all = spread(jnp.concatenate([row_grad, with_tile(gate_rows)], axis=1))
+        back_rows = back_all[:, :model_width]
+        back_gate = back_all[:, model_width].astype(jnp.float32)
         weight_of = jnp.where(slot_hit, gate2[None, :], 0.0)
         weight_of = jnp.sum(weight_of.reshape(half_axis * chunk, 2 * tok_rows, route_count), axis=2)
         partial = lax.dot_general(
@@ -180,9 +190,10 @@
             preferred_element_type=jnp.float32,
         )
         prob2 = jnp.sum(jnp.where(slot_hit, back_gate[:, None], 0.0), axis=0)
-        p_partial, p_prob = from_partner(
-            (partial[tok_rows:], prob2[entry_count:].astype(jnp.bfloat16)), "expert", swap_bit
-        )
+        send_partial, send_prob, _ = lax.optimization_barrier(
+            (partial[tok_rows:], prob2[entry_count:].astype(jnp.bfloat16), their_moments)
+        )
+        p_partial, p_prob = from_partner((send_partial, send_prob), "expert", swap_bit)
         token_grad = (partial[:tok_rows] + p_partial).astype(jnp.bfloat16)
         prob_grad = jnp.where(
             in_half[:entry_count], prob2[:entry_count], p_prob.astype(jnp.float32)

time: 374 us -> 338 us (0.904)
  waiting for transfers between devices: 256 us -> 224 us
    ppermute x9 -> x8, waiting for transfers between devices: 163 us -> 84.9 us  [from_partner(): lax.ppermute(value, axis, [(i, i ^ 1 << bit) for i in range(lax.axis_size...]
    all_gather x1, waiting for transfers between devices: 0.02 us -> 71.4 us  [on_device(): whole = lax.all_gather(weights, 'dp', axis=1, tiled=True)[0]]
    ppermute x35 -> x14, waiting for transfers between devices: 93.3 us -> 67.2 us  [xor_permute(): lax.ppermute(value, 'expert', [(i, i ^ mask) for i in range(lax.axis_size...]
    ppermute x9 -> x8, starting transfers between devices: 12.8 us -> 23.1 us  [from_partner(): lax.ppermute(value, axis, [(i, i ^ 1 << bit) for i in range(lax.axis_size...]
    ppermute x35 -> x14, starting transfers between devices: 39.8 us -> 29.9 us  [xor_permute(): lax.ppermute(value, 'expert', [(i, i ^ mask) for i in range(lax.axis_size...]
    unnamed x50 -> x30, local copies, waits for them, and re-layouts: 3.96 us -> 8.01 us
  transfers between devices with their start and end apart: 46 -> 24, of which waited for: 23 -> 10; matrix products, arithmetic and copies ran while one was open for 10% -> 10% of each run, Pallas kernels for 0% -> 0%
where the time goes in v4:
time: 338 us; the launch traced here: 337 us
  waiting for transfers between devices  224 us (66%)
  starting transfers between devices  53.3 us (16%)
  other arithmetic  20.6 us (6%)
  between operations  15.2 us (4%)
  local copies, waits for them, and re-layouts  12.7 us (4%)
  matrix products  11.9 us (4%)
    ppermute x8, waiting for transfers between devices, from_partner(): lax.ppermute(value, axis, [(i, i ^ 1 << bit) for i in range(lax.axis_size...  84.9 us
    all_gather x1, waiting for transfers between devices, on_device(): whole = lax.all_gather(weights, 'dp', axis=1, tiled=True)[0]  71.4 us
    ppermute x14, waiting for transfers between devices, xor_permute(): lax.ppermute(value, 'expert', [(i, i ^ mask) for i in range(lax.axis_size...  67.2 us
    ppermute x14, starting transfers between devices, xor_permute(): lax.ppermute(value, 'expert', [(i, i ^ mask) for i in range(lax.axis_size...  29.9 us
    ppermute x8, starting transfers between devices, from_partner(): lax.ppermute(value, axis, [(i, i ^ 1 << bit) for i in range(lax.axis_size...  23.1 us
    unnamed x30, local copies, waits for them, and re-layouts  8.01 us
  transfers between devices with their start and end apart: 24, of which 10 were waited for; matrix products, arithmetic and copies ran while one was open for 10% of the time, Pallas kernels for 0%

profile of v4, /device:TPU:6, one launch (start us, length us, event | category | flops | bytes accessed | tf_op | source)
XLA Modules:
  0.0 337.2 jit_solution(12469447269051422746)
XLA Ops:
  7.2 2.7 collective-permute-start.1
  10.2 1.0 constant_dynamic-update-slice_fusion.2
  11.2 1.0 constant_dynamic-update-slice_fusion.1
  12.1 2.7 collective-permute-start.2
  16.7 1.3 fusion.91
  20.0 0.8 pad_maximum_fusion.3
  24.3 10.4 %collective-permute-done.2 = bf16[32,7168]{1,0:T(8,128)(2,1)S(1)} collective-permute-done((bf16[32,7168]{1,0:T(8,128)(2,1)S(1)}, bf16[32,7168]{1,0:T(8,128)(2,1)S(1)}, u32[]{:S(2)}, u32[]{:S(2)}) %collective-permute-start.2) | collective-permute-done | bytes 458784 | tf_op jit(solution)/shard_map/ppermute | solution.py:8
  34.7 1.4 convolution_convert_fusion
  36.1 1.1 pad_maximum_fusion.1
  38.3 2.4 collective-permute-start.5
  41.4 1.4 collective-permute-start.7
  42.8 12.7 %collective-permute-done.3 = bf16[40,7296]{1,0:T(8,128)(2,1)S(1)} collective-permute-done((bf16[40,7296]{1,0:T(8,128)(2,1)S(1)}, bf16[40,7296]{1,0:T(8,128)(2,1)S(1)}, u32[]{:S(2)}, u32[]{:S(2)}) %collective-permute-start.3) | collective-permute-done | bytes 583712 | tf_op jit(solution)/shard_map/ppermute | solution.py:48
  55.6 2.0 collective-permute-start.9
  57.7 27.1 %collective-permute-done.5 = bf16[40,7296]{1,0:T(8,128)(2,1)S(1)} collective-permute-done((bf16[40,7296]{1,0:T(8,128)(2,1)S(1)}, bf16[40,7296]{1,0:T(8,128)(2,1)S(1)}, u32[]{:S(2)}, u32[]{:S(2)}) %collective-permute-start.5) | collective-permute-done | bytes 583712 | tf_op jit(solution)/shard_map/ppermute | solution.py:48
  85.0 56.8 %collective-permute-done.10 = bf16[1,1792,3,128]{3,1,2,0:T(8,128)(2,1)S(1)} collective-permute-done((bf16[1,1792,3,128]{3,1,2,0:T(8,128)(2,1)S(1)}, bf16[1,1792,3,128]{3,1,2,0:T(8,128)(2,1)S(1)}, u32[]{:S(2)}, u32[]{:S(2)}) %collective-permute-start.10) | collective-permute-done | bytes 1376288 | tf_op jit(solution)/shard_map/ppermute | solution.py:8
  141.9 1.2 broadcast_select_fusion
  143.4 0.9 bitcast_dynamic-update-slice_fusion.1
  144.2 0.8 bitcast_dynamic-update-slice_fusion
  145.1 0.9 slice.171
  146.2 2.9 collective-permute-start.19
  149.1 71.4 %all-gather.2.cloned.1.call-done = bf16[1,3584,3,128]{3,1,2,0:T(8,128)(2,1)} async-done(((bf16[1,1792,3,128]{3,1,2,0:T(8,128)(2,1)}), bf16[1,3584,3,128]{3,1,2,0:T(8,128)(2,1)}) %all-gather.2.cloned.1.call-update) | async-done | bytes 2752528 | tf_op jit(solution)/shard_map/all_gather | solution.py:138
  220.5 2.8 fusion.22
  223.4 1.2 copy-done.5
  224.6 0.8 fusion.33
  225.4 0.8 multiply_convert_fusion.5
  226.2 0.9 fusion.27
  227.1 1.1 fusion.2
  228.3 1.0 fusion.1
  229.2 1.0 fusion
  230.2 0.8 convolution_convert_fusion.1
  231.0 1.0 pad_maximum_fusion.2
  232.9 2.6 collective-permute-start.13
  235.6 1.8 pad_maximum_fusion
  237.5 4.8 %collective-permute-done.11 = bf16[40,3712]{1,0:T(8,128)(2,1)} collective-permute-done((bf16[40,3712]{1,0:T(8,128)(2,1)}, bf16[40,3712]{1,0:T(8,128)(2,1)}, u32[]{:S(2)}, u32[]{:S(2)}) %collective-permute-start.11) | collective-permute-done | bytes 296992 | tf_op jit(solution)/shard_map/ppermute | solution.py:48
  242.3 1.5 collective-permute-start.14
  243.8 1.0 bitcast_dynamic-update-slice_fusion.14
  244.8 3.5 %collective-permute-done.12 = bf16[40,3712]{1,0:T(8,128)(2,1)} collective-permute-done((bf16[40,3712]{1,0:T(8,128)(2,1)}, bf16[40,3712]{1,0:T(8,128)(2,1)}, u32[]{:S(2)}, u32[]{:S(2)}) %collective-permute-start.12) | collective-permute-done | bytes 296992 | tf_op jit(solution)/shard_map/ppermute | solution.py:48
  248.3 2.4 collective-permute-start.15
  250.7 1.0 bitcast_dynamic-update-slice_fusion.13
  252.3 1.0 bitcast_dynamic-update-slice_fusion.12
  253.3 14.4 %collective-permute-start.17 = (bf16[40,3712]{1,0:T(8,128)(2,1)S(1)}, bf16[40,3712]{1,0:T(8,128)(2,1)S(1)}, u32[]{:S(2)}, u32[]{:S(2)}) collective-permute-start(bf16[40,3712]{1,0:T(8,128)(2,1)S(1)} %get-tuple-element.41), channel_id=1, source_target_pairs={{0,7},{1,6},{2,5},{3,4},{4,3},{5,2},{6,1},{7,0},{8,15},{9,14},{10,... | collective-permute-start | bytes 890888 | tf_op jit(solution)/shard_map/ppermute | solution.py:48
  267.7 7.1 %collective-permute-done.15 = bf16[40,3712]{1,0:T(8,128)(2,1)S(1)} collective-permute-done((bf16[40,3712]{1,0:T(8,128)(2,1)S(1)}, bf16[40,3712]{1,0:T(8,128)(2,1)S(1)}, u32[]{:S(2)}, u32[]{:S(2)}) %collective-permute-start.15) | collective-permute-done | bytes 296992 | tf_op jit(solution)/shard_map/ppermute | solution.py:48
  274.9 11.9 %collective-permute-done.17 = bf16[40,3712]{1,0:T(8,128)(2,1)S(1)} collective-permute-done((bf16[40,3712]{1,0:T(8,128)(2,1)S(1)}, bf16[40,3712]{1,0:T(8,128)(2,1)S(1)}, u32[]{:S(2)}, u32[]{:S(2)}) %collective-permute-start.17) | collective-permute-done | bytes 296992 | tf_op jit(solution)/shard_map/ppermute | solution.py:48
  286.8 1.4 fusion.11
  288.7 14.4 %collective-permute-start.20 = (f32[32,3584]{1,0:T(8,128)S(1)}, f32[32,3584]{1,0:T(8,128)S(1)}, u32[]{:S(2)}, u32[]{:S(2)}) collective-permute-start(f32[32,3584]{1,0:T(8,128)S(1)} %slice.193), channel_id=1, source_target_pairs={{0,8},{1,9},{2,10},{3,11},{4,12},{5,13},{6,14},{7,15},{8,0},{9,1},... | collective-permute-start | bytes 1376264 | tf_op jit(solution)/shard_map/ppermute | solution.py:8
  303.2 17.7 %collective-permute-done.21 = bf16[256]{0:T(256)(128)(2,1)S(1)} collective-permute-done((bf16[256]{0:T(256)(128)(2,1)S(1)}, bf16[256]{0:T(256)(128)(2,1)S(1)}, u32[]{:S(2)}, u32[]{:S(2)}) %collective-permute-start.21) | collective-permute-done | bytes 544 | tf_op jit(solution)/shard_map/ppermute | solution.py:8
  322.4 3.2 fusion.4
  325.6 4.8 %fusion.7 = (bf16[1,1792,3,128]{3,1,2,0:T(8,128)(2,1)}, bf16[1,1792,3,128]{3,1,2,0:T(8,128)(2,1)}) fusion(bf16[1792,3,128]{2,0,1:T(8,128)(2,1)S(1)} %copy-done, bf16[1,1792,3,128]{3,1,2,0:T(8,128)(2,1)} %collective-permute-done.19, bf16[1,1792,3,128]{3,1,2,0:T(8,128)(2,1)} %param.14, pred[]{:T(512)S(6)} %eq.175, ...), kind=kLoop, calls=%fused_computation.30 | loop fusion | flops 10321920 | bytes 9633793 | tf_op jit(solution)/shard_map/convert_element_type | solution.py:175
  (111 shorter events, 13.3 us)
Async XLA Ops:
  7.2 213.3 %all-gather.2.cloned.1.call-start = ((), (), s32[]{:S(2)}) async-start(), calls=%async_computation.1 | async-start | bytes 4128768 | tf_op jit(solution)/shard_map/all_gather | solution.py:138
  7.2 12.8 %collective-permute-start.1 = (f32[32,8]{0,1:T(8,128)}, f32[32,8]{0,1:T(8,128)S(1)}, u32[]{:S(2)}, u32[]{:S(2)}) collective-permute-start(f32[32,8]{0,1:T(8,128)} %param.11), channel_id=1, source_target_pairs={{0,8},{1,9},{2,10},{3,11},{4,12},{5,13},{6,14},{7,15},{8,0},{9,1},... | collective-permute-start | bytes 3080 | tf_op jit(solution)/shard_map/ppermute | solution.py:8
  9.9 9.8 %collective-permute-start = (s32[32,8]{0,1:T(8,128)}, s32[32,8]{0,1:T(8,128)S(1)}, u32[]{:S(2)}, u32[]{:S(2)}) collective-permute-start(s32[32,8]{0,1:T(8,128)} %param.10), channel_id=1, source_target_pairs={{0,8},{1,9},{2,10},{3,11},{4,12},{5,13},{6,14},{7,15},{8,0},{9,1},... | collective-permute-start | bytes 3080 | tf_op jit(solution)/shard_map/ppermute | solution.py:8
  12.1 22.6 %collective-permute-start.2 = (bf16[32,7168]{1,0:T(8,128)(2,1)S(1)}, bf16[32,7168]{1,0:T(8,128)(2,1)S(1)}, u32[]{:S(2)}, u32[]{:S(2)}) collective-permute-start(bf16[32,7168]{1,0:T(8,128)(2,1)S(1)} %constant_dynamic-update-slice_fusion.1), channel_id=1, source_target_pairs={{0,8},{1,9},{2,10},{3,11},{4,12},{5,13},{6,14},{7,15},{8,0},{9,1},... | collective-permute-start | bytes 1376264 | tf_op jit(solution)/shard_map/ppermute | solution.py:8
  37.2 18.3 %collective-permute-start.3 = (bf16[40,7296]{1,0:T(8,128)(2,1)S(1)}, bf16[40,7296]{1,0:T(8,128)(2,1)S(1)}, u32[]{:S(2)}, u32[]{:S(2)}) collective-permute-start(bf16[40,7296]{1,0:T(8,128)(2,1)S(1)} %get-tuple-element.33), channel_id=1, source_target_pairs={{0,1},{1,0},{2,3},{3,2},{4,5},{5,4},{6,7},{7,6},{8,9},{9,8},{10,11... | collective-permute-start | bytes 1751048 | tf_op jit(solution)/shard_map/ppermute | solution.py:48
  37.8 17.8 %collective-permute-start.4 = (bf16[40,7296]{1,0:T(8,128)(2,1)S(1)}, bf16[40,7296]{1,0:T(8,128)(2,1)S(1)}, u32[]{:S(2)}, u32[]{:S(2)}) collective-permute-start(bf16[40,7296]{1,0:T(8,128)(2,1)S(1)} %get-tuple-element.34), channel_id=1, source_target_pairs={{0,2},{1,3},{2,0},{3,1},{4,6},{5,7},{6,4},{7,5},{8,10},{9,11},{10,... | collective-permute-start | bytes 1751048 | tf_op jit(solution)/shard_map/ppermute | solution.py:48
  38.3 46.5 %collective-permute-start.5 = (bf16[40,7296]{1,0:T(8,128)(2,1)S(1)}, bf16[40,7296]{1,0:T(8,128)(2,1)S(1)}, u32[]{:S(2)}, u32[]{:S(2)}) collective-permute-start(bf16[40,7296]{1,0:T(8,128)(2,1)S(1)} %get-tuple-element.35), channel_id=1, source_target_pairs={{0,3},{1,2},{2,1},{3,0},{4,7},{5,6},{6,5},{7,4},{8,11},{9,10},{10,... | collective-permute-start | bytes 1751048 | tf_op jit(solution)/shard_map/ppermute | solution.py:48
  40.8 44.1 %collective-permute-start.6 = (bf16[40,7296]{1,0:T(8,128)(2,1)S(1)}, bf16[40,7296]{1,0:T(8,128)(2,1)S(1)}, u32[]{:S(2)}, u32[]{:S(2)}) collective-permute-start(bf16[40,7296]{1,0:T(8,128)(2,1)S(1)} %get-tuple-element.36), channel_id=1, source_target_pairs={{0,4},{1,5},{2,6},{3,7},{4,0},{5,1},{6,2},{7,3},{8,12},{9,13},{10,... | collective-permute-start | bytes 1751048 | tf_op jit(solution)/shard_map/ppermute | solution.py:48
  41.4 43.4 %copy-start.1 = (bf16[1,1792,3,128]{3,1,2,0:T(8,128)(2,1)S(1)}, bf16[1,1792,3,128]{3,1,2,0:T(8,128)(2,1)}, u32[]{:S(2)}) copy-start(bf16[1,1792,3,128]{3,1,2,0:T(8,128)(2,1)} %param.12) | copy-start | bytes 4128772
  41.4 43.6 %collective-permute-start.7 = (bf16[40,7296]{1,0:T(8,128)(2,1)S(1)}, bf16[40,7296]{1,0:T(8,128)(2,1)S(1)}, u32[]{:S(2)}, u32[]{:S(2)}) collective-permute-start(bf16[40,7296]{1,0:T(8,128)(2,1)S(1)} %get-tuple-element.37), channel_id=1, source_target_pairs={{0,5},{1,4},{2,7},{3,6},{4,1},{5,0},{6,3},{7,2},{8,13},{9,12},{10,... | collective-permute-start | bytes 1751048 | tf_op jit(solution)/shard_map/ppermute | solution.py:48
  55.5 87.8 %collective-permute-start.8 = (bf16[40,7296]{1,0:T(8,128)(2,1)S(1)}, bf16[40,7296]{1,0:T(8,128)(2,1)S(1)}, u32[]{:S(2)}, u32[]{:S(2)}) collective-permute-start(bf16[40,7296]{1,0:T(8,128)(2,1)S(1)} %get-tuple-element.38), channel_id=1, source_target_pairs={{0,6},{1,7},{2,4},{3,5},{4,2},{5,3},{6,0},{7,1},{8,14},{9,15},{10,... | collective-permute-start | bytes 1751048 | tf_op jit(solution)/shard_map/ppermute | solution.py:48
  55.6 88.6 %collective-permute-start.9 = (bf16[40,7296]{1,0:T(8,128)(2,1)S(1)}, bf16[40,7296]{1,0:T(8,128)(2,1)S(1)}, u32[]{:S(2)}, u32[]{:S(2)}) collective-permute-start(bf16[40,7296]{1,0:T(8,128)(2,1)S(1)} %get-tuple-element.32), channel_id=1, source_target_pairs={{0,7},{1,6},{2,5},{3,4},{4,3},{5,2},{6,1},{7,0},{8,15},{9,14},{10,... | collective-permute-start | bytes 1751048 | tf_op jit(solution)/shard_map/ppermute | solution.py:48
  84.8 57.1 %collective-permute-start.10 = (bf16[1,1792,3,128]{3,1,2,0:T(8,128)(2,1)S(1)}, bf16[1,1792,3,128]{3,1,2,0:T(8,128)(2,1)S(1)}, u32[]{:S(2)}, u32[]{:S(2)}) collective-permute-start(bf16[1,1792,3,128]{3,1,2,0:T(8,128)(2,1)S(1)} %copy-done.1), channel_id=1, source_target_pairs={{0,8},{1,9},{2,10},{3,11},{4,12},{5,13},{6,14},{7,15},{8,0},{9,1},... | collective-permute-start | bytes 4128776 | tf_op jit(solution)/shard_map/ppermute | solution.py:8
  85.0 56.9 %copy-start.4 = (bf16[8,40,7296]{2,1,0:T(8,128)(2,1)}, bf16[8,40,7296]{2,1,0:T(8,128)(2,1)S(1)}, u32[]{:S(2)}) copy-start(bf16[8,40,7296]{2,1,0:T(8,128)(2,1)S(1)} %bitcast_dynamic-update-slice_fusion.2) | copy-start | bytes 14008324
  143.1 179.3 %reduce-scatter.2.cloned.1.call-start = ((), (), s32[]{:S(2)}) async-start(), calls=%async_computation.2 | async-start | bytes 4128768 | tf_op jit(solution)/shard_map/reduce_scatter | solution.py:165
  146.1 142.6 %collective-permute-start.18 = (bf16[1,1792,3,128]{3,1,2,0:T(8,128)(2,1)}, bf16[1,1792,3,128]{3,1,2,0:T(8,128)(2,1)}, u32[]{:S(2)}, u32[]{:S(2)}) collective-permute-start(bf16[1,1792,3,128]{3,1,2,0:T(8,128)(2,1)} %param.13), channel_id=1, source_target_pairs={{0,8},{1,9},{2,10},{3,11},{4,12},{5,13},{6,14},{7,15},{8,0},{9,1},... | collective-permute-start | bytes 4128776 | tf_op jit(solution)/shard_map/ppermute | solution.py:8
  146.2 142.5 %collective-permute-start.19 = (bf16[1,1792,3,128]{3,1,2,0:T(8,128)(2,1)}, bf16[1,1792,3,128]{3,1,2,0:T(8,128)(2,1)}, u32[]{:S(2)}, u32[]{:S(2)}) collective-permute-start(bf16[1,1792,3,128]{3,1,2,0:T(8,128)(2,1)} %param.14), channel_id=1, source_target_pairs={{0,8},{1,9},{2,10},{3,11},{4,12},{5,13},{6,14},{7,15},{8,0},{9,1},... | collective-permute-start | bytes 4128776 | tf_op jit(solution)/shard_map/ppermute | solution.py:8
  220.5 2.8 copy-start.2
  220.5 4.1 %copy-start.5 = (bf16[8,40,7296]{2,1,0:T(8,128)(2,1)S(1)}, bf16[8,40,7296]{2,1,0:T(8,128)(2,1)}, u32[]{:S(2)}) copy-start(bf16[8,40,7296]{2,1,0:T(8,128)(2,1)} %bitcast_dynamic-update-slice_fusion) | copy-start | bytes 14008324
  232.1 10.2 %collective-permute-start.11 = (bf16[40,3712]{1,0:T(8,128)(2,1)}, bf16[40,3712]{1,0:T(8,128)(2,1)}, u32[]{:S(2)}, u32[]{:S(2)}) collective-permute-start(bf16[40,3712]{1,0:T(8,128)(2,1)} %get-tuple-element.42), channel_id=1, source_target_pairs={{0,1},{1,0},{2,3},{3,2},{4,5},{5,4},{6,7},{7,6},{8,9},{9,8},{10,11... | collective-permute-start | bytes 890888 | tf_op jit(solution)/shard_map/ppermute | solution.py:48
  232.6 15.7 %collective-permute-start.12 = (bf16[40,3712]{1,0:T(8,128)(2,1)}, bf16[40,3712]{1,0:T(8,128)(2,1)}, u32[]{:S(2)}, u32[]{:S(2)}) collective-permute-start(bf16[40,3712]{1,0:T(8,128)(2,1)} %get-tuple-element.43), channel_id=1, source_target_pairs={{0,2},{1,3},{2,0},{3,1},{4,6},{5,7},{6,4},{7,5},{8,10},{9,11},{10,... | collective-permute-start | bytes 890888 | tf_op jit(solution)/shard_map/ppermute | solution.py:48
  232.9 18.8 %collective-permute-start.13 = (bf16[40,3712]{1,0:T(8,128)(2,1)}, bf16[40,3712]{1,0:T(8,128)(2,1)}, u32[]{:S(2)}, u32[]{:S(2)}) collective-permute-start(bf16[40,3712]{1,0:T(8,128)(2,1)} %get-tuple-element.44), channel_id=1, source_target_pairs={{0,3},{1,2},{2,1},{3,0},{4,7},{5,6},{6,5},{7,4},{8,11},{9,10},{10,... | collective-permute-start | bytes 890888 | tf_op jit(solution)/shard_map/ppermute | solution.py:48
  237.4 4.8 %copy-start.3 = (bf16[40,3712]{1,0:T(8,128)(2,1)S(1)}, bf16[40,3712]{1,0:T(8,128)(2,1)}, u32[]{:S(2)}) copy-start(bf16[40,3712]{1,0:T(8,128)(2,1)} %get-tuple-element.45) | copy-start | bytes 890884
  242.3 11.0 %collective-permute-start.14 = (bf16[40,3712]{1,0:T(8,128)(2,1)S(1)}, bf16[40,3712]{1,0:T(8,128)(2,1)S(1)}, u32[]{:S(2)}, u32[]{:S(2)}) collective-permute-start(bf16[40,3712]{1,0:T(8,128)(2,1)S(1)} %copy-done.3), channel_id=1, source_target_pairs={{0,4},{1,5},{2,6},{3,7},{4,0},{5,1},{6,2},{7,3},{8,12},{9,13},{10,... | collective-permute-start | bytes 890888 | tf_op jit(solution)/shard_map/ppermute | solution.py:48
  248.3 26.6 %collective-permute-start.15 = (bf16[40,3712]{1,0:T(8,128)(2,1)S(1)}, bf16[40,3712]{1,0:T(8,128)(2,1)S(1)}, u32[]{:S(2)}, u32[]{:S(2)}) collective-permute-start(bf16[40,3712]{1,0:T(8,128)(2,1)S(1)} %get-tuple-element.46), channel_id=1, source_target_pairs={{0,5},{1,4},{2,7},{3,6},{4,1},{5,0},{6,3},{7,2},{8,13},{9,12},{10,... | collective-permute-start | bytes 890888 | tf_op jit(solution)/shard_map/ppermute | solution.py:48
  251.7 23.2 %collective-permute-start.16 = (bf16[40,3712]{1,0:T(8,128)(2,1)S(1)}, bf16[40,3712]{1,0:T(8,128)(2,1)S(1)}, u32[]{:S(2)}, u32[]{:S(2)}) collective-permute-start(bf16[40,3712]{1,0:T(8,128)(2,1)S(1)} %get-tuple-element.47), channel_id=1, source_target_pairs={{0,6},{1,7},{2,4},{3,5},{4,2},{5,3},{6,0},{7,1},{8,14},{9,15},{10,... | collective-permute-start | bytes 890888 | tf_op jit(solution)/shard_map/ppermute | solution.py:48
  253.3 33.5 %collective-permute-start.17 = (bf16[40,3712]{1,0:T(8,128)(2,1)S(1)}, bf16[40,3712]{1,0:T(8,128)(2,1)S(1)}, u32[]{:S(2)}, u32[]{:S(2)}) collective-permute-start(bf16[40,3712]{1,0:T(8,128)(2,1)S(1)} %get-tuple-element.41), channel_id=1, source_target_pairs={{0,7},{1,6},{2,5},{3,4},{4,3},{5,2},{6,1},{7,0},{8,15},{9,14},{10,... | collective-permute-start | bytes 890888 | tf_op jit(solution)/shard_map/ppermute | solution.py:48
  288.7 33.0 %collective-permute-start.20 = (f32[32,3584]{1,0:T(8,128)S(1)}, f32[32,3584]{1,0:T(8,128)S(1)}, u32[]{:S(2)}, u32[]{:S(2)}) collective-permute-start(f32[32,3584]{1,0:T(8,128)S(1)} %slice.193), channel_id=1, source_target_pairs={{0,8},{1,9},{2,10},{3,11},{4,12},{5,13},{6,14},{7,15},{8,0},{9,1},... | collective-permute-start | bytes 1376264 | tf_op jit(solution)/shard_map/ppermute | solution.py:8
  303.1 17.8 %collective-permute-start.21 = (bf16[256]{0:T(256)(128)(2,1)S(1)}, bf16[256]{0:T(256)(128)(2,1)S(1)}, u32[]{:S(2)}, u32[]{:S(2)}) collective-permute-start(bf16[256]{0:T(256)(128)(2,1)S(1)} %slice.152), channel_id=1, source_target_pairs={{0,8},{1,9},{2,10},{3,11},{4,12},{5,13},{6,14},{7,15},{8,0},{9,1},... | collective-permute-start | bytes 1544 | tf_op jit(solution)/shard_map/ppermute | solution.py:8
  322.4 3.2 copy-start
Sparse Core Ops, SparseCore 0:
  143.2 77.1 all-gather.1
  237.5 11.5 reduce-scatter.1

commit v5 on v4

--- a/solution.py
+++ b/solution.py
@@ -89,10 +89,9 @@
     two_stage = half_axis <= 8
     if two_stage:
         packed = jnp.concatenate([tokens, out_grad], axis=1)
-        p_packed, p_ids, p_gate = from_partner(
-            (packed, expert_ids, gate_probs), "expert", swap_bit
-        )
-        weights, p_packed = lax.optimization_barrier((weights, p_packed))
+        p_packed, p_ids, p_gate, their_weights = from_partner(
+            (packed, expert_ids, gate_probs, weights), "expert", swap_bit
+        )
         both = jnp.concatenate([packed, p_packed], axis=0)
         ids2 = jnp.concatenate([flat_ids, p_ids.reshape(-1)])
         gate2 = jnp.concatenate([flat_gate, p_gate.reshape(-1)])
@@ -129,13 +128,22 @@
     else:
         slot_of = holder_of(flat_ids) * slot_cap + entry_ranks(flat_ids, axis_width)
         rows, grads_in, gates = send_slots(tokens, out_grad, flat_gate, slot_of, slot_cap)
-    their_weights = from_partner(weights, "expert", swap_bit)
+    if not two_stage:
+        their_weights = from_partner(weights, "expert", swap_bit)
     first_moment, second_moment, _ = lax.optimization_barrier(
         (first_moment, second_moment, their_weights)
     )
     their_moments = from_partner((first_moment, second_moment), "expert", swap_bit)
     weights = jnp.where(swapped, their_weights, weights)
-    whole = lax.all_gather(weights, "dp", axis=1, tiled=True)[0]
+    if groups == 2:
+        other = lax.ppermute(weights, "dp", [(0, 1), (1, 0)])
+        first_half = lax.axis_index("dp") == 0
+        whole = jnp.concatenate(
+            [jnp.where(first_half, weights, other), jnp.where(first_half, other, weights)],
+            axis=1,
+        )[0]
+    else:
+        whole = lax.all_gather(weights, "dp", axis=1, tiled=True)[0]
     w_gate = whole[:, 0, :]
     w_up = whole[:, 1, :]
     w_down = whole[:, 2, :]
@@ -162,12 +170,18 @@
     grad_down = lax.dot_general(
         scaled_grad, hidden, contract_rows, preferred_element_type=jnp.float32
     )
-    grad = lax.psum_scatter(
-        jnp.stack([grad_gate, grad_up, grad_down], axis=1).astype(jnp.bfloat16),
-        "dp",
-        scatter_dimension=0,
-        tiled=True,
-    ).astype(jnp.float32) * (1.0 / groups)
+    part = jnp.stack([grad_gate, grad_up, grad_down], axis=1).astype(jnp.bfloat16)
+    if groups == 2:
+        row_half = part.shape[0] // 2
+        first_half = lax.axis_index("dp") == 0
+        keep = jnp.where(first_half, part[:row_half], part[row_half:])
+        give = jnp.where(first_half, part[row_half:], part[:row_half])
+        got = lax.ppermute(give, "dp", [(0, 1), (1, 0)])
+        grad = (keep.astype(jnp.float32) + got.astype(jnp.float32)) * (1.0 / groups)
+    else:
+        grad = lax.psum_scatter(
+            part, "dp", scatter_dimension=0, tiled=True
+        ).astype(jnp.float32) * (1.0 / groups)
     grad = grad[None]
     first_moment = jnp.where(swapped, their_moments[0], first_moment)
     second_moment = jnp.where(swapped, their_moments[1], second_moment)

time: 338 us -> 311 us (0.920)
  between operations: 15.2 us -> 1.79 us
  waiting for transfers between devices: 224 us -> 215 us
  starting transfers between devices: 53.3 us -> 46.6 us
    ppermute x14, waiting for transfers between devices: 67.2 us -> 157 us  [xor_permute(): lax.ppermute(value, 'expert', [(i, i ^ mask) for i in range(lax.axis_size...]
    all_gather x1 -> x0, waiting for transfers between devices: 71.4 us -> none  [on_device(): whole = lax.all_gather(weights, 'dp', axis=1, tiled=True)[0]]
    ppermute x8, waiting for transfers between devices: 84.9 us -> 58.2 us  [from_partner(): lax.ppermute(value, axis, [(i, i ^ 1 << bit) for i in range(lax.axis_size...]
    ppermute x8, starting transfers between devices: 23.1 us -> 11.9 us  [from_partner(): lax.ppermute(value, axis, [(i, i ^ 1 << bit) for i in range(lax.axis_size...]
    ppermute x14, starting transfers between devices: 29.9 us -> 34.6 us  [xor_permute(): lax.ppermute(value, 'expert', [(i, i ^ mask) for i in range(lax.axis_size...]
    convert_element_type x0 -> x1, other arithmetic: none -> 3.72 us  [on_device(): (0.9 * first_moment.astype(jnp.float32) + 0.1 * grad).astype(jnp.bfloat16)]
    unnamed x30 -> x28, local copies, waits for them, and re-layouts: 8.01 us -> 8.19 us
  transfers between devices with their start and end apart: 24 -> 24, of which waited for: 10 -> 14; matrix products, arithmetic and copies ran while one was open for 10% -> 9% of each run, Pallas kernels for 0% -> 0%
where the time goes in v5:
time: 311 us; the launch traced here: 308 us
  waiting for transfers between devices  215 us (69%)
  starting transfers between devices  46.6 us (15%)
  other arithmetic  23.2 us (7%)
  local copies, waits for them, and re-layouts  11.2 us (4%)
  matrix products  9.85 us (3%)
    ppermute x14, waiting for transfers between devices, xor_permute(): lax.ppermute(value, 'expert', [(i, i ^ mask) for i in range(lax.axis_size...  157 us
    ppermute x8, waiting for transfers between devices, from_partner(): lax.ppermute(value, axis, [(i, i ^ 1 << bit) for i in range(lax.axis_size...  58.2 us
    ppermute x14, starting transfers between devices, xor_permute(): lax.ppermute(value, 'expert', [(i, i ^ mask) for i in range(lax.axis_size...  34.6 us
    ppermute x8, starting transfers between devices, from_partner(): lax.ppermute(value, axis, [(i, i ^ 1 << bit) for i in range(lax.axis_size...  11.9 us
    unnamed x28, local copies, waits for them, and re-layouts  8.19 us
  transfers between devices with their start and end apart: 24, of which 14 were waited for; matrix products, arithmetic and copies ran while one was open for 9% of the time, Pallas kernels for 0%

profile of v5, /device:TPU:6, one launch (start us, length us, event | category | flops | bytes accessed | tf_op | source)
XLA Modules:
  0.0 307.8 jit_solution(4000813534838037916)
XLA Ops:
  0.6 2.7 collective-permute-start.1
  3.6 1.0 constant_dynamic-update-slice_fusion.2
  4.6 1.0 constant_dynamic-update-slice_fusion.1
  5.5 2.7 collective-permute-start.2
  10.5 1.3 fusion.85
  18.1 40.5 %collective-permute-done.2 = bf16[32,7168]{1,0:T(8,128)(2,1)S(1)} collective-permute-done((bf16[32,7168]{1,0:T(8,128)(2,1)S(1)}, bf16[32,7168]{1,0:T(8,128)(2,1)S(1)}, u32[]{:S(2)}, u32[]{:S(2)}) %collective-permute-start.2) | collective-permute-done | bytes 458784 | tf_op jit(solution)/shard_map/ppermute | solution.py:8
  58.6 1.4 convolution_convert_fusion
  60.0 1.3 pad_maximum_fusion.1
  62.4 2.5 collective-permute-start.5
  64.9 12.6 %collective-permute-done.3 = bf16[40,7296]{1,0:T(8,128)(2,1)S(1)} collective-permute-done((bf16[40,7296]{1,0:T(8,128)(2,1)S(1)}, bf16[40,7296]{1,0:T(8,128)(2,1)S(1)}, u32[]{:S(2)}, u32[]{:S(2)}) %collective-permute-start.3) | collective-permute-done | bytes 583712 | tf_op jit(solution)/shard_map/ppermute | solution.py:48
  77.6 9.7 %collective-permute-done.4 = bf16[40,7296]{1,0:T(8,128)(2,1)S(1)} collective-permute-done((bf16[40,7296]{1,0:T(8,128)(2,1)S(1)}, bf16[40,7296]{1,0:T(8,128)(2,1)S(1)}, u32[]{:S(2)}, u32[]{:S(2)}) %collective-permute-start.4) | collective-permute-done | bytes 583712 | tf_op jit(solution)/shard_map/ppermute | solution.py:48
  87.4 21.3 %collective-permute-start.9 = (bf16[40,7296]{1,0:T(8,128)(2,1)S(1)}, bf16[40,7296]{1,0:T(8,128)(2,1)S(1)}, u32[]{:S(2)}, u32[]{:S(2)}) collective-permute-start(bf16[40,7296]{1,0:T(8,128)(2,1)S(1)} %get-tuple-element.30), channel_id=1, source_target_pairs={{0,7},{1,6},{2,5},{3,4},{4,3},{5,2},{6,1},{7,0},{8,15},{9,14},{10,... | collective-permute-start | bytes 1751048 | tf_op jit(solution)/shard_map/ppermute | solution.py:48
  108.8 3.3 %collective-permute-done.7 = bf16[40,7296]{1,0:T(8,128)(2,1)S(1)} collective-permute-done((bf16[40,7296]{1,0:T(8,128)(2,1)S(1)}, bf16[40,7296]{1,0:T(8,128)(2,1)S(1)}, u32[]{:S(2)}, u32[]{:S(2)}) %collective-permute-start.7) | collective-permute-done | bytes 583712 | tf_op jit(solution)/shard_map/ppermute | solution.py:48
  112.2 12.4 %collective-permute-done.8 = bf16[40,7296]{1,0:T(8,128)(2,1)S(1)} collective-permute-done((bf16[40,7296]{1,0:T(8,128)(2,1)S(1)}, bf16[40,7296]{1,0:T(8,128)(2,1)S(1)}, u32[]{:S(2)}, u32[]{:S(2)}) %collective-permute-start.8) | collective-permute-done | bytes 583712 | tf_op jit(solution)/shard_map/ppermute | solution.py:48
  125.0 12.0 %collective-permute-done.9 = bf16[40,7296]{1,0:T(8,128)(2,1)S(1)} collective-permute-done((bf16[40,7296]{1,0:T(8,128)(2,1)S(1)}, bf16[40,7296]{1,0:T(8,128)(2,1)S(1)}, u32[]{:S(2)}, u32[]{:S(2)}) %collective-permute-start.9) | collective-permute-done | bytes 583712 | tf_op jit(solution)/shard_map/ppermute | solution.py:48
  137.1 2.1 copy-done.3
  139.3 1.6 collective-permute-start.19
  141.0 1.4 collective-permute-start.20
  142.7 2.1 copy-done.4
  145.7 0.8 fusion.27
  146.6 0.8 multiply_convert_fusion.5
  147.3 0.9 fusion.21
  148.2 1.1 fusion.2
  149.4 1.0 fusion.1
  150.4 1.0 fusion
  151.4 0.8 convolution_convert_fusion.1
  152.3 1.5 collective-permute-start.12
  153.9 1.5 collective-permute-start.13
  156.2 6.2 %collective-permute-done.12 = bf16[40,3712]{1,0:T(8,128)(2,1)S(1)} collective-permute-done((bf16[40,3712]{1,0:T(8,128)(2,1)S(1)}, bf16[40,3712]{1,0:T(8,128)(2,1)S(1)}, u32[]{:S(2)}, u32[]{:S(2)}) %collective-permute-start.12) | collective-permute-done | bytes 296992 | tf_op jit(solution)/shard_map/ppermute | solution.py:48
  162.4 1.1 collective-permute-start.15
  163.6 3.8 %collective-permute-done.13 = bf16[40,3712]{1,0:T(8,128)(2,1)S(1)} collective-permute-done((bf16[40,3712]{1,0:T(8,128)(2,1)S(1)}, bf16[40,3712]{1,0:T(8,128)(2,1)S(1)}, u32[]{:S(2)}, u32[]{:S(2)}) %collective-permute-start.13) | collective-permute-done | bytes 296992 | tf_op jit(solution)/shard_map/ppermute | solution.py:48
  167.4 1.4 collective-permute-start.16
  168.9 1.2 collective-permute-done.14
  170.1 0.8 collective-permute-start.17
  170.9 36.8 %collective-permute-done.15 = bf16[40,3712]{1,0:T(8,128)(2,1)S(1)} collective-permute-done((bf16[40,3712]{1,0:T(8,128)(2,1)S(1)}, bf16[40,3712]{1,0:T(8,128)(2,1)S(1)}, u32[]{:S(2)}, u32[]{:S(2)}) %collective-permute-start.15) | collective-permute-done | bytes 296992 | tf_op jit(solution)/shard_map/ppermute | solution.py:48
  207.6 2.7 collective-permute-start.18
  210.4 3.6 %collective-permute-done.16 = bf16[40,3712]{1,0:T(8,128)(2,1)S(1)} collective-permute-done((bf16[40,3712]{1,0:T(8,128)(2,1)S(1)}, bf16[40,3712]{1,0:T(8,128)(2,1)S(1)}, u32[]{:S(2)}, u32[]{:S(2)}) %collective-permute-start.16) | collective-permute-done | bytes 296992 | tf_op jit(solution)/shard_map/ppermute | solution.py:48
  214.0 6.3 %collective-permute-done.17 = bf16[40,3712]{1,0:T(8,128)(2,1)S(1)} collective-permute-done((bf16[40,3712]{1,0:T(8,128)(2,1)S(1)}, bf16[40,3712]{1,0:T(8,128)(2,1)S(1)}, u32[]{:S(2)}, u32[]{:S(2)}) %collective-permute-start.17) | collective-permute-done | bytes 296992 | tf_op jit(solution)/shard_map/ppermute | solution.py:48
  220.4 48.9 %collective-permute-done.18 = bf16[40,3712]{1,0:T(8,128)(2,1)S(1)} collective-permute-done((bf16[40,3712]{1,0:T(8,128)(2,1)S(1)}, bf16[40,3712]{1,0:T(8,128)(2,1)S(1)}, u32[]{:S(2)}, u32[]{:S(2)}) %collective-permute-start.18) | collective-permute-done | bytes 296992 | tf_op jit(solution)/shard_map/ppermute | solution.py:48
  269.4 1.4 fusion.5
  270.8 0.9 copy-done.1
  272.2 1.2 broadcast_select_fusion
  273.4 2.9 collective-permute-start.22
  276.3 17.7 %collective-permute-done.22 = bf16[256]{0:T(256)(128)(2,1)S(1)} collective-permute-done((bf16[256]{0:T(256)(128)(2,1)S(1)}, bf16[256]{0:T(256)(128)(2,1)S(1)}, u32[]{:S(2)}, u32[]{:S(2)}) %collective-permute-start.22) | collective-permute-done | bytes 544 | tf_op jit(solution)/shard_map/ppermute | solution.py:8
  294.8 1.9 fusion.38
  296.7 4.2 %fusion.3 = (bf16[1,1792,3,128]{3,1,2,0:T(8,128)(2,1)}, bf16[1792,3,128]{2,0,1:T(8,128)(2,1)S(1)}) fusion(bf16[1792,3,128]{2,0,1:T(8,128)(2,1)} %collective-permute-done.23, bf16[1,1792,3,128]{3,1,2,0:T(8,128)(2,1)} %collective-permute-done.20, bf16[1,1792,3,128]{3,1,2,0:T(8,128)(2,1)} %param.14, pred[]{:T(512)S(6)} %eq.180, ...), kind=kLoop, calls=%fused_computation.26 | loop fusion | flops 8257536 | bytes 9633794 | tf_op jit(solution)/shard_map/convert_element_type | solution.py:189
  300.8 3.2 %multiply_bitcast_fusion = f32[1,1792,3,128]{3,1,2,0:T(8,128)} fusion(bf16[1792,3,128]{2,0,1:T(8,128)(2,1)} %collective-permute-done.23, bf16[1792,3,128]{2,0,1:T(8,128)(2,1)S(1)} %get-tuple-element.27), kind=kLoop, calls=%fused_computation.30 | loop fusion | flops 2752512 | bytes 5505024 | tf_op jit(solution)/shard_map/broadcast_in_dim | solution.py:185
  304.1 3.7 %fusion.4 = bf16[1,1792,3,128]{3,1,2,0:T(8,128)(2,1)} fusion(bf16[1792,3,128]{2,0,1:T(8,128)(2,1)} %collective-permute-done.23, bf16[1792,3,128]{2,0,1:T(8,128)(2,1)S(1)} %get-tuple-element.27, bf16[1,1792,3,128]{3,1,2,0:T(8,128)(2,1)} %collective-permute-done.19, bf16[1,1792,3,128]{3,1,2,0:T(8,128)(2,1)} %param.13, pred[]{:T(512)S(6)} %eq.180), kind=kLoop, calls=%fused_computation.28 | loop fusion | flops 6193152 | bytes 6881281 | tf_op jit(solution)/shard_map/convert_element_type | solution.py:188
  (111 shorter events, 13.8 us)
Async XLA Ops:
  0.6 13.1 %collective-permute-start.1 = (f32[32,8]{0,1:T(8,128)}, f32[32,8]{0,1:T(8,128)S(1)}, u32[]{:S(2)}, u32[]{:S(2)}) collective-permute-start(f32[32,8]{0,1:T(8,128)} %param.11), channel_id=1, source_target_pairs={{0,8},{1,9},{2,10},{3,11},{4,12},{5,13},{6,14},{7,15},{8,0},{9,1},... | collective-permute-start | bytes 3080 | tf_op jit(solution)/shard_map/ppermute | solution.py:8
  3.3 10.1 %collective-permute-start = (s32[32,8]{0,1:T(8,128)}, s32[32,8]{0,1:T(8,128)S(1)}, u32[]{:S(2)}, u32[]{:S(2)}) collective-permute-start(s32[32,8]{0,1:T(8,128)} %param.10), channel_id=1, source_target_pairs={{0,8},{1,9},{2,10},{3,11},{4,12},{5,13},{6,14},{7,15},{8,0},{9,1},... | collective-permute-start | bytes 3080 | tf_op jit(solution)/shard_map/ppermute | solution.py:8
  5.5 53.1 %collective-permute-start.2 = (bf16[32,7168]{1,0:T(8,128)(2,1)S(1)}, bf16[32,7168]{1,0:T(8,128)(2,1)S(1)}, u32[]{:S(2)}, u32[]{:S(2)}) collective-permute-start(bf16[32,7168]{1,0:T(8,128)(2,1)S(1)} %constant_dynamic-update-slice_fusion.1), channel_id=1, source_target_pairs={{0,8},{1,9},{2,10},{3,11},{4,12},{5,13},{6,14},{7,15},{8,0},{9,1},... | collective-permute-start | bytes 1376264 | tf_op jit(solution)/shard_map/ppermute | solution.py:8
  8.2 116.5 %collective-permute-start.10 = (bf16[1,1792,3,128]{3,1,2,0:T(8,128)(2,1)}, bf16[1,1792,3,128]{3,1,2,0:T(8,128)(2,1)S(1)}, u32[]{:S(2)}, u32[]{:S(2)}) collective-permute-start(bf16[1,1792,3,128]{3,1,2,0:T(8,128)(2,1)} %param.12), channel_id=1, source_target_pairs={{0,8},{1,9},{2,10},{3,11},{4,12},{5,13},{6,14},{7,15},{8,0},{9,1},... | collective-permute-start | bytes 4128776 | tf_op jit(solution)/shard_map/ppermute | solution.py:8
  61.3 16.2 %collective-permute-start.3 = (bf16[40,7296]{1,0:T(8,128)(2,1)S(1)}, bf16[40,7296]{1,0:T(8,128)(2,1)S(1)}, u32[]{:S(2)}, u32[]{:S(2)}) collective-permute-start(bf16[40,7296]{1,0:T(8,128)(2,1)S(1)} %get-tuple-element.31), channel_id=1, source_target_pairs={{0,1},{1,0},{2,3},{3,2},{4,5},{5,4},{6,7},{7,6},{8,9},{9,8},{10,11... | collective-permute-start | bytes 1751048 | tf_op jit(solution)/shard_map/ppermute | solution.py:48
  61.9 25.4 %collective-permute-start.4 = (bf16[40,7296]{1,0:T(8,128)(2,1)S(1)}, bf16[40,7296]{1,0:T(8,128)(2,1)S(1)}, u32[]{:S(2)}, u32[]{:S(2)}) collective-permute-start(bf16[40,7296]{1,0:T(8,128)(2,1)S(1)} %get-tuple-element.32), channel_id=1, source_target_pairs={{0,2},{1,3},{2,0},{3,1},{4,6},{5,7},{6,4},{7,5},{8,10},{9,11},{10,... | collective-permute-start | bytes 1751048 | tf_op jit(solution)/shard_map/ppermute | solution.py:48
  62.4 25.0 %collective-permute-start.5 = (bf16[40,7296]{1,0:T(8,128)(2,1)S(1)}, bf16[40,7296]{1,0:T(8,128)(2,1)S(1)}, u32[]{:S(2)}, u32[]{:S(2)}) collective-permute-start(bf16[40,7296]{1,0:T(8,128)(2,1)S(1)} %get-tuple-element.33), channel_id=1, source_target_pairs={{0,3},{1,2},{2,1},{3,0},{4,7},{5,6},{6,5},{7,4},{8,11},{9,10},{10,... | collective-permute-start | bytes 1751048 | tf_op jit(solution)/shard_map/ppermute | solution.py:48
  64.9 43.9 %collective-permute-start.6 = (bf16[40,7296]{1,0:T(8,128)(2,1)S(1)}, bf16[40,7296]{1,0:T(8,128)(2,1)S(1)}, u32[]{:S(2)}, u32[]{:S(2)}) collective-permute-start(bf16[40,7296]{1,0:T(8,128)(2,1)S(1)} %get-tuple-element.34), channel_id=1, source_target_pairs={{0,4},{1,5},{2,6},{3,7},{4,0},{5,1},{6,2},{7,3},{8,12},{9,13},{10,... | collective-permute-start | bytes 1751048 | tf_op jit(solution)/shard_map/ppermute | solution.py:48
  77.5 34.6 %collective-permute-start.7 = (bf16[40,7296]{1,0:T(8,128)(2,1)S(1)}, bf16[40,7296]{1,0:T(8,128)(2,1)S(1)}, u32[]{:S(2)}, u32[]{:S(2)}) collective-permute-start(bf16[40,7296]{1,0:T(8,128)(2,1)S(1)} %get-tuple-element.35), channel_id=1, source_target_pairs={{0,5},{1,4},{2,7},{3,6},{4,1},{5,0},{6,3},{7,2},{8,13},{9,12},{10,... | collective-permute-start | bytes 1751048 | tf_op jit(solution)/shard_map/ppermute | solution.py:48
  87.3 37.4 %collective-permute-start.8 = (bf16[40,7296]{1,0:T(8,128)(2,1)S(1)}, bf16[40,7296]{1,0:T(8,128)(2,1)S(1)}, u32[]{:S(2)}, u32[]{:S(2)}) collective-permute-start(bf16[40,7296]{1,0:T(8,128)(2,1)S(1)} %get-tuple-element.36), channel_id=1, source_target_pairs={{0,6},{1,7},{2,4},{3,5},{4,2},{5,3},{6,0},{7,1},{8,14},{9,15},{10,... | collective-permute-start | bytes 1751048 | tf_op jit(solution)/shard_map/ppermute | solution.py:48
  87.4 37.4 %copy-start.2 = (bf16[1,1792,3,128]{3,1,2,0:T(8,128)(2,1)S(1)}, bf16[1,1792,3,128]{3,1,2,0:T(8,128)(2,1)}, u32[]{:S(2)}) copy-start(bf16[1,1792,3,128]{3,1,2,0:T(8,128)(2,1)} %param.12) | copy-start | bytes 4128772
  87.4 49.7 %collective-permute-start.9 = (bf16[40,7296]{1,0:T(8,128)(2,1)S(1)}, bf16[40,7296]{1,0:T(8,128)(2,1)S(1)}, u32[]{:S(2)}, u32[]{:S(2)}) collective-permute-start(bf16[40,7296]{1,0:T(8,128)(2,1)S(1)} %get-tuple-element.30), channel_id=1, source_target_pairs={{0,7},{1,6},{2,5},{3,4},{4,3},{5,2},{6,1},{7,0},{8,15},{9,14},{10,... | collective-permute-start | bytes 1751048 | tf_op jit(solution)/shard_map/ppermute | solution.py:48
  124.9 17.6 %copy-start = (bf16[1,1792,3,128]{3,1,2,0:T(8,128)(2,1)}, bf16[1,1792,3,128]{3,1,2,0:T(8,128)(2,1)S(1)}, u32[]{:S(2)}) copy-start(bf16[1,1792,3,128]{3,1,2,0:T(8,128)(2,1)S(1)} %broadcast_select_fusion.2) | copy-start | bytes 4128772
  124.9 17.4 %collective-permute-start.11 = (bf16[1,1792,3,128]{3,1,2,0:T(8,128)(2,1)S(1)}, bf16[1,1792,3,128]{3,1,2,0:T(8,128)(2,1)S(1)}, u32[]{:S(2)}, u32[]{:S(2)}) collective-permute-start(bf16[1,1792,3,128]{3,1,2,0:T(8,128)(2,1)S(1)} %broadcast_select_fusion.2), channel_id=1, source_target_pairs={{0,16},{16,0},{1,17},{17,1},{2,18},{18,2},{3,19},{19,3},{4,20},{20... | collective-permute-start | bytes 4128776 | tf_op jit(solution)/shard_map/ppermute | solution.py:139
  137.1 2.1 copy-start.3
  139.3 132.7 %collective-permute-start.19 = (bf16[1,1792,3,128]{3,1,2,0:T(8,128)(2,1)}, bf16[1,1792,3,128]{3,1,2,0:T(8,128)(2,1)}, u32[]{:S(2)}, u32[]{:S(2)}) collective-permute-start(bf16[1,1792,3,128]{3,1,2,0:T(8,128)(2,1)} %param.13), channel_id=1, source_target_pairs={{0,8},{1,9},{2,10},{3,11},{4,12},{5,13},{6,14},{7,15},{8,0},{9,1},... | collective-permute-start | bytes 4128776 | tf_op jit(solution)/shard_map/ppermute | solution.py:8
  141.0 131.1 %collective-permute-start.20 = (bf16[1,1792,3,128]{3,1,2,0:T(8,128)(2,1)}, bf16[1,1792,3,128]{3,1,2,0:T(8,128)(2,1)}, u32[]{:S(2)}, u32[]{:S(2)}) collective-permute-start(bf16[1,1792,3,128]{3,1,2,0:T(8,128)(2,1)} %param.14), channel_id=1, source_target_pairs={{0,8},{1,9},{2,10},{3,11},{4,12},{5,13},{6,14},{7,15},{8,0},{9,1},... | collective-permute-start | bytes 4128776 | tf_op jit(solution)/shard_map/ppermute | solution.py:8
  142.5 2.3 copy-start.4
  152.3 10.1 %collective-permute-start.12 = (bf16[40,3712]{1,0:T(8,128)(2,1)S(1)}, bf16[40,3712]{1,0:T(8,128)(2,1)S(1)}, u32[]{:S(2)}, u32[]{:S(2)}) collective-permute-start(bf16[40,3712]{1,0:T(8,128)(2,1)S(1)} %get-tuple-element.42), channel_id=1, source_target_pairs={{0,1},{1,0},{2,3},{3,2},{4,5},{5,4},{6,7},{7,6},{8,9},{9,8},{10,11... | collective-permute-start | bytes 890888 | tf_op jit(solution)/shard_map/ppermute | solution.py:48
  153.9 13.5 %collective-permute-start.13 = (bf16[40,3712]{1,0:T(8,128)(2,1)S(1)}, bf16[40,3712]{1,0:T(8,128)(2,1)S(1)}, u32[]{:S(2)}, u32[]{:S(2)}) collective-permute-start(bf16[40,3712]{1,0:T(8,128)(2,1)S(1)} %get-tuple-element.43), channel_id=1, source_target_pairs={{0,2},{1,3},{2,0},{3,1},{4,6},{5,7},{6,4},{7,5},{8,10},{9,11},{10,... | collective-permute-start | bytes 890888 | tf_op jit(solution)/shard_map/ppermute | solution.py:48
  155.4 14.7 %collective-permute-start.14 = (bf16[40,3712]{1,0:T(8,128)(2,1)S(1)}, bf16[40,3712]{1,0:T(8,128)(2,1)S(1)}, u32[]{:S(2)}, u32[]{:S(2)}) collective-permute-start(bf16[40,3712]{1,0:T(8,128)(2,1)S(1)} %get-tuple-element.44), channel_id=1, source_target_pairs={{0,3},{1,2},{2,1},{3,0},{4,7},{5,6},{6,5},{7,4},{8,11},{9,10},{10,... | collective-permute-start | bytes 890888 | tf_op jit(solution)/shard_map/ppermute | solution.py:48
  162.4 45.2 %collective-permute-start.15 = (bf16[40,3712]{1,0:T(8,128)(2,1)S(1)}, bf16[40,3712]{1,0:T(8,128)(2,1)S(1)}, u32[]{:S(2)}, u32[]{:S(2)}) collective-permute-start(bf16[40,3712]{1,0:T(8,128)(2,1)S(1)} %get-tuple-element.45), channel_id=1, source_target_pairs={{0,4},{1,5},{2,6},{3,7},{4,0},{5,1},{6,2},{7,3},{8,12},{9,13},{10,... | collective-permute-start | bytes 890888 | tf_op jit(solution)/shard_map/ppermute | solution.py:48
  167.4 46.6 %collective-permute-start.16 = (bf16[40,3712]{1,0:T(8,128)(2,1)S(1)}, bf16[40,3712]{1,0:T(8,128)(2,1)S(1)}, u32[]{:S(2)}, u32[]{:S(2)}) collective-permute-start(bf16[40,3712]{1,0:T(8,128)(2,1)S(1)} %get-tuple-element.46), channel_id=1, source_target_pairs={{0,5},{1,4},{2,7},{3,6},{4,1},{5,0},{6,3},{7,2},{8,13},{9,12},{10,... | collective-permute-start | bytes 890888 | tf_op jit(solution)/shard_map/ppermute | solution.py:48
  170.1 50.3 %collective-permute-start.17 = (bf16[40,3712]{1,0:T(8,128)(2,1)S(1)}, bf16[40,3712]{1,0:T(8,128)(2,1)S(1)}, u32[]{:S(2)}, u32[]{:S(2)}) collective-permute-start(bf16[40,3712]{1,0:T(8,128)(2,1)S(1)} %get-tuple-element.47), channel_id=1, source_target_pairs={{0,6},{1,7},{2,4},{3,5},{4,2},{5,3},{6,0},{7,1},{8,14},{9,15},{10,... | collective-permute-start | bytes 890888 | tf_op jit(solution)/shard_map/ppermute | solution.py:48
  207.6 61.7 %collective-permute-start.18 = (bf16[40,3712]{1,0:T(8,128)(2,1)S(1)}, bf16[40,3712]{1,0:T(8,128)(2,1)S(1)}, u32[]{:S(2)}, u32[]{:S(2)}) collective-permute-start(bf16[40,3712]{1,0:T(8,128)(2,1)S(1)} %get-tuple-element.41), channel_id=1, source_target_pairs={{0,7},{1,6},{2,5},{3,4},{4,3},{5,2},{6,1},{7,0},{8,15},{9,14},{10,... | collective-permute-start | bytes 890888 | tf_op jit(solution)/shard_map/ppermute | solution.py:48
  270.8 0.9 copy-start.1
  272.1 22.7 %collective-permute-start.21 = (f32[32,3584]{1,0:T(8,128)S(1)}, f32[32,3584]{1,0:T(8,128)}, u32[]{:S(2)}, u32[]{:S(2)}) collective-permute-start(f32[32,3584]{1,0:T(8,128)S(1)} %slice.203), channel_id=1, source_target_pairs={{0,8},{1,9},{2,10},{3,11},{4,12},{5,13},{6,14},{7,15},{8,0},{9,1},... | collective-permute-start | bytes 1376264 | tf_op jit(solution)/shard_map/ppermute | solution.py:8
  273.4 23.3 %collective-permute-start.23 = (bf16[1792,3,128]{2,0,1:T(8,128)(2,1)}, bf16[1792,3,128]{2,0,1:T(8,128)(2,1)}, u32[]{:S(2)}, u32[]{:S(2)}) collective-permute-start(bf16[1792,3,128]{2,0,1:T(8,128)(2,1)} %broadcast_select_fusion), channel_id=1, source_target_pairs={{0,16},{16,0},{1,17},{17,1},{2,18},{18,2},{3,19},{19,3},{4,20},{20... | collective-permute-start | bytes 4128776 | tf_op jit(solution)/shard_map/ppermute | solution.py:179
  273.4 20.6 %collective-permute-start.22 = (bf16[256]{0:T(256)(128)(2,1)S(1)}, bf16[256]{0:T(256)(128)(2,1)S(1)}, u32[]{:S(2)}, u32[]{:S(2)}) collective-permute-start(bf16[256]{0:T(256)(128)(2,1)S(1)} %slice.160), channel_id=1, source_target_pairs={{0,8},{1,9},{2,10},{3,11},{4,12},{5,13},{6,14},{7,15},{8,0},{9,1},... | collective-permute-start | bytes 1544 | tf_op jit(solution)/shard_map/ppermute | solution.py:8

commit v6 on v5

--- a/solution.py
+++ b/solution.py
@@ -204,10 +204,9 @@
             preferred_element_type=jnp.float32,
         )
         prob2 = jnp.sum(jnp.where(slot_hit, back_gate[:, None], 0.0), axis=0)
-        send_partial, send_prob, _ = lax.optimization_barrier(
-            (partial[tok_rows:], prob2[entry_count:].astype(jnp.bfloat16), their_moments)
-        )
-        p_partial, p_prob = from_partner((send_partial, send_prob), "expert", swap_bit)
+        p_partial, p_prob = from_partner(
+            (partial[tok_rows:], prob2[entry_count:].astype(jnp.bfloat16)), "expert", swap_bit
+        )
         token_grad = (partial[:tok_rows] + p_partial).astype(jnp.bfloat16)
         prob_grad = jnp.where(
             in_half[:entry_count], prob2[:entry_count], p_prob.astype(jnp.float32)

time: 311 us -> 301 us (0.968)
  waiting for transfers between devices: 215 us -> 202 us
  starting transfers between devices: 46.6 us -> 51.2 us
    ppermute x14, waiting for transfers between devices: 157 us -> 94.5 us  [xor_permute(): lax.ppermute(value, 'expert', [(i, i ^ mask) for i in range(lax.axis_size...]
    ppermute x8, waiting for transfers between devices: 58.2 us -> 107 us  [from_partner(): lax.ppermute(value, axis, [(i, i ^ 1 << bit) for i in range(lax.axis_size...]
    ppermute x14, starting transfers between devices: 34.6 us -> 40.5 us  [xor_permute(): lax.ppermute(value, 'expert', [(i, i ^ mask) for i in range(lax.axis_size...]
    unnamed x28 -> x30, local copies, waits for them, and re-layouts: 8.19 us -> 8.19 us
  transfers between devices with their start and end apart: 24 -> 24, of which waited for: 14 -> 14; matrix products, arithmetic and copies ran while one was open for 9% -> 12% of each run, Pallas kernels for 0% -> 0%
where the time goes in v6:
time: 301 us; the launch traced here: 300 us
  waiting for transfers between devices  202 us (67%)
  starting transfers between devices  51.2 us (17%)
  other arithmetic  22.7 us (8%)
  local copies, waits for them, and re-layouts  12 us (4%)
  matrix products  9.85 us (3%)
    ppermute x8, waiting for transfers between devices, from_partner(): lax.ppermute(value, axis, [(i, i ^ 1 << bit) for i in range(lax.axis_size...  107 us
    ppermute x14, waiting for transfers between devices, xor_permute(): lax.ppermute(value, 'expert', [(i, i ^ mask) for i in range(lax.axis_size...  94.5 us
    ppermute x14, starting transfers between devices, xor_permute(): lax.ppermute(value, 'expert', [(i, i ^ mask) for i in range(lax.axis_size...  40.5 us
    ppermute x8, starting transfers between devices, from_partner(): lax.ppermute(value, axis, [(i, i ^ 1 << bit) for i in range(lax.axis_size...  10.7 us
    unnamed x30, local copies, waits for them, and re-layouts  8.19 us
  transfers between devices with their start and end apart: 24, of which 14 were waited for; matrix products, arithmetic and copies ran while one was open for 12% of the time, Pallas kernels for 0%

profile of v6, /device:TPU:6, one launch (start us, length us, event | category | flops | bytes accessed | tf_op | source)
XLA Modules:
  0.0 299.5 jit_solution(18371248215500378855)
XLA Ops:
  0.6 2.7 collective-permute-start.1
  3.6 1.0 constant_dynamic-update-slice_fusion.2
  4.6 1.0 constant_dynamic-update-slice_fusion.1
  5.5 2.7 collective-permute-start.2
  10.5 1.3 fusion.85
  13.8 0.8 pad_maximum_fusion.3
  18.1 40.5 %collective-permute-done.2 = bf16[32,7168]{1,0:T(8,128)(2,1)S(1)} collective-permute-done((bf16[32,7168]{1,0:T(8,128)(2,1)S(1)}, bf16[32,7168]{1,0:T(8,128)(2,1)S(1)}, u32[]{:S(2)}, u32[]{:S(2)}) %collective-permute-start.2) | collective-permute-done | bytes 458784 | tf_op jit(solution)/shard_map/ppermute | solution.py:8
  58.6 1.4 convolution_convert_fusion
  60.0 1.3 pad_maximum_fusion.1
  62.4 2.5 collective-permute-start.5
  64.9 12.6 %collective-permute-done.3 = bf16[40,7296]{1,0:T(8,128)(2,1)S(1)} collective-permute-done((bf16[40,7296]{1,0:T(8,128)(2,1)S(1)}, bf16[40,7296]{1,0:T(8,128)(2,1)S(1)}, u32[]{:S(2)}, u32[]{:S(2)}) %collective-permute-start.3) | collective-permute-done | bytes 583712 | tf_op jit(solution)/shard_map/ppermute | solution.py:48
  77.6 9.7 %collective-permute-done.4 = bf16[40,7296]{1,0:T(8,128)(2,1)S(1)} collective-permute-done((bf16[40,7296]{1,0:T(8,128)(2,1)S(1)}, bf16[40,7296]{1,0:T(8,128)(2,1)S(1)}, u32[]{:S(2)}, u32[]{:S(2)}) %collective-permute-start.4) | collective-permute-done | bytes 583712 | tf_op jit(solution)/shard_map/ppermute | solution.py:48
  87.4 21.3 %collective-permute-start.9 = (bf16[40,7296]{1,0:T(8,128)(2,1)S(1)}, bf16[40,7296]{1,0:T(8,128)(2,1)S(1)}, u32[]{:S(2)}, u32[]{:S(2)}) collective-permute-start(bf16[40,7296]{1,0:T(8,128)(2,1)S(1)} %get-tuple-element.26), channel_id=1, source_target_pairs={{0,7},{1,6},{2,5},{3,4},{4,3},{5,2},{6,1},{7,0},{8,15},{9,14},{10,... | collective-permute-start | bytes 1751048 | tf_op jit(solution)/shard_map/ppermute | solution.py:48
  108.8 3.3 %collective-permute-done.7 = bf16[40,7296]{1,0:T(8,128)(2,1)S(1)} collective-permute-done((bf16[40,7296]{1,0:T(8,128)(2,1)S(1)}, bf16[40,7296]{1,0:T(8,128)(2,1)S(1)}, u32[]{:S(2)}, u32[]{:S(2)}) %collective-permute-start.7) | collective-permute-done | bytes 583712 | tf_op jit(solution)/shard_map/ppermute | solution.py:48
  112.2 12.4 %collective-permute-done.8 = bf16[40,7296]{1,0:T(8,128)(2,1)S(1)} collective-permute-done((bf16[40,7296]{1,0:T(8,128)(2,1)S(1)}, bf16[40,7296]{1,0:T(8,128)(2,1)S(1)}, u32[]{:S(2)}, u32[]{:S(2)}) %collective-permute-start.8) | collective-permute-done | bytes 583712 | tf_op jit(solution)/shard_map/ppermute | solution.py:48
  125.0 12.0 %collective-permute-done.9 = bf16[40,7296]{1,0:T(8,128)(2,1)S(1)} collective-permute-done((bf16[40,7296]{1,0:T(8,128)(2,1)S(1)}, bf16[40,7296]{1,0:T(8,128)(2,1)S(1)}, u32[]{:S(2)}, u32[]{:S(2)}) %collective-permute-start.9) | collective-permute-done | bytes 583712 | tf_op jit(solution)/shard_map/ppermute | solution.py:48
  137.1 2.1 copy-done.4
  139.3 1.6 collective-permute-start.23
  141.4 2.1 copy-done.5
  144.4 0.8 fusion.27
  145.2 0.8 multiply_convert_fusion.5
  146.0 0.9 fusion.21
  146.8 1.1 fusion.2
  148.1 1.0 fusion.1
  149.0 1.0 fusion
  150.0 0.8 convolution_convert_fusion.1
  151.6 0.9 collective-permute-start.13
  152.5 2.0 collective-permute-start.14
  154.5 2.4 collective-permute-start.15
  157.3 1.2 broadcast_select_fusion
  158.5 2.5 collective-permute-done.12
  161.0 3.3 %collective-permute-start.16 = (bf16[40,3712]{1,0:T(8,128)(2,1)S(1)}, bf16[40,3712]{1,0:T(8,128)(2,1)S(1)}, u32[]{:S(2)}, u32[]{:S(2)}) collective-permute-start(bf16[40,3712]{1,0:T(8,128)(2,1)S(1)} %get-tuple-element.42), channel_id=1, source_target_pairs={{0,5},{1,4},{2,7},{3,6},{4,1},{5,0},{6,3},{7,2},{8,13},{9,12},{10,... | collective-permute-start | bytes 890888 | tf_op jit(solution)/shard_map/ppermute | solution.py:48
  164.4 6.3 %collective-permute-start.17 = (bf16[40,3712]{1,0:T(8,128)(2,1)S(1)}, bf16[40,3712]{1,0:T(8,128)(2,1)S(1)}, u32[]{:S(2)}, u32[]{:S(2)}) collective-permute-start(bf16[40,3712]{1,0:T(8,128)(2,1)S(1)} %get-tuple-element.43), channel_id=1, source_target_pairs={{0,6},{1,7},{2,4},{3,5},{4,2},{5,3},{6,0},{7,1},{8,14},{9,15},{10,... | collective-permute-start | bytes 890888 | tf_op jit(solution)/shard_map/ppermute | solution.py:48
  170.7 0.9 collective-permute-done.14
  171.6 6.5 %collective-permute-done.15 = bf16[40,3712]{1,0:T(8,128)(2,1)S(1)} collective-permute-done((bf16[40,3712]{1,0:T(8,128)(2,1)S(1)}, bf16[40,3712]{1,0:T(8,128)(2,1)S(1)}, u32[]{:S(2)}, u32[]{:S(2)}) %collective-permute-start.15) | collective-permute-done | bytes 296992 | tf_op jit(solution)/shard_map/ppermute | solution.py:48
  178.2 6.3 %collective-permute-done.16 = bf16[40,3712]{1,0:T(8,128)(2,1)S(1)} collective-permute-done((bf16[40,3712]{1,0:T(8,128)(2,1)S(1)}, bf16[40,3712]{1,0:T(8,128)(2,1)S(1)}, u32[]{:S(2)}, u32[]{:S(2)}) %collective-permute-start.16) | collective-permute-done | bytes 296992 | tf_op jit(solution)/shard_map/ppermute | solution.py:48
  184.5 22.8 %collective-permute-done.17 = bf16[40,3712]{1,0:T(8,128)(2,1)S(1)} collective-permute-done((bf16[40,3712]{1,0:T(8,128)(2,1)S(1)}, bf16[40,3712]{1,0:T(8,128)(2,1)S(1)}, u32[]{:S(2)}, u32[]{:S(2)}) %collective-permute-start.17) | collective-permute-done | bytes 296992 | tf_op jit(solution)/shard_map/ppermute | solution.py:48
  207.4 5.3 %collective-permute-done.18 = bf16[40,3712]{1,0:T(8,128)(2,1)S(1)} collective-permute-done((bf16[40,3712]{1,0:T(8,128)(2,1)S(1)}, bf16[40,3712]{1,0:T(8,128)(2,1)S(1)}, u32[]{:S(2)}, u32[]{:S(2)}) %collective-permute-start.18) | collective-permute-done | bytes 296992 | tf_op jit(solution)/shard_map/ppermute | solution.py:48
  212.7 1.4 fusion.5
  214.1 0.9 copy-done.1
  215.0 0.8 slice.203
  216.2 3.0 collective-permute-start.20
  219.3 47.5 %collective-permute-done.20 = bf16[256]{0:T(256)(128)(2,1)S(1)} collective-permute-done((bf16[256]{0:T(256)(128)(2,1)S(1)}, bf16[256]{0:T(256)(128)(2,1)S(1)}, u32[]{:S(2)}, u32[]{:S(2)}) %collective-permute-start.20) | collective-permute-done | bytes 544 | tf_op jit(solution)/shard_map/ppermute | solution.py:8
  267.6 1.8 fusion.38
  269.3 4.2 %fusion.3 = (bf16[1,1792,3,128]{3,1,2,0:T(8,128)(2,1)}, bf16[1792,3,128]{2,0,1:T(8,128)(2,1)S(1)}) fusion(bf16[1792,3,128]{2,0,1:T(8,128)(2,1)} %collective-permute-done.21, bf16[1,1792,3,128]{3,1,2,0:T(8,128)(2,1)} %collective-permute-done.23, bf16[1,1792,3,128]{3,1,2,0:T(8,128)(2,1)} %param.14, pred[]{:T(512)S(6)} %eq.180, ...), kind=kLoop, calls=%fused_computation.26 | loop fusion | flops 8257536 | bytes 9633794 | tf_op jit(solution)/shard_map/convert_element_type | solution.py:189
  273.5 3.3 %multiply_bitcast_fusion = f32[1,1792,3,128]{3,1,2,0:T(8,128)} fusion(bf16[1792,3,128]{2,0,1:T(8,128)(2,1)} %collective-permute-done.21, bf16[1792,3,128]{2,0,1:T(8,128)(2,1)S(1)} %get-tuple-element.23), kind=kLoop, calls=%fused_computation.30 | loop fusion | flops 2752512 | bytes 5505024 | tf_op jit(solution)/shard_map/broadcast_in_dim | solution.py:185
  276.8 19.4 %collective-permute-done.22 = bf16[1,1792,3,128]{3,1,2,0:T(8,128)(2,1)} collective-permute-done((bf16[1,1792,3,128]{3,1,2,0:T(8,128)(2,1)}, bf16[1,1792,3,128]{3,1,2,0:T(8,128)(2,1)}, u32[]{:S(2)}, u32[]{:S(2)}) %collective-permute-start.22) | collective-permute-done | bytes 1376288 | tf_op jit(solution)/shard_map/ppermute | solution.py:8
  296.2 3.3 %fusion.4 = bf16[1,1792,3,128]{3,1,2,0:T(8,128)(2,1)} fusion(bf16[1792,3,128]{2,0,1:T(8,128)(2,1)} %collective-permute-done.21, bf16[1792,3,128]{2,0,1:T(8,128)(2,1)S(1)} %get-tuple-element.23, bf16[1,1792,3,128]{3,1,2,0:T(8,128)(2,1)} %collective-permute-done.22, bf16[1,1792,3,128]{3,1,2,0:T(8,128)(2,1)S(1)} %copy-done.3, pred[]{:T(512)S(6)} %eq.180), kind=kLoop, calls=%fused_computation.28 | loop fusion | flops 6193152 | bytes 6881281 | tf_op jit(solution)/shard_map/convert_element_type | solution.py:188
  (113 shorter events, 13.1 us)
Async XLA Ops:
  0.6 13.1 %collective-permute-start.1 = (f32[32,8]{0,1:T(8,128)}, f32[32,8]{0,1:T(8,128)S(1)}, u32[]{:S(2)}, u32[]{:S(2)}) collective-permute-start(f32[32,8]{0,1:T(8,128)} %param.11), channel_id=1, source_target_pairs={{0,8},{1,9},{2,10},{3,11},{4,12},{5,13},{6,14},{7,15},{8,0},{9,1},... | collective-permute-start | bytes 3080 | tf_op jit(solution)/shard_map/ppermute | solution.py:8
  3.3 10.1 %collective-permute-start = (s32[32,8]{0,1:T(8,128)}, s32[32,8]{0,1:T(8,128)S(1)}, u32[]{:S(2)}, u32[]{:S(2)}) collective-permute-start(s32[32,8]{0,1:T(8,128)} %param.10), channel_id=1, source_target_pairs={{0,8},{1,9},{2,10},{3,11},{4,12},{5,13},{6,14},{7,15},{8,0},{9,1},... | collective-permute-start | bytes 3080 | tf_op jit(solution)/shard_map/ppermute | solution.py:8
  5.5 53.1 %collective-permute-start.2 = (bf16[32,7168]{1,0:T(8,128)(2,1)S(1)}, bf16[32,7168]{1,0:T(8,128)(2,1)S(1)}, u32[]{:S(2)}, u32[]{:S(2)}) collective-permute-start(bf16[32,7168]{1,0:T(8,128)(2,1)S(1)} %constant_dynamic-update-slice_fusion.1), channel_id=1, source_target_pairs={{0,8},{1,9},{2,10},{3,11},{4,12},{5,13},{6,14},{7,15},{8,0},{9,1},... | collective-permute-start | bytes 1376264 | tf_op jit(solution)/shard_map/ppermute | solution.py:8
  8.2 116.5 %collective-permute-start.10 = (bf16[1,1792,3,128]{3,1,2,0:T(8,128)(2,1)}, bf16[1,1792,3,128]{3,1,2,0:T(8,128)(2,1)S(1)}, u32[]{:S(2)}, u32[]{:S(2)}) collective-permute-start(bf16[1,1792,3,128]{3,1,2,0:T(8,128)(2,1)} %param.12), channel_id=1, source_target_pairs={{0,8},{1,9},{2,10},{3,11},{4,12},{5,13},{6,14},{7,15},{8,0},{9,1},... | collective-permute-start | bytes 4128776 | tf_op jit(solution)/shard_map/ppermute | solution.py:8
  61.3 16.2 %collective-permute-start.3 = (bf16[40,7296]{1,0:T(8,128)(2,1)S(1)}, bf16[40,7296]{1,0:T(8,128)(2,1)S(1)}, u32[]{:S(2)}, u32[]{:S(2)}) collective-permute-start(bf16[40,7296]{1,0:T(8,128)(2,1)S(1)} %get-tuple-element.27), channel_id=1, source_target_pairs={{0,1},{1,0},{2,3},{3,2},{4,5},{5,4},{6,7},{7,6},{8,9},{9,8},{10,11... | collective-permute-start | bytes 1751048 | tf_op jit(solution)/shard_map/ppermute | solution.py:48
  61.9 25.4 %collective-permute-start.4 = (bf16[40,7296]{1,0:T(8,128)(2,1)S(1)}, bf16[40,7296]{1,0:T(8,128)(2,1)S(1)}, u32[]{:S(2)}, u32[]{:S(2)}) collective-permute-start(bf16[40,7296]{1,0:T(8,128)(2,1)S(1)} %get-tuple-element.28), channel_id=1, source_target_pairs={{0,2},{1,3},{2,0},{3,1},{4,6},{5,7},{6,4},{7,5},{8,10},{9,11},{10,... | collective-permute-start | bytes 1751048 | tf_op jit(solution)/shard_map/ppermute | solution.py:48
  62.4 25.0 %collective-permute-start.5 = (bf16[40,7296]{1,0:T(8,128)(2,1)S(1)}, bf16[40,7296]{1,0:T(8,128)(2,1)S(1)}, u32[]{:S(2)}, u32[]{:S(2)}) collective-permute-start(bf16[40,7296]{1,0:T(8,128)(2,1)S(1)} %get-tuple-element.29), channel_id=1, source_target_pairs={{0,3},{1,2},{2,1},{3,0},{4,7},{5,6},{6,5},{7,4},{8,11},{9,10},{10,... | collective-permute-start | bytes 1751048 | tf_op jit(solution)/shard_map/ppermute | solution.py:48
  64.9 43.9 %collective-permute-start.6 = (bf16[40,7296]{1,0:T(8,128)(2,1)S(1)}, bf16[40,7296]{1,0:T(8,128)(2,1)S(1)}, u32[]{:S(2)}, u32[]{:S(2)}) collective-permute-start(bf16[40,7296]{1,0:T(8,128)(2,1)S(1)} %get-tuple-element.30), channel_id=1, source_target_pairs={{0,4},{1,5},{2,6},{3,7},{4,0},{5,1},{6,2},{7,3},{8,12},{9,13},{10,... | collective-permute-start | bytes 1751048 | tf_op jit(solution)/shard_map/ppermute | solution.py:48
  77.5 34.6 %collective-permute-start.7 = (bf16[40,7296]{1,0:T(8,128)(2,1)S(1)}, bf16[40,7296]{1,0:T(8,128)(2,1)S(1)}, u32[]{:S(2)}, u32[]{:S(2)}) collective-permute-start(bf16[40,7296]{1,0:T(8,128)(2,1)S(1)} %get-tuple-element.31), channel_id=1, source_target_pairs={{0,5},{1,4},{2,7},{3,6},{4,1},{5,0},{6,3},{7,2},{8,13},{9,12},{10,... | collective-permute-start | bytes 1751048 | tf_op jit(solution)/shard_map/ppermute | solution.py:48
  87.3 37.4 %collective-permute-start.8 = (bf16[40,7296]{1,0:T(8,128)(2,1)S(1)}, bf16[40,7296]{1,0:T(8,128)(2,1)S(1)}, u32[]{:S(2)}, u32[]{:S(2)}) collective-permute-start(bf16[40,7296]{1,0:T(8,128)(2,1)S(1)} %get-tuple-element.32), channel_id=1, source_target_pairs={{0,6},{1,7},{2,4},{3,5},{4,2},{5,3},{6,0},{7,1},{8,14},{9,15},{10,... | collective-permute-start | bytes 1751048 | tf_op jit(solution)/shard_map/ppermute | solution.py:48
  87.4 37.4 %copy-start.2 = (bf16[1,1792,3,128]{3,1,2,0:T(8,128)(2,1)S(1)}, bf16[1,1792,3,128]{3,1,2,0:T(8,128)(2,1)}, u32[]{:S(2)}) copy-start(bf16[1,1792,3,128]{3,1,2,0:T(8,128)(2,1)} %param.12) | copy-start | bytes 4128772
  87.4 49.7 %collective-permute-start.9 = (bf16[40,7296]{1,0:T(8,128)(2,1)S(1)}, bf16[40,7296]{1,0:T(8,128)(2,1)S(1)}, u32[]{:S(2)}, u32[]{:S(2)}) collective-permute-start(bf16[40,7296]{1,0:T(8,128)(2,1)S(1)} %get-tuple-element.26), channel_id=1, source_target_pairs={{0,7},{1,6},{2,5},{3,4},{4,3},{5,2},{6,1},{7,0},{8,15},{9,14},{10,... | collective-permute-start | bytes 1751048 | tf_op jit(solution)/shard_map/ppermute | solution.py:48
  124.9 16.2 %copy-start = (bf16[1,1792,3,128]{3,1,2,0:T(8,128)(2,1)}, bf16[1,1792,3,128]{3,1,2,0:T(8,128)(2,1)S(1)}, u32[]{:S(2)}) copy-start(bf16[1,1792,3,128]{3,1,2,0:T(8,128)(2,1)S(1)} %broadcast_select_fusion.2) | copy-start | bytes 4128772
  124.9 16.0 %collective-permute-start.11 = (bf16[1,1792,3,128]{3,1,2,0:T(8,128)(2,1)S(1)}, bf16[1,1792,3,128]{3,1,2,0:T(8,128)(2,1)S(1)}, u32[]{:S(2)}, u32[]{:S(2)}) collective-permute-start(bf16[1,1792,3,128]{3,1,2,0:T(8,128)(2,1)S(1)} %broadcast_select_fusion.2), channel_id=1, source_target_pairs={{0,16},{16,0},{1,17},{17,1},{2,18},{18,2},{3,19},{19,3},{4,20},{20... | collective-permute-start | bytes 4128776 | tf_op jit(solution)/shard_map/ppermute | solution.py:139
  137.1 2.1 copy-start.4
  139.3 130.0 %collective-permute-start.23 = (bf16[1,1792,3,128]{3,1,2,0:T(8,128)(2,1)}, bf16[1,1792,3,128]{3,1,2,0:T(8,128)(2,1)}, u32[]{:S(2)}, u32[]{:S(2)}) collective-permute-start(bf16[1,1792,3,128]{3,1,2,0:T(8,128)(2,1)} %param.14), channel_id=1, source_target_pairs={{0,8},{1,9},{2,10},{3,11},{4,12},{5,13},{6,14},{7,15},{8,0},{9,1},... | collective-permute-start | bytes 4128776 | tf_op jit(solution)/shard_map/ppermute | solution.py:8
  141.2 2.3 copy-start.5
  151.0 10.0 %collective-permute-start.12 = (bf16[40,3712]{1,0:T(8,128)(2,1)S(1)}, bf16[40,3712]{1,0:T(8,128)(2,1)S(1)}, u32[]{:S(2)}, u32[]{:S(2)}) collective-permute-start(bf16[40,3712]{1,0:T(8,128)(2,1)S(1)} %get-tuple-element.38), channel_id=1, source_target_pairs={{0,1},{1,0},{2,3},{3,2},{4,5},{5,4},{6,7},{7,6},{8,9},{9,8},{10,11... | collective-permute-start | bytes 890888 | tf_op jit(solution)/shard_map/ppermute | solution.py:48
  151.6 12.8 %collective-permute-start.13 = (bf16[40,3712]{1,0:T(8,128)(2,1)S(1)}, bf16[40,3712]{1,0:T(8,128)(2,1)S(1)}, u32[]{:S(2)}, u32[]{:S(2)}) collective-permute-start(bf16[40,3712]{1,0:T(8,128)(2,1)S(1)} %get-tuple-element.39), channel_id=1, source_target_pairs={{0,2},{1,3},{2,0},{3,1},{4,6},{5,7},{6,4},{7,5},{8,10},{9,11},{10,... | collective-permute-start | bytes 890888 | tf_op jit(solution)/shard_map/ppermute | solution.py:48
  152.5 19.1 %collective-permute-start.14 = (bf16[40,3712]{1,0:T(8,128)(2,1)S(1)}, bf16[40,3712]{1,0:T(8,128)(2,1)S(1)}, u32[]{:S(2)}, u32[]{:S(2)}) collective-permute-start(bf16[40,3712]{1,0:T(8,128)(2,1)S(1)} %get-tuple-element.40), channel_id=1, source_target_pairs={{0,3},{1,2},{2,1},{3,0},{4,7},{5,6},{6,5},{7,4},{8,11},{9,10},{10,... | collective-permute-start | bytes 890888 | tf_op jit(solution)/shard_map/ppermute | solution.py:48
  154.5 23.6 %collective-permute-start.15 = (bf16[40,3712]{1,0:T(8,128)(2,1)S(1)}, bf16[40,3712]{1,0:T(8,128)(2,1)S(1)}, u32[]{:S(2)}, u32[]{:S(2)}) collective-permute-start(bf16[40,3712]{1,0:T(8,128)(2,1)S(1)} %get-tuple-element.41), channel_id=1, source_target_pairs={{0,4},{1,5},{2,6},{3,7},{4,0},{5,1},{6,2},{7,3},{8,12},{9,13},{10,... | collective-permute-start | bytes 890888 | tf_op jit(solution)/shard_map/ppermute | solution.py:48
  161.0 23.5 %collective-permute-start.16 = (bf16[40,3712]{1,0:T(8,128)(2,1)S(1)}, bf16[40,3712]{1,0:T(8,128)(2,1)S(1)}, u32[]{:S(2)}, u32[]{:S(2)}) collective-permute-start(bf16[40,3712]{1,0:T(8,128)(2,1)S(1)} %get-tuple-element.42), channel_id=1, source_target_pairs={{0,5},{1,4},{2,7},{3,6},{4,1},{5,0},{6,3},{7,2},{8,13},{9,12},{10,... | collective-permute-start | bytes 890888 | tf_op jit(solution)/shard_map/ppermute | solution.py:48
  164.4 43.0 %collective-permute-start.17 = (bf16[40,3712]{1,0:T(8,128)(2,1)S(1)}, bf16[40,3712]{1,0:T(8,128)(2,1)S(1)}, u32[]{:S(2)}, u32[]{:S(2)}) collective-permute-start(bf16[40,3712]{1,0:T(8,128)(2,1)S(1)} %get-tuple-element.43), channel_id=1, source_target_pairs={{0,6},{1,7},{2,4},{3,5},{4,2},{5,3},{6,0},{7,1},{8,14},{9,15},{10,... | collective-permute-start | bytes 890888 | tf_op jit(solution)/shard_map/ppermute | solution.py:48
  171.6 41.1 %collective-permute-start.18 = (bf16[40,3712]{1,0:T(8,128)(2,1)S(1)}, bf16[40,3712]{1,0:T(8,128)(2,1)S(1)}, u32[]{:S(2)}, u32[]{:S(2)}) collective-permute-start(bf16[40,3712]{1,0:T(8,128)(2,1)S(1)} %get-tuple-element.37), channel_id=1, source_target_pairs={{0,7},{1,6},{2,5},{3,4},{4,3},{5,2},{6,1},{7,0},{8,15},{9,14},{10,... | collective-permute-start | bytes 890888 | tf_op jit(solution)/shard_map/ppermute | solution.py:48
  178.1 91.2 %collective-permute-start.21 = (bf16[1792,3,128]{2,0,1:T(8,128)(2,1)}, bf16[1792,3,128]{2,0,1:T(8,128)(2,1)}, u32[]{:S(2)}, u32[]{:S(2)}) collective-permute-start(bf16[1792,3,128]{2,0,1:T(8,128)(2,1)} %broadcast_select_fusion), channel_id=1, source_target_pairs={{0,16},{16,0},{1,17},{17,1},{2,18},{18,2},{3,19},{19,3},{4,20},{20... | collective-permute-start | bytes 4128776 | tf_op jit(solution)/shard_map/ppermute | solution.py:179
  214.1 0.9 copy-start.1
  215.8 51.7 %collective-permute-start.19 = (f32[32,3584]{1,0:T(8,128)}, f32[32,3584]{1,0:T(8,128)S(1)}, u32[]{:S(2)}, u32[]{:S(2)}) collective-permute-start(f32[32,3584]{1,0:T(8,128)} %slice.203), channel_id=1, source_target_pairs={{0,8},{1,9},{2,10},{3,11},{4,12},{5,13},{6,14},{7,15},{8,0},{9,1},... | collective-permute-start | bytes 1376264 | tf_op jit(solution)/shard_map/ppermute | solution.py:8
  216.2 50.6 %collective-permute-start.20 = (bf16[256]{0:T(256)(128)(2,1)S(1)}, bf16[256]{0:T(256)(128)(2,1)S(1)}, u32[]{:S(2)}, u32[]{:S(2)}) collective-permute-start(bf16[256]{0:T(256)(128)(2,1)S(1)} %slice.162), channel_id=1, source_target_pairs={{0,8},{1,9},{2,10},{3,11},{4,12},{5,13},{6,14},{7,15},{8,0},{9,1},... | collective-permute-start | bytes 1544 | tf_op jit(solution)/shard_map/ppermute | solution.py:8
  219.2 77.1 %collective-permute-start.22 = (bf16[1,1792,3,128]{3,1,2,0:T(8,128)(2,1)}, bf16[1,1792,3,128]{3,1,2,0:T(8,128)(2,1)}, u32[]{:S(2)}, u32[]{:S(2)}) collective-permute-start(bf16[1,1792,3,128]{3,1,2,0:T(8,128)(2,1)} %param.13), channel_id=1, source_target_pairs={{0,8},{1,9},{2,10},{3,11},{4,12},{5,13},{6,14},{7,15},{8,0},{9,1},... | collective-permute-start | bytes 4128776 | tf_op jit(solution)/shard_map/ppermute | solution.py:8
  273.5 22.8 %copy-start.3 = (bf16[1,1792,3,128]{3,1,2,0:T(8,128)(2,1)S(1)}, bf16[1,1792,3,128]{3,1,2,0:T(8,128)(2,1)}, u32[]{:S(2)}) copy-start(bf16[1,1792,3,128]{3,1,2,0:T(8,128)(2,1)} %param.13) | copy-start | bytes 4128772

commit v7 on v6

--- a/solution.py
+++ b/solution.py
@@ -101,7 +101,7 @@
         )
         src2 = jnp.arange(2 * entry_count, dtype=jnp.int32) // entry_count
         in_half = holder2 // half_axis == my_index // half_axis
-        lane2 = (holder2 ^ my_index) % half_axis
+        lane2 = holder2 % half_axis
         chunk = 2 * slot_cap
         slot2 = lane2 * chunk + src2 * slot_cap + rank2
         slot_hit = (
@@ -116,10 +116,14 @@
         send_gate = jnp.sum(jnp.where(slot_hit, wire2[None, :], 0.0), axis=1)
         send_all = jnp.concatenate([send_both, with_tile(send_gate)], axis=1)
 
+        halves = [list(range(h * half_axis, (h + 1) * half_axis)) for h in range(2)]
+
         def spread(value):
             parts = value.reshape((half_axis, chunk) + value.shape[1:])
-            moved = [parts[0]] + [xor_permute(parts[m], m) for m in range(1, half_axis)]
-            return jnp.stack(moved).reshape(value.shape)
+            moved = lax.all_to_all(
+                parts, "expert", 0, 0, tiled=True, axis_index_groups=halves
+            )
+            return moved.reshape(value.shape)
 
         recv_all = spread(send_all)
         rows = recv_all[:, :model_width]

time: 301 us -> 281 us (0.934)
  starting transfers between devices: 51.2 us -> 28.5 us
  matrix products: 9.85 us -> 24 us
  waiting for transfers between devices: 202 us -> 193 us
  local copies, waits for them, and re-layouts: 12 us -> 6.6 us
  other arithmetic: 22.7 us -> 26.5 us
    ppermute x14 -> x0, waiting for transfers between devices: 94.5 us -> none  [xor_permute(): lax.ppermute(value, 'expert', [(i, i ^ mask) for i in range(lax.axis_size...]
    ppermute x8, waiting for transfers between devices: 107 us -> 193 us  [from_partner(): lax.ppermute(value, axis, [(i, i ^ 1 << bit) for i in range(lax.axis_size...]
    ppermute x14 -> x0, starting transfers between devices: 40.5 us -> none  [xor_permute(): lax.ppermute(value, 'expert', [(i, i ^ mask) for i in range(lax.axis_size...]
    all_to_all x0 -> x2, starting transfers between devices: none -> 13.5 us  [spread(): lax.all_to_all(parts, 'expert', 0, 0, tiled=True, axis_index_groups=halves)]
    unnamed x30 -> x22, local copies, waits for them, and re-layouts: 8.19 us -> 2.44 us
    ppermute x8, starting transfers between devices: 10.7 us -> 14.9 us  [from_partner(): lax.ppermute(value, axis, [(i, i ^ 1 << bit) for i in range(lax.axis_size...]
  transfers between devices with their start and end apart: 24 -> 12, of which waited for: 14 -> 5; matrix products, arithmetic and copies ran while one was open for 12% -> 17% of each run, Pallas kernels for 0% -> 0%
where the time goes in v7:
time: 281 us
  waiting for transfers between devices  193 us (69%)
  starting transfers between devices  28.5 us (10%)
  other arithmetic  26.5 us (9%)
  matrix products  24 us (9%)
  local copies, waits for them, and re-layouts  6.6 us (2%)
    ppermute x8, waiting for transfers between devices, from_partner(): lax.ppermute(value, axis, [(i, i ^ 1 << bit) for i in range(lax.axis_size...  193 us
    ppermute x8, starting transfers between devices, from_partner(): lax.ppermute(value, axis, [(i, i ^ 1 << bit) for i in range(lax.axis_size...  14.9 us
    all_to_all x2, starting transfers between devices, spread(): lax.all_to_all(parts, 'expert', 0, 0, tiled=True, axis_index_groups=halves)  13.5 us
  transfers between devices with their start and end apart: 12, of which 5 were waited for; matrix products, arithmetic and copies ran while one was open for 17% of the time, Pallas kernels for 0%

profile of v7, /device:TPU:6, one launch (start us, length us, event | category | flops | bytes accessed | tf_op | source)
XLA Modules:
  0.0 280.5 jit_solution(5563652980957333425)
XLA Ops:
  0.6 2.7 collective-permute-start.1
  3.3 0.3 collective-permute-start
  3.6 1.0 constant_dynamic-update-slice_fusion.2
  4.6 1.0 constant_dynamic-update-slice_fusion.1
  5.5 2.7 collective-permute-start.2
  8.2 0.8 copy.41
  9.3 0.6 reduce-window.14
  10.2 0.7 convert.25
  11.5 0.6 reduce-window.16
  12.5 0.7 select_reduce_fusion.3
  13.9 0.2 select_reduce_fusion.2
  14.1 0.4 fusion.29
  14.6 13.5 %collective-permute-done.2 = bf16[32,7168]{1,0:T(8,128)(2,1)S(1)} collective-permute-done((bf16[32,7168]{1,0:T(8,128)(2,1)S(1)}, bf16[32,7168]{1,0:T(8,128)(2,1)S(1)}, u32[]{:S(2)}, u32[]{:S(2)}) %collective-permute-start.2) | collective-permute-done | bytes 458784 | tf_op jit(solution)/shard_map/ppermute | solution.py:8
  28.1 1.4 convolution_convert_fusion
  29.5 2.5 pad_maximum_fusion
  32.0 5.1 %all-to-all-start = ((bf16[8,40,7296]{2,1,0:T(8,128)(2,1)}), bf16[8,40,7296]{2,1,0:T(8,128)(2,1)}, u32[]{:S(2)}, u32[]{:S(2)}) async-start(bf16[8,40,7296]{2,1,0:T(8,128)(2,1)} %bitcast.79), calls=%async_computation | async-start | bytes 9338880 | tf_op jit(solution)/shard_map/all_to_all | solution.py:123
  37.0 2.7 collective-permute-start.3
  39.7 0.6 fusion.68
  41.0 82.2 %collective-permute-done.3 = bf16[1,1792,3,128]{3,1,2,0:T(8,128)(2,1)} collective-permute-done((bf16[1,1792,3,128]{3,1,2,0:T(8,128)(2,1)S(1)}, bf16[1,1792,3,128]{3,1,2,0:T(8,128)(2,1)}, u32[]{:S(2)}, u32[]{:S(2)}) %collective-permute-start.3) | collective-permute-done | bytes 1376288 | tf_op jit(solution)/shard_map/ppermute | solution.py:8
  123.2 1.5 broadcast_select_fusion.2
  124.8 3.6 %collective-permute-start.9 = (bf16[1,1792,3,128]{3,1,2,0:T(8,128)(2,1)}, bf16[1,1792,3,128]{3,1,2,0:T(8,128)(2,1)}, u32[]{:S(2)}, u32[]{:S(2)}) collective-permute-start(bf16[1,1792,3,128]{3,1,2,0:T(8,128)(2,1)} %param.14), channel_id=1, source_target_pairs={{0,8},{1,9},{2,10},{3,11},{4,12},{5,13},{6,14},{7,15},{8,0},{9,1},... | collective-permute-start | bytes 4128776 | tf_op jit(solution)/shard_map/ppermute | solution.py:8
  128.7 1.3 slice_bitcast_fusion
  130.0 1.0 convert_reduce_fusion.1
  131.0 2.4 fusion.16
  133.4 2.4 fusion.27
  135.9 2.4 multiply_convert_fusion.5
  138.3 2.5 fusion.21
  141.0 3.6 %fusion.1 = bf16[3584,1,128]{2,0,1:T(8,128)(2,1)} fusion(bf16[320,128]{1,0:T(8,128)(2,1)S(1)} %get-tuple-element.38, bf16[320,7296]{1,0:T(8,128)(2,1)} %bitcast.5), kind=kOutput, calls=%fused_computation.6 | convolution fusion | flops 294060032 | bytes 3293184 | tf_op jit(solution)/shard_map/dot_general | solution.py:173
  144.6 0.8 convolution_convert_fusion.1
  145.4 1.6 pad_maximum_fusion.2
  147.0 8.4 %all-to-all-start.1 = ((bf16[8,40,3712]{2,1,0:T(8,128)(2,1)}), bf16[8,40,3712]{2,1,0:T(8,128)(2,1)}, u32[]{:S(2)}, u32[]{:S(2)}) async-start(bf16[8,40,3712]{2,1,0:T(8,128)(2,1)} %bitcast.10), calls=%async_computation.1 | async-start | bytes 4751360 | tf_op jit(solution)/shard_map/all_to_all | solution.py:123
  155.4 2.6 fusion
  158.0 2.8 %fusion.2 = bf16[3584,1,128]{2,0,1:T(8,128)(2,1)S(1)} fusion(bf16[320,128]{1,0:T(8,128)(2,1)S(1)} %get-tuple-element.37, f32[320]{0:T(512)S(1)} %convert_reduce_fusion.1, bf16[320,7296]{1,0:T(8,128)(2,1)} %bitcast.5), kind=kOutput, calls=%fused_computation.7 | convolution fusion | flops 297500672 | bytes 3294464 | tf_op jit(solution)/shard_map/dot_general | solution.py:174
  160.9 0.3 pad_maximum_fusion.1
  161.2 1.2 broadcast_select_fusion
  162.6 0.4 select_reduce_fusion
  163.0 55.7 %collective-permute-done.9 = bf16[1,1792,3,128]{3,1,2,0:T(8,128)(2,1)} collective-permute-done((bf16[1,1792,3,128]{3,1,2,0:T(8,128)(2,1)}, bf16[1,1792,3,128]{3,1,2,0:T(8,128)(2,1)}, u32[]{:S(2)}, u32[]{:S(2)}) %collective-permute-start.9) | collective-permute-done | bytes 1376288 | tf_op jit(solution)/shard_map/ppermute | solution.py:8
  218.7 4.2 %fusion.3 = (bf16[1,1792,3,128]{3,1,2,0:T(8,128)(2,1)}, bf16[1792,3,128]{2,0,1:T(8,128)(2,1)S(1)}) fusion(bf16[1792,3,128]{2,0,1:T(8,128)(2,1)} %collective-permute-done.7, bf16[1,1792,3,128]{3,1,2,0:T(8,128)(2,1)} %collective-permute-done.9, bf16[1,1792,3,128]{3,1,2,0:T(8,128)(2,1)} %param.14, pred[]{:T(512)S(6)} %eq.180, ...), kind=kLoop, calls=%fused_computation.13 | loop fusion | flops 8257536 | bytes 9633794 | tf_op jit(solution)/shard_map/convert_element_type | solution.py:193
  222.9 25.1 %collective-permute-done.8 = bf16[1,1792,3,128]{3,1,2,0:T(8,128)(2,1)} collective-permute-done((bf16[1,1792,3,128]{3,1,2,0:T(8,128)(2,1)}, bf16[1,1792,3,128]{3,1,2,0:T(8,128)(2,1)}, u32[]{:S(2)}, u32[]{:S(2)}) %collective-permute-start.8) | collective-permute-done | bytes 1376288 | tf_op jit(solution)/shard_map/ppermute | solution.py:8
  247.9 3.7 %fusion.4 = bf16[1,1792,3,128]{3,1,2,0:T(8,128)(2,1)} fusion(bf16[1792,3,128]{2,0,1:T(8,128)(2,1)} %collective-permute-done.7, bf16[1792,3,128]{2,0,1:T(8,128)(2,1)S(1)} %get-tuple-element.29, bf16[1,1792,3,128]{3,1,2,0:T(8,128)(2,1)} %collective-permute-done.8, bf16[1,1792,3,128]{3,1,2,0:T(8,128)(2,1)} %param.13, pred[]{:T(512)S(6)} %eq.180), kind=kLoop, calls=%fused_computation.15 | loop fusion | flops 6193152 | bytes 6881281 | tf_op jit(solution)/shard_map/convert_element_type | solution.py:192
  251.6 1.1 convert_reduce_fusion
  252.8 3.1 %fusion.5 = f32[64,3584]{1,0:T(8,128)S(1)} fusion(f32[320,64]{0,1:T(8,128)S(1)} %select_reduce_fusion, bf16[320,3712]{1,0:T(8,128)(2,1)} %bitcast.11), kind=kOutput, calls=%fused_computation.19 | convolution fusion | flops 880803840 | bytes 3293184 | tf_op jit(solution)/shard_map/dot_general | solution.py:203
  255.9 0.2 select_reduce_fusion.1
  256.1 3.0 %collective-permute-start.6 = (bf16[256]{0:T(256)(128)(2,1)S(1)}, bf16[256]{0:T(256)(128)(2,1)S(1)}, u32[]{:S(2)}, u32[]{:S(2)}) collective-permute-start(bf16[256]{0:T(256)(128)(2,1)S(1)} %slice.76), channel_id=1, source_target_pairs={{0,8},{1,9},{2,10},{3,11},{4,12},{5,13},{6,14},{7,15},{8,0},{9,1},... | collective-permute-start | bytes 1544 | tf_op jit(solution)/shard_map/ppermute | solution.py:8
  259.1 3.2 %multiply_bitcast_fusion = f32[1,1792,3,128]{3,1,2,0:T(8,128)} fusion(bf16[1792,3,128]{2,0,1:T(8,128)(2,1)} %collective-permute-done.7, bf16[1792,3,128]{2,0,1:T(8,128)(2,1)S(1)} %copy-done.1), kind=kLoop, calls=%fused_computation.17 | loop fusion | flops 2752512 | bytes 5505024 | tf_op jit(solution)/shard_map/broadcast_in_dim | solution.py:189
  262.3 16.7 %collective-permute-done.6 = bf16[256]{0:T(256)(128)(2,1)S(1)} collective-permute-done((bf16[256]{0:T(256)(128)(2,1)S(1)}, bf16[256]{0:T(256)(128)(2,1)S(1)}, u32[]{:S(2)}, u32[]{:S(2)}) %collective-permute-start.6) | collective-permute-done | bytes 544 | tf_op jit(solution)/shard_map/ppermute | solution.py:8
  279.1 0.7 copy.52
  279.8 0.7 fusion.31
  (75 shorter events, 3.2 us)
Async XLA Ops:
  0.6 13.0 %collective-permute-start.1 = (f32[32,8]{0,1:T(8,128)}, f32[32,8]{0,1:T(8,128)S(1)}, u32[]{:S(2)}, u32[]{:S(2)}) collective-permute-start(f32[32,8]{0,1:T(8,128)} %param.11), channel_id=1, source_target_pairs={{0,8},{1,9},{2,10},{3,11},{4,12},{5,13},{6,14},{7,15},{8,0},{9,1},... | collective-permute-start | bytes 3080 | tf_op jit(solution)/shard_map/ppermute | solution.py:8
  3.3 7.8 %collective-permute-start = (s32[32,8]{0,1:T(8,128)}, s32[32,8]{0,1:T(8,128)S(1)}, u32[]{:S(2)}, u32[]{:S(2)}) collective-permute-start(s32[32,8]{0,1:T(8,128)} %param.10), channel_id=1, source_target_pairs={{0,8},{1,9},{2,10},{3,11},{4,12},{5,13},{6,14},{7,15},{8,0},{9,1},... | collective-permute-start | bytes 3080 | tf_op jit(solution)/shard_map/ppermute | solution.py:8
  5.5 22.6 %collective-permute-start.2 = (bf16[32,7168]{1,0:T(8,128)(2,1)S(1)}, bf16[32,7168]{1,0:T(8,128)(2,1)S(1)}, u32[]{:S(2)}, u32[]{:S(2)}) collective-permute-start(bf16[32,7168]{1,0:T(8,128)(2,1)S(1)} %constant_dynamic-update-slice_fusion.1), channel_id=1, source_target_pairs={{0,8},{1,9},{2,10},{3,11},{4,12},{5,13},{6,14},{7,15},{8,0},{9,1},... | collective-permute-start | bytes 1376264 | tf_op jit(solution)/shard_map/ppermute | solution.py:8
  32.0 5.1 %copy-start.3 = (bf16[1,1792,3,128]{3,1,2,0:T(8,128)(2,1)S(1)}, bf16[1,1792,3,128]{3,1,2,0:T(8,128)(2,1)}, u32[]{:S(2)}) copy-start(bf16[1,1792,3,128]{3,1,2,0:T(8,128)(2,1)} %param.12) | copy-start | bytes 4128772
  32.0 7.8 %copy-start.8 = (s32[8]{0:T(128)S(1)}, s32[8]{0:T(128)}, u32[]{:S(2)}) copy-start(s32[8]{0:T(128)} %param.15) | copy-start | bytes 100
  32.0 98.1 %all-to-all-start = ((bf16[8,40,7296]{2,1,0:T(8,128)(2,1)}), bf16[8,40,7296]{2,1,0:T(8,128)(2,1)}, u32[]{:S(2)}, u32[]{:S(2)}) async-start(bf16[8,40,7296]{2,1,0:T(8,128)(2,1)} %bitcast.79), calls=%async_computation | async-start | bytes 9338880 | tf_op jit(solution)/shard_map/all_to_all | solution.py:123
  37.0 86.1 %collective-permute-start.3 = (bf16[1,1792,3,128]{3,1,2,0:T(8,128)(2,1)S(1)}, bf16[1,1792,3,128]{3,1,2,0:T(8,128)(2,1)}, u32[]{:S(2)}, u32[]{:S(2)}) collective-permute-start(bf16[1,1792,3,128]{3,1,2,0:T(8,128)(2,1)S(1)} %copy-done.3), channel_id=1, source_target_pairs={{0,8},{1,9},{2,10},{3,11},{4,12},{5,13},{6,14},{7,15},{8,0},{9,1},... | collective-permute-start | bytes 4128776 | tf_op jit(solution)/shard_map/ppermute | solution.py:8
  124.7 3.8 %copy-start.2 = (bf16[1,1792,3,128]{3,1,2,0:T(8,128)(2,1)}, bf16[1,1792,3,128]{3,1,2,0:T(8,128)(2,1)S(1)}, u32[]{:S(2)}) copy-start(bf16[1,1792,3,128]{3,1,2,0:T(8,128)(2,1)S(1)} %broadcast_select_fusion.2) | copy-start | bytes 4128772
  124.7 3.6 %collective-permute-start.4 = (bf16[1,1792,3,128]{3,1,2,0:T(8,128)(2,1)S(1)}, bf16[1,1792,3,128]{3,1,2,0:T(8,128)(2,1)S(1)}, u32[]{:S(2)}, u32[]{:S(2)}) collective-permute-start(bf16[1,1792,3,128]{3,1,2,0:T(8,128)(2,1)S(1)} %broadcast_select_fusion.2), channel_id=1, source_target_pairs={{0,16},{16,0},{1,17},{17,1},{2,18},{18,2},{3,19},{19,3},{4,20},{20... | collective-permute-start | bytes 4128776 | tf_op jit(solution)/shard_map/ppermute | solution.py:143
  124.8 93.9 %collective-permute-start.9 = (bf16[1,1792,3,128]{3,1,2,0:T(8,128)(2,1)}, bf16[1,1792,3,128]{3,1,2,0:T(8,128)(2,1)}, u32[]{:S(2)}, u32[]{:S(2)}) collective-permute-start(bf16[1,1792,3,128]{3,1,2,0:T(8,128)(2,1)} %param.14), channel_id=1, source_target_pairs={{0,8},{1,9},{2,10},{3,11},{4,12},{5,13},{6,14},{7,15},{8,0},{9,1},... | collective-permute-start | bytes 4128776 | tf_op jit(solution)/shard_map/ppermute | solution.py:8
  140.8 3.8 %copy-start.4 = (bf16[3584,128]{1,0:T(8,128)(2,1)S(1)}, bf16[3584,128]{1,0:T(8,128)(2,1)}, u32[]{:S(2)}) copy-start(bf16[3584,128]{1,0:T(8,128)(2,1)} %get-tuple-element.32) | copy-start | bytes 2752516
  140.8 3.7 %copy-start.5 = (bf16[3584,128]{1,0:T(8,128)(2,1)S(1)}, bf16[3584,128]{1,0:T(8,128)(2,1)}, u32[]{:S(2)}) copy-start(bf16[3584,128]{1,0:T(8,128)(2,1)} %get-tuple-element.33) | copy-start | bytes 2752516
  147.0 104.7 %all-to-all-start.1 = ((bf16[8,40,3712]{2,1,0:T(8,128)(2,1)}), bf16[8,40,3712]{2,1,0:T(8,128)(2,1)}, u32[]{:S(2)}, u32[]{:S(2)}) async-start(bf16[8,40,3712]{2,1,0:T(8,128)(2,1)} %bitcast.10), calls=%async_computation.1 | async-start | bytes 4751360 | tf_op jit(solution)/shard_map/all_to_all | solution.py:123
  158.0 2.8 %copy-start.6 = (bf16[3584,1,128]{2,0,1:T(8,128)(2,1)S(1)}, bf16[3584,1,128]{2,0,1:T(8,128)(2,1)}, u32[]{:S(2)}) copy-start(bf16[3584,1,128]{2,0,1:T(8,128)(2,1)} %fusion.1) | copy-start | bytes 2752516
  161.2 1.2 copy-start.7
  162.4 56.3 %collective-permute-start.7 = (bf16[1792,3,128]{2,0,1:T(8,128)(2,1)}, bf16[1792,3,128]{2,0,1:T(8,128)(2,1)}, u32[]{:S(2)}, u32[]{:S(2)}) collective-permute-start(bf16[1792,3,128]{2,0,1:T(8,128)(2,1)} %broadcast_select_fusion), channel_id=1, source_target_pairs={{0,16},{16,0},{1,17},{17,1},{2,18},{18,2},{3,19},{19,3},{4,20},{20... | collective-permute-start | bytes 4128776 | tf_op jit(solution)/shard_map/ppermute | solution.py:183
  162.4 85.5 %collective-permute-start.8 = (bf16[1,1792,3,128]{3,1,2,0:T(8,128)(2,1)}, bf16[1,1792,3,128]{3,1,2,0:T(8,128)(2,1)}, u32[]{:S(2)}, u32[]{:S(2)}) collective-permute-start(bf16[1,1792,3,128]{3,1,2,0:T(8,128)(2,1)} %param.13), channel_id=1, source_target_pairs={{0,8},{1,9},{2,10},{3,11},{4,12},{5,13},{6,14},{7,15},{8,0},{9,1},... | collective-permute-start | bytes 4128776 | tf_op jit(solution)/shard_map/ppermute | solution.py:8
  222.9 25.1 %copy-start = (bf16[1792,3,128]{2,0,1:T(8,128)(2,1)}, bf16[1792,3,128]{2,0,1:T(8,128)(2,1)S(1)}, u32[]{:S(2)}) copy-start(bf16[1792,3,128]{2,0,1:T(8,128)(2,1)S(1)} %get-tuple-element.29) | copy-start | bytes 4128772
  251.6 7.5 %copy-start.1 = (bf16[1792,3,128]{2,0,1:T(8,128)(2,1)S(1)}, bf16[1792,3,128]{2,0,1:T(8,128)(2,1)}, u32[]{:S(2)}) copy-start(bf16[1792,3,128]{2,0,1:T(8,128)(2,1)} %copy-done) | copy-start | bytes 4128772
  255.9 23.9 %collective-permute-start.5 = (f32[32,3584]{1,0:T(8,128)S(1)}, f32[32,3584]{1,0:T(8,128)S(1)}, u32[]{:S(2)}, u32[]{:S(2)}) collective-permute-start(f32[32,3584]{1,0:T(8,128)S(1)} %slice.89), channel_id=1, source_target_pairs={{0,8},{1,9},{2,10},{3,11},{4,12},{5,13},{6,14},{7,15},{8,0},{9,1},... | collective-permute-start | bytes 1376264 | tf_op jit(solution)/shard_map/ppermute | solution.py:8
  256.1 22.9 %collective-permute-start.6 = (bf16[256]{0:T(256)(128)(2,1)S(1)}, bf16[256]{0:T(256)(128)(2,1)S(1)}, u32[]{:S(2)}, u32[]{:S(2)}) collective-permute-start(bf16[256]{0:T(256)(128)(2,1)S(1)} %slice.76), channel_id=1, source_target_pairs={{0,8},{1,9},{2,10},{3,11},{4,12},{5,13},{6,14},{7,15},{8,0},{9,1},... | collective-permute-start | bytes 1544 | tf_op jit(solution)/shard_map/ppermute | solution.py:8

commit v8 on v7

--- a/solution.py
+++ b/solution.py
@@ -209,9 +209,11 @@
         )
         prob2 = jnp.sum(jnp.where(slot_hit, back_gate[:, None], 0.0), axis=0)
         p_partial, p_prob = from_partner(
-            (partial[tok_rows:], prob2[entry_count:].astype(jnp.bfloat16)), "expert", swap_bit
-        )
-        token_grad = (partial[:tok_rows] + p_partial).astype(jnp.bfloat16)
+            (partial[tok_rows:].astype(jnp.bfloat16), prob2[entry_count:].astype(jnp.bfloat16)),
+            "expert",
+            swap_bit,
+        )
+        token_grad = (partial[:tok_rows] + p_partial.astype(jnp.float32)).astype(jnp.bfloat16)
         prob_grad = jnp.where(
             in_half[:entry_count], prob2[:entry_count], p_prob.astype(jnp.float32)
         )

time: 281 us -> 271 us (0.964)
  waiting for transfers between devices: 193 us -> 183 us
    ppermute x8, waiting for transfers between devices: 193 us -> 183 us  [from_partner(): lax.ppermute(value, axis, [(i, i ^ 1 << bit) for i in range(lax.axis_size...]
  transfers between devices with their start and end apart: 12 -> 12, of which waited for: 5 -> 5; matrix products, arithmetic and copies ran while one was open for 17% -> 18% of each run, Pallas kernels for 0% -> 0%
where the time goes in v8:
time: 271 us
  waiting for transfers between devices  183 us (68%)
  starting transfers between devices  28.5 us (11%)
  other arithmetic  26.5 us (10%)
  matrix products  24 us (9%)
  local copies, waits for them, and re-layouts  6.59 us (2%)
    ppermute x8, waiting for transfers between devices, from_partner(): lax.ppermute(value, axis, [(i, i ^ 1 << bit) for i in range(lax.axis_size...  183 us
    ppermute x8, starting transfers between devices, from_partner(): lax.ppermute(value, axis, [(i, i ^ 1 << bit) for i in range(lax.axis_size...  14.9 us
    all_to_all x2, starting transfers between devices, spread(): lax.all_to_all(parts, 'expert', 0, 0, tiled=True, axis_index_groups=halves)  13.5 us
  transfers between devices with their start and end apart: 12, of which 5 were waited for; matrix products, arithmetic and copies ran while one was open for 18% of the time, Pallas kernels for 0%

profile of v8, /device:TPU:6, one launch (start us, length us, event | category | flops | bytes accessed | tf_op | source)
XLA Modules:
  0.0 270.7 jit_solution(7937942872271905468)
XLA Ops:
  0.6 2.7 collective-permute-start.1
  3.3 0.3 collective-permute-start
  3.6 1.0 constant_dynamic-update-slice_fusion.2
  4.6 1.0 constant_dynamic-update-slice_fusion.1
  5.5 2.7 collective-permute-start.2
  8.2 0.8 copy.41
  9.3 0.6 reduce-window.14
  10.2 0.7 convert.28
  11.5 0.6 reduce-window.16
  12.5 0.7 select_reduce_fusion.3
  13.9 0.2 select_reduce_fusion.2
  14.1 0.4 fusion.29
  14.6 13.5 %collective-permute-done.2 = bf16[32,7168]{1,0:T(8,128)(2,1)S(1)} collective-permute-done((bf16[32,7168]{1,0:T(8,128)(2,1)S(1)}, bf16[32,7168]{1,0:T(8,128)(2,1)S(1)}, u32[]{:S(2)}, u32[]{:S(2)}) %collective-permute-start.2) | collective-permute-done | bytes 458784 | tf_op jit(solution)/shard_map/ppermute | solution.py:8
  28.1 1.4 convolution_convert_fusion
  29.5 2.5 pad_maximum_fusion
  32.0 5.1 %all-to-all-start = ((bf16[8,40,7296]{2,1,0:T(8,128)(2,1)}), bf16[8,40,7296]{2,1,0:T(8,128)(2,1)}, u32[]{:S(2)}, u32[]{:S(2)}) async-start(bf16[8,40,7296]{2,1,0:T(8,128)(2,1)} %bitcast.79), calls=%async_computation | async-start | bytes 9338880 | tf_op jit(solution)/shard_map/all_to_all | solution.py:123
  37.0 2.7 collective-permute-start.3
  39.7 0.6 fusion.68
  41.0 82.2 %collective-permute-done.3 = bf16[1,1792,3,128]{3,1,2,0:T(8,128)(2,1)} collective-permute-done((bf16[1,1792,3,128]{3,1,2,0:T(8,128)(2,1)S(1)}, bf16[1,1792,3,128]{3,1,2,0:T(8,128)(2,1)}, u32[]{:S(2)}, u32[]{:S(2)}) %collective-permute-start.3) | collective-permute-done | bytes 1376288 | tf_op jit(solution)/shard_map/ppermute | solution.py:8
  123.2 1.5 broadcast_select_fusion.2
  124.8 3.6 %collective-permute-start.9 = (bf16[1,1792,3,128]{3,1,2,0:T(8,128)(2,1)}, bf16[1,1792,3,128]{3,1,2,0:T(8,128)(2,1)}, u32[]{:S(2)}, u32[]{:S(2)}) collective-permute-start(bf16[1,1792,3,128]{3,1,2,0:T(8,128)(2,1)} %param.14), channel_id=1, source_target_pairs={{0,8},{1,9},{2,10},{3,11},{4,12},{5,13},{6,14},{7,15},{8,0},{9,1},... | collective-permute-start | bytes 4128776 | tf_op jit(solution)/shard_map/ppermute | solution.py:8
  128.7 1.3 slice_bitcast_fusion
  130.0 1.0 convert_reduce_fusion.1
  131.0 2.4 fusion.16
  133.4 2.4 fusion.27
  135.9 2.4 multiply_convert_fusion.5
  138.3 2.5 fusion.21
  141.0 3.6 %fusion.1 = bf16[3584,1,128]{2,0,1:T(8,128)(2,1)} fusion(bf16[320,128]{1,0:T(8,128)(2,1)S(1)} %get-tuple-element.38, bf16[320,7296]{1,0:T(8,128)(2,1)} %bitcast.5), kind=kOutput, calls=%fused_computation.6 | convolution fusion | flops 294060032 | bytes 3293184 | tf_op jit(solution)/shard_map/dot_general | solution.py:173
  144.6 0.8 convolution_convert_fusion.1
  145.4 1.6 pad_maximum_fusion.2
  147.0 8.5 %all-to-all-start.1 = ((bf16[8,40,3712]{2,1,0:T(8,128)(2,1)}), bf16[8,40,3712]{2,1,0:T(8,128)(2,1)}, u32[]{:S(2)}, u32[]{:S(2)}) async-start(bf16[8,40,3712]{2,1,0:T(8,128)(2,1)} %bitcast.10), calls=%async_computation.1 | async-start | bytes 4751360 | tf_op jit(solution)/shard_map/all_to_all | solution.py:123
  155.4 2.6 fusion
  158.0 2.8 %fusion.2 = bf16[3584,1,128]{2,0,1:T(8,128)(2,1)S(1)} fusion(bf16[320,128]{1,0:T(8,128)(2,1)S(1)} %get-tuple-element.37, f32[320]{0:T(512)S(1)} %convert_reduce_fusion.1, bf16[320,7296]{1,0:T(8,128)(2,1)} %bitcast.5), kind=kOutput, calls=%fused_computation.7 | convolution fusion | flops 297500672 | bytes 3294464 | tf_op jit(solution)/shard_map/dot_general | solution.py:174
  160.9 0.3 pad_maximum_fusion.1
  161.2 1.2 broadcast_select_fusion
  162.6 0.4 select_reduce_fusion
  163.0 55.7 %collective-permute-done.9 = bf16[1,1792,3,128]{3,1,2,0:T(8,128)(2,1)} collective-permute-done((bf16[1,1792,3,128]{3,1,2,0:T(8,128)(2,1)}, bf16[1,1792,3,128]{3,1,2,0:T(8,128)(2,1)}, u32[]{:S(2)}, u32[]{:S(2)}) %collective-permute-start.9) | collective-permute-done | bytes 1376288 | tf_op jit(solution)/shard_map/ppermute | solution.py:8
  218.7 4.2 %fusion.3 = (bf16[1,1792,3,128]{3,1,2,0:T(8,128)(2,1)}, bf16[1792,3,128]{2,0,1:T(8,128)(2,1)S(1)}) fusion(bf16[1792,3,128]{2,0,1:T(8,128)(2,1)} %collective-permute-done.7, bf16[1,1792,3,128]{3,1,2,0:T(8,128)(2,1)} %collective-permute-done.9, bf16[1,1792,3,128]{3,1,2,0:T(8,128)(2,1)} %param.14, pred[]{:T(512)S(6)} %eq.180, ...), kind=kLoop, calls=%fused_computation.13 | loop fusion | flops 8257536 | bytes 9633794 | tf_op jit(solution)/shard_map/convert_element_type | solution.py:193
  222.9 25.1 %collective-permute-done.8 = bf16[1,1792,3,128]{3,1,2,0:T(8,128)(2,1)} collective-permute-done((bf16[1,1792,3,128]{3,1,2,0:T(8,128)(2,1)}, bf16[1,1792,3,128]{3,1,2,0:T(8,128)(2,1)}, u32[]{:S(2)}, u32[]{:S(2)}) %collective-permute-start.8) | collective-permute-done | bytes 1376288 | tf_op jit(solution)/shard_map/ppermute | solution.py:8
  247.9 3.7 %fusion.4 = bf16[1,1792,3,128]{3,1,2,0:T(8,128)(2,1)} fusion(bf16[1792,3,128]{2,0,1:T(8,128)(2,1)} %collective-permute-done.7, bf16[1792,3,128]{2,0,1:T(8,128)(2,1)S(1)} %get-tuple-element.29, bf16[1,1792,3,128]{3,1,2,0:T(8,128)(2,1)} %collective-permute-done.8, bf16[1,1792,3,128]{3,1,2,0:T(8,128)(2,1)} %param.13, pred[]{:T(512)S(6)} %eq.180), kind=kLoop, calls=%fused_computation.15 | loop fusion | flops 6193152 | bytes 6881281 | tf_op jit(solution)/shard_map/convert_element_type | solution.py:192
  251.6 1.1 convert_reduce_fusion
  252.8 3.1 %fusion.5 = f32[64,3584]{1,0:T(8,128)S(1)} fusion(f32[320,64]{0,1:T(8,128)S(1)} %select_reduce_fusion, bf16[320,3712]{1,0:T(8,128)(2,1)} %bitcast.11), kind=kOutput, calls=%fused_computation.19 | convolution fusion | flops 880803840 | bytes 3293184 | tf_op jit(solution)/shard_map/dot_general | solution.py:203
  255.9 0.2 select_reduce_fusion.1
  256.1 3.0 %collective-permute-start.6 = (bf16[256]{0:T(256)(128)(2,1)S(1)}, bf16[256]{0:T(256)(128)(2,1)S(1)}, u32[]{:S(2)}, u32[]{:S(2)}) collective-permute-start(bf16[256]{0:T(256)(128)(2,1)S(1)} %slice.77), channel_id=1, source_target_pairs={{0,8},{1,9},{2,10},{3,11},{4,12},{5,13},{6,14},{7,15},{8,0},{9,1},... | collective-permute-start | bytes 1544 | tf_op jit(solution)/shard_map/ppermute | solution.py:8
  259.1 3.2 %multiply_bitcast_fusion = f32[1,1792,3,128]{3,1,2,0:T(8,128)} fusion(bf16[1792,3,128]{2,0,1:T(8,128)(2,1)} %collective-permute-done.7, bf16[1792,3,128]{2,0,1:T(8,128)(2,1)S(1)} %copy-done.1), kind=kLoop, calls=%fused_computation.17 | loop fusion | flops 2752512 | bytes 5505024 | tf_op jit(solution)/shard_map/broadcast_in_dim | solution.py:189
  262.3 6.8 %collective-permute-done.6 = bf16[256]{0:T(256)(128)(2,1)S(1)} collective-permute-done((bf16[256]{0:T(256)(128)(2,1)S(1)}, bf16[256]{0:T(256)(128)(2,1)S(1)}, u32[]{:S(2)}, u32[]{:S(2)}) %collective-permute-start.6) | collective-permute-done | bytes 544 | tf_op jit(solution)/shard_map/ppermute | solution.py:8
  269.3 0.7 copy.52
  269.9 0.7 fusion.31
  (75 shorter events, 3.2 us)
Async XLA Ops:
  0.6 13.0 %collective-permute-start.1 = (f32[32,8]{0,1:T(8,128)}, f32[32,8]{0,1:T(8,128)S(1)}, u32[]{:S(2)}, u32[]{:S(2)}) collective-permute-start(f32[32,8]{0,1:T(8,128)} %param.11), channel_id=1, source_target_pairs={{0,8},{1,9},{2,10},{3,11},{4,12},{5,13},{6,14},{7,15},{8,0},{9,1},... | collective-permute-start | bytes 3080 | tf_op jit(solution)/shard_map/ppermute | solution.py:8
  3.3 7.8 %collective-permute-start = (s32[32,8]{0,1:T(8,128)}, s32[32,8]{0,1:T(8,128)S(1)}, u32[]{:S(2)}, u32[]{:S(2)}) collective-permute-start(s32[32,8]{0,1:T(8,128)} %param.10), channel_id=1, source_target_pairs={{0,8},{1,9},{2,10},{3,11},{4,12},{5,13},{6,14},{7,15},{8,0},{9,1},... | collective-permute-start | bytes 3080 | tf_op jit(solution)/shard_map/ppermute | solution.py:8
  5.5 22.6 %collective-permute-start.2 = (bf16[32,7168]{1,0:T(8,128)(2,1)S(1)}, bf16[32,7168]{1,0:T(8,128)(2,1)S(1)}, u32[]{:S(2)}, u32[]{:S(2)}) collective-permute-start(bf16[32,7168]{1,0:T(8,128)(2,1)S(1)} %constant_dynamic-update-slice_fusion.1), channel_id=1, source_target_pairs={{0,8},{1,9},{2,10},{3,11},{4,12},{5,13},{6,14},{7,15},{8,0},{9,1},... | collective-permute-start | bytes 1376264 | tf_op jit(solution)/shard_map/ppermute | solution.py:8
  32.0 5.1 %copy-start.3 = (bf16[1,1792,3,128]{3,1,2,0:T(8,128)(2,1)S(1)}, bf16[1,1792,3,128]{3,1,2,0:T(8,128)(2,1)}, u32[]{:S(2)}) copy-start(bf16[1,1792,3,128]{3,1,2,0:T(8,128)(2,1)} %param.12) | copy-start | bytes 4128772
  32.0 7.8 %copy-start.8 = (s32[8]{0:T(128)S(1)}, s32[8]{0:T(128)}, u32[]{:S(2)}) copy-start(s32[8]{0:T(128)} %param.15) | copy-start | bytes 100
  32.0 98.1 %all-to-all-start = ((bf16[8,40,7296]{2,1,0:T(8,128)(2,1)}), bf16[8,40,7296]{2,1,0:T(8,128)(2,1)}, u32[]{:S(2)}, u32[]{:S(2)}) async-start(bf16[8,40,7296]{2,1,0:T(8,128)(2,1)} %bitcast.79), calls=%async_computation | async-start | bytes 9338880 | tf_op jit(solution)/shard_map/all_to_all | solution.py:123
  37.0 86.1 %collective-permute-start.3 = (bf16[1,1792,3,128]{3,1,2,0:T(8,128)(2,1)S(1)}, bf16[1,1792,3,128]{3,1,2,0:T(8,128)(2,1)}, u32[]{:S(2)}, u32[]{:S(2)}) collective-permute-start(bf16[1,1792,3,128]{3,1,2,0:T(8,128)(2,1)S(1)} %copy-done.3), channel_id=1, source_target_pairs={{0,8},{1,9},{2,10},{3,11},{4,12},{5,13},{6,14},{7,15},{8,0},{9,1},... | collective-permute-start | bytes 4128776 | tf_op jit(solution)/shard_map/ppermute | solution.py:8
  124.7 3.8 %copy-start.2 = (bf16[1,1792,3,128]{3,1,2,0:T(8,128)(2,1)}, bf16[1,1792,3,128]{3,1,2,0:T(8,128)(2,1)S(1)}, u32[]{:S(2)}) copy-start(bf16[1,1792,3,128]{3,1,2,0:T(8,128)(2,1)S(1)} %broadcast_select_fusion.2) | copy-start | bytes 4128772
  124.7 3.6 %collective-permute-start.4 = (bf16[1,1792,3,128]{3,1,2,0:T(8,128)(2,1)S(1)}, bf16[1,1792,3,128]{3,1,2,0:T(8,128)(2,1)S(1)}, u32[]{:S(2)}, u32[]{:S(2)}) collective-permute-start(bf16[1,1792,3,128]{3,1,2,0:T(8,128)(2,1)S(1)} %broadcast_select_fusion.2), channel_id=1, source_target_pairs={{0,16},{16,0},{1,17},{17,1},{2,18},{18,2},{3,19},{19,3},{4,20},{20... | collective-permute-start | bytes 4128776 | tf_op jit(solution)/shard_map/ppermute | solution.py:143
  124.8 93.9 %collective-permute-start.9 = (bf16[1,1792,3,128]{3,1,2,0:T(8,128)(2,1)}, bf16[1,1792,3,128]{3,1,2,0:T(8,128)(2,1)}, u32[]{:S(2)}, u32[]{:S(2)}) collective-permute-start(bf16[1,1792,3,128]{3,1,2,0:T(8,128)(2,1)} %param.14), channel_id=1, source_target_pairs={{0,8},{1,9},{2,10},{3,11},{4,12},{5,13},{6,14},{7,15},{8,0},{9,1},... | collective-permute-start | bytes 4128776 | tf_op jit(solution)/shard_map/ppermute | solution.py:8
  140.8 3.8 %copy-start.4 = (bf16[3584,128]{1,0:T(8,128)(2,1)S(1)}, bf16[3584,128]{1,0:T(8,128)(2,1)}, u32[]{:S(2)}) copy-start(bf16[3584,128]{1,0:T(8,128)(2,1)} %get-tuple-element.32) | copy-start | bytes 2752516
  140.8 3.8 %copy-start.5 = (bf16[3584,128]{1,0:T(8,128)(2,1)S(1)}, bf16[3584,128]{1,0:T(8,128)(2,1)}, u32[]{:S(2)}) copy-start(bf16[3584,128]{1,0:T(8,128)(2,1)} %get-tuple-element.33) | copy-start | bytes 2752516
  147.0 104.7 %all-to-all-start.1 = ((bf16[8,40,3712]{2,1,0:T(8,128)(2,1)}), bf16[8,40,3712]{2,1,0:T(8,128)(2,1)}, u32[]{:S(2)}, u32[]{:S(2)}) async-start(bf16[8,40,3712]{2,1,0:T(8,128)(2,1)} %bitcast.10), calls=%async_computation.1 | async-start | bytes 4751360 | tf_op jit(solution)/shard_map/all_to_all | solution.py:123
  158.0 2.8 %copy-start.6 = (bf16[3584,1,128]{2,0,1:T(8,128)(2,1)S(1)}, bf16[3584,1,128]{2,0,1:T(8,128)(2,1)}, u32[]{:S(2)}) copy-start(bf16[3584,1,128]{2,0,1:T(8,128)(2,1)} %fusion.1) | copy-start | bytes 2752516
  161.2 1.2 copy-start.7
  162.4 56.3 %collective-permute-start.7 = (bf16[1792,3,128]{2,0,1:T(8,128)(2,1)}, bf16[1792,3,128]{2,0,1:T(8,128)(2,1)}, u32[]{:S(2)}, u32[]{:S(2)}) collective-permute-start(bf16[1792,3,128]{2,0,1:T(8,128)(2,1)} %broadcast_select_fusion), channel_id=1, source_target_pairs={{0,16},{16,0},{1,17},{17,1},{2,18},{18,2},{3,19},{19,3},{4,20},{20... | collective-permute-start | bytes 4128776 | tf_op jit(solution)/shard_map/ppermute | solution.py:183
  162.4 85.5 %collective-permute-start.8 = (bf16[1,1792,3,128]{3,1,2,0:T(8,128)(2,1)}, bf16[1,1792,3,128]{3,1,2,0:T(8,128)(2,1)}, u32[]{:S(2)}, u32[]{:S(2)}) collective-permute-start(bf16[1,1792,3,128]{3,1,2,0:T(8,128)(2,1)} %param.13), channel_id=1, source_target_pairs={{0,8},{1,9},{2,10},{3,11},{4,12},{5,13},{6,14},{7,15},{8,0},{9,1},... | collective-permute-start | bytes 4128776 | tf_op jit(solution)/shard_map/ppermute | solution.py:8
  222.9 25.1 %copy-start = (bf16[1792,3,128]{2,0,1:T(8,128)(2,1)}, bf16[1792,3,128]{2,0,1:T(8,128)(2,1)S(1)}, u32[]{:S(2)}) copy-start(bf16[1792,3,128]{2,0,1:T(8,128)(2,1)S(1)} %get-tuple-element.29) | copy-start | bytes 4128772
  251.6 7.5 %copy-start.1 = (bf16[1792,3,128]{2,0,1:T(8,128)(2,1)S(1)}, bf16[1792,3,128]{2,0,1:T(8,128)(2,1)}, u32[]{:S(2)}) copy-start(bf16[1792,3,128]{2,0,1:T(8,128)(2,1)} %copy-done) | copy-start | bytes 4128772
  255.9 14.1 %collective-permute-start.5 = (bf16[32,3584]{1,0:T(8,128)(2,1)S(1)}, bf16[32,3584]{1,0:T(8,128)(2,1)S(1)}, u32[]{:S(2)}, u32[]{:S(2)}) collective-permute-start(bf16[32,3584]{1,0:T(8,128)(2,1)S(1)} %slice.136), channel_id=1, source_target_pairs={{0,8},{1,9},{2,10},{3,11},{4,12},{5,13},{6,14},{7,15},{8,0},{9,1},... | collective-permute-start | bytes 688136 | tf_op jit(solution)/shard_map/ppermute | solution.py:8
  256.1 13.0 %collective-permute-start.6 = (bf16[256]{0:T(256)(128)(2,1)S(1)}, bf16[256]{0:T(256)(128)(2,1)S(1)}, u32[]{:S(2)}, u32[]{:S(2)}) collective-permute-start(bf16[256]{0:T(256)(128)(2,1)S(1)} %slice.77), channel_id=1, source_target_pairs={{0,8},{1,9},{2,10},{3,11},{4,12},{5,13},{6,14},{7,15},{8,0},{9,1},... | collective-permute-start | bytes 1544 | tf_op jit(solution)/shard_map/ppermute | solution.py:8

commit v9 on v8

--- a/solution.py
+++ b/solution.py
@@ -134,10 +134,10 @@
         rows, grads_in, gates = send_slots(tokens, out_grad, flat_gate, slot_of, slot_cap)
     if not two_stage:
         their_weights = from_partner(weights, "expert", swap_bit)
-    first_moment, second_moment, _ = lax.optimization_barrier(
-        (first_moment, second_moment, their_weights)
-    )
-    their_moments = from_partner((first_moment, second_moment), "expert", swap_bit)
+    moments, _ = lax.optimization_barrier(
+        (jnp.stack([first_moment, second_moment]), their_weights)
+    )
+    their_moments = from_partner(moments, "expert", swap_bit)
     weights = jnp.where(swapped, their_weights, weights)
     if groups == 2:
         other = lax.ppermute(weights, "dp", [(0, 1), (1, 0)])

time: 271 us -> 280 us (1.033)
  other arithmetic: 26.5 us -> 31.5 us
  waiting for transfers between devices: 183 us -> 187 us
    ppermute x8 -> x7, waiting for transfers between devices: 183 us -> 187 us  [from_partner(): lax.ppermute(value, axis, [(i, i ^ 1 << bit) for i in range(lax.axis_size...]
    ppermute x8 -> x7, starting transfers between devices: 14.9 us -> 14.7 us  [from_partner(): lax.ppermute(value, axis, [(i, i ^ 1 << bit) for i in range(lax.axis_size...]
  transfers between devices with their start and end apart: 12 -> 11, of which waited for: 5 -> 4; matrix products, arithmetic and copies ran while one was open for 18% -> 19% of each run, Pallas kernels for 0% -> 0%
where the time goes in v9:
time: 280 us; the launch traced here: 279 us
  waiting for transfers between devices  187 us (67%)
  other arithmetic  31.5 us (11%)
  starting transfers between devices  26.9 us (10%)
  matrix products  24.1 us (9%)
  local copies, waits for them, and re-layouts  7.67 us (3%)
    ppermute x7, waiting for transfers between devices, from_partner(): lax.ppermute(value, axis, [(i, i ^ 1 << bit) for i in range(lax.axis_size...  187 us
    ppermute x7, starting transfers between devices, from_partner(): lax.ppermute(value, axis, [(i, i ^ 1 << bit) for i in range(lax.axis_size...  14.7 us
    all_to_all x2, starting transfers between devices, spread(): lax.all_to_all(parts, 'expert', 0, 0, tiled=True, axis_index_groups=halves)  12.2 us
  transfers between devices with their start and end apart: 11, of which 4 were waited for; matrix products, arithmetic and copies ran while one was open for 19% of the time, Pallas kernels for 0%

profile of v9, /device:TPU:6, one launch (start us, length us, event | category | flops | bytes accessed | tf_op | source)
XLA Modules:
  0.0 279.2 jit_solution(13593716633613814680)
XLA Ops:
  0.6 2.7 collective-permute-start.1
  3.3 0.3 collective-permute-start
  3.6 1.0 constant_dynamic-update-slice_fusion.2
  4.6 1.0 constant_dynamic-update-slice_fusion.1
  5.5 2.7 collective-permute-start.2
  8.2 0.8 copy.41
  9.3 0.6 reduce-window.14
  10.2 0.7 convert.28
  11.5 0.6 reduce-window.16
  12.5 0.7 select_reduce_fusion.3
  14.1 0.4 fusion.31
  14.6 13.5 %collective-permute-done.2 = bf16[32,7168]{1,0:T(8,128)(2,1)S(1)} collective-permute-done((bf16[32,7168]{1,0:T(8,128)(2,1)S(1)}, bf16[32,7168]{1,0:T(8,128)(2,1)S(1)}, u32[]{:S(2)}, u32[]{:S(2)}) %collective-permute-start.2) | collective-permute-done | bytes 458784 | tf_op jit(solution)/shard_map/ppermute | solution.py:8
  28.1 1.4 convolution_convert_fusion
  29.5 2.5 pad_maximum_fusion
  32.0 5.1 %all-to-all-start = ((bf16[8,40,7296]{2,1,0:T(8,128)(2,1)}), bf16[8,40,7296]{2,1,0:T(8,128)(2,1)}, u32[]{:S(2)}, u32[]{:S(2)}) async-start(bf16[8,40,7296]{2,1,0:T(8,128)(2,1)} %bitcast.93), calls=%async_computation | async-start | bytes 9338880 | tf_op jit(solution)/shard_map/all_to_all | solution.py:123
  37.1 2.7 collective-permute-start.3
  39.7 0.6 fusion.70
  41.0 82.3 %collective-permute-done.3 = bf16[1,1792,3,128]{3,1,2,0:T(8,128)(2,1)} collective-permute-done((bf16[1,1792,3,128]{3,1,2,0:T(8,128)(2,1)}, bf16[1,1792,3,128]{3,1,2,0:T(8,128)(2,1)}, u32[]{:S(2)}, u32[]{:S(2)}) %collective-permute-start.3) | collective-permute-done | bytes 1376288 | tf_op jit(solution)/shard_map/ppermute | solution.py:8
  123.3 2.6 broadcast_select_fusion.2
  125.9 1.8 pad_maximum_fusion.2
  127.7 3.4 %collective-permute-start.8 = (bf16[2,1,1792,3,128]{4,2,3,1,0:T(8,128)(2,1)}, bf16[2,1,1792,3,128]{4,2,3,1,0:T(8,128)(2,1)}, u32[]{:S(2)}, u32[]{:S(2)}) collective-permute-start(bf16[2,1,1792,3,128]{4,2,3,1,0:T(8,128)(2,1)} %pad_maximum_fusion.2), channel_id=1, source_target_pairs={{0,8},{1,9},{2,10},{3,11},{4,12},{5,13},{6,14},{7,15},{8,0},{9,1},... | collective-permute-start | bytes 8257544 | tf_op jit(solution)/shard_map/ppermute | solution.py:8
  131.0 1.9 broadcast_select_fusion.4
  133.2 1.3 slice_bitcast_fusion.2
  134.5 1.0 convert_reduce_fusion.1
  135.5 2.4 fusion.16
  137.9 2.4 fusion.29
  140.4 2.4 multiply_convert_fusion.5
  142.8 2.5 fusion.23
  145.4 3.7 %fusion.1 = bf16[3584,1,128]{2,0,1:T(8,128)(2,1)} fusion(bf16[320,128]{1,0:T(8,128)(2,1)S(1)} %get-tuple-element.36, bf16[320,7296]{1,0:T(8,128)(2,1)} %bitcast.5), kind=kOutput, calls=%fused_computation.6 | convolution fusion | flops 294060032 | bytes 3293184 | tf_op jit(solution)/shard_map/dot_general | solution.py:173
  149.1 0.8 convolution_convert_fusion.1
  149.9 1.6 pad_maximum_fusion.3
  151.5 7.1 %all-to-all-start.1 = ((bf16[8,40,3712]{2,1,0:T(8,128)(2,1)}), bf16[8,40,3712]{2,1,0:T(8,128)(2,1)}, u32[]{:S(2)}, u32[]{:S(2)}) async-start(bf16[8,40,3712]{2,1,0:T(8,128)(2,1)} %bitcast.10), calls=%async_computation.1 | async-start | bytes 4751360 | tf_op jit(solution)/shard_map/all_to_all | solution.py:123
  158.6 2.6 fusion
  161.2 2.8 %fusion.2 = bf16[3584,1,128]{2,0,1:T(8,128)(2,1)S(1)} fusion(bf16[320,128]{1,0:T(8,128)(2,1)S(1)} %get-tuple-element.35, f32[320]{0:T(512)S(1)} %convert_reduce_fusion.1, bf16[320,7296]{1,0:T(8,128)(2,1)} %bitcast.5), kind=kOutput, calls=%fused_computation.7 | convolution fusion | flops 297500672 | bytes 3294464 | tf_op jit(solution)/shard_map/dot_general | solution.py:174
  164.0 0.3 pad_maximum_fusion.1
  164.3 1.2 broadcast_select_fusion
  165.7 0.4 select_reduce_fusion
  166.1 84.5 %collective-permute-done.8 = bf16[2,1,1792,3,128]{4,2,3,1,0:T(8,128)(2,1)} collective-permute-done((bf16[2,1,1792,3,128]{4,2,3,1,0:T(8,128)(2,1)}, bf16[2,1,1792,3,128]{4,2,3,1,0:T(8,128)(2,1)}, u32[]{:S(2)}, u32[]{:S(2)}) %collective-permute-start.8) | collective-permute-done | bytes 2752544 | tf_op jit(solution)/shard_map/ppermute | solution.py:8
  250.7 4.6 %fusion.3 = (bf16[1,1792,3,128]{3,1,2,0:T(8,128)(2,1)}, bf16[1792,3,128]{2,0,1:T(8,128)(2,1)S(1)}) fusion(bf16[1792,3,128]{2,0,1:T(8,128)(2,1)} %collective-permute-done.7, bf16[1,1792,3,128]{3,1,2,0:T(8,128)(2,1)} %param.14, bf16[2,1,1792,3,128]{4,2,3,1,0:T(8,128)(2,1)} %collective-permute-done.8, pred[]{:T(512)S(6)} %eq.180, ...), kind=kLoop, calls=%fused_computation.14 | loop fusion | flops 8257536 | bytes 9633794 | tf_op jit(solution)/shard_map/convert_element_type | solution.py:193
  255.3 1.1 copy-done
  256.3 3.7 %fusion.4 = bf16[1,1792,3,128]{3,1,2,0:T(8,128)(2,1)} fusion(bf16[1792,3,128]{2,0,1:T(8,128)(2,1)} %collective-permute-done.7, bf16[1792,3,128]{2,0,1:T(8,128)(2,1)S(1)} %get-tuple-element.27, bf16[1,1792,3,128]{3,1,2,0:T(8,128)(2,1)S(1)} %copy-done.4, bf16[2,1,1792,3,128]{4,2,3,1,0:T(8,128)(2,1)} %collective-permute-done.8, pred[]{:T(512)S(6)} %eq.180), kind=kLoop, calls=%fused_computation.16 | loop fusion | flops 6193152 | bytes 6881281 | tf_op jit(solution)/shard_map/convert_element_type | solution.py:192
  260.1 1.1 convert_reduce_fusion
  261.2 3.1 %fusion.5 = f32[64,3584]{1,0:T(8,128)S(1)} fusion(f32[320,64]{0,1:T(8,128)S(1)} %select_reduce_fusion, bf16[320,3712]{1,0:T(8,128)(2,1)} %bitcast.11), kind=kOutput, calls=%fused_computation.20 | convolution fusion | flops 880803840 | bytes 3293184 | tf_op jit(solution)/shard_map/dot_general | solution.py:203
  264.6 3.0 %collective-permute-start.6 = (bf16[256]{0:T(256)(128)(2,1)S(1)}, bf16[256]{0:T(256)(128)(2,1)S(1)}, u32[]{:S(2)}, u32[]{:S(2)}) collective-permute-start(bf16[256]{0:T(256)(128)(2,1)S(1)} %slice.83), channel_id=1, source_target_pairs={{0,8},{1,9},{2,10},{3,11},{4,12},{5,13},{6,14},{7,15},{8,0},{9,1},... | collective-permute-start | bytes 1544 | tf_op jit(solution)/shard_map/ppermute | solution.py:8
  267.5 3.2 %multiply_bitcast_fusion = f32[1,1792,3,128]{3,1,2,0:T(8,128)} fusion(bf16[1792,3,128]{2,0,1:T(8,128)(2,1)} %collective-permute-done.7, bf16[1792,3,128]{2,0,1:T(8,128)(2,1)S(1)} %copy-done.1), kind=kLoop, calls=%fused_computation.18 | loop fusion | flops 2752512 | bytes 5505024 | tf_op jit(solution)/shard_map/broadcast_in_dim | solution.py:189
  270.8 6.9 %collective-permute-done.6 = bf16[256]{0:T(256)(128)(2,1)S(1)} collective-permute-done((bf16[256]{0:T(256)(128)(2,1)S(1)}, bf16[256]{0:T(256)(128)(2,1)S(1)}, u32[]{:S(2)}, u32[]{:S(2)}) %collective-permute-start.6) | collective-permute-done | bytes 544 | tf_op jit(solution)/shard_map/ppermute | solution.py:8
  277.8 0.7 copy.52
  278.4 0.7 fusion.33
  (76 shorter events, 3.4 us)
Async XLA Ops:
  0.6 13.0 %collective-permute-start.1 = (f32[32,8]{0,1:T(8,128)}, f32[32,8]{0,1:T(8,128)S(1)}, u32[]{:S(2)}, u32[]{:S(2)}) collective-permute-start(f32[32,8]{0,1:T(8,128)} %param.11), channel_id=1, source_target_pairs={{0,8},{1,9},{2,10},{3,11},{4,12},{5,13},{6,14},{7,15},{8,0},{9,1},... | collective-permute-start | bytes 3080 | tf_op jit(solution)/shard_map/ppermute | solution.py:8
  3.3 7.8 %collective-permute-start = (s32[32,8]{0,1:T(8,128)}, s32[32,8]{0,1:T(8,128)S(1)}, u32[]{:S(2)}, u32[]{:S(2)}) collective-permute-start(s32[32,8]{0,1:T(8,128)} %param.10), channel_id=1, source_target_pairs={{0,8},{1,9},{2,10},{3,11},{4,12},{5,13},{6,14},{7,15},{8,0},{9,1},... | collective-permute-start | bytes 3080 | tf_op jit(solution)/shard_map/ppermute | solution.py:8
  5.5 22.6 %collective-permute-start.2 = (bf16[32,7168]{1,0:T(8,128)(2,1)S(1)}, bf16[32,7168]{1,0:T(8,128)(2,1)S(1)}, u32[]{:S(2)}, u32[]{:S(2)}) collective-permute-start(bf16[32,7168]{1,0:T(8,128)(2,1)S(1)} %constant_dynamic-update-slice_fusion.1), channel_id=1, source_target_pairs={{0,8},{1,9},{2,10},{3,11},{4,12},{5,13},{6,14},{7,15},{8,0},{9,1},... | collective-permute-start | bytes 1376264 | tf_op jit(solution)/shard_map/ppermute | solution.py:8
  32.0 7.8 %copy-start.9 = (s32[8]{0:T(128)S(1)}, s32[8]{0:T(128)}, u32[]{:S(2)}) copy-start(s32[8]{0:T(128)} %param.15) | copy-start | bytes 100
  32.0 102.5 %all-to-all-start = ((bf16[8,40,7296]{2,1,0:T(8,128)(2,1)}), bf16[8,40,7296]{2,1,0:T(8,128)(2,1)}, u32[]{:S(2)}, u32[]{:S(2)}) async-start(bf16[8,40,7296]{2,1,0:T(8,128)(2,1)} %bitcast.93), calls=%async_computation | async-start | bytes 9338880 | tf_op jit(solution)/shard_map/all_to_all | solution.py:123
  37.1 88.8 %copy-start.2 = (bf16[1,1792,3,128]{3,1,2,0:T(8,128)(2,1)S(1)}, bf16[1,1792,3,128]{3,1,2,0:T(8,128)(2,1)}, u32[]{:S(2)}) copy-start(bf16[1,1792,3,128]{3,1,2,0:T(8,128)(2,1)} %param.14) | copy-start | bytes 4128772
  37.1 88.8 %copy-start.3 = (bf16[1,1792,3,128]{3,1,2,0:T(8,128)(2,1)S(1)}, bf16[1,1792,3,128]{3,1,2,0:T(8,128)(2,1)}, u32[]{:S(2)}) copy-start(bf16[1,1792,3,128]{3,1,2,0:T(8,128)(2,1)} %param.13) | copy-start | bytes 4128772
  37.1 86.2 %collective-permute-start.3 = (bf16[1,1792,3,128]{3,1,2,0:T(8,128)(2,1)}, bf16[1,1792,3,128]{3,1,2,0:T(8,128)(2,1)}, u32[]{:S(2)}, u32[]{:S(2)}) collective-permute-start(bf16[1,1792,3,128]{3,1,2,0:T(8,128)(2,1)} %param.12), channel_id=1, source_target_pairs={{0,8},{1,9},{2,10},{3,11},{4,12},{5,13},{6,14},{7,15},{8,0},{9,1},... | collective-permute-start | bytes 4128776 | tf_op jit(solution)/shard_map/ppermute | solution.py:8
  125.9 5.2 %collective-permute-start.4 = (bf16[1,1792,3,128]{3,1,2,0:T(8,128)(2,1)}, bf16[1,1792,3,128]{3,1,2,0:T(8,128)(2,1)}, u32[]{:S(2)}, u32[]{:S(2)}) collective-permute-start(bf16[1,1792,3,128]{3,1,2,0:T(8,128)(2,1)} %broadcast_select_fusion.2), channel_id=1, source_target_pairs={{0,16},{16,0},{1,17},{17,1},{2,18},{18,2},{3,19},{19,3},{4,20},{20... | collective-permute-start | bytes 4128776 | tf_op jit(solution)/shard_map/ppermute | solution.py:143
  127.7 123.0 %collective-permute-start.8 = (bf16[2,1,1792,3,128]{4,2,3,1,0:T(8,128)(2,1)}, bf16[2,1,1792,3,128]{4,2,3,1,0:T(8,128)(2,1)}, u32[]{:S(2)}, u32[]{:S(2)}) collective-permute-start(bf16[2,1,1792,3,128]{4,2,3,1,0:T(8,128)(2,1)} %pad_maximum_fusion.2), channel_id=1, source_target_pairs={{0,8},{1,9},{2,10},{3,11},{4,12},{5,13},{6,14},{7,15},{8,0},{9,1},... | collective-permute-start | bytes 8257544 | tf_op jit(solution)/shard_map/ppermute | solution.py:8
  145.3 3.8 %copy-start.5 = (bf16[3584,128]{1,0:T(8,128)(2,1)S(1)}, bf16[3584,128]{1,0:T(8,128)(2,1)}, u32[]{:S(2)}) copy-start(bf16[3584,128]{1,0:T(8,128)(2,1)} %get-tuple-element.30) | copy-start | bytes 2752516
  145.3 3.8 %copy-start.6 = (bf16[3584,128]{1,0:T(8,128)(2,1)S(1)}, bf16[3584,128]{1,0:T(8,128)(2,1)}, u32[]{:S(2)}) copy-start(bf16[3584,128]{1,0:T(8,128)(2,1)} %get-tuple-element.31) | copy-start | bytes 2752516
  151.5 108.6 %all-to-all-start.1 = ((bf16[8,40,3712]{2,1,0:T(8,128)(2,1)}), bf16[8,40,3712]{2,1,0:T(8,128)(2,1)}, u32[]{:S(2)}, u32[]{:S(2)}) async-start(bf16[8,40,3712]{2,1,0:T(8,128)(2,1)} %bitcast.10), calls=%async_computation.1 | async-start | bytes 4751360 | tf_op jit(solution)/shard_map/all_to_all | solution.py:123
  161.2 2.8 %copy-start.7 = (bf16[3584,1,128]{2,0,1:T(8,128)(2,1)S(1)}, bf16[3584,1,128]{2,0,1:T(8,128)(2,1)}, u32[]{:S(2)}) copy-start(bf16[3584,1,128]{2,0,1:T(8,128)(2,1)} %fusion.1) | copy-start | bytes 2752516
  164.3 1.2 copy-start.8
  165.5 85.1 %collective-permute-start.7 = (bf16[1792,3,128]{2,0,1:T(8,128)(2,1)}, bf16[1792,3,128]{2,0,1:T(8,128)(2,1)}, u32[]{:S(2)}, u32[]{:S(2)}) collective-permute-start(bf16[1792,3,128]{2,0,1:T(8,128)(2,1)} %broadcast_select_fusion), channel_id=1, source_target_pairs={{0,16},{16,0},{1,17},{17,1},{2,18},{18,2},{3,19},{19,3},{4,20},{20... | collective-permute-start | bytes 4128776 | tf_op jit(solution)/shard_map/ppermute | solution.py:183
  166.1 90.2 %copy-start.4 = (bf16[1,1792,3,128]{3,1,2,0:T(8,128)(2,1)S(1)}, bf16[1,1792,3,128]{3,1,2,0:T(8,128)(2,1)}, u32[]{:S(2)}) copy-start(bf16[1,1792,3,128]{3,1,2,0:T(8,128)(2,1)} %param.13) | copy-start | bytes 4128772
  255.3 1.1 copy-start
  260.1 7.5 %copy-start.1 = (bf16[1792,3,128]{2,0,1:T(8,128)(2,1)S(1)}, bf16[1792,3,128]{2,0,1:T(8,128)(2,1)}, u32[]{:S(2)}) copy-start(bf16[1792,3,128]{2,0,1:T(8,128)(2,1)} %copy-done) | copy-start | bytes 4128772
  264.3 14.2 %collective-permute-start.5 = (bf16[32,3584]{1,0:T(8,128)(2,1)S(1)}, bf16[32,3584]{1,0:T(8,128)(2,1)S(1)}, u32[]{:S(2)}, u32[]{:S(2)}) collective-permute-start(bf16[32,3584]{1,0:T(8,128)(2,1)S(1)} %slice.156), channel_id=1, source_target_pairs={{0,8},{1,9},{2,10},{3,11},{4,12},{5,13},{6,14},{7,15},{8,0},{9,1},... | collective-permute-start | bytes 688136 | tf_op jit(solution)/shard_map/ppermute | solution.py:8
  264.6 13.1 %collective-permute-start.6 = (bf16[256]{0:T(256)(128)(2,1)S(1)}, bf16[256]{0:T(256)(128)(2,1)S(1)}, u32[]{:S(2)}, u32[]{:S(2)}) collective-permute-start(bf16[256]{0:T(256)(128)(2,1)S(1)} %slice.83), channel_id=1, source_target_pairs={{0,8},{1,9},{2,10},{3,11},{4,12},{5,13},{6,14},{7,15},{8,0},{9,1},... | collective-permute-start | bytes 1544 | tf_op jit(solution)/shard_map/ppermute | solution.py:8

commit v10 on v7

--- a/solution.py
+++ b/solution.py
@@ -88,26 +88,34 @@
 
     two_stage = half_axis <= 8
     if two_stage:
+        plane = min(4, half_axis)
+        column = axis_width // plane
         packed = jnp.concatenate([tokens, out_grad], axis=1)
-        p_packed, p_ids, p_gate, their_weights = from_partner(
-            (packed, expert_ids, gate_probs, weights), "expert", swap_bit
-        )
-        both = jnp.concatenate([packed, p_packed], axis=0)
-        ids2 = jnp.concatenate([flat_ids, p_ids.reshape(-1)])
-        gate2 = jnp.concatenate([flat_gate, p_gate.reshape(-1)])
+        got = [(packed, expert_ids, gate_probs)]
+        for k in range(1, column):
+            if k * plane == half_axis:
+                p_packed, p_ids, p_gate, their_weights = xor_permute(
+                    (packed, expert_ids, gate_probs, weights), k * plane
+                )
+            else:
+                p_packed, p_ids, p_gate = xor_permute((packed, expert_ids, gate_probs), k * plane)
+            got.append((p_packed, p_ids, p_gate))
+        both = jnp.concatenate([g[0] for g in got], axis=0)
+        ids2 = jnp.concatenate([g[1].reshape(-1) for g in got])
+        gate2 = jnp.concatenate([g[2].reshape(-1) for g in got])
         holder2 = holder_of(ids2)
-        rank2 = jnp.concatenate(
-            [entry_ranks(flat_ids, axis_width), entry_ranks(p_ids.reshape(-1), axis_width)]
-        )
-        src2 = jnp.arange(2 * entry_count, dtype=jnp.int32) // entry_count
-        in_half = holder2 // half_axis == my_index // half_axis
-        lane2 = holder2 % half_axis
-        chunk = 2 * slot_cap
+        rank2 = jnp.concatenate([entry_ranks(g[1].reshape(-1), axis_width) for g in got])
+        src2 = jnp.arange(column * entry_count, dtype=jnp.int32) // entry_count
+        in_half = holder2 // plane == my_index // plane
+        lane2 = holder2 % plane
+        chunk = column * slot_cap
         slot2 = lane2 * chunk + src2 * slot_cap + rank2
         slot_hit = (
-            jnp.arange(half_axis * chunk, dtype=jnp.int32)[:, None] == slot2[None, :]
+            jnp.arange(plane * chunk, dtype=jnp.int32)[:, None] == slot2[None, :]
         ) & in_half[None, :]
-        tok_hit = jnp.any(slot_hit.reshape(half_axis * chunk, 2 * tok_rows, route_count), axis=2)
+        tok_hit = jnp.any(
+            slot_hit.reshape(plane * chunk, column * tok_rows, route_count), axis=2
+        )
         tok_pick = tok_hit.astype(jnp.bfloat16)
         send_both = jnp.dot(tok_pick, both, preferred_element_type=jnp.float32).astype(
             jnp.bfloat16
@@ -116,12 +124,12 @@
         send_gate = jnp.sum(jnp.where(slot_hit, wire2[None, :], 0.0), axis=1)
         send_all = jnp.concatenate([send_both, with_tile(send_gate)], axis=1)
 
-        halves = [list(range(h * half_axis, (h + 1) * half_axis)) for h in range(2)]
+        planes = [list(range(h * plane, (h + 1) * plane)) for h in range(column)]
 
         def spread(value):
-            parts = value.reshape((half_axis, chunk) + value.shape[1:])
+            parts = value.reshape((plane, chunk) + value.shape[1:])
             moved = lax.all_to_all(
-                parts, "expert", 0, 0, tiled=True, axis_index_groups=halves
+                parts, "expert", 0, 0, tiled=True, axis_index_groups=planes
             )
             return moved.reshape(value.shape)
 
@@ -199,7 +207,9 @@
         back_rows = back_all[:, :model_width]
         back_gate = back_all[:, model_width].astype(jnp.float32)
         weight_of = jnp.where(slot_hit, gate2[None, :], 0.0)
-        weight_of = jnp.sum(weight_of.reshape(half_axis * chunk, 2 * tok_rows, route_count), axis=2)
+        weight_of = jnp.sum(
+            weight_of.reshape(plane * chunk, column * tok_rows, route_count), axis=2
+        )
         partial = lax.dot_general(
             weight_of,
             back_rows.astype(jnp.float32),
@@ -208,13 +218,23 @@
             preferred_element_type=jnp.float32,
         )
         prob2 = jnp.sum(jnp.where(slot_hit, back_gate[:, None], 0.0), axis=0)
-        p_partial, p_prob = from_partner(
-            (partial[tok_rows:], prob2[entry_count:].astype(jnp.bfloat16)), "expert", swap_bit
-        )
-        token_grad = (partial[:tok_rows] + p_partial).astype(jnp.bfloat16)
-        prob_grad = jnp.where(
-            in_half[:entry_count], prob2[:entry_count], p_prob.astype(jnp.float32)
-        )
+        token_acc = partial[:tok_rows]
+        prob_parts = [prob2[:entry_count]]
+        for k in range(1, column):
+            k_partial, k_prob = xor_permute(
+                (
+                    partial[k * tok_rows : (k + 1) * tok_rows].astype(jnp.bfloat16),
+                    prob2[k * entry_count : (k + 1) * entry_count].astype(jnp.bfloat16),
+                ),
+                k * plane,
+            )
+            token_acc = token_acc + k_partial.astype(jnp.float32)
+            prob_parts.append(k_prob.astype(jnp.float32))
+        token_grad = token_acc.astype(jnp.bfloat16)
+        served_by = (holder2[:entry_count] // plane) ^ (my_index // plane)
+        prob_grad = jnp.zeros((entry_count,), jnp.float32)
+        for k in range(column):
+            prob_grad = jnp.where(served_by == k, prob_parts[k], prob_grad)
         prob_grad = prob_grad.astype(jnp.bfloat16).reshape(tok_rows, route_count)
     else:
         back_rows, back_gate = [

time: 281 us -> 274 us (0.975)
  waiting for transfers between devices: 193 us -> 173 us
  starting transfers between devices: 28.5 us -> 37.5 us
    ppermute x8 -> x2, waiting for transfers between devices: 193 us -> 58.4 us  [from_partner(): lax.ppermute(value, axis, [(i, i ^ 1 << bit) for i in range(lax.axis_size...]
    ppermute x0 -> x16, waiting for transfers between devices: none -> 90.8 us  [xor_permute(): lax.ppermute(value, 'expert', [(i, i ^ mask) for i in range(lax.axis_size...]
    all_to_all x2, waiting for transfers between devices: 0.01 us -> 23.8 us  [spread(): lax.all_to_all(parts, 'expert', 0, 0, tiled=True, axis_index_groups=planes)]
    ppermute x0 -> x16, starting transfers between devices: none -> 22.8 us  [xor_permute(): lax.ppermute(value, 'expert', [(i, i ^ mask) for i in range(lax.axis_size...]
    ppermute x8 -> x2, starting transfers between devices: 14.9 us -> 2.98 us  [from_partner(): lax.ppermute(value, axis, [(i, i ^ 1 << bit) for i in range(lax.axis_size...]
  transfers between devices with their start and end apart: 12 -> 22, of which waited for: 5 -> 8; matrix products, arithmetic and copies ran while one was open for 17% -> 20% of each run, Pallas kernels for 0% -> 0%
where the time goes in v10:
time: 274 us
  waiting for transfers between devices  173 us (63%)
  starting transfers between devices  37.5 us (14%)
  other arithmetic  29.1 us (11%)
  matrix products  23.8 us (9%)
  local copies, waits for them, and re-layouts  8.3 us (3%)
    ppermute x16, waiting for transfers between devices, xor_permute(): lax.ppermute(value, 'expert', [(i, i ^ mask) for i in range(lax.axis_size...  90.8 us
    ppermute x2, waiting for transfers between devices, from_partner(): lax.ppermute(value, axis, [(i, i ^ 1 << bit) for i in range(lax.axis_size...  58.4 us
    all_to_all x2, waiting for transfers between devices, spread(): lax.all_to_all(parts, 'expert', 0, 0, tiled=True, axis_index_groups=planes)  23.8 us
    ppermute x16, starting transfers between devices, xor_permute(): lax.ppermute(value, 'expert', [(i, i ^ mask) for i in range(lax.axis_size...  22.8 us
    all_to_all x2, starting transfers between devices, spread(): lax.all_to_all(parts, 'expert', 0, 0, tiled=True, axis_index_groups=planes)  11.6 us
  transfers between devices with their start and end apart: 22, of which 8 were waited for; matrix products, arithmetic and copies ran while one was open for 20% of the time, Pallas kernels for 0%

profile of v10, /device:TPU:6, one launch (start us, length us, event | category | flops | bytes accessed | tf_op | source)
XLA Modules:
  0.0 273.6 jit_solution(16774774936285128287)
XLA Ops:
  0.6 3.7 %collective-permute-start.5 = (f32[32,8]{0,1:T(8,128)}, f32[32,8]{0,1:T(8,128)S(1)}, u32[]{:S(2)}, u32[]{:S(2)}) collective-permute-start(f32[32,8]{0,1:T(8,128)} %param.11), channel_id=1, source_target_pairs={{0,12},{1,13},{2,14},{3,15},{4,8},{5,9},{6,10},{7,11},{8,4},{9,5},... | collective-permute-start | bytes 3080 | tf_op jit(solution)/shard_map/ppermute | solution.py:48
  4.3 1.9 collective-permute-start.2
  6.2 1.0 collective-permute-start.1
  7.2 1.5 collective-permute-start
  8.7 0.8 copy.84
  10.7 1.0 constant_dynamic-update-slice_fusion.2
  11.7 1.0 constant_dynamic-update-slice_fusion.1
  12.7 1.3 fusion.84
  16.5 3.0 %collective-permute-start.8 = (bf16[32,7168]{1,0:T(8,128)(2,1)S(1)}, bf16[32,7168]{1,0:T(8,128)(2,1)S(1)}, u32[]{:S(2)}, u32[]{:S(2)}) collective-permute-start(bf16[32,7168]{1,0:T(8,128)(2,1)S(1)} %constant_dynamic-update-slice_fusion.1), channel_id=1, source_target_pairs={{0,12},{1,13},{2,14},{3,15},{4,8},{5,9},{6,10},{7,11},{8,4},{9,5},... | collective-permute-start | bytes 1376264 | tf_op jit(solution)/shard_map/ppermute | solution.py:48
  23.2 0.7 select_reduce_fusion.3
  24.4 1.5 collective-permute-start.6
  26.1 1.5 collective-permute-start.9
  29.1 2.8 %collective-permute-done.8 = bf16[32,7168]{1,0:T(8,128)(2,1)S(1)} collective-permute-done((bf16[32,7168]{1,0:T(8,128)(2,1)S(1)}, bf16[32,7168]{1,0:T(8,128)(2,1)S(1)}, u32[]{:S(2)}, u32[]{:S(2)}) %collective-permute-start.8) | collective-permute-done | bytes 458784 | tf_op jit(solution)/shard_map/ppermute | solution.py:48
  31.9 56.5 %collective-permute-done.7 = bf16[32,7168]{1,0:T(8,128)(2,1)S(1)} collective-permute-done((bf16[32,7168]{1,0:T(8,128)(2,1)S(1)}, bf16[32,7168]{1,0:T(8,128)(2,1)S(1)}, u32[]{:S(2)}, u32[]{:S(2)}) %collective-permute-start.7) | collective-permute-done | bytes 458784 | tf_op jit(solution)/shard_map/ppermute | solution.py:48
  88.4 1.5 convolution_convert_fusion
  89.9 2.5 pad_maximum_fusion
  92.4 5.5 %all-to-all-start = ((bf16[4,80,7296]{2,1,0:T(8,128)(2,1)}), bf16[4,80,7296]{2,1,0:T(8,128)(2,1)}, u32[]{:S(2)}, u32[]{:S(2)}) async-start(bf16[4,80,7296]{2,1,0:T(8,128)(2,1)} %bitcast.119), calls=%async_computation | async-start | bytes 9338880 | tf_op jit(solution)/shard_map/all_to_all | solution.py:131
  97.9 19.0 %collective-permute-done.9 = bf16[1,1792,3,128]{3,1,2,0:T(8,128)(2,1)} collective-permute-done((bf16[1,1792,3,128]{3,1,2,0:T(8,128)(2,1)}, bf16[1,1792,3,128]{3,1,2,0:T(8,128)(2,1)}, u32[]{:S(2)}, u32[]{:S(2)}) %collective-permute-start.9) | collective-permute-done | bytes 1376288 | tf_op jit(solution)/shard_map/ppermute | solution.py:48
  116.9 1.5 broadcast_select_fusion.2
  118.6 2.9 %collective-permute-start.18 = (bf16[1,1792,3,128]{3,1,2,0:T(8,128)(2,1)}, bf16[1,1792,3,128]{3,1,2,0:T(8,128)(2,1)}, u32[]{:S(2)}, u32[]{:S(2)}) collective-permute-start(bf16[1,1792,3,128]{3,1,2,0:T(8,128)(2,1)} %param.13), channel_id=1, source_target_pairs={{0,8},{1,9},{2,10},{3,11},{4,12},{5,13},{6,14},{7,15},{8,0},{9,1},... | collective-permute-start | bytes 4128776 | tf_op jit(solution)/shard_map/ppermute | solution.py:8
  122.0 1.5 slice_bitcast_fusion
  123.5 23.8 %all-to-all-done = bf16[4,80,7296]{2,1,0:T(8,128)(2,1)} async-done(((bf16[4,80,7296]{2,1,0:T(8,128)(2,1)}), bf16[4,80,7296]{2,1,0:T(8,128)(2,1)}, u32[]{:S(2)}, u32[]{:S(2)}) %all-to-all-start) | async-done | bytes 4669472 | tf_op jit(solution)/shard_map/all_to_all | solution.py:131
  147.3 1.0 convert_reduce_fusion.1
  148.3 2.4 fusion.23
  150.7 2.4 fusion.34
  153.2 2.4 multiply_convert_fusion.5
  155.6 2.7 %fusion.2 = bf16[3584,1,128]{2,0,1:T(8,128)(2,1)S(1)} fusion(bf16[320,128]{1,0:T(8,128)(2,1)S(1)} %get-tuple-element.47, f32[320]{0:T(512)S(1)} %convert_reduce_fusion.1, bf16[320,7296]{1,0:T(8,128)(2,1)} %bitcast.9), kind=kOutput, calls=%fused_computation.7 | convolution fusion | flops 297500672 | bytes 3294464 | tf_op jit(solution)/shard_map/dot_general | solution.py:182
  158.3 2.6 fusion.1
  160.9 2.6 fusion
  163.9 1.2 broadcast_select_fusion
  165.1 2.9 %fusion.31 = bf16[320]{0:T(512)(128)(2,1)S(1)} fusion(bf16[320,7296]{1,0:T(8,128)(2,1)} %bitcast.9, bf16[3584,3,128]{2,0,1:T(8,128)(2,1)} %copy-done.2, bf16[320,128]{1,0:T(8,128)(2,1)S(1)} %get-tuple-element.47), kind=kOutput, calls=%fused_computation.53 | convolution fusion | flops 293723840 | bytes 3293824 | tf_op jit(solution)/shard_map/dot_general | solution.py:168
  168.0 0.8 convolution_convert_fusion.1
  168.9 1.6 pad_maximum_fusion.2
  170.4 6.1 %all-to-all-start.1 = ((bf16[4,80,3712]{2,1,0:T(8,128)(2,1)}), bf16[4,80,3712]{2,1,0:T(8,128)(2,1)}, u32[]{:S(2)}, u32[]{:S(2)}) async-start(bf16[4,80,3712]{2,1,0:T(8,128)(2,1)} %bitcast.120), calls=%async_computation.1 | async-start | bytes 4751360 | tf_op jit(solution)/shard_map/all_to_all | solution.py:131
  177.2 33.1 %collective-permute-done.19 = bf16[1,1792,3,128]{3,1,2,0:T(8,128)(2,1)} collective-permute-done((bf16[1,1792,3,128]{3,1,2,0:T(8,128)(2,1)}, bf16[1,1792,3,128]{3,1,2,0:T(8,128)(2,1)}, u32[]{:S(2)}, u32[]{:S(2)}) %collective-permute-start.19) | collective-permute-done | bytes 1376288 | tf_op jit(solution)/shard_map/ppermute | solution.py:8
  210.3 4.2 %fusion.3 = (bf16[1,1792,3,128]{3,1,2,0:T(8,128)(2,1)}, bf16[1792,3,128]{2,0,1:T(8,128)(2,1)S(1)}) fusion(bf16[1792,3,128]{2,0,1:T(8,128)(2,1)} %collective-permute-done.17, bf16[1,1792,3,128]{3,1,2,0:T(8,128)(2,1)} %collective-permute-done.19, bf16[1,1792,3,128]{3,1,2,0:T(8,128)(2,1)} %param.14, pred[]{:T(512)S(6)} %eq.256, ...), kind=kLoop, calls=%fused_computation.13 | loop fusion | flops 8257536 | bytes 9633794 | tf_op jit(solution)/shard_map/convert_element_type | solution.py:201
  214.5 25.3 %collective-permute-done.18 = bf16[1,1792,3,128]{3,1,2,0:T(8,128)(2,1)} collective-permute-done((bf16[1,1792,3,128]{3,1,2,0:T(8,128)(2,1)}, bf16[1,1792,3,128]{3,1,2,0:T(8,128)(2,1)}, u32[]{:S(2)}, u32[]{:S(2)}) %collective-permute-start.18) | collective-permute-done | bytes 1376288 | tf_op jit(solution)/shard_map/ppermute | solution.py:8
  239.8 3.7 %fusion.4 = bf16[1,1792,3,128]{3,1,2,0:T(8,128)(2,1)} fusion(bf16[1792,3,128]{2,0,1:T(8,128)(2,1)} %collective-permute-done.17, bf16[1792,3,128]{2,0,1:T(8,128)(2,1)S(1)} %get-tuple-element.35, bf16[1,1792,3,128]{3,1,2,0:T(8,128)(2,1)} %collective-permute-done.18, bf16[1,1792,3,128]{3,1,2,0:T(8,128)(2,1)S(1)} %copy-done.5, pred[]{:T(512)S(6)} %eq.256), kind=kLoop, calls=%fused_computation.15 | loop fusion | flops 6193152 | bytes 6881281 | tf_op jit(solution)/shard_map/convert_element_type | solution.py:200
  243.5 1.0 convert_reduce_fusion
  244.5 3.4 %fusion.90 = (bf16[128,3584]{1,0:T(8,128)(2,1)S(1)}, f32[128,3584]{1,0:T(8,128)S(1)}) fusion(f32[320,128]{1,0:T(8,128)S(1)} %select_reduce_fusion.2, bf16[320,3712]{1,0:T(8,128)(2,1)} %bitcast.15), kind=kOutput, calls=%fused_computation.193 | convolution fusion | flops 1762066432 | bytes 5210112 | tf_op jit(solution)/shard_map/dot_general | solution.py:213
  248.4 2.3 collective-permute-start.13
  250.6 1.3 collective-permute-start.12
  251.9 0.9 collective-permute-start.11
  252.8 1.8 collective-permute-start.15
  254.6 1.6 collective-permute-start.14
  256.3 3.2 %multiply_bitcast_fusion = f32[1,1792,3,128]{3,1,2,0:T(8,128)} fusion(bf16[1792,3,128]{2,0,1:T(8,128)(2,1)} %collective-permute-done.17, bf16[1792,3,128]{2,0,1:T(8,128)(2,1)S(1)} %copy-done.1), kind=kLoop, calls=%fused_computation.17 | loop fusion | flops 2752512 | bytes 5505024 | tf_op jit(solution)/shard_map/broadcast_in_dim | solution.py:197
  259.5 12.5 %collective-permute-done.15 = bf16[256]{0:T(256)(128)(2,1)S(1)} collective-permute-done((bf16[256]{0:T(256)(128)(2,1)S(1)}, bf16[256]{0:T(256)(128)(2,1)S(1)}, u32[]{:S(2)}, u32[]{:S(2)}) %collective-permute-start.15) | collective-permute-done | bytes 544 | tf_op jit(solution)/shard_map/ppermute | solution.py:48
  272.8 0.8 fusion.37
  (125 shorter events, 11.6 us)
Async XLA Ops:
  0.6 23.8 %collective-permute-start.5 = (f32[32,8]{0,1:T(8,128)}, f32[32,8]{0,1:T(8,128)S(1)}, u32[]{:S(2)}, u32[]{:S(2)}) collective-permute-start(f32[32,8]{0,1:T(8,128)} %param.11), channel_id=1, source_target_pairs={{0,12},{1,13},{2,14},{3,15},{4,8},{5,9},{6,10},{7,11},{8,4},{9,5},... | collective-permute-start | bytes 3080 | tf_op jit(solution)/shard_map/ppermute | solution.py:48
  4.3 21.8 %collective-permute-start.4 = (f32[32,8]{0,1:T(8,128)}, f32[32,8]{0,1:T(8,128)S(1)}, u32[]{:S(2)}, u32[]{:S(2)}) collective-permute-start(f32[32,8]{0,1:T(8,128)} %param.11), channel_id=1, source_target_pairs={{0,8},{1,9},{2,10},{3,11},{4,12},{5,13},{6,14},{7,15},{8,0},{9,1},... | collective-permute-start | bytes 3080 | tf_op jit(solution)/shard_map/ppermute | solution.py:48
  4.3 11.2 %collective-permute-start.2 = (s32[32,8]{0,1:T(8,128)}, s32[32,8]{0,1:T(8,128)S(1)}, u32[]{:S(2)}, u32[]{:S(2)}) collective-permute-start(s32[32,8]{0,1:T(8,128)} %param.10), channel_id=1, source_target_pairs={{0,12},{1,13},{2,14},{3,15},{4,8},{5,9},{6,10},{7,11},{8,4},{9,5},... | collective-permute-start | bytes 3080 | tf_op jit(solution)/shard_map/ppermute | solution.py:48
  6.2 10.3 %collective-permute-start.1 = (s32[32,8]{0,1:T(8,128)}, s32[32,8]{0,1:T(8,128)S(1)}, u32[]{:S(2)}, u32[]{:S(2)}) collective-permute-start(s32[32,8]{0,1:T(8,128)} %param.10), channel_id=1, source_target_pairs={{0,8},{1,9},{2,10},{3,11},{4,12},{5,13},{6,14},{7,15},{8,0},{9,1},... | collective-permute-start | bytes 3080 | tf_op jit(solution)/shard_map/ppermute | solution.py:48
  7.2 12.6 %collective-permute-start = (s32[32,8]{0,1:T(8,128)}, s32[32,8]{0,1:T(8,128)S(1)}, u32[]{:S(2)}, u32[]{:S(2)}) collective-permute-start(s32[32,8]{0,1:T(8,128)} %param.10), channel_id=1, source_target_pairs={{0,4},{1,5},{2,6},{3,7},{4,0},{5,1},{6,2},{7,3},{8,12},{9,13},{10,... | collective-permute-start | bytes 3080 | tf_op jit(solution)/shard_map/ppermute | solution.py:48
  15.5 12.4 %collective-permute-start.3 = (f32[32,8]{0,1:T(8,128)}, f32[32,8]{0,1:T(8,128)S(1)}, u32[]{:S(2)}, u32[]{:S(2)}) collective-permute-start(f32[32,8]{0,1:T(8,128)} %param.11), channel_id=1, source_target_pairs={{0,4},{1,5},{2,6},{3,7},{4,0},{5,1},{6,2},{7,3},{8,12},{9,13},{10,... | collective-permute-start | bytes 3080 | tf_op jit(solution)/shard_map/ppermute | solution.py:48
  16.5 15.4 %collective-permute-start.8 = (bf16[32,7168]{1,0:T(8,128)(2,1)S(1)}, bf16[32,7168]{1,0:T(8,128)(2,1)S(1)}, u32[]{:S(2)}, u32[]{:S(2)}) collective-permute-start(bf16[32,7168]{1,0:T(8,128)(2,1)S(1)} %constant_dynamic-update-slice_fusion.1), channel_id=1, source_target_pairs={{0,12},{1,13},{2,14},{3,15},{4,8},{5,9},{6,10},{7,11},{8,4},{9,5},... | collective-permute-start | bytes 1376264 | tf_op jit(solution)/shard_map/ppermute | solution.py:48
  19.8 68.5 %collective-permute-start.7 = (bf16[32,7168]{1,0:T(8,128)(2,1)S(1)}, bf16[32,7168]{1,0:T(8,128)(2,1)S(1)}, u32[]{:S(2)}, u32[]{:S(2)}) collective-permute-start(bf16[32,7168]{1,0:T(8,128)(2,1)S(1)} %constant_dynamic-update-slice_fusion.1), channel_id=1, source_target_pairs={{0,8},{1,9},{2,10},{3,11},{4,12},{5,13},{6,14},{7,15},{8,0},{9,1},... | collective-permute-start | bytes 1376264 | tf_op jit(solution)/shard_map/ppermute | solution.py:48
  24.4 64.0 %collective-permute-start.6 = (bf16[32,7168]{1,0:T(8,128)(2,1)S(1)}, bf16[32,7168]{1,0:T(8,128)(2,1)S(1)}, u32[]{:S(2)}, u32[]{:S(2)}) collective-permute-start(bf16[32,7168]{1,0:T(8,128)(2,1)S(1)} %constant_dynamic-update-slice_fusion.1), channel_id=1, source_target_pairs={{0,4},{1,5},{2,6},{3,7},{4,0},{5,1},{6,2},{7,3},{8,12},{9,13},{10,... | collective-permute-start | bytes 1376264 | tf_op jit(solution)/shard_map/ppermute | solution.py:48
  26.1 90.8 %collective-permute-start.9 = (bf16[1,1792,3,128]{3,1,2,0:T(8,128)(2,1)}, bf16[1,1792,3,128]{3,1,2,0:T(8,128)(2,1)}, u32[]{:S(2)}, u32[]{:S(2)}) collective-permute-start(bf16[1,1792,3,128]{3,1,2,0:T(8,128)(2,1)} %param.12), channel_id=1, source_target_pairs={{0,8},{1,9},{2,10},{3,11},{4,12},{5,13},{6,14},{7,15},{8,0},{9,1},... | collective-permute-start | bytes 4128776 | tf_op jit(solution)/shard_map/ppermute | solution.py:48
  92.4 24.5 %copy-start.4 = (bf16[1,1792,3,128]{3,1,2,0:T(8,128)(2,1)S(1)}, bf16[1,1792,3,128]{3,1,2,0:T(8,128)(2,1)}, u32[]{:S(2)}) copy-start(bf16[1,1792,3,128]{3,1,2,0:T(8,128)(2,1)} %param.12) | copy-start | bytes 4128772
  92.4 54.9 %all-to-all-start = ((bf16[4,80,7296]{2,1,0:T(8,128)(2,1)}), bf16[4,80,7296]{2,1,0:T(8,128)(2,1)}, u32[]{:S(2)}, u32[]{:S(2)}) async-start(bf16[4,80,7296]{2,1,0:T(8,128)(2,1)} %bitcast.119), calls=%async_computation | async-start | bytes 9338880 | tf_op jit(solution)/shard_map/all_to_all | solution.py:131
  118.4 3.4 %copy-start.3 = (bf16[1,1792,3,128]{3,1,2,0:T(8,128)(2,1)}, bf16[1,1792,3,128]{3,1,2,0:T(8,128)(2,1)S(1)}, u32[]{:S(2)}) copy-start(bf16[1,1792,3,128]{3,1,2,0:T(8,128)(2,1)S(1)} %broadcast_select_fusion.2) | copy-start | bytes 4128772
  118.4 3.2 %collective-permute-start.10 = (bf16[1,1792,3,128]{3,1,2,0:T(8,128)(2,1)S(1)}, bf16[1,1792,3,128]{3,1,2,0:T(8,128)(2,1)S(1)}, u32[]{:S(2)}, u32[]{:S(2)}) collective-permute-start(bf16[1,1792,3,128]{3,1,2,0:T(8,128)(2,1)S(1)} %broadcast_select_fusion.2), channel_id=1, source_target_pairs={{0,16},{16,0},{1,17},{17,1},{2,18},{18,2},{3,19},{19,3},{4,20},{20... | collective-permute-start | bytes 4128776 | tf_op jit(solution)/shard_map/ppermute | solution.py:151
  118.5 91.8 %collective-permute-start.19 = (bf16[1,1792,3,128]{3,1,2,0:T(8,128)(2,1)}, bf16[1,1792,3,128]{3,1,2,0:T(8,128)(2,1)}, u32[]{:S(2)}, u32[]{:S(2)}) collective-permute-start(bf16[1,1792,3,128]{3,1,2,0:T(8,128)(2,1)} %param.14), channel_id=1, source_target_pairs={{0,8},{1,9},{2,10},{3,11},{4,12},{5,13},{6,14},{7,15},{8,0},{9,1},... | collective-permute-start | bytes 4128776 | tf_op jit(solution)/shard_map/ppermute | solution.py:8
  118.6 121.2 %collective-permute-start.18 = (bf16[1,1792,3,128]{3,1,2,0:T(8,128)(2,1)}, bf16[1,1792,3,128]{3,1,2,0:T(8,128)(2,1)}, u32[]{:S(2)}, u32[]{:S(2)}) collective-permute-start(bf16[1,1792,3,128]{3,1,2,0:T(8,128)(2,1)} %param.13), channel_id=1, source_target_pairs={{0,8},{1,9},{2,10},{3,11},{4,12},{5,13},{6,14},{7,15},{8,0},{9,1},... | collective-permute-start | bytes 4128776 | tf_op jit(solution)/shard_map/ppermute | solution.py:8
  122.0 31.2 %copy-start.2 = (bf16[3584,3,128]{2,0,1:T(8,128)(2,1)}, bf16[3584,3,128]{2,0,1:T(8,128)(2,1)S(1)}, u32[]{:S(2)}) copy-start(bf16[3584,3,128]{2,0,1:T(8,128)(2,1)S(1)} %maximum_bitcast_fusion) | copy-start | bytes 8257540
  165.1 2.9 %copy-start.6 = (bf16[3584,128]{1,0:T(8,128)(2,1)S(1)}, bf16[3584,128]{1,0:T(8,128)(2,1)}, u32[]{:S(2)}) copy-start(bf16[3584,128]{1,0:T(8,128)(2,1)} %get-tuple-element.39) | copy-start | bytes 2752516
  165.1 2.9 %copy-start.7 = (bf16[3584,128]{1,0:T(8,128)(2,1)S(1)}, bf16[3584,128]{1,0:T(8,128)(2,1)}, u32[]{:S(2)}) copy-start(bf16[3584,128]{1,0:T(8,128)(2,1)} %get-tuple-element.40) | copy-start | bytes 2752516
  165.1 45.2 %collective-permute-start.17 = (bf16[1792,3,128]{2,0,1:T(8,128)(2,1)}, bf16[1792,3,128]{2,0,1:T(8,128)(2,1)}, u32[]{:S(2)}, u32[]{:S(2)}) collective-permute-start(bf16[1792,3,128]{2,0,1:T(8,128)(2,1)} %broadcast_select_fusion), channel_id=1, source_target_pairs={{0,16},{16,0},{1,17},{17,1},{2,18},{18,2},{3,19},{19,3},{4,20},{20... | collective-permute-start | bytes 4128776 | tf_op jit(solution)/shard_map/ppermute | solution.py:191
  170.4 6.1 %copy-start.8 = (f32[32,8]{0,1:T(8,128)S(1)}, f32[32,8]{0,1:T(8,128)}, u32[]{:S(2)}) copy-start(f32[32,8]{0,1:T(8,128)} %param.11) | copy-start | bytes 3076
  170.4 73.0 %all-to-all-start.1 = ((bf16[4,80,3712]{2,1,0:T(8,128)(2,1)}), bf16[4,80,3712]{2,1,0:T(8,128)(2,1)}, u32[]{:S(2)}, u32[]{:S(2)}) async-start(bf16[4,80,3712]{2,1,0:T(8,128)(2,1)} %bitcast.120), calls=%async_computation.1 | async-start | bytes 4751360 | tf_op jit(solution)/shard_map/all_to_all | solution.py:131
  177.2 62.6 %copy-start.5 = (bf16[1,1792,3,128]{3,1,2,0:T(8,128)(2,1)S(1)}, bf16[1,1792,3,128]{3,1,2,0:T(8,128)(2,1)}, u32[]{:S(2)}) copy-start(bf16[1,1792,3,128]{3,1,2,0:T(8,128)(2,1)} %param.13) | copy-start | bytes 4128772
  214.5 25.3 %copy-start = (bf16[1792,3,128]{2,0,1:T(8,128)(2,1)}, bf16[1792,3,128]{2,0,1:T(8,128)(2,1)S(1)}, u32[]{:S(2)}) copy-start(bf16[1792,3,128]{2,0,1:T(8,128)(2,1)S(1)} %get-tuple-element.35) | copy-start | bytes 4128772
  244.5 11.8 %copy-start.1 = (bf16[1792,3,128]{2,0,1:T(8,128)(2,1)S(1)}, bf16[1792,3,128]{2,0,1:T(8,128)(2,1)}, u32[]{:S(2)}) copy-start(bf16[1792,3,128]{2,0,1:T(8,128)(2,1)} %copy-done) | copy-start | bytes 4128772
  248.2 6.4 %collective-permute-start.16 = (bf16[256]{0:T(256)(128)(2,1)S(1)}, bf16[256]{0:T(256)(128)(2,1)S(1)}, u32[]{:S(2)}, u32[]{:S(2)}) collective-permute-start(bf16[256]{0:T(256)(128)(2,1)S(1)} %get-tuple-element.51), channel_id=1, source_target_pairs={{0,4},{1,5},{2,6},{3,7},{4,0},{5,1},{6,2},{7,3},{8,12},{9,13},{10,... | collective-permute-start | bytes 1544 | tf_op jit(solution)/shard_map/ppermute | solution.py:48
  248.4 24.4 %collective-permute-start.13 = (bf16[32,3584]{1,0:T(8,128)(2,1)S(1)}, bf16[32,3584]{1,0:T(8,128)(2,1)S(1)}, u32[]{:S(2)}, u32[]{:S(2)}) collective-permute-start(bf16[32,3584]{1,0:T(8,128)(2,1)S(1)} %get-tuple-element.44), channel_id=1, source_target_pairs={{0,12},{1,13},{2,14},{3,15},{4,8},{5,9},{6,10},{7,11},{8,4},{9,5},... | collective-permute-start | bytes 688136 | tf_op jit(solution)/shard_map/ppermute | solution.py:48
  250.6 22.2 %collective-permute-start.12 = (bf16[32,3584]{1,0:T(8,128)(2,1)S(1)}, bf16[32,3584]{1,0:T(8,128)(2,1)S(1)}, u32[]{:S(2)}, u32[]{:S(2)}) collective-permute-start(bf16[32,3584]{1,0:T(8,128)(2,1)S(1)} %get-tuple-element.45), channel_id=1, source_target_pairs={{0,8},{1,9},{2,10},{3,11},{4,12},{5,13},{6,14},{7,15},{8,0},{9,1},... | collective-permute-start | bytes 688136 | tf_op jit(solution)/shard_map/ppermute | solution.py:48
  251.9 20.9 %collective-permute-start.11 = (bf16[32,3584]{1,0:T(8,128)(2,1)S(1)}, bf16[32,3584]{1,0:T(8,128)(2,1)S(1)}, u32[]{:S(2)}, u32[]{:S(2)}) collective-permute-start(bf16[32,3584]{1,0:T(8,128)(2,1)S(1)} %get-tuple-element.43), channel_id=1, source_target_pairs={{0,4},{1,5},{2,6},{3,7},{4,0},{5,1},{6,2},{7,3},{8,12},{9,13},{10,... | collective-permute-start | bytes 688136 | tf_op jit(solution)/shard_map/ppermute | solution.py:48
  252.8 19.2 %collective-permute-start.15 = (bf16[256]{0:T(256)(128)(2,1)S(1)}, bf16[256]{0:T(256)(128)(2,1)S(1)}, u32[]{:S(2)}, u32[]{:S(2)}) collective-permute-start(bf16[256]{0:T(256)(128)(2,1)S(1)} %get-tuple-element.50), channel_id=1, source_target_pairs={{0,8},{1,9},{2,10},{3,11},{4,12},{5,13},{6,14},{7,15},{8,0},{9,1},... | collective-permute-start | bytes 1544 | tf_op jit(solution)/shard_map/ppermute | solution.py:48
  254.6 17.4 %collective-permute-start.14 = (bf16[256]{0:T(256)(128)(2,1)S(1)}, bf16[256]{0:T(256)(128)(2,1)S(1)}, u32[]{:S(2)}, u32[]{:S(2)}) collective-permute-start(bf16[256]{0:T(256)(128)(2,1)S(1)} %get-tuple-element.49), channel_id=1, source_target_pairs={{0,12},{1,13},{2,14},{3,15},{4,8},{5,9},{6,10},{7,11},{8,4},{9,5},... | collective-permute-start | bytes 1544 | tf_op jit(solution)/shard_map/ppermute | solution.py:48

commit v11 on v10

--- a/solution.py
+++ b/solution.py
@@ -145,7 +145,15 @@
     first_moment, second_moment, _ = lax.optimization_barrier(
         (first_moment, second_moment, their_weights)
     )
-    their_moments = from_partner((first_moment, second_moment), "expert", swap_bit)
+    if two_stage:
+        pairs = [[p, p + half_axis] for p in range(half_axis)]
+        pair_both = lax.all_gather(
+            jnp.stack([first_moment, second_moment]), "expert", axis_index_groups=pairs
+        )
+        mine_first = my_index < half_axis
+        their_moments = jnp.where(mine_first, pair_both[1], pair_both[0])
+    else:
+        their_moments = from_partner((first_moment, second_moment), "expert", swap_bit)
     weights = jnp.where(swapped, their_weights, weights)
     if groups == 2:
         other = lax.ppermute(weights, "dp", [(0, 1), (1, 0)])

time: 274 us -> 301 us (1.099)
  between operations: 1.81 us -> 15.2 us
  other arithmetic: 29.1 us -> 37.1 us
  waiting for transfers between devices: 173 us -> 179 us
  starting transfers between devices: 37.5 us -> 34.3 us
    ppermute x2 -> x0, waiting for transfers between devices: 58.4 us -> none  [from_partner(): lax.ppermute(value, axis, [(i, i ^ 1 << bit) for i in range(lax.axis_size...]
    all_gather x0 -> x1, waiting for transfers between devices: none -> 37.4 us  [on_device(): lax.all_gather(jnp.stack([first_moment, second_moment]), 'expert', axis_i...]
    all_to_all x2, waiting for transfers between devices: 23.8 us -> 37.9 us  [spread(): lax.all_to_all(parts, 'expert', 0, 0, tiled=True, axis_index_groups=planes)]
    ppermute x16, waiting for transfers between devices: 90.8 us -> 102 us  [xor_permute(): lax.ppermute(value, 'expert', [(i, i ^ mask) for i in range(lax.axis_size...]
  transfers between devices with their start and end apart: 22 -> 21, of which waited for: 8 -> 8; matrix products, arithmetic and copies ran while one was open for 20% -> 20% of each run, Pallas kernels for 0% -> 0%
where the time goes in v11:
time: 301 us; the launch traced here: 299 us
  waiting for transfers between devices  179 us (59%)
  other arithmetic  37.1 us (12%)
  starting transfers between devices  34.3 us (11%)
  matrix products  24.7 us (8%)
  between operations  15.2 us (5%)
  local copies, waits for them, and re-layouts  8.92 us (3%)
    ppermute x16, waiting for transfers between devices, xor_permute(): lax.ppermute(value, 'expert', [(i, i ^ mask) for i in range(lax.axis_size...  102 us
    all_to_all x2, waiting for transfers between devices, spread(): lax.all_to_all(parts, 'expert', 0, 0, tiled=True, axis_index_groups=planes)  37.9 us
    all_gather x1, waiting for transfers between devices, on_device(): lax.all_gather(jnp.stack([first_moment, second_moment]), 'expert', axis_i...  37.4 us
    ppermute x16, starting transfers between devices, xor_permute(): lax.ppermute(value, 'expert', [(i, i ^ mask) for i in range(lax.axis_size...  22.7 us
    all_to_all x2, starting transfers between devices, spread(): lax.all_to_all(parts, 'expert', 0, 0, tiled=True, axis_index_groups=planes)  11.5 us
  transfers between devices with their start and end apart: 21, of which 8 were waited for; matrix products, arithmetic and copies ran while one was open for 20% of the time, Pallas kernels for 0%

profile of v11, /device:TPU:6, one launch (start us, length us, event | category | flops | bytes accessed | tf_op | source)
XLA Modules:
  0.0 298.8 jit_solution(8939943999359862639)
XLA Ops:
  7.2 3.7 %collective-permute-start.5 = (f32[32,8]{0,1:T(8,128)}, f32[32,8]{0,1:T(8,128)S(1)}, u32[]{:S(2)}, u32[]{:S(2)}) collective-permute-start(f32[32,8]{0,1:T(8,128)} %param.11), channel_id=1, source_target_pairs={{0,12},{1,13},{2,14},{3,15},{4,8},{5,9},{6,10},{7,11},{8,4},{9,5},... | collective-permute-start | bytes 3080 | tf_op jit(solution)/shard_map/ppermute | solution.py:48
  10.8 1.9 collective-permute-start.2
  12.7 1.0 collective-permute-start.1
  13.8 1.5 collective-permute-start
  17.3 1.0 constant_dynamic-update-slice_fusion.2
  18.2 1.0 constant_dynamic-update-slice_fusion.1
  19.2 1.3 fusion.87
  23.0 3.0 collective-permute-start.8
  30.9 1.5 collective-permute-start.6
  32.7 1.5 collective-permute-start.9
  35.6 2.8 collective-permute-done.8
  38.4 56.5 %collective-permute-done.7 = bf16[32,7168]{1,0:T(8,128)(2,1)S(1)} collective-permute-done((bf16[32,7168]{1,0:T(8,128)(2,1)S(1)}, bf16[32,7168]{1,0:T(8,128)(2,1)S(1)}, u32[]{:S(2)}, u32[]{:S(2)}) %collective-permute-start.7) | collective-permute-done | bytes 458784 | tf_op jit(solution)/shard_map/ppermute | solution.py:48
  94.9 1.5 convolution_convert_fusion
  96.4 2.5 pad_maximum_fusion
  99.0 5.4 %all-to-all-start = ((bf16[4,80,7296]{2,1,0:T(8,128)(2,1)}), bf16[4,80,7296]{2,1,0:T(8,128)(2,1)}, u32[]{:S(2)}, u32[]{:S(2)}) async-start(bf16[4,80,7296]{2,1,0:T(8,128)(2,1)} %bitcast.137), calls=%async_computation | async-start | bytes 9338880 | tf_op jit(solution)/shard_map/all_to_all | solution.py:131
  104.4 19.1 %collective-permute-done.9 = bf16[1,1792,3,128]{3,1,2,0:T(8,128)(2,1)} collective-permute-done((bf16[1,1792,3,128]{3,1,2,0:T(8,128)(2,1)}, bf16[1,1792,3,128]{3,1,2,0:T(8,128)(2,1)}, u32[]{:S(2)}, u32[]{:S(2)}) %collective-permute-start.9) | collective-permute-done | bytes 1376288 | tf_op jit(solution)/shard_map/ppermute | solution.py:48
  123.4 2.6 broadcast_select_fusion.2
  126.0 1.8 pad_maximum_fusion.2
  127.8 1.7 collective-permute-done.10
  129.5 1.9 broadcast_select_fusion.4
  131.6 1.3 slice_bitcast_fusion.2
  132.9 20.9 %all-to-all-done = bf16[4,80,7296]{2,1,0:T(8,128)(2,1)} async-done(((bf16[4,80,7296]{2,1,0:T(8,128)(2,1)}), bf16[4,80,7296]{2,1,0:T(8,128)(2,1)}, u32[]{:S(2)}, u32[]{:S(2)}) %all-to-all-start) | async-done | bytes 4669472 | tf_op jit(solution)/shard_map/all_to_all | solution.py:131
  153.8 1.0 convert_reduce_fusion.1
  154.8 2.4 fusion.24
  157.2 2.4 fusion.37
  159.7 2.4 multiply_convert_fusion.5
  162.1 2.6 fusion.34
  165.7 1.6 pad_maximum_fusion.3
  167.3 6.1 %all-to-all-start.1 = ((bf16[4,80,3712]{2,1,0:T(8,128)(2,1)}), bf16[4,80,3712]{2,1,0:T(8,128)(2,1)}, u32[]{:S(2)}, u32[]{:S(2)}) async-start(bf16[4,80,3712]{2,1,0:T(8,128)(2,1)} %bitcast.14), calls=%async_computation.1 | async-start | bytes 4751360 | tf_op jit(solution)/shard_map/all_to_all | solution.py:131
  174.0 2.6 fusion.1
  176.6 2.6 fusion
  179.2 2.7 fusion.2
  182.3 17.0 %all-to-all-done.1 = bf16[4,80,3712]{2,1,0:T(8,128)(2,1)} async-done(((bf16[4,80,3712]{2,1,0:T(8,128)(2,1)}), bf16[4,80,3712]{2,1,0:T(8,128)(2,1)}, u32[]{:S(2)}, u32[]{:S(2)}) %all-to-all-start.1) | async-done | bytes 2375712 | tf_op jit(solution)/shard_map/all_to_all | solution.py:131
  199.3 1.0 convert_reduce_fusion
  200.7 4.6 %fusion.93 = (bf16[128,3584]{1,0:T(8,128)(2,1)S(1)}, f32[128,3584]{1,0:T(8,128)}) fusion(f32[320,128]{1,0:T(8,128)S(1)} %select_reduce_fusion.2, bf16[320,3712]{1,0:T(8,128)(2,1)} %bitcast.15), kind=kOutput, calls=%fused_computation.200 | convolution fusion | flops 1762066432 | bytes 5210112 | tf_op jit(solution)/shard_map/dot_general | solution.py:221
  205.3 0.8 fusion.91
  206.1 1.0 collective-permute-start.13
  207.1 2.5 collective-permute-start.12
  209.6 0.9 collective-permute-start.11
  211.0 2.9 collective-permute-start.14
  214.0 1.2 broadcast_select_fusion
  215.2 23.3 %collective-permute-done.15 = bf16[256]{0:T(256)(128)(2,1)S(1)} collective-permute-done((bf16[256]{0:T(256)(128)(2,1)S(1)}, bf16[256]{0:T(256)(128)(2,1)S(1)}, u32[]{:S(2)}, u32[]{:S(2)}) %collective-permute-start.15) | collective-permute-done | bytes 544 | tf_op jit(solution)/shard_map/ppermute | solution.py:48
  239.3 1.9 fusion.40
  241.1 37.4 %all-gather.3.cloned.1.call-done = bf16[4,1,1792,3,128]{4,2,3,1,0:T(8,128)(2,1)} async-done(((bf16[2,1,1792,3,128]{4,2,3,1,0:T(8,128)(2,1)}), bf16[4,1,1792,3,128]{4,2,3,1,0:T(8,128)(2,1)}) %all-gather.3.cloned.1.call-update) | async-done | bytes 5505040 | tf_op jit(solution)/shard_map/all_gather | solution.py:150
  278.5 3.0 %fusion.3 = bf16[1,2,1,1792,3,128]{5,3,4,2,1,0:T(8,128)(2,1)S(1)} fusion(bf16[4,1,1792,3,128]{4,2,3,0,1:T(8,128)(2,1)} %bitcast.140, pred[]{:T(512)S(6)} %lt.33), kind=kLoop, calls=%fused_computation.11 | loop fusion | flops 1376256 | bytes 8257537 | tf_op jit(solution)/shard_map/jit(_where)/select_n | solution.py:154
  281.5 3.8 %fusion.4 = (bf16[1,1792,3,128]{3,1,2,0:T(8,128)(2,1)}, bf16[1792,3,128]{2,0,1:T(8,128)(2,1)S(1)}) fusion(bf16[1792,3,128]{2,0,1:T(8,128)(2,1)} %collective-permute-done.17, bf16[1,1792,3,128]{3,1,2,0:T(8,128)(2,1)S(1)} %copy-done.1, bf16[1,2,1,1792,3,128]{5,3,4,2,1,0:T(8,128)(2,1)S(1)} %fusion.3, pred[]{:T(512)S(6)} %eq.256, ...), kind=kLoop, calls=%fused_computation.16 | loop fusion | flops 8257536 | bytes 9633794 | tf_op jit(solution)/shard_map/convert_element_type | solution.py:209
  285.3 3.3 %multiply_bitcast_fusion = f32[1,1792,3,128]{3,1,2,0:T(8,128)} fusion(bf16[1792,3,128]{2,0,1:T(8,128)(2,1)} %collective-permute-done.17, bf16[1792,3,128]{2,0,1:T(8,128)(2,1)S(1)} %get-tuple-element.41), kind=kLoop, calls=%fused_computation.20 | loop fusion | flops 2752512 | bytes 5505024 | tf_op jit(solution)/shard_map/broadcast_in_dim | solution.py:205
  288.6 3.3 %fusion.5 = bf16[1,1792,3,128]{3,1,2,0:T(8,128)(2,1)} fusion(bf16[1792,3,128]{2,0,1:T(8,128)(2,1)} %collective-permute-done.17, bf16[1792,3,128]{2,0,1:T(8,128)(2,1)S(1)} %get-tuple-element.41, bf16[1,1792,3,128]{3,1,2,0:T(8,128)(2,1)S(1)} %copy-done.3, bf16[1,2,1,1792,3,128]{5,3,4,2,1,0:T(8,128)(2,1)S(1)} %fusion.3, pred[]{:T(512)S(6)} %eq.256), kind=kLoop, calls=%fused_computation.18 | loop fusion | flops 6193152 | bytes 6881281 | tf_op jit(solution)/shard_map/convert_element_type | solution.py:208
  (122 shorter events, 14.0 us)
Async XLA Ops:
  7.2 23.8 %collective-permute-start.5 = (f32[32,8]{0,1:T(8,128)}, f32[32,8]{0,1:T(8,128)S(1)}, u32[]{:S(2)}, u32[]{:S(2)}) collective-permute-start(f32[32,8]{0,1:T(8,128)} %param.11), channel_id=1, source_target_pairs={{0,12},{1,13},{2,14},{3,15},{4,8},{5,9},{6,10},{7,11},{8,4},{9,5},... | collective-permute-start | bytes 3080 | tf_op jit(solution)/shard_map/ppermute | solution.py:48
  10.8 21.8 %collective-permute-start.4 = (f32[32,8]{0,1:T(8,128)}, f32[32,8]{0,1:T(8,128)S(1)}, u32[]{:S(2)}, u32[]{:S(2)}) collective-permute-start(f32[32,8]{0,1:T(8,128)} %param.11), channel_id=1, source_target_pairs={{0,8},{1,9},{2,10},{3,11},{4,12},{5,13},{6,14},{7,15},{8,0},{9,1},... | collective-permute-start | bytes 3080 | tf_op jit(solution)/shard_map/ppermute | solution.py:48
  10.8 11.2 %collective-permute-start.2 = (s32[32,8]{0,1:T(8,128)}, s32[32,8]{0,1:T(8,128)S(1)}, u32[]{:S(2)}, u32[]{:S(2)}) collective-permute-start(s32[32,8]{0,1:T(8,128)} %param.10), channel_id=1, source_target_pairs={{0,12},{1,13},{2,14},{3,15},{4,8},{5,9},{6,10},{7,11},{8,4},{9,5},... | collective-permute-start | bytes 3080 | tf_op jit(solution)/shard_map/ppermute | solution.py:48
  12.7 10.3 %collective-permute-start.1 = (s32[32,8]{0,1:T(8,128)}, s32[32,8]{0,1:T(8,128)S(1)}, u32[]{:S(2)}, u32[]{:S(2)}) collective-permute-start(s32[32,8]{0,1:T(8,128)} %param.10), channel_id=1, source_target_pairs={{0,8},{1,9},{2,10},{3,11},{4,12},{5,13},{6,14},{7,15},{8,0},{9,1},... | collective-permute-start | bytes 3080 | tf_op jit(solution)/shard_map/ppermute | solution.py:48
  13.8 12.6 %collective-permute-start = (s32[32,8]{0,1:T(8,128)}, s32[32,8]{0,1:T(8,128)S(1)}, u32[]{:S(2)}, u32[]{:S(2)}) collective-permute-start(s32[32,8]{0,1:T(8,128)} %param.10), channel_id=1, source_target_pairs={{0,4},{1,5},{2,6},{3,7},{4,0},{5,1},{6,2},{7,3},{8,12},{9,13},{10,... | collective-permute-start | bytes 3080 | tf_op jit(solution)/shard_map/ppermute | solution.py:48
  22.0 12.4 %collective-permute-start.3 = (f32[32,8]{0,1:T(8,128)}, f32[32,8]{0,1:T(8,128)S(1)}, u32[]{:S(2)}, u32[]{:S(2)}) collective-permute-start(f32[32,8]{0,1:T(8,128)} %param.11), channel_id=1, source_target_pairs={{0,4},{1,5},{2,6},{3,7},{4,0},{5,1},{6,2},{7,3},{8,12},{9,13},{10,... | collective-permute-start | bytes 3080 | tf_op jit(solution)/shard_map/ppermute | solution.py:48
  23.0 15.4 %collective-permute-start.8 = (bf16[32,7168]{1,0:T(8,128)(2,1)S(1)}, bf16[32,7168]{1,0:T(8,128)(2,1)S(1)}, u32[]{:S(2)}, u32[]{:S(2)}) collective-permute-start(bf16[32,7168]{1,0:T(8,128)(2,1)S(1)} %constant_dynamic-update-slice_fusion.1), channel_id=1, source_target_pairs={{0,12},{1,13},{2,14},{3,15},{4,8},{5,9},{6,10},{7,11},{8,4},{9,5},... | collective-permute-start | bytes 1376264 | tf_op jit(solution)/shard_map/ppermute | solution.py:48
  26.4 68.5 %collective-permute-start.7 = (bf16[32,7168]{1,0:T(8,128)(2,1)S(1)}, bf16[32,7168]{1,0:T(8,128)(2,1)S(1)}, u32[]{:S(2)}, u32[]{:S(2)}) collective-permute-start(bf16[32,7168]{1,0:T(8,128)(2,1)S(1)} %constant_dynamic-update-slice_fusion.1), channel_id=1, source_target_pairs={{0,8},{1,9},{2,10},{3,11},{4,12},{5,13},{6,14},{7,15},{8,0},{9,1},... | collective-permute-start | bytes 1376264 | tf_op jit(solution)/shard_map/ppermute | solution.py:48
  30.9 64.0 %collective-permute-start.6 = (bf16[32,7168]{1,0:T(8,128)(2,1)S(1)}, bf16[32,7168]{1,0:T(8,128)(2,1)S(1)}, u32[]{:S(2)}, u32[]{:S(2)}) collective-permute-start(bf16[32,7168]{1,0:T(8,128)(2,1)S(1)} %constant_dynamic-update-slice_fusion.1), channel_id=1, source_target_pairs={{0,4},{1,5},{2,6},{3,7},{4,0},{5,1},{6,2},{7,3},{8,12},{9,13},{10,... | collective-permute-start | bytes 1376264 | tf_op jit(solution)/shard_map/ppermute | solution.py:48
  32.7 90.8 %collective-permute-start.9 = (bf16[1,1792,3,128]{3,1,2,0:T(8,128)(2,1)}, bf16[1,1792,3,128]{3,1,2,0:T(8,128)(2,1)}, u32[]{:S(2)}, u32[]{:S(2)}) collective-permute-start(bf16[1,1792,3,128]{3,1,2,0:T(8,128)(2,1)} %param.12), channel_id=1, source_target_pairs={{0,8},{1,9},{2,10},{3,11},{4,12},{5,13},{6,14},{7,15},{8,0},{9,1},... | collective-permute-start | bytes 4128776 | tf_op jit(solution)/shard_map/ppermute | solution.py:48
  99.0 54.8 %all-to-all-start = ((bf16[4,80,7296]{2,1,0:T(8,128)(2,1)}), bf16[4,80,7296]{2,1,0:T(8,128)(2,1)}, u32[]{:S(2)}, u32[]{:S(2)}) async-start(bf16[4,80,7296]{2,1,0:T(8,128)(2,1)} %bitcast.137), calls=%async_computation | async-start | bytes 9338880 | tf_op jit(solution)/shard_map/all_to_all | solution.py:131
  104.4 21.6 %copy-start = (bf16[1,1792,3,128]{3,1,2,0:T(8,128)(2,1)S(1)}, bf16[1,1792,3,128]{3,1,2,0:T(8,128)(2,1)}, u32[]{:S(2)}) copy-start(bf16[1,1792,3,128]{3,1,2,0:T(8,128)(2,1)} %param.14) | copy-start | bytes 4128772
  104.4 21.7 %copy-start.2 = (bf16[1,1792,3,128]{3,1,2,0:T(8,128)(2,1)S(1)}, bf16[1,1792,3,128]{3,1,2,0:T(8,128)(2,1)}, u32[]{:S(2)}) copy-start(bf16[1,1792,3,128]{3,1,2,0:T(8,128)(2,1)} %param.13) | copy-start | bytes 4128772
  104.4 174.1 %all-gather.3.cloned.1.call-start = ((), (), s32[]{:S(2)}) async-start(), calls=%async_computation.2 | async-start | bytes 8257536 | tf_op jit(solution)/shard_map/all_gather | solution.py:150
  126.0 3.5 %collective-permute-start.10 = (bf16[1,1792,3,128]{3,1,2,0:T(8,128)(2,1)}, bf16[1,1792,3,128]{3,1,2,0:T(8,128)(2,1)}, u32[]{:S(2)}, u32[]{:S(2)}) collective-permute-start(bf16[1,1792,3,128]{3,1,2,0:T(8,128)(2,1)} %broadcast_select_fusion.2), channel_id=1, source_target_pairs={{0,16},{16,0},{1,17},{17,1},{2,18},{18,2},{3,19},{19,3},{4,20},{20... | collective-permute-start | bytes 4128776 | tf_op jit(solution)/shard_map/ppermute | solution.py:159
  162.1 2.8 copy-start.4
  162.1 2.8 copy-start.5
  167.3 6.1 %copy-start.6 = (f32[32,8]{0,1:T(8,128)S(1)}, f32[32,8]{0,1:T(8,128)}, u32[]{:S(2)}) copy-start(f32[32,8]{0,1:T(8,128)} %param.11) | copy-start | bytes 3076
  167.3 32.0 %all-to-all-start.1 = ((bf16[4,80,3712]{2,1,0:T(8,128)(2,1)}), bf16[4,80,3712]{2,1,0:T(8,128)(2,1)}, u32[]{:S(2)}, u32[]{:S(2)}) async-start(bf16[4,80,3712]{2,1,0:T(8,128)(2,1)} %bitcast.14), calls=%async_computation.1 | async-start | bytes 4751360 | tf_op jit(solution)/shard_map/all_to_all | solution.py:131
  200.6 10.4 %collective-permute-start.16 = (bf16[256]{0:T(256)(128)(2,1)S(1)}, bf16[256]{0:T(256)(128)(2,1)S(1)}, u32[]{:S(2)}, u32[]{:S(2)}) collective-permute-start(bf16[256]{0:T(256)(128)(2,1)S(1)} %get-tuple-element.57), channel_id=1, source_target_pairs={{0,4},{1,5},{2,6},{3,7},{4,0},{5,1},{6,2},{7,3},{8,12},{9,13},{10,... | collective-permute-start | bytes 1544 | tf_op jit(solution)/shard_map/ppermute | solution.py:48
  206.1 33.1 %collective-permute-start.13 = (bf16[32,3584]{1,0:T(8,128)(2,1)}, bf16[32,3584]{1,0:T(8,128)(2,1)S(1)}, u32[]{:S(2)}, u32[]{:S(2)}) collective-permute-start(bf16[32,3584]{1,0:T(8,128)(2,1)} %get-tuple-element.50), channel_id=1, source_target_pairs={{0,12},{1,13},{2,14},{3,15},{4,8},{5,9},{6,10},{7,11},{8,4},{9,5},... | collective-permute-start | bytes 688136 | tf_op jit(solution)/shard_map/ppermute | solution.py:48
  207.1 32.1 %collective-permute-start.12 = (bf16[32,3584]{1,0:T(8,128)(2,1)}, bf16[32,3584]{1,0:T(8,128)(2,1)S(1)}, u32[]{:S(2)}, u32[]{:S(2)}) collective-permute-start(bf16[32,3584]{1,0:T(8,128)(2,1)} %get-tuple-element.51), channel_id=1, source_target_pairs={{0,8},{1,9},{2,10},{3,11},{4,12},{5,13},{6,14},{7,15},{8,0},{9,1},... | collective-permute-start | bytes 688136 | tf_op jit(solution)/shard_map/ppermute | solution.py:48
  209.6 29.7 %collective-permute-start.11 = (bf16[32,3584]{1,0:T(8,128)(2,1)S(1)}, bf16[32,3584]{1,0:T(8,128)(2,1)}, u32[]{:S(2)}, u32[]{:S(2)}) collective-permute-start(bf16[32,3584]{1,0:T(8,128)(2,1)S(1)} %get-tuple-element.49), channel_id=1, source_target_pairs={{0,4},{1,5},{2,6},{3,7},{4,0},{5,1},{6,2},{7,3},{8,12},{9,13},{10,... | collective-permute-start | bytes 688136 | tf_op jit(solution)/shard_map/ppermute | solution.py:48
  210.5 28.0 %collective-permute-start.15 = (bf16[256]{0:T(256)(128)(2,1)S(1)}, bf16[256]{0:T(256)(128)(2,1)S(1)}, u32[]{:S(2)}, u32[]{:S(2)}) collective-permute-start(bf16[256]{0:T(256)(128)(2,1)S(1)} %get-tuple-element.56), channel_id=1, source_target_pairs={{0,8},{1,9},{2,10},{3,11},{4,12},{5,13},{6,14},{7,15},{8,0},{9,1},... | collective-permute-start | bytes 1544 | tf_op jit(solution)/shard_map/ppermute | solution.py:48
  211.0 27.4 %collective-permute-start.14 = (bf16[256]{0:T(256)(128)(2,1)S(1)}, bf16[256]{0:T(256)(128)(2,1)S(1)}, u32[]{:S(2)}, u32[]{:S(2)}) collective-permute-start(bf16[256]{0:T(256)(128)(2,1)S(1)} %get-tuple-element.55), channel_id=1, source_target_pairs={{0,12},{1,13},{2,14},{3,15},{4,8},{5,9},{6,10},{7,11},{8,4},{9,5},... | collective-permute-start | bytes 1544 | tf_op jit(solution)/shard_map/ppermute | solution.py:48
  238.5 43.0 %collective-permute-start.17 = (bf16[1792,3,128]{2,0,1:T(8,128)(2,1)}, bf16[1792,3,128]{2,0,1:T(8,128)(2,1)}, u32[]{:S(2)}, u32[]{:S(2)}) collective-permute-start(bf16[1792,3,128]{2,0,1:T(8,128)(2,1)} %broadcast_select_fusion), channel_id=1, source_target_pairs={{0,16},{16,0},{1,17},{17,1},{2,18},{18,2},{3,19},{19,3},{4,20},{20... | collective-permute-start | bytes 4128776 | tf_op jit(solution)/shard_map/ppermute | solution.py:199
  278.5 3.0 %copy-start.1 = (bf16[1,1792,3,128]{3,1,2,0:T(8,128)(2,1)S(1)}, bf16[1,1792,3,128]{3,1,2,0:T(8,128)(2,1)}, u32[]{:S(2)}) copy-start(bf16[1,1792,3,128]{3,1,2,0:T(8,128)(2,1)} %param.14) | copy-start | bytes 4128772
  285.3 3.3 %copy-start.3 = (bf16[1,1792,3,128]{3,1,2,0:T(8,128)(2,1)S(1)}, bf16[1,1792,3,128]{3,1,2,0:T(8,128)(2,1)}, u32[]{:S(2)}) copy-start(bf16[1,1792,3,128]{3,1,2,0:T(8,128)(2,1)} %param.13) | copy-start | bytes 4128772
Sparse Core Ops, SparseCore 0:
  127.9 150.5 all-gather.2

commit v12 on v11

--- a/solution.py
+++ b/solution.py
@@ -142,9 +142,6 @@
         rows, grads_in, gates = send_slots(tokens, out_grad, flat_gate, slot_of, slot_cap)
     if not two_stage:
         their_weights = from_partner(weights, "expert", swap_bit)
-    first_moment, second_moment, _ = lax.optimization_barrier(
-        (first_moment, second_moment, their_weights)
-    )
     if two_stage:
         pairs = [[p, p + half_axis] for p in range(half_axis)]
         pair_both = lax.all_gather(
@@ -153,6 +150,9 @@
         mine_first = my_index < half_axis
         their_moments = jnp.where(mine_first, pair_both[1], pair_both[0])
     else:
+        first_moment, second_moment, _ = lax.optimization_barrier(
+            (first_moment, second_moment, their_weights)
+        )
         their_moments = from_partner((first_moment, second_moment), "expert", swap_bit)
     weights = jnp.where(swapped, their_weights, weights)
     if groups == 2:

time: 301 us -> 309 us (1.027)
  waiting for transfers between devices: 179 us -> 188 us
    all_gather x1, waiting for transfers between devices: 37.4 us -> 75.7 us  [on_device(): lax.all_gather(jnp.stack([first_moment, second_moment]), 'expert', axis_i...]
    all_to_all x2, waiting for transfers between devices: 37.9 us -> 20.7 us  [spread(): lax.all_to_all(parts, 'expert', 0, 0, tiled=True, axis_index_groups=planes)]
    ppermute x16, waiting for transfers between devices: 102 us -> 90.6 us  [xor_permute(): lax.ppermute(value, 'expert', [(i, i ^ mask) for i in range(lax.axis_size...]
  transfers between devices with their start and end apart: 21 -> 21, of which waited for: 8 -> 7; matrix products, arithmetic and copies ran while one was open for 20% -> 20% of each run, Pallas kernels for 0% -> 0%
where the time goes in v12:
time: 309 us; the launch traced here: 307 us
  waiting for transfers between devices  188 us (61%)
  other arithmetic  36 us (12%)
  starting transfers between devices  34.2 us (11%)
  matrix products  23.8 us (8%)
  between operations  15.2 us (5%)
  local copies, waits for them, and re-layouts  10.1 us (3%)
    ppermute x16, waiting for transfers between devices, xor_permute(): lax.ppermute(value, 'expert', [(i, i ^ mask) for i in range(lax.axis_size...  90.6 us
    all_gather x1, waiting for transfers between devices, on_device(): lax.all_gather(jnp.stack([first_moment, second_moment]), 'expert', axis_i...  75.7 us
    ppermute x16, starting transfers between devices, xor_permute(): lax.ppermute(value, 'expert', [(i, i ^ mask) for i in range(lax.axis_size...  22.8 us
    all_to_all x2, waiting for transfers between devices, spread(): lax.all_to_all(parts, 'expert', 0, 0, tiled=True, axis_index_groups=planes)  20.7 us
    all_to_all x2, starting transfers between devices, spread(): lax.all_to_all(parts, 'expert', 0, 0, tiled=True, axis_index_groups=planes)  11.4 us
  transfers between devices with their start and end apart: 21, of which 7 were waited for; matrix products, arithmetic and copies ran while one was open for 20% of the time, Pallas kernels for 0%

profile of v12, /device:TPU:6, one launch (start us, length us, event | category | flops | bytes accessed | tf_op | source)
XLA Modules:
  0.0 306.8 jit_solution(9049813798763031124)
XLA Ops:
  7.2 3.7 %collective-permute-start.5 = (f32[32,8]{0,1:T(8,128)}, f32[32,8]{0,1:T(8,128)S(1)}, u32[]{:S(2)}, u32[]{:S(2)}) collective-permute-start(f32[32,8]{0,1:T(8,128)} %param.11), channel_id=1, source_target_pairs={{0,12},{1,13},{2,14},{3,15},{4,8},{5,9},{6,10},{7,11},{8,4},{9,5},... | collective-permute-start | bytes 3080 | tf_op jit(solution)/shard_map/ppermute | solution.py:48
  10.8 1.9 collective-permute-start.2
  12.7 1.0 collective-permute-start.1
  13.8 1.5 collective-permute-start
  15.2 0.8 copy.110
  17.3 1.0 constant_dynamic-update-slice_fusion.2
  18.2 1.0 constant_dynamic-update-slice_fusion.1
  19.2 1.3 fusion.87
  23.0 3.0 collective-permute-start.8
  30.9 1.5 collective-permute-start.6
  32.7 1.5 collective-permute-start.9
  35.6 2.8 collective-permute-done.8
  38.4 56.5 %collective-permute-done.7 = bf16[32,7168]{1,0:T(8,128)(2,1)S(1)} collective-permute-done((bf16[32,7168]{1,0:T(8,128)(2,1)S(1)}, bf16[32,7168]{1,0:T(8,128)(2,1)S(1)}, u32[]{:S(2)}, u32[]{:S(2)}) %collective-permute-start.7) | collective-permute-done | bytes 458784 | tf_op jit(solution)/shard_map/ppermute | solution.py:48
  94.9 1.5 convolution_convert_fusion
  96.4 2.5 pad_maximum_fusion
  99.0 5.4 %all-to-all-start = ((bf16[4,80,7296]{2,1,0:T(8,128)(2,1)}), bf16[4,80,7296]{2,1,0:T(8,128)(2,1)}, u32[]{:S(2)}, u32[]{:S(2)}) async-start(bf16[4,80,7296]{2,1,0:T(8,128)(2,1)} %bitcast.137), calls=%async_computation | async-start | bytes 9338880 | tf_op jit(solution)/shard_map/all_to_all | solution.py:131
  104.4 19.1 %collective-permute-done.9 = bf16[1,1792,3,128]{3,1,2,0:T(8,128)(2,1)} collective-permute-done((bf16[1,1792,3,128]{3,1,2,0:T(8,128)(2,1)}, bf16[1,1792,3,128]{3,1,2,0:T(8,128)(2,1)}, u32[]{:S(2)}, u32[]{:S(2)}) %collective-permute-start.9) | collective-permute-done | bytes 1376288 | tf_op jit(solution)/shard_map/ppermute | solution.py:48
  123.4 2.6 broadcast_select_fusion.2
  126.0 1.7 pad_maximum_fusion.2
  129.5 1.9 broadcast_select_fusion.4
  131.6 1.5 slice_bitcast_fusion.2
  133.1 20.7 %all-to-all-done = bf16[4,80,7296]{2,1,0:T(8,128)(2,1)} async-done(((bf16[4,80,7296]{2,1,0:T(8,128)(2,1)}), bf16[4,80,7296]{2,1,0:T(8,128)(2,1)}, u32[]{:S(2)}, u32[]{:S(2)}) %all-to-all-start) | async-done | bytes 4669472 | tf_op jit(solution)/shard_map/all_to_all | solution.py:131
  153.8 1.0 convert_reduce_fusion.1
  154.8 2.4 fusion.24
  157.2 2.4 fusion.37
  159.7 2.4 multiply_convert_fusion.5
  162.1 2.6 fusion.1
  164.7 2.6 fusion
  167.3 2.7 fusion.2
  170.4 1.2 broadcast_select_fusion
  171.6 2.9 fusion.34
  174.5 0.8 convolution_convert_fusion.1
  175.4 1.6 pad_maximum_fusion.3
  177.0 6.0 %all-to-all-start.1 = ((bf16[4,80,3712]{2,1,0:T(8,128)(2,1)}), bf16[4,80,3712]{2,1,0:T(8,128)(2,1)}, u32[]{:S(2)}, u32[]{:S(2)}) async-start(bf16[4,80,3712]{2,1,0:T(8,128)(2,1)} %bitcast.138), calls=%async_computation.1 | async-start | bytes 4751360 | tf_op jit(solution)/shard_map/all_to_all | solution.py:131
  183.0 75.7 %all-gather.3.cloned.1.call-done = bf16[4,1,1792,3,128]{4,2,3,1,0:T(8,128)(2,1)} async-done(((bf16[2,1,1792,3,128]{4,2,3,1,0:T(8,128)(2,1)}), bf16[4,1,1792,3,128]{4,2,3,1,0:T(8,128)(2,1)}) %all-gather.3.cloned.1.call-update) | async-done | bytes 5505040 | tf_op jit(solution)/shard_map/all_gather | solution.py:147
  258.7 3.0 fusion.3
  261.8 3.9 %fusion.4 = (bf16[1,1792,3,128]{3,1,2,0:T(8,128)(2,1)}, bf16[1792,3,128]{2,0,1:T(8,128)(2,1)S(1)}) fusion(bf16[1792,3,128]{2,0,1:T(8,128)(2,1)} %collective-permute-done.17, bf16[1,1792,3,128]{3,1,2,0:T(8,128)(2,1)S(1)} %copy-done.4, bf16[1,2,1,1792,3,128]{5,3,4,2,1,0:T(8,128)(2,1)S(1)} %fusion.3, pred[]{:T(512)S(6)} %eq.256, ...), kind=kLoop, calls=%fused_computation.16 | loop fusion | flops 8257536 | bytes 9633794 | tf_op jit(solution)/shard_map/convert_element_type | solution.py:209
  265.6 1.2 copy-done
  266.8 3.3 %fusion.5 = bf16[1,1792,3,128]{3,1,2,0:T(8,128)(2,1)} fusion(bf16[1792,3,128]{2,0,1:T(8,128)(2,1)} %collective-permute-done.17, bf16[1792,3,128]{2,0,1:T(8,128)(2,1)S(1)} %get-tuple-element.37, bf16[1,1792,3,128]{3,1,2,0:T(8,128)(2,1)S(1)} %copy-done.6, bf16[1,2,1,1792,3,128]{5,3,4,2,1,0:T(8,128)(2,1)S(1)} %fusion.3, pred[]{:T(512)S(6)} %eq.256), kind=kLoop, calls=%fused_computation.18 | loop fusion | flops 6193152 | bytes 6881281 | tf_op jit(solution)/shard_map/convert_element_type | solution.py:208
  270.1 1.0 convert_reduce_fusion
  271.1 3.4 %fusion.93 = (bf16[128,3584]{1,0:T(8,128)(2,1)S(1)}, f32[128,3584]{1,0:T(8,128)S(1)}) fusion(f32[320,128]{1,0:T(8,128)S(1)} %select_reduce_fusion.2, bf16[320,3712]{1,0:T(8,128)(2,1)} %bitcast.15), kind=kOutput, calls=%fused_computation.200 | convolution fusion | flops 1762066432 | bytes 5210112 | tf_op jit(solution)/shard_map/dot_general | solution.py:221
  275.0 1.5 collective-permute-start.13
  276.5 2.1 collective-permute-start.12
  278.5 0.9 collective-permute-start.11
  279.4 1.1 collective-permute-start.15
  280.5 2.4 collective-permute-start.14
  282.9 3.2 %multiply_bitcast_fusion = f32[1,1792,3,128]{3,1,2,0:T(8,128)} fusion(bf16[1792,3,128]{2,0,1:T(8,128)(2,1)} %collective-permute-done.17, bf16[1792,3,128]{2,0,1:T(8,128)(2,1)S(1)} %copy-done.1), kind=kLoop, calls=%fused_computation.20 | loop fusion | flops 2752512 | bytes 5505024 | tf_op jit(solution)/shard_map/broadcast_in_dim | solution.py:205
  286.1 12.3 %collective-permute-done.15 = bf16[256]{0:T(256)(128)(2,1)S(1)} collective-permute-done((bf16[256]{0:T(256)(128)(2,1)S(1)}, bf16[256]{0:T(256)(128)(2,1)S(1)}, u32[]{:S(2)}, u32[]{:S(2)}) %collective-permute-start.15) | collective-permute-done | bytes 544 | tf_op jit(solution)/shard_map/ppermute | solution.py:48
  (128 shorter events, 13.8 us)
Async XLA Ops:
  7.2 23.8 %collective-permute-start.5 = (f32[32,8]{0,1:T(8,128)}, f32[32,8]{0,1:T(8,128)S(1)}, u32[]{:S(2)}, u32[]{:S(2)}) collective-permute-start(f32[32,8]{0,1:T(8,128)} %param.11), channel_id=1, source_target_pairs={{0,12},{1,13},{2,14},{3,15},{4,8},{5,9},{6,10},{7,11},{8,4},{9,5},... | collective-permute-start | bytes 3080 | tf_op jit(solution)/shard_map/ppermute | solution.py:48
  10.8 21.8 %collective-permute-start.4 = (f32[32,8]{0,1:T(8,128)}, f32[32,8]{0,1:T(8,128)S(1)}, u32[]{:S(2)}, u32[]{:S(2)}) collective-permute-start(f32[32,8]{0,1:T(8,128)} %param.11), channel_id=1, source_target_pairs={{0,8},{1,9},{2,10},{3,11},{4,12},{5,13},{6,14},{7,15},{8,0},{9,1},... | collective-permute-start | bytes 3080 | tf_op jit(solution)/shard_map/ppermute | solution.py:48
  10.8 11.2 %collective-permute-start.2 = (s32[32,8]{0,1:T(8,128)}, s32[32,8]{0,1:T(8,128)S(1)}, u32[]{:S(2)}, u32[]{:S(2)}) collective-permute-start(s32[32,8]{0,1:T(8,128)} %param.10), channel_id=1, source_target_pairs={{0,12},{1,13},{2,14},{3,15},{4,8},{5,9},{6,10},{7,11},{8,4},{9,5},... | collective-permute-start | bytes 3080 | tf_op jit(solution)/shard_map/ppermute | solution.py:48
  12.7 10.3 %collective-permute-start.1 = (s32[32,8]{0,1:T(8,128)}, s32[32,8]{0,1:T(8,128)S(1)}, u32[]{:S(2)}, u32[]{:S(2)}) collective-permute-start(s32[32,8]{0,1:T(8,128)} %param.10), channel_id=1, source_target_pairs={{0,8},{1,9},{2,10},{3,11},{4,12},{5,13},{6,14},{7,15},{8,0},{9,1},... | collective-permute-start | bytes 3080 | tf_op jit(solution)/shard_map/ppermute | solution.py:48
  13.8 12.6 %collective-permute-start = (s32[32,8]{0,1:T(8,128)}, s32[32,8]{0,1:T(8,128)S(1)}, u32[]{:S(2)}, u32[]{:S(2)}) collective-permute-start(s32[32,8]{0,1:T(8,128)} %param.10), channel_id=1, source_target_pairs={{0,4},{1,5},{2,6},{3,7},{4,0},{5,1},{6,2},{7,3},{8,12},{9,13},{10,... | collective-permute-start | bytes 3080 | tf_op jit(solution)/shard_map/ppermute | solution.py:48
  22.0 12.4 %collective-permute-start.3 = (f32[32,8]{0,1:T(8,128)}, f32[32,8]{0,1:T(8,128)S(1)}, u32[]{:S(2)}, u32[]{:S(2)}) collective-permute-start(f32[32,8]{0,1:T(8,128)} %param.11), channel_id=1, source_target_pairs={{0,4},{1,5},{2,6},{3,7},{4,0},{5,1},{6,2},{7,3},{8,12},{9,13},{10,... | collective-permute-start | bytes 3080 | tf_op jit(solution)/shard_map/ppermute | solution.py:48
  23.0 15.4 %collective-permute-start.8 = (bf16[32,7168]{1,0:T(8,128)(2,1)S(1)}, bf16[32,7168]{1,0:T(8,128)(2,1)S(1)}, u32[]{:S(2)}, u32[]{:S(2)}) collective-permute-start(bf16[32,7168]{1,0:T(8,128)(2,1)S(1)} %constant_dynamic-update-slice_fusion.1), channel_id=1, source_target_pairs={{0,12},{1,13},{2,14},{3,15},{4,8},{5,9},{6,10},{7,11},{8,4},{9,5},... | collective-permute-start | bytes 1376264 | tf_op jit(solution)/shard_map/ppermute | solution.py:48
  26.4 68.5 %collective-permute-start.7 = (bf16[32,7168]{1,0:T(8,128)(2,1)S(1)}, bf16[32,7168]{1,0:T(8,128)(2,1)S(1)}, u32[]{:S(2)}, u32[]{:S(2)}) collective-permute-start(bf16[32,7168]{1,0:T(8,128)(2,1)S(1)} %constant_dynamic-update-slice_fusion.1), channel_id=1, source_target_pairs={{0,8},{1,9},{2,10},{3,11},{4,12},{5,13},{6,14},{7,15},{8,0},{9,1},... | collective-permute-start | bytes 1376264 | tf_op jit(solution)/shard_map/ppermute | solution.py:48
  30.9 64.0 %collective-permute-start.6 = (bf16[32,7168]{1,0:T(8,128)(2,1)S(1)}, bf16[32,7168]{1,0:T(8,128)(2,1)S(1)}, u32[]{:S(2)}, u32[]{:S(2)}) collective-permute-start(bf16[32,7168]{1,0:T(8,128)(2,1)S(1)} %constant_dynamic-update-slice_fusion.1), channel_id=1, source_target_pairs={{0,4},{1,5},{2,6},{3,7},{4,0},{5,1},{6,2},{7,3},{8,12},{9,13},{10,... | collective-permute-start | bytes 1376264 | tf_op jit(solution)/shard_map/ppermute | solution.py:48
  32.7 90.8 %collective-permute-start.9 = (bf16[1,1792,3,128]{3,1,2,0:T(8,128)(2,1)}, bf16[1,1792,3,128]{3,1,2,0:T(8,128)(2,1)}, u32[]{:S(2)}, u32[]{:S(2)}) collective-permute-start(bf16[1,1792,3,128]{3,1,2,0:T(8,128)(2,1)} %param.12), channel_id=1, source_target_pairs={{0,8},{1,9},{2,10},{3,11},{4,12},{5,13},{6,14},{7,15},{8,0},{9,1},... | collective-permute-start | bytes 4128776 | tf_op jit(solution)/shard_map/ppermute | solution.py:48
  99.0 54.8 %all-to-all-start = ((bf16[4,80,7296]{2,1,0:T(8,128)(2,1)}), bf16[4,80,7296]{2,1,0:T(8,128)(2,1)}, u32[]{:S(2)}, u32[]{:S(2)}) async-start(bf16[4,80,7296]{2,1,0:T(8,128)(2,1)} %bitcast.137), calls=%async_computation | async-start | bytes 9338880 | tf_op jit(solution)/shard_map/all_to_all | solution.py:131
  104.4 21.6 %copy-start.3 = (bf16[1,1792,3,128]{3,1,2,0:T(8,128)(2,1)S(1)}, bf16[1,1792,3,128]{3,1,2,0:T(8,128)(2,1)}, u32[]{:S(2)}) copy-start(bf16[1,1792,3,128]{3,1,2,0:T(8,128)(2,1)} %param.14) | copy-start | bytes 4128772
  104.4 21.6 %copy-start.5 = (bf16[1,1792,3,128]{3,1,2,0:T(8,128)(2,1)S(1)}, bf16[1,1792,3,128]{3,1,2,0:T(8,128)(2,1)}, u32[]{:S(2)}) copy-start(bf16[1,1792,3,128]{3,1,2,0:T(8,128)(2,1)} %param.13) | copy-start | bytes 4128772
  104.4 154.4 %all-gather.3.cloned.1.call-start = ((), (), s32[]{:S(2)}) async-start(), calls=%async_computation.2 | async-start | bytes 8257536 | tf_op jit(solution)/shard_map/all_gather | solution.py:147
  126.0 3.5 %collective-permute-start.10 = (bf16[1,1792,3,128]{3,1,2,0:T(8,128)(2,1)}, bf16[1,1792,3,128]{3,1,2,0:T(8,128)(2,1)}, u32[]{:S(2)}, u32[]{:S(2)}) collective-permute-start(bf16[1,1792,3,128]{3,1,2,0:T(8,128)(2,1)} %broadcast_select_fusion.2), channel_id=1, source_target_pairs={{0,16},{16,0},{1,17},{17,1},{2,18},{18,2},{3,19},{19,3},{4,20},{20... | collective-permute-start | bytes 4128776 | tf_op jit(solution)/shard_map/ppermute | solution.py:159
  127.7 0.7 copy-start.9
  131.6 28.1 %copy-start.2 = (bf16[3584,3,128]{2,0,1:T(8,128)(2,1)}, bf16[3584,3,128]{2,0,1:T(8,128)(2,1)S(1)}, u32[]{:S(2)}) copy-start(bf16[3584,3,128]{2,0,1:T(8,128)(2,1)S(1)} %maximum_bitcast_fusion) | copy-start | bytes 8257540
  171.6 2.9 copy-start.7
  171.6 2.9 copy-start.8
  171.6 90.2 %collective-permute-start.17 = (bf16[1792,3,128]{2,0,1:T(8,128)(2,1)}, bf16[1792,3,128]{2,0,1:T(8,128)(2,1)}, u32[]{:S(2)}, u32[]{:S(2)}) collective-permute-start(bf16[1792,3,128]{2,0,1:T(8,128)(2,1)} %broadcast_select_fusion), channel_id=1, source_target_pairs={{0,16},{16,0},{1,17},{17,1},{2,18},{18,2},{3,19},{19,3},{4,20},{20... | collective-permute-start | bytes 4128776 | tf_op jit(solution)/shard_map/ppermute | solution.py:199
  177.0 93.1 %all-to-all-start.1 = ((bf16[4,80,3712]{2,1,0:T(8,128)(2,1)}), bf16[4,80,3712]{2,1,0:T(8,128)(2,1)}, u32[]{:S(2)}, u32[]{:S(2)}) async-start(bf16[4,80,3712]{2,1,0:T(8,128)(2,1)} %bitcast.138), calls=%async_computation.1 | async-start | bytes 4751360 | tf_op jit(solution)/shard_map/all_to_all | solution.py:131
  258.7 3.0 copy-start.4
  261.7 5.1 %copy-start.6 = (bf16[1,1792,3,128]{3,1,2,0:T(8,128)(2,1)S(1)}, bf16[1,1792,3,128]{3,1,2,0:T(8,128)(2,1)}, u32[]{:S(2)}) copy-start(bf16[1,1792,3,128]{3,1,2,0:T(8,128)(2,1)} %param.13) | copy-start | bytes 4128772
  265.6 1.2 copy-start
  271.1 11.8 %copy-start.1 = (bf16[1792,3,128]{2,0,1:T(8,128)(2,1)S(1)}, bf16[1792,3,128]{2,0,1:T(8,128)(2,1)}, u32[]{:S(2)}) copy-start(bf16[1792,3,128]{2,0,1:T(8,128)(2,1)} %copy-done) | copy-start | bytes 4128772
  274.8 5.7 %collective-permute-start.16 = (bf16[256]{0:T(256)(128)(2,1)S(1)}, bf16[256]{0:T(256)(128)(2,1)S(1)}, u32[]{:S(2)}, u32[]{:S(2)}) collective-permute-start(bf16[256]{0:T(256)(128)(2,1)S(1)} %get-tuple-element.53), channel_id=1, source_target_pairs={{0,4},{1,5},{2,6},{3,7},{4,0},{5,1},{6,2},{7,3},{8,12},{9,13},{10,... | collective-permute-start | bytes 1544 | tf_op jit(solution)/shard_map/ppermute | solution.py:48
  275.0 24.2 %collective-permute-start.13 = (bf16[32,3584]{1,0:T(8,128)(2,1)S(1)}, bf16[32,3584]{1,0:T(8,128)(2,1)S(1)}, u32[]{:S(2)}, u32[]{:S(2)}) collective-permute-start(bf16[32,3584]{1,0:T(8,128)(2,1)S(1)} %get-tuple-element.46), channel_id=1, source_target_pairs={{0,12},{1,13},{2,14},{3,15},{4,8},{5,9},{6,10},{7,11},{8,4},{9,5},... | collective-permute-start | bytes 688136 | tf_op jit(solution)/shard_map/ppermute | solution.py:48
  276.5 22.7 %collective-permute-start.12 = (bf16[32,3584]{1,0:T(8,128)(2,1)S(1)}, bf16[32,3584]{1,0:T(8,128)(2,1)S(1)}, u32[]{:S(2)}, u32[]{:S(2)}) collective-permute-start(bf16[32,3584]{1,0:T(8,128)(2,1)S(1)} %get-tuple-element.47), channel_id=1, source_target_pairs={{0,8},{1,9},{2,10},{3,11},{4,12},{5,13},{6,14},{7,15},{8,0},{9,1},... | collective-permute-start | bytes 688136 | tf_op jit(solution)/shard_map/ppermute | solution.py:48
  278.5 20.7 %collective-permute-start.11 = (bf16[32,3584]{1,0:T(8,128)(2,1)S(1)}, bf16[32,3584]{1,0:T(8,128)(2,1)S(1)}, u32[]{:S(2)}, u32[]{:S(2)}) collective-permute-start(bf16[32,3584]{1,0:T(8,128)(2,1)S(1)} %get-tuple-element.45), channel_id=1, source_target_pairs={{0,4},{1,5},{2,6},{3,7},{4,0},{5,1},{6,2},{7,3},{8,12},{9,13},{10,... | collective-permute-start | bytes 688136 | tf_op jit(solution)/shard_map/ppermute | solution.py:48
  279.4 19.0 %collective-permute-start.15 = (bf16[256]{0:T(256)(128)(2,1)S(1)}, bf16[256]{0:T(256)(128)(2,1)S(1)}, u32[]{:S(2)}, u32[]{:S(2)}) collective-permute-start(bf16[256]{0:T(256)(128)(2,1)S(1)} %get-tuple-element.52), channel_id=1, source_target_pairs={{0,8},{1,9},{2,10},{3,11},{4,12},{5,13},{6,14},{7,15},{8,0},{9,1},... | collective-permute-start | bytes 1544 | tf_op jit(solution)/shard_map/ppermute | solution.py:48
  280.5 17.9 %collective-permute-start.14 = (bf16[256]{0:T(256)(128)(2,1)S(1)}, bf16[256]{0:T(256)(128)(2,1)S(1)}, u32[]{:S(2)}, u32[]{:S(2)}) collective-permute-start(bf16[256]{0:T(256)(128)(2,1)S(1)} %get-tuple-element.51), channel_id=1, source_target_pairs={{0,12},{1,13},{2,14},{3,15},{4,8},{5,9},{6,10},{7,11},{8,4},{9,5},... | collective-permute-start | bytes 1544 | tf_op jit(solution)/shard_map/ppermute | solution.py:48
Sparse Core Ops, SparseCore 0:
  127.9 130.7 all-gather.2

commit v13 on v9

--- a/solution.py
+++ b/solution.py
@@ -134,10 +134,10 @@
         rows, grads_in, gates = send_slots(tokens, out_grad, flat_gate, slot_of, slot_cap)
     if not two_stage:
         their_weights = from_partner(weights, "expert", swap_bit)
-    moments, _ = lax.optimization_barrier(
-        (jnp.stack([first_moment, second_moment]), their_weights)
-    )
-    their_moments = from_partner(moments, "expert", swap_bit)
+    moments = (first_moment, second_moment)
+    if not two_stage:
+        moments, _ = lax.optimization_barrier((moments, their_weights))
+        their_moments = from_partner(moments, "expert", swap_bit)
     weights = jnp.where(swapped, their_weights, weights)
     if groups == 2:
         other = lax.ppermute(weights, "dp", [(0, 1), (1, 0)])
@@ -187,15 +187,12 @@
             part, "dp", scatter_dimension=0, tiled=True
         ).astype(jnp.float32) * (1.0 / groups)
     grad = grad[None]
-    first_moment = jnp.where(swapped, their_moments[0], first_moment)
-    second_moment = jnp.where(swapped, their_moments[1], second_moment)
-    new_first = (0.9 * first_moment.astype(jnp.float32) + 0.1 * grad).astype(jnp.bfloat16)
-    new_second = (0.95 * second_moment.astype(jnp.float32) + 0.05 * grad * grad).astype(
-        jnp.bfloat16
-    )
 
     if two_stage:
-        back_all = spread(jnp.concatenate([row_grad, with_tile(gate_rows)], axis=1))
+        back_in = jnp.concatenate([row_grad, with_tile(gate_rows)], axis=1)
+        back_in, moments = lax.optimization_barrier((back_in, moments))
+        back_all = spread(back_in)
+        their_moments = from_partner(moments, "expert", swap_bit)
         back_rows = back_all[:, :model_width]
         back_gate = back_all[:, model_width].astype(jnp.float32)
         weight_of = jnp.where(slot_hit, gate2[None, :], 0.0)
@@ -237,6 +234,12 @@
             .astype(jnp.bfloat16)
         )
         prob_grad = back_gate.reshape(slot_count)[slot_of].reshape(tok_rows, route_count)
+    first_moment = jnp.where(swapped, their_moments[0], first_moment)
+    second_moment = jnp.where(swapped, their_moments[1], second_moment)
+    new_first = (0.9 * first_moment.astype(jnp.float32) + 0.1 * grad).astype(jnp.bfloat16)
+    new_second = (0.95 * second_moment.astype(jnp.float32) + 0.05 * grad * grad).astype(
+        jnp.bfloat16
+    )
     return (token_grad, prob_grad, weights, grad, new_first, new_second)
 
 

time: 280 us -> 308 us (1.10)
  waiting for transfers between devices: 187 us -> 219 us
  other arithmetic: 31.5 us -> 25.2 us
    ppermute x7 -> x8, waiting for transfers between devices: 187 us -> 216 us  [from_partner(): lax.ppermute(value, axis, [(i, i ^ 1 << bit) for i in range(lax.axis_size...]
    all_to_all x2, starting transfers between devices: 12.2 us -> 15.3 us  [spread(): lax.all_to_all(parts, 'expert', 0, 0, tiled=True, axis_index_groups=halves)]
    ppermute x1, waiting for transfers between devices: 0.01 us -> 3.11 us  [on_device(): other = lax.ppermute(weights, 'dp', [(0, 1), (1, 0)])]
    ppermute x7 -> x8, starting transfers between devices: 14.7 us -> 14.3 us  [from_partner(): lax.ppermute(value, axis, [(i, i ^ 1 << bit) for i in range(lax.axis_size...]
  transfers between devices with their start and end apart: 11 -> 12, of which waited for: 4 -> 6; matrix products, arithmetic and copies ran while one was open for 19% -> 10% of each run, Pallas kernels for 0% -> 0%
where the time goes in v13:
time: 308 us; the launch traced here: 306 us
  waiting for transfers between devices  219 us (71%)
  starting transfers between devices  29.7 us (10%)
  other arithmetic  25.2 us (8%)
  matrix products  24 us (8%)
  local copies, waits for them, and re-layouts  6.59 us (2%)
    ppermute x8, waiting for transfers between devices, from_partner(): lax.ppermute(value, axis, [(i, i ^ 1 << bit) for i in range(lax.axis_size...  216 us
    all_to_all x2, starting transfers between devices, spread(): lax.all_to_all(parts, 'expert', 0, 0, tiled=True, axis_index_groups=halves)  15.3 us
    ppermute x8, starting transfers between devices, from_partner(): lax.ppermute(value, axis, [(i, i ^ 1 << bit) for i in range(lax.axis_size...  14.3 us
  transfers between devices with their start and end apart: 12, of which 6 were waited for; matrix products, arithmetic and copies ran while one was open for 10% of the time, Pallas kernels for 0%

profile of v13, /device:TPU:6, one launch (start us, length us, event | category | flops | bytes accessed | tf_op | source)
XLA Modules:
  0.0 306.1 jit_solution(11296723831910628528)
XLA Ops:
  0.6 2.7 collective-permute-start.1
  3.3 0.3 collective-permute-start
  3.6 1.0 constant_dynamic-update-slice_fusion.2
  4.6 1.0 constant_dynamic-update-slice_fusion.1
  5.5 2.7 collective-permute-start.2
  8.2 0.8 copy.41
  9.3 0.6 reduce-window.14
  10.2 0.7 convert.28
  11.5 0.6 reduce-window.16
  12.5 0.7 select_reduce_fusion.3
  13.9 0.2 select_reduce_fusion.2
  14.1 0.4 fusion.29
  14.6 13.5 %collective-permute-done.2 = bf16[32,7168]{1,0:T(8,128)(2,1)S(1)} collective-permute-done((bf16[32,7168]{1,0:T(8,128)(2,1)S(1)}, bf16[32,7168]{1,0:T(8,128)(2,1)S(1)}, u32[]{:S(2)}, u32[]{:S(2)}) %collective-permute-start.2) | collective-permute-done | bytes 458784 | tf_op jit(solution)/shard_map/ppermute | solution.py:8
  28.1 1.4 convolution_convert_fusion
  29.5 2.5 pad_maximum_fusion
  32.0 5.1 %all-to-all-start = ((bf16[8,40,7296]{2,1,0:T(8,128)(2,1)}), bf16[8,40,7296]{2,1,0:T(8,128)(2,1)}, u32[]{:S(2)}, u32[]{:S(2)}) async-start(bf16[8,40,7296]{2,1,0:T(8,128)(2,1)} %bitcast.79), calls=%async_computation | async-start | bytes 9338880 | tf_op jit(solution)/shard_map/all_to_all | solution.py:123
  37.0 2.7 collective-permute-start.3
  39.7 0.6 fusion.68
  41.0 82.2 %collective-permute-done.3 = bf16[1,1792,3,128]{3,1,2,0:T(8,128)(2,1)} collective-permute-done((bf16[1,1792,3,128]{3,1,2,0:T(8,128)(2,1)S(1)}, bf16[1,1792,3,128]{3,1,2,0:T(8,128)(2,1)}, u32[]{:S(2)}, u32[]{:S(2)}) %collective-permute-start.3) | collective-permute-done | bytes 1376288 | tf_op jit(solution)/shard_map/ppermute | solution.py:8
  123.4 3.1 %collective-permute-done.4 = bf16[1,1792,3,128]{3,1,2,0:T(8,128)(2,1)S(1)} collective-permute-done((bf16[1,1792,3,128]{3,1,2,0:T(8,128)(2,1)S(1)}, bf16[1,1792,3,128]{3,1,2,0:T(8,128)(2,1)S(1)}, u32[]{:S(2)}, u32[]{:S(2)}) %collective-permute-start.4) | collective-permute-done | bytes 1376288 | tf_op jit(solution)/shard_map/ppermute | solution.py:143
  126.9 1.3 slice_bitcast_fusion
  128.3 1.0 convert_reduce_fusion.1
  129.3 2.4 fusion.16
  131.7 2.4 fusion.27
  134.1 2.4 multiply_convert_fusion.5
  136.6 2.5 fusion.21
  139.2 3.6 %fusion.1 = bf16[3584,1,128]{2,0,1:T(8,128)(2,1)} fusion(bf16[320,128]{1,0:T(8,128)(2,1)S(1)} %get-tuple-element.40, bf16[320,7296]{1,0:T(8,128)(2,1)} %bitcast.5), kind=kOutput, calls=%fused_computation.6 | convolution fusion | flops 294060032 | bytes 3293184 | tf_op jit(solution)/shard_map/dot_general | solution.py:173
  142.8 0.8 convolution_convert_fusion.1
  143.6 1.6 pad_maximum_fusion.2
  145.2 10.2 %all-to-all-start.1 = ((bf16[8,40,3712]{2,1,0:T(8,128)(2,1)}), bf16[8,40,3712]{2,1,0:T(8,128)(2,1)}, u32[]{:S(2)}, u32[]{:S(2)}) async-start(bf16[8,40,3712]{2,1,0:T(8,128)(2,1)} %bitcast.10), calls=%async_computation.1 | async-start | bytes 4751360 | tf_op jit(solution)/shard_map/all_to_all | solution.py:123
  155.4 2.6 fusion
  158.0 2.8 fusion.2
  160.9 0.3 pad_maximum_fusion.1
  161.2 1.2 broadcast_select_fusion
  162.4 2.9 collective-permute-start.8
  165.5 0.4 select_reduce_fusion
  165.9 89.7 %collective-permute-done.9 = bf16[1,1792,3,128]{3,1,2,0:T(8,128)(2,1)} collective-permute-done((bf16[1,1792,3,128]{3,1,2,0:T(8,128)(2,1)}, bf16[1,1792,3,128]{3,1,2,0:T(8,128)(2,1)}, u32[]{:S(2)}, u32[]{:S(2)}) %collective-permute-start.9) | collective-permute-done | bytes 1376288 | tf_op jit(solution)/shard_map/ppermute | solution.py:8
  255.6 4.2 %fusion.3 = (bf16[1,1792,3,128]{3,1,2,0:T(8,128)(2,1)}, bf16[1792,3,128]{2,0,1:T(8,128)(2,1)S(1)}) fusion(bf16[1792,3,128]{2,0,1:T(8,128)(2,1)} %collective-permute-done.7, bf16[1,1792,3,128]{3,1,2,0:T(8,128)(2,1)} %collective-permute-done.9, bf16[1,1792,3,128]{3,1,2,0:T(8,128)(2,1)} %param.14, pred[]{:T(512)S(6)} %eq.180, ...), kind=kLoop, calls=%fused_computation.13 | loop fusion | flops 8257536 | bytes 9633794 | tf_op jit(solution)/shard_map/convert_element_type | solution.py:240
  259.8 24.9 %collective-permute-done.8 = bf16[1,1792,3,128]{3,1,2,0:T(8,128)(2,1)} collective-permute-done((bf16[1,1792,3,128]{3,1,2,0:T(8,128)(2,1)}, bf16[1,1792,3,128]{3,1,2,0:T(8,128)(2,1)}, u32[]{:S(2)}, u32[]{:S(2)}) %collective-permute-start.8) | collective-permute-done | bytes 1376288 | tf_op jit(solution)/shard_map/ppermute | solution.py:8
  284.7 3.7 %fusion.4 = bf16[1,1792,3,128]{3,1,2,0:T(8,128)(2,1)} fusion(bf16[1792,3,128]{2,0,1:T(8,128)(2,1)} %collective-permute-done.7, bf16[1792,3,128]{2,0,1:T(8,128)(2,1)S(1)} %get-tuple-element.31, bf16[1,1792,3,128]{3,1,2,0:T(8,128)(2,1)} %collective-permute-done.8, bf16[1,1792,3,128]{3,1,2,0:T(8,128)(2,1)} %param.13, pred[]{:T(512)S(6)} %eq.180), kind=kLoop, calls=%fused_computation.15 | loop fusion | flops 6193152 | bytes 6881281 | tf_op jit(solution)/shard_map/convert_element_type | solution.py:239
  288.5 1.1 convert_reduce_fusion
  289.6 3.1 fusion.5
  292.8 0.2 select_reduce_fusion.1
  293.0 3.0 collective-permute-start.6
  295.9 3.2 %multiply_bitcast_fusion = f32[1,1792,3,128]{3,1,2,0:T(8,128)} fusion(bf16[1792,3,128]{2,0,1:T(8,128)(2,1)} %collective-permute-done.7, bf16[1792,3,128]{2,0,1:T(8,128)(2,1)S(1)} %copy-done.1), kind=kLoop, calls=%fused_computation.17 | loop fusion | flops 2752512 | bytes 5505024 | tf_op jit(solution)/shard_map/broadcast_in_dim | solution.py:189
  299.2 5.5 %collective-permute-done.6 = bf16[256]{0:T(256)(128)(2,1)S(1)} collective-permute-done((bf16[256]{0:T(256)(128)(2,1)S(1)}, bf16[256]{0:T(256)(128)(2,1)S(1)}, u32[]{:S(2)}, u32[]{:S(2)}) %collective-permute-start.6) | collective-permute-done | bytes 544 | tf_op jit(solution)/shard_map/ppermute | solution.py:8
  304.7 0.7 copy.52
  305.4 0.7 fusion.31
  (75 shorter events, 3.3 us)
Async XLA Ops:
  0.6 13.0 %collective-permute-start.1 = (f32[32,8]{0,1:T(8,128)}, f32[32,8]{0,1:T(8,128)S(1)}, u32[]{:S(2)}, u32[]{:S(2)}) collective-permute-start(f32[32,8]{0,1:T(8,128)} %param.11), channel_id=1, source_target_pairs={{0,8},{1,9},{2,10},{3,11},{4,12},{5,13},{6,14},{7,15},{8,0},{9,1},... | collective-permute-start | bytes 3080 | tf_op jit(solution)/shard_map/ppermute | solution.py:8
  3.3 7.8 %collective-permute-start = (s32[32,8]{0,1:T(8,128)}, s32[32,8]{0,1:T(8,128)S(1)}, u32[]{:S(2)}, u32[]{:S(2)}) collective-permute-start(s32[32,8]{0,1:T(8,128)} %param.10), channel_id=1, source_target_pairs={{0,8},{1,9},{2,10},{3,11},{4,12},{5,13},{6,14},{7,15},{8,0},{9,1},... | collective-permute-start | bytes 3080 | tf_op jit(solution)/shard_map/ppermute | solution.py:8
  5.5 22.6 %collective-permute-start.2 = (bf16[32,7168]{1,0:T(8,128)(2,1)S(1)}, bf16[32,7168]{1,0:T(8,128)(2,1)S(1)}, u32[]{:S(2)}, u32[]{:S(2)}) collective-permute-start(bf16[32,7168]{1,0:T(8,128)(2,1)S(1)} %constant_dynamic-update-slice_fusion.1), channel_id=1, source_target_pairs={{0,8},{1,9},{2,10},{3,11},{4,12},{5,13},{6,14},{7,15},{8,0},{9,1},... | collective-permute-start | bytes 1376264 | tf_op jit(solution)/shard_map/ppermute | solution.py:8
  32.0 5.1 %copy-start.3 = (bf16[1,1792,3,128]{3,1,2,0:T(8,128)(2,1)S(1)}, bf16[1,1792,3,128]{3,1,2,0:T(8,128)(2,1)}, u32[]{:S(2)}) copy-start(bf16[1,1792,3,128]{3,1,2,0:T(8,128)(2,1)} %param.12) | copy-start | bytes 4128772
  32.0 7.8 %copy-start.8 = (s32[8]{0:T(128)S(1)}, s32[8]{0:T(128)}, u32[]{:S(2)}) copy-start(s32[8]{0:T(128)} %param.15) | copy-start | bytes 100
  32.0 96.3 %all-to-all-start = ((bf16[8,40,7296]{2,1,0:T(8,128)(2,1)}), bf16[8,40,7296]{2,1,0:T(8,128)(2,1)}, u32[]{:S(2)}, u32[]{:S(2)}) async-start(bf16[8,40,7296]{2,1,0:T(8,128)(2,1)} %bitcast.79), calls=%async_computation | async-start | bytes 9338880 | tf_op jit(solution)/shard_map/all_to_all | solution.py:123
  37.0 86.1 %collective-permute-start.3 = (bf16[1,1792,3,128]{3,1,2,0:T(8,128)(2,1)S(1)}, bf16[1,1792,3,128]{3,1,2,0:T(8,128)(2,1)}, u32[]{:S(2)}, u32[]{:S(2)}) collective-permute-start(bf16[1,1792,3,128]{3,1,2,0:T(8,128)(2,1)S(1)} %copy-done.3), channel_id=1, source_target_pairs={{0,8},{1,9},{2,10},{3,11},{4,12},{5,13},{6,14},{7,15},{8,0},{9,1},... | collective-permute-start | bytes 4128776 | tf_op jit(solution)/shard_map/ppermute | solution.py:8
  123.3 3.4 %copy-start.2 = (bf16[1,1792,3,128]{3,1,2,0:T(8,128)(2,1)}, bf16[1,1792,3,128]{3,1,2,0:T(8,128)(2,1)S(1)}, u32[]{:S(2)}) copy-start(bf16[1,1792,3,128]{3,1,2,0:T(8,128)(2,1)S(1)} %broadcast_select_fusion.2) | copy-start | bytes 4128772
  123.3 3.2 %collective-permute-start.4 = (bf16[1,1792,3,128]{3,1,2,0:T(8,128)(2,1)S(1)}, bf16[1,1792,3,128]{3,1,2,0:T(8,128)(2,1)S(1)}, u32[]{:S(2)}, u32[]{:S(2)}) collective-permute-start(bf16[1,1792,3,128]{3,1,2,0:T(8,128)(2,1)S(1)} %broadcast_select_fusion.2), channel_id=1, source_target_pairs={{0,16},{16,0},{1,17},{17,1},{2,18},{18,2},{3,19},{19,3},{4,20},{20... | collective-permute-start | bytes 4128776 | tf_op jit(solution)/shard_map/ppermute | solution.py:143
  139.1 3.8 %copy-start.4 = (bf16[3584,128]{1,0:T(8,128)(2,1)S(1)}, bf16[3584,128]{1,0:T(8,128)(2,1)}, u32[]{:S(2)}) copy-start(bf16[3584,128]{1,0:T(8,128)(2,1)} %get-tuple-element.34) | copy-start | bytes 2752516
  139.1 3.8 %copy-start.5 = (bf16[3584,128]{1,0:T(8,128)(2,1)S(1)}, bf16[3584,128]{1,0:T(8,128)(2,1)}, u32[]{:S(2)}) copy-start(bf16[3584,128]{1,0:T(8,128)(2,1)} %get-tuple-element.35) | copy-start | bytes 2752516
  145.2 143.3 %all-to-all-start.1 = ((bf16[8,40,3712]{2,1,0:T(8,128)(2,1)}), bf16[8,40,3712]{2,1,0:T(8,128)(2,1)}, u32[]{:S(2)}, u32[]{:S(2)}) async-start(bf16[8,40,3712]{2,1,0:T(8,128)(2,1)} %bitcast.10), calls=%async_computation.1 | async-start | bytes 4751360 | tf_op jit(solution)/shard_map/all_to_all | solution.py:123
  158.0 2.8 copy-start.6
  161.2 4.2 %copy-start.7 = (f32[32,8]{0,1:T(8,128)S(1)}, f32[32,8]{0,1:T(8,128)}, u32[]{:S(2)}) copy-start(f32[32,8]{0,1:T(8,128)} %param.11) | copy-start | bytes 3076
  162.4 3.5 %collective-permute-start.7 = (bf16[1792,3,128]{2,0,1:T(8,128)(2,1)}, bf16[1792,3,128]{2,0,1:T(8,128)(2,1)}, u32[]{:S(2)}, u32[]{:S(2)}) collective-permute-start(bf16[1792,3,128]{2,0,1:T(8,128)(2,1)} %broadcast_select_fusion), channel_id=1, source_target_pairs={{0,16},{16,0},{1,17},{17,1},{2,18},{18,2},{3,19},{19,3},{4,20},{20... | collective-permute-start | bytes 4128776 | tf_op jit(solution)/shard_map/ppermute | solution.py:183
  162.4 93.2 %collective-permute-start.9 = (bf16[1,1792,3,128]{3,1,2,0:T(8,128)(2,1)}, bf16[1,1792,3,128]{3,1,2,0:T(8,128)(2,1)}, u32[]{:S(2)}, u32[]{:S(2)}) collective-permute-start(bf16[1,1792,3,128]{3,1,2,0:T(8,128)(2,1)} %param.14), channel_id=1, source_target_pairs={{0,8},{1,9},{2,10},{3,11},{4,12},{5,13},{6,14},{7,15},{8,0},{9,1},... | collective-permute-start | bytes 4128776 | tf_op jit(solution)/shard_map/ppermute | solution.py:8
  162.4 122.3 %collective-permute-start.8 = (bf16[1,1792,3,128]{3,1,2,0:T(8,128)(2,1)}, bf16[1,1792,3,128]{3,1,2,0:T(8,128)(2,1)}, u32[]{:S(2)}, u32[]{:S(2)}) collective-permute-start(bf16[1,1792,3,128]{3,1,2,0:T(8,128)(2,1)} %param.13), channel_id=1, source_target_pairs={{0,8},{1,9},{2,10},{3,11},{4,12},{5,13},{6,14},{7,15},{8,0},{9,1},... | collective-permute-start | bytes 4128776 | tf_op jit(solution)/shard_map/ppermute | solution.py:8
  259.8 24.9 %copy-start = (bf16[1792,3,128]{2,0,1:T(8,128)(2,1)}, bf16[1792,3,128]{2,0,1:T(8,128)(2,1)S(1)}, u32[]{:S(2)}) copy-start(bf16[1792,3,128]{2,0,1:T(8,128)(2,1)S(1)} %get-tuple-element.31) | copy-start | bytes 4128772
  288.5 7.5 %copy-start.1 = (bf16[1792,3,128]{2,0,1:T(8,128)(2,1)S(1)}, bf16[1792,3,128]{2,0,1:T(8,128)(2,1)}, u32[]{:S(2)}) copy-start(bf16[1792,3,128]{2,0,1:T(8,128)(2,1)} %copy-done) | copy-start | bytes 4128772
  292.7 12.7 %collective-permute-start.5 = (bf16[32,3584]{1,0:T(8,128)(2,1)S(1)}, bf16[32,3584]{1,0:T(8,128)(2,1)S(1)}, u32[]{:S(2)}, u32[]{:S(2)}) collective-permute-start(bf16[32,3584]{1,0:T(8,128)(2,1)S(1)} %slice.136), channel_id=1, source_target_pairs={{0,8},{1,9},{2,10},{3,11},{4,12},{5,13},{6,14},{7,15},{8,0},{9,1},... | collective-permute-start | bytes 688136 | tf_op jit(solution)/shard_map/ppermute | solution.py:8
  293.0 11.7 %collective-permute-start.6 = (bf16[256]{0:T(256)(128)(2,1)S(1)}, bf16[256]{0:T(256)(128)(2,1)S(1)}, u32[]{:S(2)}, u32[]{:S(2)}) collective-permute-start(bf16[256]{0:T(256)(128)(2,1)S(1)} %slice.77), channel_id=1, source_target_pairs={{0,8},{1,9},{2,10},{3,11},{4,12},{5,13},{6,14},{7,15},{8,0},{9,1},... | collective-permute-start | bytes 1544 | tf_op jit(solution)/shard_map/ppermute | solution.py:8

commit v14 on v9

--- a/solution.py
+++ b/solution.py
@@ -89,9 +89,11 @@
     two_stage = half_axis <= 8
     if two_stage:
         packed = jnp.concatenate([tokens, out_grad], axis=1)
-        p_packed, p_ids, p_gate, their_weights = from_partner(
-            (packed, expert_ids, gate_probs, weights), "expert", swap_bit
-        )
+        slabs = jnp.stack([weights, first_moment, second_moment])
+        p_packed, p_ids, p_gate, p_slabs = from_partner(
+            (packed, expert_ids, gate_probs, slabs), "expert", swap_bit
+        )
+        their_weights = p_slabs[0]
         both = jnp.concatenate([packed, p_packed], axis=0)
         ids2 = jnp.concatenate([flat_ids, p_ids.reshape(-1)])
         gate2 = jnp.concatenate([flat_gate, p_gate.reshape(-1)])
@@ -134,10 +136,13 @@
         rows, grads_in, gates = send_slots(tokens, out_grad, flat_gate, slot_of, slot_cap)
     if not two_stage:
         their_weights = from_partner(weights, "expert", swap_bit)
-    moments, _ = lax.optimization_barrier(
-        (jnp.stack([first_moment, second_moment]), their_weights)
-    )
-    their_moments = from_partner(moments, "expert", swap_bit)
+    if two_stage:
+        their_moments = (p_slabs[1], p_slabs[2])
+    else:
+        first_moment, second_moment, _ = lax.optimization_barrier(
+            (first_moment, second_moment, their_weights)
+        )
+        their_moments = from_partner((first_moment, second_moment), "expert", swap_bit)
     weights = jnp.where(swapped, their_weights, weights)
     if groups == 2:
         other = lax.ppermute(weights, "dp", [(0, 1), (1, 0)])

time: 280 us -> 328 us (1.17)
  waiting for transfers between devices: 187 us -> 246 us
  starting transfers between devices: 26.9 us -> 18.9 us
    all_to_all x2, waiting for transfers between devices: 0.01 us -> 55.5 us  [spread(): lax.all_to_all(parts, 'expert', 0, 0, tiled=True, axis_index_groups=halves)]
    ppermute x7 -> x6, starting transfers between devices: 14.7 us -> 9.04 us  [from_partner(): lax.ppermute(value, axis, [(i, i ^ 1 << bit) for i in range(lax.axis_size...]
    ppermute x7 -> x6, waiting for transfers between devices: 187 us -> 185 us  [from_partner(): lax.ppermute(value, axis, [(i, i ^ 1 << bit) for i in range(lax.axis_size...]
  transfers between devices with their start and end apart: 11 -> 10, of which waited for: 4 -> 7; matrix products, arithmetic and copies ran while one was open for 19% -> 11% of each run, Pallas kernels for 0% -> 0%
where the time goes in v14:
time: 328 us; the launch traced here: 327 us
  waiting for transfers between devices  246 us (75%)
  other arithmetic  29.2 us (9%)
  matrix products  24 us (7%)
  starting transfers between devices  18.9 us (6%)
  local copies, waits for them, and re-layouts  6.99 us (2%)
    ppermute x6, waiting for transfers between devices, from_partner(): lax.ppermute(value, axis, [(i, i ^ 1 << bit) for i in range(lax.axis_size...  185 us
    all_to_all x2, waiting for transfers between devices, spread(): lax.all_to_all(parts, 'expert', 0, 0, tiled=True, axis_index_groups=halves)  55.5 us
    all_to_all x2, starting transfers between devices, spread(): lax.all_to_all(parts, 'expert', 0, 0, tiled=True, axis_index_groups=halves)  9.84 us
    ppermute x6, starting transfers between devices, from_partner(): lax.ppermute(value, axis, [(i, i ^ 1 << bit) for i in range(lax.axis_size...  9.04 us
  transfers between devices with their start and end apart: 10, of which 7 were waited for; matrix products, arithmetic and copies ran while one was open for 11% of the time, Pallas kernels for 0%

profile of v14, /device:TPU:6, one launch (start us, length us, event | category | flops | bytes accessed | tf_op | source)
XLA Modules:
  0.0 326.9 jit_solution(2313859876371546891)
XLA Ops:
  0.6 2.7 collective-permute-start.1
  3.3 0.3 collective-permute-start
  3.6 1.0 constant_dynamic-update-slice_fusion.2
  4.6 1.0 constant_dynamic-update-slice_fusion.1
  5.5 2.7 collective-permute-start.2
  8.2 3.7 %pad_maximum_fusion.1 = bf16[3,1,1792,3,128]{4,2,3,1,0:T(8,128)(2,1)} fusion(bf16[1,1,1792,3,128]{4,2,3,1,0:T(8,128)(2,1)} %bitcast.99, bf16[1,1,1792,3,128]{4,2,3,1,0:T(8,128)(2,1)} %bitcast.101, bf16[1,1,1792,3,128]{4,2,3,1,0:T(8,128)(2,1)} %bitcast.100), kind=kLoop, calls=%fused_computation.10 | loop fusion | flops 4128768 | bytes 8257536 | tf_op jit(solution)/shard_map/stack | solution.py:92
  11.9 0.3 collective-permute-start.3
  12.6 0.6 reduce-window.14
  14.1 0.6 reduce-window.16
  15.9 0.2 select_reduce_fusion.2
  16.1 0.4 fusion.32
  16.6 101.0 %collective-permute-done.2 = bf16[32,7168]{1,0:T(8,128)(2,1)S(1)} collective-permute-done((bf16[32,7168]{1,0:T(8,128)(2,1)S(1)}, bf16[32,7168]{1,0:T(8,128)(2,1)S(1)}, u32[]{:S(2)}, u32[]{:S(2)}) %collective-permute-start.2) | collective-permute-done | bytes 458784 | tf_op jit(solution)/shard_map/ppermute | solution.py:8
  117.6 1.4 convolution_convert_fusion
  119.0 2.5 pad_maximum_fusion
  121.5 5.1 %all-to-all-start = ((bf16[8,40,7296]{2,1,0:T(8,128)(2,1)}), bf16[8,40,7296]{2,1,0:T(8,128)(2,1)}, u32[]{:S(2)}, u32[]{:S(2)}) async-start(bf16[8,40,7296]{2,1,0:T(8,128)(2,1)} %bitcast.98), calls=%async_computation | async-start | bytes 9338880 | tf_op jit(solution)/shard_map/all_to_all | solution.py:125
  126.5 0.6 fusion.71
  127.8 77.4 %collective-permute-done.3 = bf16[3,1,1792,3,128]{4,2,3,1,0:T(8,128)(2,1)} collective-permute-done((bf16[3,1,1792,3,128]{4,2,3,1,0:T(8,128)(2,1)}, bf16[3,1,1792,3,128]{4,2,3,1,0:T(8,128)(2,1)}, u32[]{:S(2)}, u32[]{:S(2)}) %collective-permute-start.3) | collective-permute-done | bytes 4128800 | tf_op jit(solution)/shard_map/ppermute | solution.py:8
  205.3 1.5 fusion.20
  206.8 3.1 collective-permute-done.4
  210.3 1.3 slice_bitcast_fusion.3
  211.7 43.5 %all-to-all-done = bf16[8,40,7296]{2,1,0:T(8,128)(2,1)} async-done(((bf16[8,40,7296]{2,1,0:T(8,128)(2,1)}), bf16[8,40,7296]{2,1,0:T(8,128)(2,1)}, u32[]{:S(2)}, u32[]{:S(2)}) %all-to-all-start) | async-done | bytes 4669472 | tf_op jit(solution)/shard_map/all_to_all | solution.py:125
  255.2 1.0 convert_reduce_fusion.1
  256.2 2.4 fusion.16
  258.6 2.4 fusion.30
  261.1 2.4 multiply_convert_fusion.5
  263.5 2.5 fusion.24
  266.1 3.6 %fusion.1 = bf16[3584,1,128]{2,0,1:T(8,128)(2,1)} fusion(bf16[320,128]{1,0:T(8,128)(2,1)S(1)} %get-tuple-element.34, bf16[320,7296]{1,0:T(8,128)(2,1)} %bitcast.5), kind=kOutput, calls=%fused_computation.6 | convolution fusion | flops 294060032 | bytes 3293184 | tf_op jit(solution)/shard_map/dot_general | solution.py:178
  269.8 0.8 convolution_convert_fusion.1
  270.6 1.6 pad_maximum_fusion.3
  272.1 4.8 %all-to-all-start.1 = ((bf16[8,40,3712]{2,1,0:T(8,128)(2,1)}), bf16[8,40,3712]{2,1,0:T(8,128)(2,1)}, u32[]{:S(2)}, u32[]{:S(2)}) async-start(bf16[8,40,3712]{2,1,0:T(8,128)(2,1)} %bitcast.14), calls=%async_computation.1 | async-start | bytes 4751360 | tf_op jit(solution)/shard_map/all_to_all | solution.py:125
  276.9 2.6 fusion
  279.5 2.8 fusion.2
  282.3 0.3 pad_maximum_fusion.2
  282.6 1.2 broadcast_select_fusion
  284.0 0.4 select_reduce_fusion
  284.4 2.9 collective-permute-done.7
  287.3 4.6 %fusion.3 = (bf16[1,1792,3,128]{3,1,2,0:T(8,128)(2,1)}, bf16[1792,3,128]{2,0,1:T(8,128)(2,1)S(1)}) fusion(bf16[1792,3,128]{2,0,1:T(8,128)(2,1)} %collective-permute-done.7, bf16[1,1792,3,128]{3,1,2,0:T(8,128)(2,1)} %param.14, bf16[3,1,1792,3,128]{4,2,3,1,0:T(8,128)(2,1)} %collective-permute-done.3, pred[]{:T(512)S(6)} %eq.180, ...), kind=kLoop, calls=%fused_computation.14 | loop fusion | flops 8257536 | bytes 9633794 | tf_op jit(solution)/shard_map/convert_element_type | solution.py:198
  291.9 1.1 copy-done
  293.0 3.7 %fusion.4 = bf16[1,1792,3,128]{3,1,2,0:T(8,128)(2,1)} fusion(bf16[1792,3,128]{2,0,1:T(8,128)(2,1)} %collective-permute-done.7, bf16[1792,3,128]{2,0,1:T(8,128)(2,1)S(1)} %get-tuple-element.25, bf16[1,1792,3,128]{3,1,2,0:T(8,128)(2,1)S(1)} %copy-done.4, bf16[3,1,1792,3,128]{4,2,3,1,0:T(8,128)(2,1)} %collective-permute-done.3, pred[]{:T(512)S(6)} %eq.180), kind=kLoop, calls=%fused_computation.16 | loop fusion | flops 6193152 | bytes 6881281 | tf_op jit(solution)/shard_map/convert_element_type | solution.py:197
  296.7 12.0 %all-to-all-done.1 = bf16[8,40,3712]{2,1,0:T(8,128)(2,1)} async-done(((bf16[8,40,3712]{2,1,0:T(8,128)(2,1)}), bf16[8,40,3712]{2,1,0:T(8,128)(2,1)}, u32[]{:S(2)}, u32[]{:S(2)}) %all-to-all-start.1) | async-done | bytes 2375712 | tf_op jit(solution)/shard_map/all_to_all | solution.py:125
  308.7 1.0 convert_reduce_fusion
  309.7 3.1 fusion.5
  312.8 2.3 collective-permute-start.5
  315.3 0.8 collective-permute-start.6
  316.1 3.2 multiply_bitcast_fusion
  319.3 6.1 %collective-permute-done.6 = bf16[256]{0:T(256)(128)(2,1)S(1)} collective-permute-done((bf16[256]{0:T(256)(128)(2,1)S(1)}, bf16[256]{0:T(256)(128)(2,1)S(1)}, u32[]{:S(2)}, u32[]{:S(2)}) %collective-permute-start.6) | collective-permute-done | bytes 544 | tf_op jit(solution)/shard_map/ppermute | solution.py:8
  325.5 0.7 copy.52
  326.2 0.7 fusion.34
  (76 shorter events, 3.5 us)
Async XLA Ops:
  0.6 15.0 %collective-permute-start.1 = (f32[32,8]{0,1:T(8,128)}, f32[32,8]{0,1:T(8,128)S(1)}, u32[]{:S(2)}, u32[]{:S(2)}) collective-permute-start(f32[32,8]{0,1:T(8,128)} %param.11), channel_id=1, source_target_pairs={{0,8},{1,9},{2,10},{3,11},{4,12},{5,13},{6,14},{7,15},{8,0},{9,1},... | collective-permute-start | bytes 3080 | tf_op jit(solution)/shard_map/ppermute | solution.py:8
  3.3 10.5 %collective-permute-start = (s32[32,8]{0,1:T(8,128)}, s32[32,8]{0,1:T(8,128)S(1)}, u32[]{:S(2)}, u32[]{:S(2)}) collective-permute-start(s32[32,8]{0,1:T(8,128)} %param.10), channel_id=1, source_target_pairs={{0,8},{1,9},{2,10},{3,11},{4,12},{5,13},{6,14},{7,15},{8,0},{9,1},... | collective-permute-start | bytes 3080 | tf_op jit(solution)/shard_map/ppermute | solution.py:8
  5.5 112.1 %collective-permute-start.2 = (bf16[32,7168]{1,0:T(8,128)(2,1)S(1)}, bf16[32,7168]{1,0:T(8,128)(2,1)S(1)}, u32[]{:S(2)}, u32[]{:S(2)}) collective-permute-start(bf16[32,7168]{1,0:T(8,128)(2,1)S(1)} %constant_dynamic-update-slice_fusion.1), channel_id=1, source_target_pairs={{0,8},{1,9},{2,10},{3,11},{4,12},{5,13},{6,14},{7,15},{8,0},{9,1},... | collective-permute-start | bytes 1376264 | tf_op jit(solution)/shard_map/ppermute | solution.py:8
  8.2 4.0 %copy-start.9 = (s32[32,8]{0,1:T(8,128)S(1)}, s32[32,8]{0,1:T(8,128)}, u32[]{:S(2)}) copy-start(s32[32,8]{0,1:T(8,128)} %param.10) | copy-start | bytes 3076
  8.2 5.4 %copy-start.8 = (f32[32,8]{0,1:T(8,128)S(1)}, f32[32,8]{0,1:T(8,128)}, u32[]{:S(2)}) copy-start(f32[32,8]{0,1:T(8,128)} %param.11) | copy-start | bytes 3076
  8.2 7.0 %copy-start.10 = (s32[8]{0:T(128)S(1)}, s32[8]{0:T(128)}, u32[]{:S(2)}) copy-start(s32[8]{0:T(128)} %param.15) | copy-start | bytes 100
  11.9 193.4 %collective-permute-start.3 = (bf16[3,1,1792,3,128]{4,2,3,1,0:T(8,128)(2,1)}, bf16[3,1,1792,3,128]{4,2,3,1,0:T(8,128)(2,1)}, u32[]{:S(2)}, u32[]{:S(2)}) collective-permute-start(bf16[3,1,1792,3,128]{4,2,3,1,0:T(8,128)(2,1)} %pad_maximum_fusion.1), channel_id=1, source_target_pairs={{0,8},{1,9},{2,10},{3,11},{4,12},{5,13},{6,14},{7,15},{8,0},{9,1},... | collective-permute-start | bytes 12386312 | tf_op jit(solution)/shard_map/ppermute | solution.py:8
  121.5 83.8 %copy-start.3 = (bf16[1,1792,3,128]{3,1,2,0:T(8,128)(2,1)S(1)}, bf16[1,1792,3,128]{3,1,2,0:T(8,128)(2,1)}, u32[]{:S(2)}) copy-start(bf16[1,1792,3,128]{3,1,2,0:T(8,128)(2,1)} %param.12) | copy-start | bytes 4128772
  121.5 133.7 %all-to-all-start = ((bf16[8,40,7296]{2,1,0:T(8,128)(2,1)}), bf16[8,40,7296]{2,1,0:T(8,128)(2,1)}, u32[]{:S(2)}, u32[]{:S(2)}) async-start(bf16[8,40,7296]{2,1,0:T(8,128)(2,1)} %bitcast.98), calls=%async_computation | async-start | bytes 9338880 | tf_op jit(solution)/shard_map/all_to_all | solution.py:125
  206.8 3.4 %copy-start.2 = (bf16[1,1792,3,128]{3,1,2,0:T(8,128)(2,1)}, bf16[1,1792,3,128]{3,1,2,0:T(8,128)(2,1)S(1)}, u32[]{:S(2)}) copy-start(bf16[1,1792,3,128]{3,1,2,0:T(8,128)(2,1)S(1)} %fusion.20) | copy-start | bytes 4128772
  206.8 3.2 collective-permute-start.4
  266.0 3.8 %copy-start.5 = (bf16[3584,128]{1,0:T(8,128)(2,1)S(1)}, bf16[3584,128]{1,0:T(8,128)(2,1)}, u32[]{:S(2)}) copy-start(bf16[3584,128]{1,0:T(8,128)(2,1)} %get-tuple-element.28) | copy-start | bytes 2752516
  266.0 3.8 %copy-start.6 = (bf16[3584,128]{1,0:T(8,128)(2,1)S(1)}, bf16[3584,128]{1,0:T(8,128)(2,1)}, u32[]{:S(2)}) copy-start(bf16[3584,128]{1,0:T(8,128)(2,1)} %get-tuple-element.29) | copy-start | bytes 2752516
  272.1 36.6 %all-to-all-start.1 = ((bf16[8,40,3712]{2,1,0:T(8,128)(2,1)}), bf16[8,40,3712]{2,1,0:T(8,128)(2,1)}, u32[]{:S(2)}, u32[]{:S(2)}) async-start(bf16[8,40,3712]{2,1,0:T(8,128)(2,1)} %bitcast.14), calls=%async_computation.1 | async-start | bytes 4751360 | tf_op jit(solution)/shard_map/all_to_all | solution.py:125
  279.5 2.8 copy-start.7
  283.9 3.5 %collective-permute-start.7 = (bf16[1792,3,128]{2,0,1:T(8,128)(2,1)}, bf16[1792,3,128]{2,0,1:T(8,128)(2,1)}, u32[]{:S(2)}, u32[]{:S(2)}) collective-permute-start(bf16[1792,3,128]{2,0,1:T(8,128)(2,1)} %broadcast_select_fusion), channel_id=1, source_target_pairs={{0,16},{16,0},{1,17},{17,1},{2,18},{18,2},{3,19},{19,3},{4,20},{20... | collective-permute-start | bytes 4128776 | tf_op jit(solution)/shard_map/ppermute | solution.py:188
  284.4 8.6 %copy-start.4 = (bf16[1,1792,3,128]{3,1,2,0:T(8,128)(2,1)S(1)}, bf16[1,1792,3,128]{3,1,2,0:T(8,128)(2,1)}, u32[]{:S(2)}) copy-start(bf16[1,1792,3,128]{3,1,2,0:T(8,128)(2,1)} %param.13) | copy-start | bytes 4128772
  291.9 1.1 copy-start
  296.7 19.4 %copy-start.1 = (bf16[1792,3,128]{2,0,1:T(8,128)(2,1)S(1)}, bf16[1792,3,128]{2,0,1:T(8,128)(2,1)}, u32[]{:S(2)}) copy-start(bf16[1792,3,128]{2,0,1:T(8,128)(2,1)} %copy-done) | copy-start | bytes 4128772
  312.8 13.4 %collective-permute-start.5 = (bf16[32,3584]{1,0:T(8,128)(2,1)S(1)}, bf16[32,3584]{1,0:T(8,128)(2,1)S(1)}, u32[]{:S(2)}, u32[]{:S(2)}) collective-permute-start(bf16[32,3584]{1,0:T(8,128)(2,1)S(1)} %slice.164), channel_id=1, source_target_pairs={{0,8},{1,9},{2,10},{3,11},{4,12},{5,13},{6,14},{7,15},{8,0},{9,1},... | collective-permute-start | bytes 688136 | tf_op jit(solution)/shard_map/ppermute | solution.py:8
  315.3 10.1 %collective-permute-start.6 = (bf16[256]{0:T(256)(128)(2,1)S(1)}, bf16[256]{0:T(256)(128)(2,1)S(1)}, u32[]{:S(2)}, u32[]{:S(2)}) collective-permute-start(bf16[256]{0:T(256)(128)(2,1)S(1)} %slice.87), channel_id=1, source_target_pairs={{0,8},{1,9},{2,10},{3,11},{4,12},{5,13},{6,14},{7,15},{8,0},{9,1},... | collective-permute-start | bytes 1544 | tf_op jit(solution)/shard_map/ppermute | solution.py:8

commit v15 on v8

--- a/solution.py
+++ b/solution.py
@@ -88,11 +88,29 @@
 
     two_stage = half_axis <= 8
     if two_stage:
-        packed = jnp.concatenate([tokens, out_grad], axis=1)
-        p_packed, p_ids, p_gate, their_weights = from_partner(
-            (packed, expert_ids, gate_probs, weights), "expert", swap_bit
-        )
-        both = jnp.concatenate([packed, p_packed], axis=0)
+        gate_hi = gate_probs.astype(jnp.bfloat16)
+        gate_rest = gate_probs - gate_hi.astype(jnp.float32)
+        gate_mid = gate_rest.astype(jnp.bfloat16)
+        gate_lo = (gate_rest - gate_mid.astype(jnp.float32)).astype(jnp.bfloat16)
+        side = jnp.concatenate(
+            [
+                expert_ids.astype(jnp.bfloat16),
+                gate_hi,
+                gate_mid,
+                gate_lo,
+                jnp.zeros((tok_rows, 128 - 4 * route_count), jnp.bfloat16),
+            ],
+            axis=1,
+        )
+        packed = jnp.concatenate([tokens, out_grad, side], axis=1)
+        p_packed, their_weights = from_partner((packed, weights), "expert", swap_bit)
+        p_side = p_packed[:, 2 * model_width :].astype(jnp.float32)
+        p_ids = p_side[:, :route_count].astype(jnp.int32)
+        p_gate = (
+            p_side[:, route_count : 2 * route_count]
+            + p_side[:, 2 * route_count : 3 * route_count]
+        ) + p_side[:, 3 * route_count : 4 * route_count]
+        both = jnp.concatenate([packed, p_packed], axis=0)[:, : 2 * model_width]
         ids2 = jnp.concatenate([flat_ids, p_ids.reshape(-1)])
         gate2 = jnp.concatenate([flat_gate, p_gate.reshape(-1)])
         holder2 = holder_of(ids2)

time: 271 us -> 274 us (1.011)
  waiting for transfers between devices: 183 us -> 189 us
  starting transfers between devices: 28.5 us -> 25.5 us
    ppermute x8 -> x6, waiting for transfers between devices: 183 us -> 189 us  [from_partner(): lax.ppermute(value, axis, [(i, i ^ 1 << bit) for i in range(lax.axis_size...]
    ppermute x8 -> x6, starting transfers between devices: 14.9 us -> 12 us  [from_partner(): lax.ppermute(value, axis, [(i, i ^ 1 << bit) for i in range(lax.axis_size...]
  transfers between devices with their start and end apart: 12 -> 10, of which waited for: 5 -> 5; matrix products, arithmetic and copies ran while one was open for 18% -> 15% of each run, Pallas kernels for 0% -> 0%
where the time goes in v15:
time: 274 us; the launch traced here: 273 us
  waiting for transfers between devices  189 us (69%)
  other arithmetic  27.3 us (10%)
  starting transfers between devices  25.5 us (9%)
  matrix products  24 us (9%)
  local copies, waits for them, and re-layouts  5.91 us (2%)
    ppermute x6, waiting for transfers between devices, from_partner(): lax.ppermute(value, axis, [(i, i ^ 1 << bit) for i in range(lax.axis_size...  189 us
    all_to_all x2, starting transfers between devices, spread(): lax.all_to_all(parts, 'expert', 0, 0, tiled=True, axis_index_groups=halves)  13.4 us
    ppermute x6, starting transfers between devices, from_partner(): lax.ppermute(value, axis, [(i, i ^ 1 << bit) for i in range(lax.axis_size...  12 us
  transfers between devices with their start and end apart: 10, of which 5 were waited for; matrix products, arithmetic and copies ran while one was open for 15% of the time, Pallas kernels for 0%

profile of v15, /device:TPU:6, one launch (start us, length us, event | category | flops | bytes accessed | tf_op | source)
XLA Modules:
  0.0 273.0 jit_solution(11996486726801167068)
XLA Ops:
  0.6 0.7 convert_element_type.127
  1.4 0.8 subtract_convert_fusion
  2.5 1.1 concatenate.89
  3.6 2.6 collective-permute-start
  6.3 0.8 copy.78
  7.4 0.6 reduce-window.14
  8.0 0.2 slice_reduce_fusion.1
  8.3 18.7 %collective-permute-done = bf16[32,7296]{1,0:T(8,128)(2,1)S(1)} collective-permute-done((bf16[32,7296]{1,0:T(8,128)(2,1)S(1)}, bf16[32,7296]{1,0:T(8,128)(2,1)S(1)}, u32[]{:S(2)}, u32[]{:S(2)}) %collective-permute-start) | collective-permute-done | bytes 466976 | tf_op jit(solution)/shard_map/ppermute | solution.py:8
  27.4 0.6 reduce-window.16
  28.0 0.2 slice_reduce_fusion
  28.3 0.7 select_reduce_fusion.3
  29.6 0.2 select_reduce_fusion.2
  30.0 0.4 fusion.27
  30.4 1.4 convolution_convert_fusion
  31.7 2.5 pad_maximum_fusion
  34.2 5.0 %all-to-all-start = ((bf16[8,40,7296]{2,1,0:T(8,128)(2,1)}), bf16[8,40,7296]{2,1,0:T(8,128)(2,1)}, u32[]{:S(2)}, u32[]{:S(2)}) async-start(bf16[8,40,7296]{2,1,0:T(8,128)(2,1)} %bitcast.79), calls=%async_computation | async-start | bytes 9338880 | tf_op jit(solution)/shard_map/all_to_all | solution.py:141
  39.2 2.8 %collective-permute-start.1 = (bf16[1,1792,3,128]{3,1,2,0:T(8,128)(2,1)S(1)}, bf16[1,1792,3,128]{3,1,2,0:T(8,128)(2,1)}, u32[]{:S(2)}, u32[]{:S(2)}) collective-permute-start(bf16[1,1792,3,128]{3,1,2,0:T(8,128)(2,1)S(1)} %copy-done.3), channel_id=1, source_target_pairs={{0,8},{1,9},{2,10},{3,11},{4,12},{5,13},{6,14},{7,15},{8,0},{9,1},... | collective-permute-start | bytes 4128776 | tf_op jit(solution)/shard_map/ppermute | solution.py:8
  42.0 0.6 fusion.67
  43.3 82.2 %collective-permute-done.1 = bf16[1,1792,3,128]{3,1,2,0:T(8,128)(2,1)} collective-permute-done((bf16[1,1792,3,128]{3,1,2,0:T(8,128)(2,1)S(1)}, bf16[1,1792,3,128]{3,1,2,0:T(8,128)(2,1)}, u32[]{:S(2)}, u32[]{:S(2)}) %collective-permute-start.1) | collective-permute-done | bytes 1376288 | tf_op jit(solution)/shard_map/ppermute | solution.py:8
  125.5 1.5 broadcast_select_fusion.2
  127.1 3.6 %collective-permute-start.7 = (bf16[1,1792,3,128]{3,1,2,0:T(8,128)(2,1)}, bf16[1,1792,3,128]{3,1,2,0:T(8,128)(2,1)}, u32[]{:S(2)}, u32[]{:S(2)}) collective-permute-start(bf16[1,1792,3,128]{3,1,2,0:T(8,128)(2,1)} %param.14), channel_id=1, source_target_pairs={{0,8},{1,9},{2,10},{3,11},{4,12},{5,13},{6,14},{7,15},{8,0},{9,1},... | collective-permute-start | bytes 4128776 | tf_op jit(solution)/shard_map/ppermute | solution.py:8
  131.1 1.3 slice_bitcast_fusion
  132.4 1.0 convert_reduce_fusion.1
  133.4 2.4 fusion.16
  135.8 2.4 fusion.25
  138.3 2.4 multiply_convert_fusion.5
  140.7 2.5 fusion.21
  143.3 3.6 %fusion.1 = bf16[3584,1,128]{2,0,1:T(8,128)(2,1)} fusion(bf16[320,128]{1,0:T(8,128)(2,1)S(1)} %get-tuple-element.58, bf16[320,7296]{1,0:T(8,128)(2,1)} %bitcast.5), kind=kOutput, calls=%fused_computation.6 | convolution fusion | flops 294060032 | bytes 3293184 | tf_op jit(solution)/shard_map/dot_general | solution.py:191
  147.0 0.8 convolution_convert_fusion.1
  147.8 1.6 pad_maximum_fusion.2
  149.3 8.4 %all-to-all-start.1 = ((bf16[8,40,3712]{2,1,0:T(8,128)(2,1)}), bf16[8,40,3712]{2,1,0:T(8,128)(2,1)}, u32[]{:S(2)}, u32[]{:S(2)}) async-start(bf16[8,40,3712]{2,1,0:T(8,128)(2,1)} %bitcast.10), calls=%async_computation.1 | async-start | bytes 4751360 | tf_op jit(solution)/shard_map/all_to_all | solution.py:141
  157.8 2.6 fusion
  160.4 2.8 %fusion.2 = bf16[3584,1,128]{2,0,1:T(8,128)(2,1)S(1)} fusion(bf16[320,128]{1,0:T(8,128)(2,1)S(1)} %get-tuple-element.57, f32[320]{0:T(512)S(1)} %convert_reduce_fusion.1, bf16[320,7296]{1,0:T(8,128)(2,1)} %bitcast.5), kind=kOutput, calls=%fused_computation.7 | convolution fusion | flops 297500672 | bytes 3294464 | tf_op jit(solution)/shard_map/dot_general | solution.py:192
  163.2 0.3 pad_maximum_fusion.1
  163.5 1.2 broadcast_select_fusion
  164.8 0.4 select_reduce_fusion
  165.2 55.8 %collective-permute-done.7 = bf16[1,1792,3,128]{3,1,2,0:T(8,128)(2,1)} collective-permute-done((bf16[1,1792,3,128]{3,1,2,0:T(8,128)(2,1)}, bf16[1,1792,3,128]{3,1,2,0:T(8,128)(2,1)}, u32[]{:S(2)}, u32[]{:S(2)}) %collective-permute-start.7) | collective-permute-done | bytes 1376288 | tf_op jit(solution)/shard_map/ppermute | solution.py:8
  221.1 4.2 %fusion.3 = (bf16[1,1792,3,128]{3,1,2,0:T(8,128)(2,1)}, bf16[1792,3,128]{2,0,1:T(8,128)(2,1)S(1)}) fusion(bf16[1792,3,128]{2,0,1:T(8,128)(2,1)} %collective-permute-done.5, bf16[1,1792,3,128]{3,1,2,0:T(8,128)(2,1)} %collective-permute-done.7, bf16[1,1792,3,128]{3,1,2,0:T(8,128)(2,1)} %param.14, pred[]{:T(512)S(6)} %eq.180, ...), kind=kLoop, calls=%fused_computation.13 | loop fusion | flops 8257536 | bytes 9633794 | tf_op jit(solution)/shard_map/convert_element_type | solution.py:211
  225.2 25.1 %collective-permute-done.6 = bf16[1,1792,3,128]{3,1,2,0:T(8,128)(2,1)} collective-permute-done((bf16[1,1792,3,128]{3,1,2,0:T(8,128)(2,1)}, bf16[1,1792,3,128]{3,1,2,0:T(8,128)(2,1)}, u32[]{:S(2)}, u32[]{:S(2)}) %collective-permute-start.6) | collective-permute-done | bytes 1376288 | tf_op jit(solution)/shard_map/ppermute | solution.py:8
  250.3 3.7 %fusion.4 = bf16[1,1792,3,128]{3,1,2,0:T(8,128)(2,1)} fusion(bf16[1792,3,128]{2,0,1:T(8,128)(2,1)} %collective-permute-done.5, bf16[1792,3,128]{2,0,1:T(8,128)(2,1)S(1)} %get-tuple-element.47, bf16[1,1792,3,128]{3,1,2,0:T(8,128)(2,1)} %collective-permute-done.6, bf16[1,1792,3,128]{3,1,2,0:T(8,128)(2,1)} %param.13, pred[]{:T(512)S(6)} %eq.180), kind=kLoop, calls=%fused_computation.15 | loop fusion | flops 6193152 | bytes 6881281 | tf_op jit(solution)/shard_map/convert_element_type | solution.py:210
  254.0 1.1 convert_reduce_fusion
  255.1 3.1 %fusion.5 = f32[64,3584]{1,0:T(8,128)S(1)} fusion(f32[320,64]{0,1:T(8,128)S(1)} %select_reduce_fusion, bf16[320,3712]{1,0:T(8,128)(2,1)} %bitcast.11), kind=kOutput, calls=%fused_computation.19 | convolution fusion | flops 880803840 | bytes 3293184 | tf_op jit(solution)/shard_map/dot_general | solution.py:221
  258.3 0.2 select_reduce_fusion.1
  258.5 3.0 %collective-permute-start.4 = (bf16[256]{0:T(256)(128)(2,1)S(1)}, bf16[256]{0:T(256)(128)(2,1)S(1)}, u32[]{:S(2)}, u32[]{:S(2)}) collective-permute-start(bf16[256]{0:T(256)(128)(2,1)S(1)} %slice.101), channel_id=1, source_target_pairs={{0,8},{1,9},{2,10},{3,11},{4,12},{5,13},{6,14},{7,15},{8,0},{9,1},... | collective-permute-start | bytes 1544 | tf_op jit(solution)/shard_map/ppermute | solution.py:8
  261.5 3.2 %multiply_bitcast_fusion = f32[1,1792,3,128]{3,1,2,0:T(8,128)} fusion(bf16[1792,3,128]{2,0,1:T(8,128)(2,1)} %collective-permute-done.5, bf16[1792,3,128]{2,0,1:T(8,128)(2,1)S(1)} %copy-done.1), kind=kLoop, calls=%fused_computation.17 | loop fusion | flops 2752512 | bytes 5505024 | tf_op jit(solution)/shard_map/broadcast_in_dim | solution.py:207
  264.7 6.8 %collective-permute-done.4 = bf16[256]{0:T(256)(128)(2,1)S(1)} collective-permute-done((bf16[256]{0:T(256)(128)(2,1)S(1)}, bf16[256]{0:T(256)(128)(2,1)S(1)}, u32[]{:S(2)}, u32[]{:S(2)}) %collective-permute-start.4) | collective-permute-done | bytes 544 | tf_op jit(solution)/shard_map/ppermute | solution.py:8
  271.6 0.7 copy.89
  272.3 0.7 fusion.29
  (74 shorter events, 2.9 us)
Async XLA Ops:
  3.6 23.4 %collective-permute-start = (bf16[32,7296]{1,0:T(8,128)(2,1)S(1)}, bf16[32,7296]{1,0:T(8,128)(2,1)S(1)}, u32[]{:S(2)}, u32[]{:S(2)}) collective-permute-start(bf16[32,7296]{1,0:T(8,128)(2,1)S(1)} %concatenate.89), channel_id=1, source_target_pairs={{0,8},{1,9},{2,10},{3,11},{4,12},{5,13},{6,14},{7,15},{8,0},{9,1},... | collective-permute-start | bytes 1400840 | tf_op jit(solution)/shard_map/ppermute | solution.py:8
  34.2 5.0 %copy-start.3 = (bf16[1,1792,3,128]{3,1,2,0:T(8,128)(2,1)S(1)}, bf16[1,1792,3,128]{3,1,2,0:T(8,128)(2,1)}, u32[]{:S(2)}) copy-start(bf16[1,1792,3,128]{3,1,2,0:T(8,128)(2,1)} %param.12) | copy-start | bytes 4128772
  34.2 7.8 %copy-start.8 = (s32[8]{0:T(128)S(1)}, s32[8]{0:T(128)}, u32[]{:S(2)}) copy-start(s32[8]{0:T(128)} %param.15) | copy-start | bytes 100
  34.2 98.2 %all-to-all-start = ((bf16[8,40,7296]{2,1,0:T(8,128)(2,1)}), bf16[8,40,7296]{2,1,0:T(8,128)(2,1)}, u32[]{:S(2)}, u32[]{:S(2)}) async-start(bf16[8,40,7296]{2,1,0:T(8,128)(2,1)} %bitcast.79), calls=%async_computation | async-start | bytes 9338880 | tf_op jit(solution)/shard_map/all_to_all | solution.py:141
  39.2 86.3 %collective-permute-start.1 = (bf16[1,1792,3,128]{3,1,2,0:T(8,128)(2,1)S(1)}, bf16[1,1792,3,128]{3,1,2,0:T(8,128)(2,1)}, u32[]{:S(2)}, u32[]{:S(2)}) collective-permute-start(bf16[1,1792,3,128]{3,1,2,0:T(8,128)(2,1)S(1)} %copy-done.3), channel_id=1, source_target_pairs={{0,8},{1,9},{2,10},{3,11},{4,12},{5,13},{6,14},{7,15},{8,0},{9,1},... | collective-permute-start | bytes 4128776 | tf_op jit(solution)/shard_map/ppermute | solution.py:8
  127.0 3.8 %copy-start.2 = (bf16[1,1792,3,128]{3,1,2,0:T(8,128)(2,1)}, bf16[1,1792,3,128]{3,1,2,0:T(8,128)(2,1)S(1)}, u32[]{:S(2)}) copy-start(bf16[1,1792,3,128]{3,1,2,0:T(8,128)(2,1)S(1)} %broadcast_select_fusion.2) | copy-start | bytes 4128772
  127.0 3.6 %collective-permute-start.2 = (bf16[1,1792,3,128]{3,1,2,0:T(8,128)(2,1)S(1)}, bf16[1,1792,3,128]{3,1,2,0:T(8,128)(2,1)S(1)}, u32[]{:S(2)}, u32[]{:S(2)}) collective-permute-start(bf16[1,1792,3,128]{3,1,2,0:T(8,128)(2,1)S(1)} %broadcast_select_fusion.2), channel_id=1, source_target_pairs={{0,16},{16,0},{1,17},{17,1},{2,18},{18,2},{3,19},{19,3},{4,20},{20... | collective-permute-start | bytes 4128776 | tf_op jit(solution)/shard_map/ppermute | solution.py:161
  127.1 93.9 %collective-permute-start.7 = (bf16[1,1792,3,128]{3,1,2,0:T(8,128)(2,1)}, bf16[1,1792,3,128]{3,1,2,0:T(8,128)(2,1)}, u32[]{:S(2)}, u32[]{:S(2)}) collective-permute-start(bf16[1,1792,3,128]{3,1,2,0:T(8,128)(2,1)} %param.14), channel_id=1, source_target_pairs={{0,8},{1,9},{2,10},{3,11},{4,12},{5,13},{6,14},{7,15},{8,0},{9,1},... | collective-permute-start | bytes 4128776 | tf_op jit(solution)/shard_map/ppermute | solution.py:8
  143.2 3.8 %copy-start.4 = (bf16[3584,128]{1,0:T(8,128)(2,1)S(1)}, bf16[3584,128]{1,0:T(8,128)(2,1)}, u32[]{:S(2)}) copy-start(bf16[3584,128]{1,0:T(8,128)(2,1)} %get-tuple-element.52) | copy-start | bytes 2752516
  143.2 3.8 %copy-start.5 = (bf16[3584,128]{1,0:T(8,128)(2,1)S(1)}, bf16[3584,128]{1,0:T(8,128)(2,1)}, u32[]{:S(2)}) copy-start(bf16[3584,128]{1,0:T(8,128)(2,1)} %get-tuple-element.53) | copy-start | bytes 2752516
  149.3 104.7 %all-to-all-start.1 = ((bf16[8,40,3712]{2,1,0:T(8,128)(2,1)}), bf16[8,40,3712]{2,1,0:T(8,128)(2,1)}, u32[]{:S(2)}, u32[]{:S(2)}) async-start(bf16[8,40,3712]{2,1,0:T(8,128)(2,1)} %bitcast.10), calls=%async_computation.1 | async-start | bytes 4751360 | tf_op jit(solution)/shard_map/all_to_all | solution.py:141
  160.3 2.8 %copy-start.6 = (bf16[3584,1,128]{2,0,1:T(8,128)(2,1)S(1)}, bf16[3584,1,128]{2,0,1:T(8,128)(2,1)}, u32[]{:S(2)}) copy-start(bf16[3584,1,128]{2,0,1:T(8,128)(2,1)} %fusion.1) | copy-start | bytes 2752516
  163.5 1.2 copy-start.7
  164.7 56.3 %collective-permute-start.5 = (bf16[1792,3,128]{2,0,1:T(8,128)(2,1)}, bf16[1792,3,128]{2,0,1:T(8,128)(2,1)}, u32[]{:S(2)}, u32[]{:S(2)}) collective-permute-start(bf16[1792,3,128]{2,0,1:T(8,128)(2,1)} %broadcast_select_fusion), channel_id=1, source_target_pairs={{0,16},{16,0},{1,17},{17,1},{2,18},{18,2},{3,19},{19,3},{4,20},{20... | collective-permute-start | bytes 4128776 | tf_op jit(solution)/shard_map/ppermute | solution.py:201
  164.7 85.6 %collective-permute-start.6 = (bf16[1,1792,3,128]{3,1,2,0:T(8,128)(2,1)}, bf16[1,1792,3,128]{3,1,2,0:T(8,128)(2,1)}, u32[]{:S(2)}, u32[]{:S(2)}) collective-permute-start(bf16[1,1792,3,128]{3,1,2,0:T(8,128)(2,1)} %param.13), channel_id=1, source_target_pairs={{0,8},{1,9},{2,10},{3,11},{4,12},{5,13},{6,14},{7,15},{8,0},{9,1},... | collective-permute-start | bytes 4128776 | tf_op jit(solution)/shard_map/ppermute | solution.py:8
  225.2 25.1 %copy-start = (bf16[1792,3,128]{2,0,1:T(8,128)(2,1)}, bf16[1792,3,128]{2,0,1:T(8,128)(2,1)S(1)}, u32[]{:S(2)}) copy-start(bf16[1792,3,128]{2,0,1:T(8,128)(2,1)S(1)} %get-tuple-element.47) | copy-start | bytes 4128772
  254.0 7.5 %copy-start.1 = (bf16[1792,3,128]{2,0,1:T(8,128)(2,1)S(1)}, bf16[1792,3,128]{2,0,1:T(8,128)(2,1)}, u32[]{:S(2)}) copy-start(bf16[1792,3,128]{2,0,1:T(8,128)(2,1)} %copy-done) | copy-start | bytes 4128772
  258.2 14.1 %collective-permute-start.3 = (bf16[32,3584]{1,0:T(8,128)(2,1)S(1)}, bf16[32,3584]{1,0:T(8,128)(2,1)S(1)}, u32[]{:S(2)}, u32[]{:S(2)}) collective-permute-start(bf16[32,3584]{1,0:T(8,128)(2,1)S(1)} %slice.172), channel_id=1, source_target_pairs={{0,8},{1,9},{2,10},{3,11},{4,12},{5,13},{6,14},{7,15},{8,0},{9,1},... | collective-permute-start | bytes 688136 | tf_op jit(solution)/shard_map/ppermute | solution.py:8
  258.5 13.0 %collective-permute-start.4 = (bf16[256]{0:T(256)(128)(2,1)S(1)}, bf16[256]{0:T(256)(128)(2,1)S(1)}, u32[]{:S(2)}, u32[]{:S(2)}) collective-permute-start(bf16[256]{0:T(256)(128)(2,1)S(1)} %slice.101), channel_id=1, source_target_pairs={{0,8},{1,9},{2,10},{3,11},{4,12},{5,13},{6,14},{7,15},{8,0},{9,1},... | collective-permute-start | bytes 1544 | tf_op jit(solution)/shard_map/ppermute | solution.py:8

commit v16 on v10

--- a/solution.py
+++ b/solution.py
@@ -93,13 +93,9 @@
         packed = jnp.concatenate([tokens, out_grad], axis=1)
         got = [(packed, expert_ids, gate_probs)]
         for k in range(1, column):
-            if k * plane == half_axis:
-                p_packed, p_ids, p_gate, their_weights = xor_permute(
-                    (packed, expert_ids, gate_probs, weights), k * plane
-                )
-            else:
-                p_packed, p_ids, p_gate = xor_permute((packed, expert_ids, gate_probs), k * plane)
-            got.append((p_packed, p_ids, p_gate))
+            got.append(xor_permute((packed, expert_ids, gate_probs), k * plane))
+        weights, got = lax.optimization_barrier((weights, got))
+        their_weights = from_partner(weights, "expert", swap_bit)
         both = jnp.concatenate([g[0] for g in got], axis=0)
         ids2 = jnp.concatenate([g[1].reshape(-1) for g in got])
         gate2 = jnp.concatenate([g[2].reshape(-1) for g in got])

time: 274 us -> 280 us (1.022)
  waiting for transfers between devices: 173 us -> 181 us
    ppermute x2 -> x3, waiting for transfers between devices: 58.4 us -> 132 us  [from_partner(): lax.ppermute(value, axis, [(i, i ^ 1 << bit) for i in range(lax.axis_size...]
    ppermute x16 -> x15, waiting for transfers between devices: 90.8 us -> 49.2 us  [xor_permute(): lax.ppermute(value, 'expert', [(i, i ^ mask) for i in range(lax.axis_size...]
    all_to_all x2, waiting for transfers between devices: 23.8 us -> 0.01 us  [spread(): lax.all_to_all(parts, 'expert', 0, 0, tiled=True, axis_index_groups=planes)]
    ppermute x16 -> x15, starting transfers between devices: 22.8 us -> 21.8 us  [xor_permute(): lax.ppermute(value, 'expert', [(i, i ^ mask) for i in range(lax.axis_size...]
  transfers between devices with their start and end apart: 22 -> 22, of which waited for: 8 -> 9; matrix products, arithmetic and copies ran while one was open for 20% -> 16% of each run, Pallas kernels for 0% -> 0%
where the time goes in v16:
time: 280 us
  waiting for transfers between devices  181 us (65%)
  starting transfers between devices  35.5 us (13%)
  other arithmetic  29.1 us (10%)
  matrix products  23.8 us (8%)
  local copies, waits for them, and re-layouts  8.27 us (3%)
    ppermute x3, waiting for transfers between devices, from_partner(): lax.ppermute(value, axis, [(i, i ^ 1 << bit) for i in range(lax.axis_size...  132 us
    ppermute x15, waiting for transfers between devices, xor_permute(): lax.ppermute(value, 'expert', [(i, i ^ mask) for i in range(lax.axis_size...  49.2 us
    ppermute x15, starting transfers between devices, xor_permute(): lax.ppermute(value, 'expert', [(i, i ^ mask) for i in range(lax.axis_size...  21.8 us
    all_to_all x2, starting transfers between devices, spread(): lax.all_to_all(parts, 'expert', 0, 0, tiled=True, axis_index_groups=planes)  10.4 us
  transfers between devices with their start and end apart: 22, of which 9 were waited for; matrix products, arithmetic and copies ran while one was open for 16% of the time, Pallas kernels for 0%

profile of v16, /device:TPU:6, one launch (start us, length us, event | category | flops | bytes accessed | tf_op | source)
XLA Modules:
  0.0 279.7 jit_solution(6325425222845789726)
XLA Ops:
  0.6 1.0 constant_dynamic-update-slice_fusion.1
  1.6 1.0 constant_dynamic-update-slice_fusion
  2.5 1.6 collective-permute-start
  4.2 2.6 collective-permute-start.3
  7.7 1.3 collective-permute-start.2
  9.0 24.8 %collective-permute-done.1 = s32[32,8]{0,1:T(8,128)S(1)} collective-permute-done((s32[32,8]{0,1:T(8,128)}, s32[32,8]{0,1:T(8,128)S(1)}, u32[]{:S(2)}, u32[]{:S(2)}) %collective-permute-start.1) | collective-permute-done | bytes 1056 | tf_op jit(solution)/shard_map/ppermute | solution.py:48
  33.8 3.5 %collective-permute-start.4 = (s32[32,8]{0,1:T(8,128)}, s32[32,8]{0,1:T(8,128)S(1)}, u32[]{:S(2)}, u32[]{:S(2)}) collective-permute-start(s32[32,8]{0,1:T(8,128)} %param.10), channel_id=1, source_target_pairs={{0,8},{1,9},{2,10},{3,11},{4,12},{5,13},{6,14},{7,15},{8,0},{9,1},... | collective-permute-start | bytes 3080 | tf_op jit(solution)/shard_map/ppermute | solution.py:48
  37.3 1.3 fusion.84
  38.6 8.3 %collective-permute-done.4 = s32[32,8]{0,1:T(8,128)S(1)} collective-permute-done((s32[32,8]{0,1:T(8,128)}, s32[32,8]{0,1:T(8,128)S(1)}, u32[]{:S(2)}, u32[]{:S(2)}) %collective-permute-start.4) | collective-permute-done | bytes 1056 | tf_op jit(solution)/shard_map/ppermute | solution.py:48
  46.9 2.5 collective-permute-start.7
  49.4 1.3 collective-permute-start.8
  51.4 1.1 collective-permute-done.7
  52.5 2.5 collective-permute-done.8
  56.1 0.8 copy.84
  61.1 0.7 select_reduce_fusion.3
  64.8 1.5 convolution_convert_fusion
  66.3 2.5 pad_maximum_fusion
  68.8 5.5 %all-to-all-start = ((bf16[4,80,7296]{2,1,0:T(8,128)(2,1)}), bf16[4,80,7296]{2,1,0:T(8,128)(2,1)}, u32[]{:S(2)}, u32[]{:S(2)}) async-start(bf16[4,80,7296]{2,1,0:T(8,128)(2,1)} %bitcast.119), calls=%async_computation | async-start | bytes 9338880 | tf_op jit(solution)/shard_map/all_to_all | solution.py:127
  74.3 47.9 %collective-permute-done.9 = bf16[1,1792,3,128]{3,1,2,0:T(8,128)(2,1)} collective-permute-done((bf16[1,1792,3,128]{3,1,2,0:T(8,128)(2,1)}, bf16[1,1792,3,128]{3,1,2,0:T(8,128)(2,1)}, u32[]{:S(2)}, u32[]{:S(2)}) %collective-permute-start.9) | collective-permute-done | bytes 1376288 | tf_op jit(solution)/shard_map/ppermute | solution.py:8
  122.2 1.5 broadcast_select_fusion.2
  123.8 2.9 %collective-permute-start.18 = (bf16[1,1792,3,128]{3,1,2,0:T(8,128)(2,1)}, bf16[1,1792,3,128]{3,1,2,0:T(8,128)(2,1)}, u32[]{:S(2)}, u32[]{:S(2)}) collective-permute-start(bf16[1,1792,3,128]{3,1,2,0:T(8,128)(2,1)} %param.13), channel_id=1, source_target_pairs={{0,8},{1,9},{2,10},{3,11},{4,12},{5,13},{6,14},{7,15},{8,0},{9,1},... | collective-permute-start | bytes 4128776 | tf_op jit(solution)/shard_map/ppermute | solution.py:8
  127.3 1.5 slice_bitcast_fusion
  128.7 1.1 convert_reduce_fusion.1
  129.8 2.4 fusion.23
  132.2 2.4 fusion.34
  134.7 2.4 multiply_convert_fusion.5
  137.1 2.7 fusion.2
  139.8 2.6 fusion.1
  142.4 2.6 fusion
  145.3 1.2 broadcast_select_fusion
  146.7 2.8 %fusion.31 = bf16[320]{0:T(512)(128)(2,1)S(1)} fusion(bf16[320,7296]{1,0:T(8,128)(2,1)} %bitcast.9, bf16[3584,3,128]{2,0,1:T(8,128)(2,1)} %copy-done.2, bf16[320,128]{1,0:T(8,128)(2,1)S(1)} %get-tuple-element.73), kind=kOutput, calls=%fused_computation.53 | convolution fusion | flops 293723840 | bytes 3293824 | tf_op jit(solution)/shard_map/dot_general | solution.py:164
  149.6 0.8 convolution_convert_fusion.1
  150.5 1.6 pad_maximum_fusion.2
  152.0 4.9 %all-to-all-start.1 = ((bf16[4,80,3712]{2,1,0:T(8,128)(2,1)}), bf16[4,80,3712]{2,1,0:T(8,128)(2,1)}, u32[]{:S(2)}, u32[]{:S(2)}) async-start(bf16[4,80,3712]{2,1,0:T(8,128)(2,1)} %bitcast.120), calls=%async_computation.1 | async-start | bytes 4751360 | tf_op jit(solution)/shard_map/all_to_all | solution.py:127
  157.6 58.8 %collective-permute-done.19 = bf16[1,1792,3,128]{3,1,2,0:T(8,128)(2,1)} collective-permute-done((bf16[1,1792,3,128]{3,1,2,0:T(8,128)(2,1)}, bf16[1,1792,3,128]{3,1,2,0:T(8,128)(2,1)}, u32[]{:S(2)}, u32[]{:S(2)}) %collective-permute-start.19) | collective-permute-done | bytes 1376288 | tf_op jit(solution)/shard_map/ppermute | solution.py:8
  216.4 4.2 %fusion.3 = (bf16[1,1792,3,128]{3,1,2,0:T(8,128)(2,1)}, bf16[1792,3,128]{2,0,1:T(8,128)(2,1)S(1)}) fusion(bf16[1792,3,128]{2,0,1:T(8,128)(2,1)} %collective-permute-done.17, bf16[1,1792,3,128]{3,1,2,0:T(8,128)(2,1)} %collective-permute-done.19, bf16[1,1792,3,128]{3,1,2,0:T(8,128)(2,1)} %param.14, pred[]{:T(512)S(6)} %eq.256, ...), kind=kLoop, calls=%fused_computation.13 | loop fusion | flops 8257536 | bytes 9633794 | tf_op jit(solution)/shard_map/convert_element_type | solution.py:197
  220.6 25.3 %collective-permute-done.18 = bf16[1,1792,3,128]{3,1,2,0:T(8,128)(2,1)} collective-permute-done((bf16[1,1792,3,128]{3,1,2,0:T(8,128)(2,1)}, bf16[1,1792,3,128]{3,1,2,0:T(8,128)(2,1)}, u32[]{:S(2)}, u32[]{:S(2)}) %collective-permute-start.18) | collective-permute-done | bytes 1376288 | tf_op jit(solution)/shard_map/ppermute | solution.py:8
  245.9 3.7 %fusion.4 = bf16[1,1792,3,128]{3,1,2,0:T(8,128)(2,1)} fusion(bf16[1792,3,128]{2,0,1:T(8,128)(2,1)} %collective-permute-done.17, bf16[1792,3,128]{2,0,1:T(8,128)(2,1)S(1)} %get-tuple-element.61, bf16[1,1792,3,128]{3,1,2,0:T(8,128)(2,1)} %collective-permute-done.18, bf16[1,1792,3,128]{3,1,2,0:T(8,128)(2,1)S(1)} %copy-done.5, pred[]{:T(512)S(6)} %eq.256), kind=kLoop, calls=%fused_computation.15 | loop fusion | flops 6193152 | bytes 6881281 | tf_op jit(solution)/shard_map/convert_element_type | solution.py:196
  249.6 1.0 convert_reduce_fusion
  250.6 3.4 %fusion.90 = (bf16[128,3584]{1,0:T(8,128)(2,1)S(1)}, f32[128,3584]{1,0:T(8,128)S(1)}) fusion(f32[320,128]{1,0:T(8,128)S(1)} %select_reduce_fusion.2, bf16[320,3712]{1,0:T(8,128)(2,1)} %bitcast.15), kind=kOutput, calls=%fused_computation.193 | convolution fusion | flops 1762066432 | bytes 5210112 | tf_op jit(solution)/shard_map/dot_general | solution.py:209
  254.5 1.4 collective-permute-start.13
  255.9 2.1 collective-permute-start.12
  258.0 0.9 collective-permute-start.11
  258.9 1.0 collective-permute-start.15
  259.9 2.5 collective-permute-start.14
  262.4 3.2 %multiply_bitcast_fusion = f32[1,1792,3,128]{3,1,2,0:T(8,128)} fusion(bf16[1792,3,128]{2,0,1:T(8,128)(2,1)} %collective-permute-done.17, bf16[1792,3,128]{2,0,1:T(8,128)(2,1)S(1)} %copy-done.1), kind=kLoop, calls=%fused_computation.17 | loop fusion | flops 2752512 | bytes 5505024 | tf_op jit(solution)/shard_map/broadcast_in_dim | solution.py:193
  265.6 12.5 %collective-permute-done.15 = bf16[256]{0:T(256)(128)(2,1)S(1)} collective-permute-done((bf16[256]{0:T(256)(128)(2,1)S(1)}, bf16[256]{0:T(256)(128)(2,1)S(1)}, u32[]{:S(2)}, u32[]{:S(2)}) %collective-permute-start.15) | collective-permute-done | bytes 544 | tf_op jit(solution)/shard_map/ppermute | solution.py:48
  278.9 0.8 fusion.37
  (125 shorter events, 12.1 us)
Async XLA Ops:
  2.5 52.5 %collective-permute-start = (bf16[32,7168]{1,0:T(8,128)(2,1)S(1)}, bf16[32,7168]{1,0:T(8,128)(2,1)S(1)}, u32[]{:S(2)}, u32[]{:S(2)}) collective-permute-start(bf16[32,7168]{1,0:T(8,128)(2,1)S(1)} %constant_dynamic-update-slice_fusion), channel_id=1, source_target_pairs={{0,4},{1,5},{2,6},{3,7},{4,0},{5,1},{6,2},{7,3},{8,12},{9,13},{10,... | collective-permute-start | bytes 1376264 | tf_op jit(solution)/shard_map/ppermute | solution.py:48
  4.2 50.9 %collective-permute-start.3 = (bf16[32,7168]{1,0:T(8,128)(2,1)S(1)}, bf16[32,7168]{1,0:T(8,128)(2,1)S(1)}, u32[]{:S(2)}, u32[]{:S(2)}) collective-permute-start(bf16[32,7168]{1,0:T(8,128)(2,1)S(1)} %constant_dynamic-update-slice_fusion), channel_id=1, source_target_pairs={{0,8},{1,9},{2,10},{3,11},{4,12},{5,13},{6,14},{7,15},{8,0},{9,1},... | collective-permute-start | bytes 1376264 | tf_op jit(solution)/shard_map/ppermute | solution.py:48
  6.8 48.3 %collective-permute-start.6 = (bf16[32,7168]{1,0:T(8,128)(2,1)S(1)}, bf16[32,7168]{1,0:T(8,128)(2,1)S(1)}, u32[]{:S(2)}, u32[]{:S(2)}) collective-permute-start(bf16[32,7168]{1,0:T(8,128)(2,1)S(1)} %constant_dynamic-update-slice_fusion), channel_id=1, source_target_pairs={{0,12},{1,13},{2,14},{3,15},{4,8},{5,9},{6,10},{7,11},{8,4},{9,5},... | collective-permute-start | bytes 1376264 | tf_op jit(solution)/shard_map/ppermute | solution.py:48
  7.0 26.8 %collective-permute-start.1 = (s32[32,8]{0,1:T(8,128)}, s32[32,8]{0,1:T(8,128)S(1)}, u32[]{:S(2)}, u32[]{:S(2)}) collective-permute-start(s32[32,8]{0,1:T(8,128)} %param.10), channel_id=1, source_target_pairs={{0,4},{1,5},{2,6},{3,7},{4,0},{5,1},{6,2},{7,3},{8,12},{9,13},{10,... | collective-permute-start | bytes 3080 | tf_op jit(solution)/shard_map/ppermute | solution.py:48
  7.7 29.6 %collective-permute-start.2 = (f32[32,8]{0,1:T(8,128)}, f32[32,8]{0,1:T(8,128)S(1)}, u32[]{:S(2)}, u32[]{:S(2)}) collective-permute-start(f32[32,8]{0,1:T(8,128)} %param.11), channel_id=1, source_target_pairs={{0,4},{1,5},{2,6},{3,7},{4,0},{5,1},{6,2},{7,3},{8,12},{9,13},{10,... | collective-permute-start | bytes 3080 | tf_op jit(solution)/shard_map/ppermute | solution.py:48
  33.8 13.1 %collective-permute-start.4 = (s32[32,8]{0,1:T(8,128)}, s32[32,8]{0,1:T(8,128)S(1)}, u32[]{:S(2)}, u32[]{:S(2)}) collective-permute-start(s32[32,8]{0,1:T(8,128)} %param.10), channel_id=1, source_target_pairs={{0,8},{1,9},{2,10},{3,11},{4,12},{5,13},{6,14},{7,15},{8,0},{9,1},... | collective-permute-start | bytes 3080 | tf_op jit(solution)/shard_map/ppermute | solution.py:48
  37.3 12.1 %collective-permute-start.5 = (f32[32,8]{0,1:T(8,128)}, f32[32,8]{0,1:T(8,128)S(1)}, u32[]{:S(2)}, u32[]{:S(2)}) collective-permute-start(f32[32,8]{0,1:T(8,128)} %param.11), channel_id=1, source_target_pairs={{0,8},{1,9},{2,10},{3,11},{4,12},{5,13},{6,14},{7,15},{8,0},{9,1},... | collective-permute-start | bytes 3080 | tf_op jit(solution)/shard_map/ppermute | solution.py:48
  46.9 5.6 %collective-permute-start.7 = (s32[32,8]{0,1:T(8,128)}, s32[32,8]{0,1:T(8,128)S(1)}, u32[]{:S(2)}, u32[]{:S(2)}) collective-permute-start(s32[32,8]{0,1:T(8,128)} %param.10), channel_id=1, source_target_pairs={{0,12},{1,13},{2,14},{3,15},{4,8},{5,9},{6,10},{7,11},{8,4},{9,5},... | collective-permute-start | bytes 3080 | tf_op jit(solution)/shard_map/ppermute | solution.py:48
  49.4 5.6 %collective-permute-start.8 = (f32[32,8]{0,1:T(8,128)}, f32[32,8]{0,1:T(8,128)S(1)}, u32[]{:S(2)}, u32[]{:S(2)}) collective-permute-start(f32[32,8]{0,1:T(8,128)} %param.11), channel_id=1, source_target_pairs={{0,12},{1,13},{2,14},{3,15},{4,8},{5,9},{6,10},{7,11},{8,4},{9,5},... | collective-permute-start | bytes 3080 | tf_op jit(solution)/shard_map/ppermute | solution.py:48
  63.7 58.5 %collective-permute-start.9 = (bf16[1,1792,3,128]{3,1,2,0:T(8,128)(2,1)}, bf16[1,1792,3,128]{3,1,2,0:T(8,128)(2,1)}, u32[]{:S(2)}, u32[]{:S(2)}) collective-permute-start(bf16[1,1792,3,128]{3,1,2,0:T(8,128)(2,1)} %param.12), channel_id=1, source_target_pairs={{0,8},{1,9},{2,10},{3,11},{4,12},{5,13},{6,14},{7,15},{8,0},{9,1},... | collective-permute-start | bytes 4128776 | tf_op jit(solution)/shard_map/ppermute | solution.py:8
  68.8 53.4 %copy-start.4 = (bf16[1,1792,3,128]{3,1,2,0:T(8,128)(2,1)S(1)}, bf16[1,1792,3,128]{3,1,2,0:T(8,128)(2,1)}, u32[]{:S(2)}) copy-start(bf16[1,1792,3,128]{3,1,2,0:T(8,128)(2,1)} %param.12) | copy-start | bytes 4128772
  68.8 59.9 %all-to-all-start = ((bf16[4,80,7296]{2,1,0:T(8,128)(2,1)}), bf16[4,80,7296]{2,1,0:T(8,128)(2,1)}, u32[]{:S(2)}, u32[]{:S(2)}) async-start(bf16[4,80,7296]{2,1,0:T(8,128)(2,1)} %bitcast.119), calls=%async_computation | async-start | bytes 9338880 | tf_op jit(solution)/shard_map/all_to_all | solution.py:127
  123.7 3.4 %copy-start.3 = (bf16[1,1792,3,128]{3,1,2,0:T(8,128)(2,1)}, bf16[1,1792,3,128]{3,1,2,0:T(8,128)(2,1)S(1)}, u32[]{:S(2)}) copy-start(bf16[1,1792,3,128]{3,1,2,0:T(8,128)(2,1)S(1)} %broadcast_select_fusion.2) | copy-start | bytes 4128772
  123.7 3.2 %collective-permute-start.10 = (bf16[1,1792,3,128]{3,1,2,0:T(8,128)(2,1)S(1)}, bf16[1,1792,3,128]{3,1,2,0:T(8,128)(2,1)S(1)}, u32[]{:S(2)}, u32[]{:S(2)}) collective-permute-start(bf16[1,1792,3,128]{3,1,2,0:T(8,128)(2,1)S(1)} %broadcast_select_fusion.2), channel_id=1, source_target_pairs={{0,16},{16,0},{1,17},{17,1},{2,18},{18,2},{3,19},{19,3},{4,20},{20... | collective-permute-start | bytes 4128776 | tf_op jit(solution)/shard_map/ppermute | solution.py:147
  123.8 92.7 %collective-permute-start.19 = (bf16[1,1792,3,128]{3,1,2,0:T(8,128)(2,1)}, bf16[1,1792,3,128]{3,1,2,0:T(8,128)(2,1)}, u32[]{:S(2)}, u32[]{:S(2)}) collective-permute-start(bf16[1,1792,3,128]{3,1,2,0:T(8,128)(2,1)} %param.14), channel_id=1, source_target_pairs={{0,8},{1,9},{2,10},{3,11},{4,12},{5,13},{6,14},{7,15},{8,0},{9,1},... | collective-permute-start | bytes 4128776 | tf_op jit(solution)/shard_map/ppermute | solution.py:8
  123.8 122.0 %collective-permute-start.18 = (bf16[1,1792,3,128]{3,1,2,0:T(8,128)(2,1)}, bf16[1,1792,3,128]{3,1,2,0:T(8,128)(2,1)}, u32[]{:S(2)}, u32[]{:S(2)}) collective-permute-start(bf16[1,1792,3,128]{3,1,2,0:T(8,128)(2,1)} %param.13), channel_id=1, source_target_pairs={{0,8},{1,9},{2,10},{3,11},{4,12},{5,13},{6,14},{7,15},{8,0},{9,1},... | collective-permute-start | bytes 4128776 | tf_op jit(solution)/shard_map/ppermute | solution.py:8
  127.3 7.4 %copy-start.2 = (bf16[3584,3,128]{2,0,1:T(8,128)(2,1)}, bf16[3584,3,128]{2,0,1:T(8,128)(2,1)S(1)}, u32[]{:S(2)}) copy-start(bf16[3584,3,128]{2,0,1:T(8,128)(2,1)S(1)} %maximum_bitcast_fusion) | copy-start | bytes 8257540
  146.6 3.0 %copy-start.6 = (bf16[3584,128]{1,0:T(8,128)(2,1)S(1)}, bf16[3584,128]{1,0:T(8,128)(2,1)}, u32[]{:S(2)}) copy-start(bf16[3584,128]{1,0:T(8,128)(2,1)} %get-tuple-element.65) | copy-start | bytes 2752516
  146.6 3.0 %copy-start.7 = (bf16[3584,128]{1,0:T(8,128)(2,1)S(1)}, bf16[3584,128]{1,0:T(8,128)(2,1)}, u32[]{:S(2)}) copy-start(bf16[3584,128]{1,0:T(8,128)(2,1)} %get-tuple-element.66) | copy-start | bytes 2752516
  146.6 69.8 %collective-permute-start.17 = (bf16[1792,3,128]{2,0,1:T(8,128)(2,1)}, bf16[1792,3,128]{2,0,1:T(8,128)(2,1)}, u32[]{:S(2)}, u32[]{:S(2)}) collective-permute-start(bf16[1792,3,128]{2,0,1:T(8,128)(2,1)} %broadcast_select_fusion), channel_id=1, source_target_pairs={{0,16},{16,0},{1,17},{17,1},{2,18},{18,2},{3,19},{19,3},{4,20},{20... | collective-permute-start | bytes 4128776 | tf_op jit(solution)/shard_map/ppermute | solution.py:187
  152.0 4.9 %copy-start.8 = (f32[32,8]{0,1:T(8,128)S(1)}, f32[32,8]{0,1:T(8,128)}, u32[]{:S(2)}) copy-start(f32[32,8]{0,1:T(8,128)} %param.11) | copy-start | bytes 3076
  152.0 97.5 %all-to-all-start.1 = ((bf16[4,80,3712]{2,1,0:T(8,128)(2,1)}), bf16[4,80,3712]{2,1,0:T(8,128)(2,1)}, u32[]{:S(2)}, u32[]{:S(2)}) async-start(bf16[4,80,3712]{2,1,0:T(8,128)(2,1)} %bitcast.120), calls=%async_computation.1 | async-start | bytes 4751360 | tf_op jit(solution)/shard_map/all_to_all | solution.py:127
  157.6 88.3 %copy-start.5 = (bf16[1,1792,3,128]{3,1,2,0:T(8,128)(2,1)S(1)}, bf16[1,1792,3,128]{3,1,2,0:T(8,128)(2,1)}, u32[]{:S(2)}) copy-start(bf16[1,1792,3,128]{3,1,2,0:T(8,128)(2,1)} %param.13) | copy-start | bytes 4128772
  220.6 25.3 %copy-start = (bf16[1792,3,128]{2,0,1:T(8,128)(2,1)}, bf16[1792,3,128]{2,0,1:T(8,128)(2,1)S(1)}, u32[]{:S(2)}) copy-start(bf16[1792,3,128]{2,0,1:T(8,128)(2,1)S(1)} %get-tuple-element.61) | copy-start | bytes 4128772
  250.6 11.8 %copy-start.1 = (bf16[1792,3,128]{2,0,1:T(8,128)(2,1)S(1)}, bf16[1792,3,128]{2,0,1:T(8,128)(2,1)}, u32[]{:S(2)}) copy-start(bf16[1792,3,128]{2,0,1:T(8,128)(2,1)} %copy-done) | copy-start | bytes 4128772
  254.3 5.6 %collective-permute-start.16 = (bf16[256]{0:T(256)(128)(2,1)S(1)}, bf16[256]{0:T(256)(128)(2,1)S(1)}, u32[]{:S(2)}, u32[]{:S(2)}) collective-permute-start(bf16[256]{0:T(256)(128)(2,1)S(1)} %get-tuple-element.77), channel_id=1, source_target_pairs={{0,4},{1,5},{2,6},{3,7},{4,0},{5,1},{6,2},{7,3},{8,12},{9,13},{10,... | collective-permute-start | bytes 1544 | tf_op jit(solution)/shard_map/ppermute | solution.py:48
  254.5 24.4 %collective-permute-start.13 = (bf16[32,3584]{1,0:T(8,128)(2,1)S(1)}, bf16[32,3584]{1,0:T(8,128)(2,1)S(1)}, u32[]{:S(2)}, u32[]{:S(2)}) collective-permute-start(bf16[32,3584]{1,0:T(8,128)(2,1)S(1)} %get-tuple-element.70), channel_id=1, source_target_pairs={{0,12},{1,13},{2,14},{3,15},{4,8},{5,9},{6,10},{7,11},{8,4},{9,5},... | collective-permute-start | bytes 688136 | tf_op jit(solution)/shard_map/ppermute | solution.py:48
  255.9 23.0 %collective-permute-start.12 = (bf16[32,3584]{1,0:T(8,128)(2,1)S(1)}, bf16[32,3584]{1,0:T(8,128)(2,1)S(1)}, u32[]{:S(2)}, u32[]{:S(2)}) collective-permute-start(bf16[32,3584]{1,0:T(8,128)(2,1)S(1)} %get-tuple-element.71), channel_id=1, source_target_pairs={{0,8},{1,9},{2,10},{3,11},{4,12},{5,13},{6,14},{7,15},{8,0},{9,1},... | collective-permute-start | bytes 688136 | tf_op jit(solution)/shard_map/ppermute | solution.py:48
  258.0 20.9 %collective-permute-start.11 = (bf16[32,3584]{1,0:T(8,128)(2,1)S(1)}, bf16[32,3584]{1,0:T(8,128)(2,1)S(1)}, u32[]{:S(2)}, u32[]{:S(2)}) collective-permute-start(bf16[32,3584]{1,0:T(8,128)(2,1)S(1)} %get-tuple-element.69), channel_id=1, source_target_pairs={{0,4},{1,5},{2,6},{3,7},{4,0},{5,1},{6,2},{7,3},{8,12},{9,13},{10,... | collective-permute-start | bytes 688136 | tf_op jit(solution)/shard_map/ppermute | solution.py:48
  258.9 19.2 %collective-permute-start.15 = (bf16[256]{0:T(256)(128)(2,1)S(1)}, bf16[256]{0:T(256)(128)(2,1)S(1)}, u32[]{:S(2)}, u32[]{:S(2)}) collective-permute-start(bf16[256]{0:T(256)(128)(2,1)S(1)} %get-tuple-element.76), channel_id=1, source_target_pairs={{0,8},{1,9},{2,10},{3,11},{4,12},{5,13},{6,14},{7,15},{8,0},{9,1},... | collective-permute-start | bytes 1544 | tf_op jit(solution)/shard_map/ppermute | solution.py:48
  259.9 18.2 %collective-permute-start.14 = (bf16[256]{0:T(256)(128)(2,1)S(1)}, bf16[256]{0:T(256)(128)(2,1)S(1)}, u32[]{:S(2)}, u32[]{:S(2)}) collective-permute-start(bf16[256]{0:T(256)(128)(2,1)S(1)} %get-tuple-element.75), channel_id=1, source_target_pairs={{0,12},{1,13},{2,14},{3,15},{4,8},{5,9},{6,10},{7,11},{8,4},{9,5},... | collective-permute-start | bytes 1544 | tf_op jit(solution)/shard_map/ppermute | solution.py:48

commit v17 on v8

--- a/solution.py
+++ b/solution.py
@@ -137,7 +137,13 @@
     first_moment, second_moment, _ = lax.optimization_barrier(
         (first_moment, second_moment, their_weights)
     )
-    their_moments = from_partner((first_moment, second_moment), "expert", swap_bit)
+    if two_stage:
+        pairs = [[p, p + half_axis] for p in range(half_axis)]
+        pair_second = lax.all_gather(second_moment, "expert", axis_index_groups=pairs)
+        their_second = jnp.where(my_index < half_axis, pair_second[1], pair_second[0])
+        their_moments = (from_partner(first_moment, "expert", swap_bit), their_second)
+    else:
+        their_moments = from_partner((first_moment, second_moment), "expert", swap_bit)
     weights = jnp.where(swapped, their_weights, weights)
     if groups == 2:
         other = lax.ppermute(weights, "dp", [(0, 1), (1, 0)])

time: 271 us -> 296 us (1.092)
  between operations: 1.67 us -> 15.1 us
  waiting for transfers between devices: 183 us -> 195 us
  starting transfers between devices: 28.5 us -> 25.4 us
    all_gather x0 -> x1, waiting for transfers between devices: none -> 88.6 us  [on_device(): lax.all_gather(second_moment, 'expert', axis_index_groups=pairs)]
    ppermute x8 -> x7, waiting for transfers between devices: 183 us -> 103 us  [from_partner(): lax.ppermute(value, axis, [(i, i ^ 1 << bit) for i in range(lax.axis_size...]
    ppermute x8 -> x7, starting transfers between devices: 14.9 us -> 11.4 us  [from_partner(): lax.ppermute(value, axis, [(i, i ^ 1 << bit) for i in range(lax.axis_size...]
    ppermute x1, waiting for transfers between devices: 0.01 us -> 3.08 us  [on_device(): other = lax.ppermute(weights, 'dp', [(0, 1), (1, 0)])]
  transfers between devices with their start and end apart: 12 -> 12, of which waited for: 5 -> 6; matrix products, arithmetic and copies ran while one was open for 18% -> 17% of each run, Pallas kernels for 0% -> 0%
where the time goes in v17:
time: 296 us; the launch traced here: 294 us
  waiting for transfers between devices  195 us (66%)
  other arithmetic  27.1 us (9%)
  starting transfers between devices  25.4 us (9%)
  matrix products  24.6 us (8%)
  between operations  15.1 us (5%)
  local copies, waits for them, and re-layouts  6.77 us (2%)
    ppermute x7, waiting for transfers between devices, from_partner(): lax.ppermute(value, axis, [(i, i ^ 1 << bit) for i in range(lax.axis_size...  103 us
    all_gather x1, waiting for transfers between devices, on_device(): lax.all_gather(second_moment, 'expert', axis_index_groups=pairs)  88.6 us
    all_to_all x2, starting transfers between devices, spread(): lax.all_to_all(parts, 'expert', 0, 0, tiled=True, axis_index_groups=halves)  13.9 us
    ppermute x7, starting transfers between devices, from_partner(): lax.ppermute(value, axis, [(i, i ^ 1 << bit) for i in range(lax.axis_size...  11.4 us
  transfers between devices with their start and end apart: 12, of which 6 were waited for; matrix products, arithmetic and copies ran while one was open for 17% of the time, Pallas kernels for 0%

profile of v17, /device:TPU:6, one launch (start us, length us, event | category | flops | bytes accessed | tf_op | source)
XLA Modules:
  0.0 294.0 jit_solution(10266474771193603790)
XLA Ops:
  7.2 2.7 collective-permute-start.1
  9.8 0.3 collective-permute-start
  10.2 1.0 constant_dynamic-update-slice_fusion.2
  11.1 1.0 constant_dynamic-update-slice_fusion.1
  12.1 2.7 collective-permute-start.2
  14.7 0.8 copy.53
  15.8 0.6 reduce-window.14
  16.7 0.7 convert.28
  18.0 0.6 reduce-window.16
  19.1 0.7 select_reduce_fusion.3
  20.4 0.2 select_reduce_fusion.2
  20.6 0.4 fusion.30
  21.1 13.5 %collective-permute-done.2 = bf16[32,7168]{1,0:T(8,128)(2,1)S(1)} collective-permute-done((bf16[32,7168]{1,0:T(8,128)(2,1)S(1)}, bf16[32,7168]{1,0:T(8,128)(2,1)S(1)}, u32[]{:S(2)}, u32[]{:S(2)}) %collective-permute-start.2) | collective-permute-done | bytes 458784 | tf_op jit(solution)/shard_map/ppermute | solution.py:8
  34.6 1.4 convolution_convert_fusion
  36.0 2.5 pad_maximum_fusion
  38.5 5.1 %all-to-all-start = ((bf16[8,40,7296]{2,1,0:T(8,128)(2,1)}), bf16[8,40,7296]{2,1,0:T(8,128)(2,1)}, u32[]{:S(2)}, u32[]{:S(2)}) async-start(bf16[8,40,7296]{2,1,0:T(8,128)(2,1)} %bitcast.79), calls=%async_computation | async-start | bytes 9338880 | tf_op jit(solution)/shard_map/all_to_all | solution.py:123
  43.6 2.7 collective-permute-start.3
  46.3 0.6 fusion.69
  47.6 82.1 %collective-permute-done.3 = bf16[1,1792,3,128]{3,1,2,0:T(8,128)(2,1)} collective-permute-done((bf16[1,1792,3,128]{3,1,2,0:T(8,128)(2,1)S(1)}, bf16[1,1792,3,128]{3,1,2,0:T(8,128)(2,1)}, u32[]{:S(2)}, u32[]{:S(2)}) %collective-permute-start.3) | collective-permute-done | bytes 1376288 | tf_op jit(solution)/shard_map/ppermute | solution.py:8
  129.7 1.5 broadcast_select_fusion.2
  131.3 3.1 %collective-permute-done.4 = bf16[1,1792,3,128]{3,1,2,0:T(8,128)(2,1)S(1)} collective-permute-done((bf16[1,1792,3,128]{3,1,2,0:T(8,128)(2,1)S(1)}, bf16[1,1792,3,128]{3,1,2,0:T(8,128)(2,1)S(1)}, u32[]{:S(2)}, u32[]{:S(2)}) %collective-permute-start.4) | collective-permute-done | bytes 1376288 | tf_op jit(solution)/shard_map/ppermute | solution.py:149
  134.8 1.3 slice_bitcast_fusion
  136.1 1.0 convert_reduce_fusion.1
  137.1 2.4 fusion.16
  139.5 2.7 fusion.28
  142.2 2.6 multiply_convert_fusion.5
  144.8 2.6 fusion.22
  147.6 3.6 %fusion.1 = bf16[3584,1,128]{2,0,1:T(8,128)(2,1)} fusion(bf16[320,128]{1,0:T(8,128)(2,1)S(1)} %get-tuple-element.44, bf16[320,7296]{1,0:T(8,128)(2,1)} %bitcast.5), kind=kOutput, calls=%fused_computation.6 | convolution fusion | flops 294060032 | bytes 3293184 | tf_op jit(solution)/shard_map/dot_general | solution.py:179
  151.2 0.8 convolution_convert_fusion.1
  152.0 1.6 pad_maximum_fusion.2
  153.6 8.8 %all-to-all-start.1 = ((bf16[8,40,3712]{2,1,0:T(8,128)(2,1)}), bf16[8,40,3712]{2,1,0:T(8,128)(2,1)}, u32[]{:S(2)}, u32[]{:S(2)}) async-start(bf16[8,40,3712]{2,1,0:T(8,128)(2,1)} %bitcast.10), calls=%async_computation.1 | async-start | bytes 4751360 | tf_op jit(solution)/shard_map/all_to_all | solution.py:123
  162.5 2.6 fusion
  165.1 2.8 fusion.2
  167.9 0.3 pad_maximum_fusion.1
  168.2 1.2 broadcast_select_fusion
  169.6 0.4 select_reduce_fusion
  170.0 88.6 %all-gather.3.cloned.1.call-done = bf16[2,1792,3,128]{3,1,2,0:T(8,128)(2,1)} async-done(((bf16[1,1792,3,128]{3,1,2,0:T(8,128)(2,1)}), bf16[2,1792,3,128]{3,1,2,0:T(8,128)(2,1)}) %all-gather.3.cloned.1.call-update) | async-done | bytes 2752528 | tf_op jit(solution)/shard_map/all_gather | solution.py:142
  258.6 4.8 %fusion.3 = (bf16[1,1792,3,128]{3,1,2,0:T(8,128)(2,1)}, bf16[1792,3,128]{2,0,1:T(8,128)(2,1)S(1)}) fusion(bf16[1792,3,128]{2,0,1:T(8,128)(2,1)} %collective-permute-done.7, bf16[1,1792,3,128]{3,1,2,0:T(8,128)(2,1)} %param.14, bf16[2,1792,3,128]{3,1,2,0:T(8,128)(2,1)} %all-gather.3.cloned.1.call-done, pred[]{:T(512)S(6)} %lt.33, pred[]{:T(512)S(6)} %eq.180, ...), kind=kLoop, calls=%fused_computation.13 | loop fusion | flops 8945664 | bytes 11010051 | tf_op jit(solution)/shard_map/convert_element_type | solution.py:199
  263.3 0.9 collective-permute-done.8
  264.2 0.2 copy-done
  264.4 3.7 %fusion.4 = bf16[1,1792,3,128]{3,1,2,0:T(8,128)(2,1)} fusion(bf16[1792,3,128]{2,0,1:T(8,128)(2,1)} %collective-permute-done.7, bf16[1792,3,128]{2,0,1:T(8,128)(2,1)S(1)} %get-tuple-element.35, bf16[1,1792,3,128]{3,1,2,0:T(8,128)(2,1)} %collective-permute-done.8, bf16[1,1792,3,128]{3,1,2,0:T(8,128)(2,1)} %param.13, pred[]{:T(512)S(6)} %eq.180), kind=kLoop, calls=%fused_computation.15 | loop fusion | flops 6193152 | bytes 6881281 | tf_op jit(solution)/shard_map/convert_element_type | solution.py:198
  268.1 1.1 convert_reduce_fusion
  269.2 3.1 %fusion.5 = f32[64,3584]{1,0:T(8,128)S(1)} fusion(f32[320,64]{0,1:T(8,128)S(1)} %select_reduce_fusion, bf16[320,3712]{1,0:T(8,128)(2,1)} %bitcast.11), kind=kOutput, calls=%fused_computation.19 | convolution fusion | flops 880803840 | bytes 3293184 | tf_op jit(solution)/shard_map/dot_general | solution.py:209
  272.6 3.0 %collective-permute-start.6 = (bf16[256]{0:T(256)(128)(2,1)S(1)}, bf16[256]{0:T(256)(128)(2,1)S(1)}, u32[]{:S(2)}, u32[]{:S(2)}) collective-permute-start(bf16[256]{0:T(256)(128)(2,1)S(1)} %slice.83), channel_id=1, source_target_pairs={{0,8},{1,9},{2,10},{3,11},{4,12},{5,13},{6,14},{7,15},{8,0},{9,1},... | collective-permute-start | bytes 1544 | tf_op jit(solution)/shard_map/ppermute | solution.py:8
  275.6 3.2 %multiply_bitcast_fusion = f32[1,1792,3,128]{3,1,2,0:T(8,128)} fusion(bf16[1792,3,128]{2,0,1:T(8,128)(2,1)} %collective-permute-done.7, bf16[1792,3,128]{2,0,1:T(8,128)(2,1)S(1)} %copy-done.1), kind=kLoop, calls=%fused_computation.17 | loop fusion | flops 2752512 | bytes 5505024 | tf_op jit(solution)/shard_map/broadcast_in_dim | solution.py:195
  278.8 6.8 %collective-permute-done.6 = bf16[256]{0:T(256)(128)(2,1)S(1)} collective-permute-done((bf16[256]{0:T(256)(128)(2,1)S(1)}, bf16[256]{0:T(256)(128)(2,1)S(1)}, u32[]{:S(2)}, u32[]{:S(2)}) %collective-permute-start.6) | collective-permute-done | bytes 544 | tf_op jit(solution)/shard_map/ppermute | solution.py:8
  285.8 0.7 copy.64
  286.4 0.7 fusion.32
  (76 shorter events, 3.4 us)
Async XLA Ops:
  7.2 13.0 %collective-permute-start.1 = (f32[32,8]{0,1:T(8,128)}, f32[32,8]{0,1:T(8,128)S(1)}, u32[]{:S(2)}, u32[]{:S(2)}) collective-permute-start(f32[32,8]{0,1:T(8,128)} %param.11), channel_id=1, source_target_pairs={{0,8},{1,9},{2,10},{3,11},{4,12},{5,13},{6,14},{7,15},{8,0},{9,1},... | collective-permute-start | bytes 3080 | tf_op jit(solution)/shard_map/ppermute | solution.py:8
  9.8 7.8 %collective-permute-start = (s32[32,8]{0,1:T(8,128)}, s32[32,8]{0,1:T(8,128)S(1)}, u32[]{:S(2)}, u32[]{:S(2)}) collective-permute-start(s32[32,8]{0,1:T(8,128)} %param.10), channel_id=1, source_target_pairs={{0,8},{1,9},{2,10},{3,11},{4,12},{5,13},{6,14},{7,15},{8,0},{9,1},... | collective-permute-start | bytes 3080 | tf_op jit(solution)/shard_map/ppermute | solution.py:8
  12.1 22.6 %collective-permute-start.2 = (bf16[32,7168]{1,0:T(8,128)(2,1)S(1)}, bf16[32,7168]{1,0:T(8,128)(2,1)S(1)}, u32[]{:S(2)}, u32[]{:S(2)}) collective-permute-start(bf16[32,7168]{1,0:T(8,128)(2,1)S(1)} %constant_dynamic-update-slice_fusion.1), channel_id=1, source_target_pairs={{0,8},{1,9},{2,10},{3,11},{4,12},{5,13},{6,14},{7,15},{8,0},{9,1},... | collective-permute-start | bytes 1376264 | tf_op jit(solution)/shard_map/ppermute | solution.py:8
  38.5 5.1 %copy-start.3 = (bf16[1,1792,3,128]{3,1,2,0:T(8,128)(2,1)S(1)}, bf16[1,1792,3,128]{3,1,2,0:T(8,128)(2,1)}, u32[]{:S(2)}) copy-start(bf16[1,1792,3,128]{3,1,2,0:T(8,128)(2,1)} %param.12) | copy-start | bytes 4128772
  38.5 7.8 %copy-start.8 = (s32[8]{0:T(128)S(1)}, s32[8]{0:T(128)}, u32[]{:S(2)}) copy-start(s32[8]{0:T(128)} %param.15) | copy-start | bytes 100
  38.5 97.6 %all-to-all-start = ((bf16[8,40,7296]{2,1,0:T(8,128)(2,1)}), bf16[8,40,7296]{2,1,0:T(8,128)(2,1)}, u32[]{:S(2)}, u32[]{:S(2)}) async-start(bf16[8,40,7296]{2,1,0:T(8,128)(2,1)} %bitcast.79), calls=%async_computation | async-start | bytes 9338880 | tf_op jit(solution)/shard_map/all_to_all | solution.py:123
  43.6 215.0 %all-gather.3.cloned.1.call-start = ((), (), s32[]{:S(2)}) async-start(), calls=%async_computation.2 | async-start | bytes 4128768 | tf_op jit(solution)/shard_map/all_gather | solution.py:142
  43.6 86.1 %collective-permute-start.3 = (bf16[1,1792,3,128]{3,1,2,0:T(8,128)(2,1)S(1)}, bf16[1,1792,3,128]{3,1,2,0:T(8,128)(2,1)}, u32[]{:S(2)}, u32[]{:S(2)}) collective-permute-start(bf16[1,1792,3,128]{3,1,2,0:T(8,128)(2,1)S(1)} %copy-done.3), channel_id=1, source_target_pairs={{0,8},{1,9},{2,10},{3,11},{4,12},{5,13},{6,14},{7,15},{8,0},{9,1},... | collective-permute-start | bytes 4128776 | tf_op jit(solution)/shard_map/ppermute | solution.py:8
  131.2 3.4 %copy-start.2 = (bf16[1,1792,3,128]{3,1,2,0:T(8,128)(2,1)}, bf16[1,1792,3,128]{3,1,2,0:T(8,128)(2,1)S(1)}, u32[]{:S(2)}) copy-start(bf16[1,1792,3,128]{3,1,2,0:T(8,128)(2,1)S(1)} %broadcast_select_fusion.2) | copy-start | bytes 4128772
  131.2 3.2 %collective-permute-start.4 = (bf16[1,1792,3,128]{3,1,2,0:T(8,128)(2,1)S(1)}, bf16[1,1792,3,128]{3,1,2,0:T(8,128)(2,1)S(1)}, u32[]{:S(2)}, u32[]{:S(2)}) collective-permute-start(bf16[1,1792,3,128]{3,1,2,0:T(8,128)(2,1)S(1)} %broadcast_select_fusion.2), channel_id=1, source_target_pairs={{0,16},{16,0},{1,17},{17,1},{2,18},{18,2},{3,19},{19,3},{4,20},{20... | collective-permute-start | bytes 4128776 | tf_op jit(solution)/shard_map/ppermute | solution.py:149
  147.5 3.8 %copy-start.4 = (bf16[3584,128]{1,0:T(8,128)(2,1)S(1)}, bf16[3584,128]{1,0:T(8,128)(2,1)}, u32[]{:S(2)}) copy-start(bf16[3584,128]{1,0:T(8,128)(2,1)} %get-tuple-element.38) | copy-start | bytes 2752516
  147.5 3.8 %copy-start.5 = (bf16[3584,128]{1,0:T(8,128)(2,1)S(1)}, bf16[3584,128]{1,0:T(8,128)(2,1)}, u32[]{:S(2)}) copy-start(bf16[3584,128]{1,0:T(8,128)(2,1)} %get-tuple-element.39) | copy-start | bytes 2752516
  153.6 114.5 %all-to-all-start.1 = ((bf16[8,40,3712]{2,1,0:T(8,128)(2,1)}), bf16[8,40,3712]{2,1,0:T(8,128)(2,1)}, u32[]{:S(2)}, u32[]{:S(2)}) async-start(bf16[8,40,3712]{2,1,0:T(8,128)(2,1)} %bitcast.10), calls=%async_computation.1 | async-start | bytes 4751360 | tf_op jit(solution)/shard_map/all_to_all | solution.py:123
  165.1 2.8 copy-start.6
  168.2 1.2 copy-start.7
  169.4 89.1 %collective-permute-start.7 = (bf16[1792,3,128]{2,0,1:T(8,128)(2,1)}, bf16[1792,3,128]{2,0,1:T(8,128)(2,1)}, u32[]{:S(2)}, u32[]{:S(2)}) collective-permute-start(bf16[1792,3,128]{2,0,1:T(8,128)(2,1)} %broadcast_select_fusion), channel_id=1, source_target_pairs={{0,16},{16,0},{1,17},{17,1},{2,18},{18,2},{3,19},{19,3},{4,20},{20... | collective-permute-start | bytes 4128776 | tf_op jit(solution)/shard_map/ppermute | solution.py:189
  169.4 94.8 %collective-permute-start.8 = (bf16[1,1792,3,128]{3,1,2,0:T(8,128)(2,1)}, bf16[1,1792,3,128]{3,1,2,0:T(8,128)(2,1)}, u32[]{:S(2)}, u32[]{:S(2)}) collective-permute-start(bf16[1,1792,3,128]{3,1,2,0:T(8,128)(2,1)} %param.13), channel_id=1, source_target_pairs={{0,8},{1,9},{2,10},{3,11},{4,12},{5,13},{6,14},{7,15},{8,0},{9,1},... | collective-permute-start | bytes 4128776 | tf_op jit(solution)/shard_map/ppermute | solution.py:8
  263.3 1.1 copy-start
  268.1 7.5 %copy-start.1 = (bf16[1792,3,128]{2,0,1:T(8,128)(2,1)S(1)}, bf16[1792,3,128]{2,0,1:T(8,128)(2,1)}, u32[]{:S(2)}) copy-start(bf16[1792,3,128]{2,0,1:T(8,128)(2,1)} %copy-done) | copy-start | bytes 4128772
  272.4 14.1 %collective-permute-start.5 = (bf16[32,3584]{1,0:T(8,128)(2,1)S(1)}, bf16[32,3584]{1,0:T(8,128)(2,1)S(1)}, u32[]{:S(2)}, u32[]{:S(2)}) collective-permute-start(bf16[32,3584]{1,0:T(8,128)(2,1)S(1)} %slice.154), channel_id=1, source_target_pairs={{0,8},{1,9},{2,10},{3,11},{4,12},{5,13},{6,14},{7,15},{8,0},{9,1},... | collective-permute-start | bytes 688136 | tf_op jit(solution)/shard_map/ppermute | solution.py:8
  272.6 13.0 %collective-permute-start.6 = (bf16[256]{0:T(256)(128)(2,1)S(1)}, bf16[256]{0:T(256)(128)(2,1)S(1)}, u32[]{:S(2)}, u32[]{:S(2)}) collective-permute-start(bf16[256]{0:T(256)(128)(2,1)S(1)} %slice.83), channel_id=1, source_target_pairs={{0,8},{1,9},{2,10},{3,11},{4,12},{5,13},{6,14},{7,15},{8,0},{9,1},... | collective-permute-start | bytes 1544 | tf_op jit(solution)/shard_map/ppermute | solution.py:8
Sparse Core Ops, SparseCore 0:
  131.4 127.0 all-gather.2

commit v18 on v13

--- a/solution.py
+++ b/solution.py
@@ -134,10 +134,10 @@
         rows, grads_in, gates = send_slots(tokens, out_grad, flat_gate, slot_of, slot_cap)
     if not two_stage:
         their_weights = from_partner(weights, "expert", swap_bit)
-    moments = (first_moment, second_moment)
-    if not two_stage:
-        moments, _ = lax.optimization_barrier((moments, their_weights))
-        their_moments = from_partner(moments, "expert", swap_bit)
+    first_moment, second_moment, _ = lax.optimization_barrier(
+        (first_moment, second_moment, their_weights)
+    )
+    their_moments = from_partner((first_moment, second_moment), "expert", swap_bit)
     weights = jnp.where(swapped, their_weights, weights)
     if groups == 2:
         other = lax.ppermute(weights, "dp", [(0, 1), (1, 0)])
@@ -190,9 +190,8 @@
 
     if two_stage:
         back_in = jnp.concatenate([row_grad, with_tile(gate_rows)], axis=1)
-        back_in, moments = lax.optimization_barrier((back_in, moments))
+        back_in, their_moments = lax.optimization_barrier((back_in, their_moments))
         back_all = spread(back_in)
-        their_moments = from_partner(moments, "expert", swap_bit)
         back_rows = back_all[:, :model_width]
         back_gate = back_all[:, model_width].astype(jnp.float32)
         weight_of = jnp.where(slot_hit, gate2[None, :], 0.0)

time: 308 us -> 303 us (0.984)
  starting transfers between devices: 29.7 us -> 25.2 us
    ppermute x8, waiting for transfers between devices: 216 us -> 203 us  [from_partner(): lax.ppermute(value, axis, [(i, i ^ 1 << bit) for i in range(lax.axis_size...]
    all_to_all x2, waiting for transfers between devices: 0.01 us -> 11.8 us  [spread(): lax.all_to_all(parts, 'expert', 0, 0, tiled=True, axis_index_groups=halves)]
    all_to_all x2, starting transfers between devices: 15.3 us -> 9.62 us  [spread(): lax.all_to_all(parts, 'expert', 0, 0, tiled=True, axis_index_groups=halves)]
    ppermute x1, waiting for transfers between devices: 3.11 us -> 0.01 us  [on_device(): other = lax.ppermute(weights, 'dp', [(0, 1), (1, 0)])]
  transfers between devices with their start and end apart: 12 -> 12, of which waited for: 6 -> 7; matrix products, arithmetic and copies ran while one was open for 10% -> 16% of each run, Pallas kernels for 0% -> 0%
where the time goes in v18:
time: 303 us; the launch traced here: 302 us
  waiting for transfers between devices  217 us (72%)
  other arithmetic  26.4 us (9%)
  starting transfers between devices  25.2 us (8%)
  matrix products  24.1 us (8%)
  local copies, waits for them, and re-layouts  7.68 us (3%)
    ppermute x8, waiting for transfers between devices, from_partner(): lax.ppermute(value, axis, [(i, i ^ 1 << bit) for i in range(lax.axis_size...  203 us
    ppermute x8, starting transfers between devices, from_partner(): lax.ppermute(value, axis, [(i, i ^ 1 << bit) for i in range(lax.axis_size...  15.5 us
    all_to_all x2, waiting for transfers between devices, spread(): lax.all_to_all(parts, 'expert', 0, 0, tiled=True, axis_index_groups=halves)  11.8 us
    all_to_all x2, starting transfers between devices, spread(): lax.all_to_all(parts, 'expert', 0, 0, tiled=True, axis_index_groups=halves)  9.62 us
  transfers between devices with their start and end apart: 12, of which 7 were waited for; matrix products, arithmetic and copies ran while one was open for 16% of the time, Pallas kernels for 0%

profile of v18, /device:TPU:6, one launch (start us, length us, event | category | flops | bytes accessed | tf_op | source)
XLA Modules:
  0.0 302.4 jit_solution(2077769121871293831)
XLA Ops:
  0.6 2.7 collective-permute-start.1
  3.3 0.3 collective-permute-start
  3.6 1.0 constant_dynamic-update-slice_fusion.2
  4.6 1.0 constant_dynamic-update-slice_fusion.1
  5.5 2.7 collective-permute-start.2
  8.2 0.8 copy.41
  9.3 0.6 reduce-window.14
  10.2 0.7 convert.28
  11.5 0.6 reduce-window.16
  12.5 0.7 select_reduce_fusion.3
  14.1 0.4 fusion.29
  14.6 13.5 %collective-permute-done.2 = bf16[32,7168]{1,0:T(8,128)(2,1)S(1)} collective-permute-done((bf16[32,7168]{1,0:T(8,128)(2,1)S(1)}, bf16[32,7168]{1,0:T(8,128)(2,1)S(1)}, u32[]{:S(2)}, u32[]{:S(2)}) %collective-permute-start.2) | collective-permute-done | bytes 458784 | tf_op jit(solution)/shard_map/ppermute | solution.py:8
  28.1 1.4 convolution_convert_fusion
  29.5 2.5 pad_maximum_fusion
  32.0 5.1 %all-to-all-start = ((bf16[8,40,7296]{2,1,0:T(8,128)(2,1)}), bf16[8,40,7296]{2,1,0:T(8,128)(2,1)}, u32[]{:S(2)}, u32[]{:S(2)}) async-start(bf16[8,40,7296]{2,1,0:T(8,128)(2,1)} %bitcast.79), calls=%async_computation | async-start | bytes 9338880 | tf_op jit(solution)/shard_map/all_to_all | solution.py:123
  37.0 2.7 collective-permute-start.3
  39.7 0.6 fusion.68
  41.0 82.2 %collective-permute-done.3 = bf16[1,1792,3,128]{3,1,2,0:T(8,128)(2,1)} collective-permute-done((bf16[1,1792,3,128]{3,1,2,0:T(8,128)(2,1)S(1)}, bf16[1,1792,3,128]{3,1,2,0:T(8,128)(2,1)}, u32[]{:S(2)}, u32[]{:S(2)}) %collective-permute-start.3) | collective-permute-done | bytes 1376288 | tf_op jit(solution)/shard_map/ppermute | solution.py:8
  123.2 1.5 broadcast_select_fusion.2
  124.8 3.6 %collective-permute-start.5 = (bf16[1,1792,3,128]{3,1,2,0:T(8,128)(2,1)}, bf16[1,1792,3,128]{3,1,2,0:T(8,128)(2,1)}, u32[]{:S(2)}, u32[]{:S(2)}) collective-permute-start(bf16[1,1792,3,128]{3,1,2,0:T(8,128)(2,1)} %param.13), channel_id=1, source_target_pairs={{0,8},{1,9},{2,10},{3,11},{4,12},{5,13},{6,14},{7,15},{8,0},{9,1},... | collective-permute-start | bytes 4128776 | tf_op jit(solution)/shard_map/ppermute | solution.py:8
  128.8 1.3 slice_bitcast_fusion
  130.1 1.0 convert_reduce_fusion.1
  131.1 2.4 fusion.16
  133.5 2.4 fusion.27
  136.0 2.6 multiply_convert_fusion.5
  138.6 0.8 convolution_convert_fusion.1
  139.4 2.5 fusion.21
  142.0 3.5 %fusion.1 = bf16[3584,1,128]{2,0,1:T(8,128)(2,1)} fusion(bf16[320,128]{1,0:T(8,128)(2,1)S(1)} %get-tuple-element.44, bf16[320,7296]{1,0:T(8,128)(2,1)} %bitcast.5), kind=kOutput, calls=%fused_computation.6 | convolution fusion | flops 294060032 | bytes 3293184 | tf_op jit(solution)/shard_map/dot_general | solution.py:173
  145.6 1.6 pad_maximum_fusion.2
  147.1 71.5 %collective-permute-done.5 = bf16[1,1792,3,128]{3,1,2,0:T(8,128)(2,1)} collective-permute-done((bf16[1,1792,3,128]{3,1,2,0:T(8,128)(2,1)}, bf16[1,1792,3,128]{3,1,2,0:T(8,128)(2,1)}, u32[]{:S(2)}, u32[]{:S(2)}) %collective-permute-start.5) | collective-permute-done | bytes 1376288 | tf_op jit(solution)/shard_map/ppermute | solution.py:8
  218.6 29.2 %collective-permute-done.6 = bf16[1,1792,3,128]{3,1,2,0:T(8,128)(2,1)} collective-permute-done((bf16[1,1792,3,128]{3,1,2,0:T(8,128)(2,1)}, bf16[1,1792,3,128]{3,1,2,0:T(8,128)(2,1)}, u32[]{:S(2)}, u32[]{:S(2)}) %collective-permute-start.6) | collective-permute-done | bytes 1376288 | tf_op jit(solution)/shard_map/ppermute | solution.py:8
  247.9 4.5 %all-to-all-start.1 = ((bf16[8,40,3712]{2,1,0:T(8,128)(2,1)}), bf16[8,40,3712]{2,1,0:T(8,128)(2,1)}, u32[]{:S(2)}, u32[]{:S(2)}) async-start(bf16[8,40,3712]{2,1,0:T(8,128)(2,1)} %bitcast.10), calls=%async_computation.1 | async-start | bytes 4751360 | tf_op jit(solution)/shard_map/all_to_all | solution.py:123
  252.4 2.6 fusion
  255.0 2.8 fusion.2
  258.2 1.2 broadcast_select_fusion
  259.6 0.4 select_reduce_fusion
  260.0 2.9 collective-permute-done.9
  262.9 4.2 %fusion.3 = (bf16[1,1792,3,128]{3,1,2,0:T(8,128)(2,1)}, bf16[1792,3,128]{2,0,1:T(8,128)(2,1)S(1)}) fusion(bf16[1792,3,128]{2,0,1:T(8,128)(2,1)} %collective-permute-done.9, bf16[1,1792,3,128]{3,1,2,0:T(8,128)(2,1)} %collective-permute-done.6, bf16[1,1792,3,128]{3,1,2,0:T(8,128)(2,1)} %param.14, pred[]{:T(512)S(6)} %eq.180, ...), kind=kLoop, calls=%fused_computation.13 | loop fusion | flops 8257536 | bytes 9633794 | tf_op jit(solution)/shard_map/convert_element_type | solution.py:239
  267.0 1.1 copy-done
  268.1 3.7 %fusion.4 = bf16[1,1792,3,128]{3,1,2,0:T(8,128)(2,1)} fusion(bf16[1792,3,128]{2,0,1:T(8,128)(2,1)} %collective-permute-done.9, bf16[1792,3,128]{2,0,1:T(8,128)(2,1)S(1)} %get-tuple-element.35, bf16[1,1792,3,128]{3,1,2,0:T(8,128)(2,1)} %collective-permute-done.5, bf16[1,1792,3,128]{3,1,2,0:T(8,128)(2,1)S(1)} %copy-done.4, pred[]{:T(512)S(6)} %eq.180), kind=kLoop, calls=%fused_computation.15 | loop fusion | flops 6193152 | bytes 6881281 | tf_op jit(solution)/shard_map/convert_element_type | solution.py:238
  271.8 11.8 %all-to-all-done.1 = bf16[8,40,3712]{2,1,0:T(8,128)(2,1)} async-done(((bf16[8,40,3712]{2,1,0:T(8,128)(2,1)}), bf16[8,40,3712]{2,1,0:T(8,128)(2,1)}, u32[]{:S(2)}, u32[]{:S(2)}) %all-to-all-start.1) | async-done | bytes 2375712 | tf_op jit(solution)/shard_map/all_to_all | solution.py:123
  283.7 1.0 convert_reduce_fusion
  284.7 3.1 %fusion.5 = f32[64,3584]{1,0:T(8,128)S(1)} fusion(f32[320,64]{0,1:T(8,128)S(1)} %select_reduce_fusion, bf16[320,3712]{1,0:T(8,128)(2,1)} %bitcast.11), kind=kOutput, calls=%fused_computation.19 | convolution fusion | flops 880803840 | bytes 3293184 | tf_op jit(solution)/shard_map/dot_general | solution.py:199
  287.8 3.5 %collective-permute-start.7 = (bf16[32,3584]{1,0:T(8,128)(2,1)S(1)}, bf16[32,3584]{1,0:T(8,128)(2,1)S(1)}, u32[]{:S(2)}, u32[]{:S(2)}) collective-permute-start(bf16[32,3584]{1,0:T(8,128)(2,1)S(1)} %slice.136), channel_id=1, source_target_pairs={{0,8},{1,9},{2,10},{3,11},{4,12},{5,13},{6,14},{7,15},{8,0},{9,1},... | collective-permute-start | bytes 688136 | tf_op jit(solution)/shard_map/ppermute | solution.py:8
  291.5 3.2 %multiply_bitcast_fusion = f32[1,1792,3,128]{3,1,2,0:T(8,128)} fusion(bf16[1792,3,128]{2,0,1:T(8,128)(2,1)} %collective-permute-done.9, bf16[1792,3,128]{2,0,1:T(8,128)(2,1)S(1)} %copy-done.1), kind=kLoop, calls=%fused_computation.17 | loop fusion | flops 2752512 | bytes 5505024 | tf_op jit(solution)/shard_map/broadcast_in_dim | solution.py:189
  294.7 6.2 %collective-permute-done.8 = bf16[256]{0:T(256)(128)(2,1)S(1)} collective-permute-done((bf16[256]{0:T(256)(128)(2,1)S(1)}, bf16[256]{0:T(256)(128)(2,1)S(1)}, u32[]{:S(2)}, u32[]{:S(2)}) %collective-permute-start.8) | collective-permute-done | bytes 544 | tf_op jit(solution)/shard_map/ppermute | solution.py:8
  301.0 0.7 copy.52
  301.7 0.7 fusion.31
  (77 shorter events, 4.0 us)
Async XLA Ops:
  0.6 13.0 %collective-permute-start.1 = (f32[32,8]{0,1:T(8,128)}, f32[32,8]{0,1:T(8,128)S(1)}, u32[]{:S(2)}, u32[]{:S(2)}) collective-permute-start(f32[32,8]{0,1:T(8,128)} %param.11), channel_id=1, source_target_pairs={{0,8},{1,9},{2,10},{3,11},{4,12},{5,13},{6,14},{7,15},{8,0},{9,1},... | collective-permute-start | bytes 3080 | tf_op jit(solution)/shard_map/ppermute | solution.py:8
  3.3 7.8 %collective-permute-start = (s32[32,8]{0,1:T(8,128)}, s32[32,8]{0,1:T(8,128)S(1)}, u32[]{:S(2)}, u32[]{:S(2)}) collective-permute-start(s32[32,8]{0,1:T(8,128)} %param.10), channel_id=1, source_target_pairs={{0,8},{1,9},{2,10},{3,11},{4,12},{5,13},{6,14},{7,15},{8,0},{9,1},... | collective-permute-start | bytes 3080 | tf_op jit(solution)/shard_map/ppermute | solution.py:8
  5.5 22.6 %collective-permute-start.2 = (bf16[32,7168]{1,0:T(8,128)(2,1)S(1)}, bf16[32,7168]{1,0:T(8,128)(2,1)S(1)}, u32[]{:S(2)}, u32[]{:S(2)}) collective-permute-start(bf16[32,7168]{1,0:T(8,128)(2,1)S(1)} %constant_dynamic-update-slice_fusion.1), channel_id=1, source_target_pairs={{0,8},{1,9},{2,10},{3,11},{4,12},{5,13},{6,14},{7,15},{8,0},{9,1},... | collective-permute-start | bytes 1376264 | tf_op jit(solution)/shard_map/ppermute | solution.py:8
  32.0 5.1 %copy-start.3 = (bf16[1,1792,3,128]{3,1,2,0:T(8,128)(2,1)S(1)}, bf16[1,1792,3,128]{3,1,2,0:T(8,128)(2,1)}, u32[]{:S(2)}) copy-start(bf16[1,1792,3,128]{3,1,2,0:T(8,128)(2,1)} %param.12) | copy-start | bytes 4128772
  32.0 7.8 %copy-start.9 = (s32[8]{0:T(128)S(1)}, s32[8]{0:T(128)}, u32[]{:S(2)}) copy-start(s32[8]{0:T(128)} %param.15) | copy-start | bytes 100
  32.0 98.2 %all-to-all-start = ((bf16[8,40,7296]{2,1,0:T(8,128)(2,1)}), bf16[8,40,7296]{2,1,0:T(8,128)(2,1)}, u32[]{:S(2)}, u32[]{:S(2)}) async-start(bf16[8,40,7296]{2,1,0:T(8,128)(2,1)} %bitcast.79), calls=%async_computation | async-start | bytes 9338880 | tf_op jit(solution)/shard_map/all_to_all | solution.py:123
  37.0 86.1 %collective-permute-start.3 = (bf16[1,1792,3,128]{3,1,2,0:T(8,128)(2,1)S(1)}, bf16[1,1792,3,128]{3,1,2,0:T(8,128)(2,1)}, u32[]{:S(2)}, u32[]{:S(2)}) collective-permute-start(bf16[1,1792,3,128]{3,1,2,0:T(8,128)(2,1)S(1)} %copy-done.3), channel_id=1, source_target_pairs={{0,8},{1,9},{2,10},{3,11},{4,12},{5,13},{6,14},{7,15},{8,0},{9,1},... | collective-permute-start | bytes 4128776 | tf_op jit(solution)/shard_map/ppermute | solution.py:8
  124.7 3.9 %copy-start.2 = (bf16[1,1792,3,128]{3,1,2,0:T(8,128)(2,1)}, bf16[1,1792,3,128]{3,1,2,0:T(8,128)(2,1)S(1)}, u32[]{:S(2)}) copy-start(bf16[1,1792,3,128]{3,1,2,0:T(8,128)(2,1)S(1)} %broadcast_select_fusion.2) | copy-start | bytes 4128772
  124.7 3.7 %collective-permute-start.4 = (bf16[1,1792,3,128]{3,1,2,0:T(8,128)(2,1)S(1)}, bf16[1,1792,3,128]{3,1,2,0:T(8,128)(2,1)S(1)}, u32[]{:S(2)}, u32[]{:S(2)}) collective-permute-start(bf16[1,1792,3,128]{3,1,2,0:T(8,128)(2,1)S(1)} %broadcast_select_fusion.2), channel_id=1, source_target_pairs={{0,16},{16,0},{1,17},{17,1},{2,18},{18,2},{3,19},{19,3},{4,20},{20... | collective-permute-start | bytes 4128776 | tf_op jit(solution)/shard_map/ppermute | solution.py:143
  124.8 93.9 %collective-permute-start.5 = (bf16[1,1792,3,128]{3,1,2,0:T(8,128)(2,1)}, bf16[1,1792,3,128]{3,1,2,0:T(8,128)(2,1)}, u32[]{:S(2)}, u32[]{:S(2)}) collective-permute-start(bf16[1,1792,3,128]{3,1,2,0:T(8,128)(2,1)} %param.13), channel_id=1, source_target_pairs={{0,8},{1,9},{2,10},{3,11},{4,12},{5,13},{6,14},{7,15},{8,0},{9,1},... | collective-permute-start | bytes 4128776 | tf_op jit(solution)/shard_map/ppermute | solution.py:8
  128.3 119.6 %collective-permute-start.6 = (bf16[1,1792,3,128]{3,1,2,0:T(8,128)(2,1)}, bf16[1,1792,3,128]{3,1,2,0:T(8,128)(2,1)}, u32[]{:S(2)}, u32[]{:S(2)}) collective-permute-start(bf16[1,1792,3,128]{3,1,2,0:T(8,128)(2,1)} %param.14), channel_id=1, source_target_pairs={{0,8},{1,9},{2,10},{3,11},{4,12},{5,13},{6,14},{7,15},{8,0},{9,1},... | collective-permute-start | bytes 4128776 | tf_op jit(solution)/shard_map/ppermute | solution.py:8
  136.0 2.6 copy-start.5
  136.0 2.6 copy-start.6
  247.9 35.8 %all-to-all-start.1 = ((bf16[8,40,3712]{2,1,0:T(8,128)(2,1)}), bf16[8,40,3712]{2,1,0:T(8,128)(2,1)}, u32[]{:S(2)}, u32[]{:S(2)}) async-start(bf16[8,40,3712]{2,1,0:T(8,128)(2,1)} %bitcast.10), calls=%async_computation.1 | async-start | bytes 4751360 | tf_op jit(solution)/shard_map/all_to_all | solution.py:123
  255.0 2.8 copy-start.7
  258.2 1.2 copy-start.8
  259.4 3.5 %collective-permute-start.9 = (bf16[1792,3,128]{2,0,1:T(8,128)(2,1)}, bf16[1792,3,128]{2,0,1:T(8,128)(2,1)}, u32[]{:S(2)}, u32[]{:S(2)}) collective-permute-start(bf16[1792,3,128]{2,0,1:T(8,128)(2,1)} %broadcast_select_fusion), channel_id=1, source_target_pairs={{0,16},{16,0},{1,17},{17,1},{2,18},{18,2},{3,19},{19,3},{4,20},{20... | collective-permute-start | bytes 4128776 | tf_op jit(solution)/shard_map/ppermute | solution.py:183
  260.0 8.2 %copy-start.4 = (bf16[1,1792,3,128]{3,1,2,0:T(8,128)(2,1)S(1)}, bf16[1,1792,3,128]{3,1,2,0:T(8,128)(2,1)}, u32[]{:S(2)}) copy-start(bf16[1,1792,3,128]{3,1,2,0:T(8,128)(2,1)} %param.13) | copy-start | bytes 4128772
  267.0 1.1 copy-start
  271.8 19.7 %copy-start.1 = (bf16[1792,3,128]{2,0,1:T(8,128)(2,1)S(1)}, bf16[1792,3,128]{2,0,1:T(8,128)(2,1)}, u32[]{:S(2)}) copy-start(bf16[1792,3,128]{2,0,1:T(8,128)(2,1)} %copy-done) | copy-start | bytes 4128772
  287.8 14.0 %collective-permute-start.7 = (bf16[32,3584]{1,0:T(8,128)(2,1)S(1)}, bf16[32,3584]{1,0:T(8,128)(2,1)S(1)}, u32[]{:S(2)}, u32[]{:S(2)}) collective-permute-start(bf16[32,3584]{1,0:T(8,128)(2,1)S(1)} %slice.136), channel_id=1, source_target_pairs={{0,8},{1,9},{2,10},{3,11},{4,12},{5,13},{6,14},{7,15},{8,0},{9,1},... | collective-permute-start | bytes 688136 | tf_op jit(solution)/shard_map/ppermute | solution.py:8
  291.4 9.5 %collective-permute-start.8 = (bf16[256]{0:T(256)(128)(2,1)S(1)}, bf16[256]{0:T(256)(128)(2,1)S(1)}, u32[]{:S(2)}, u32[]{:S(2)}) collective-permute-start(bf16[256]{0:T(256)(128)(2,1)S(1)} %slice.77), channel_id=1, source_target_pairs={{0,8},{1,9},{2,10},{3,11},{4,12},{5,13},{6,14},{7,15},{8,0},{9,1},... | collective-permute-start | bytes 1544 | tf_op jit(solution)/shard_map/ppermute | solution.py:8

commit v19 on v8

--- a/solution.py
+++ b/solution.py
@@ -208,11 +208,20 @@
             preferred_element_type=jnp.float32,
         )
         prob2 = jnp.sum(jnp.where(slot_hit, back_gate[:, None], 0.0), axis=0)
-        p_partial, p_prob = from_partner(
-            (partial[tok_rows:].astype(jnp.bfloat16), prob2[entry_count:].astype(jnp.bfloat16)),
+        prob_tile = jnp.concatenate(
+            [
+                prob2[entry_count:].reshape(tok_rows, route_count),
+                jnp.zeros((tok_rows, 128 - route_count), jnp.float32),
+            ],
+            axis=1,
+        )
+        p_back = from_partner(
+            jnp.concatenate([partial[tok_rows:], prob_tile], axis=1).astype(jnp.bfloat16),
             "expert",
             swap_bit,
         )
+        p_partial = p_back[:, :model_width]
+        p_prob = p_back[:, model_width : model_width + route_count].reshape(-1)
         token_grad = (partial[:tok_rows] + p_partial.astype(jnp.float32)).astype(jnp.bfloat16)
         prob_grad = jnp.where(
             in_half[:entry_count], prob2[:entry_count], p_prob.astype(jnp.float32)

time: 271 us -> 271 us (level)
  starting transfers between devices: 28.5 us -> 25.5 us
  waiting for transfers between devices: 183 us -> 186 us
    ppermute x8 -> x7, starting transfers between devices: 14.9 us -> 11.9 us  [from_partner(): lax.ppermute(value, axis, [(i, i ^ 1 << bit) for i in range(lax.axis_size...]
    ppermute x8 -> x7, waiting for transfers between devices: 183 us -> 186 us  [from_partner(): lax.ppermute(value, axis, [(i, i ^ 1 << bit) for i in range(lax.axis_size...]
  transfers between devices with their start and end apart: 12 -> 11, of which waited for: 5 -> 5; matrix products, arithmetic and copies ran while one was open for 18% -> 18% of each run, Pallas kernels for 0% -> 0%
where the time goes in v19:
time: 271 us
  waiting for transfers between devices  186 us (69%)
  other arithmetic  27.3 us (10%)
  starting transfers between devices  25.5 us (9%)
  matrix products  24.1 us (9%)
  local copies, waits for them, and re-layouts  6.85 us (3%)
    ppermute x7, waiting for transfers between devices, from_partner(): lax.ppermute(value, axis, [(i, i ^ 1 << bit) for i in range(lax.axis_size...  186 us
    all_to_all x2, starting transfers between devices, spread(): lax.all_to_all(parts, 'expert', 0, 0, tiled=True, axis_index_groups=halves)  13.5 us
    ppermute x7, starting transfers between devices, from_partner(): lax.ppermute(value, axis, [(i, i ^ 1 << bit) for i in range(lax.axis_size...  11.9 us
  transfers between devices with their start and end apart: 11, of which 5 were waited for; matrix products, arithmetic and copies ran while one was open for 18% of the time, Pallas kernels for 0%

profile of v19, /device:TPU:6, one launch (start us, length us, event | category | flops | bytes accessed | tf_op | source)
XLA Modules:
  0.0 271.2 jit_solution(3281428443787925820)
XLA Ops:
  0.6 2.7 collective-permute-start.1
  3.3 0.3 collective-permute-start
  3.6 1.0 constant_dynamic-update-slice_fusion.2
  4.6 1.0 constant_dynamic-update-slice_fusion.1
  5.5 2.7 collective-permute-start.2
  8.2 0.8 copy.56
  9.3 0.6 reduce-window.14
  10.2 0.7 convert.33
  11.5 0.6 reduce-window.16
  12.5 0.7 select_reduce_fusion.3
  13.5 0.8 pad_add_fusion
  14.7 0.2 select_reduce_fusion.2
  14.9 0.4 fusion.29
  15.4 12.7 %collective-permute-done.2 = bf16[32,7168]{1,0:T(8,128)(2,1)S(1)} collective-permute-done((bf16[32,7168]{1,0:T(8,128)(2,1)S(1)}, bf16[32,7168]{1,0:T(8,128)(2,1)S(1)}, u32[]{:S(2)}, u32[]{:S(2)}) %collective-permute-start.2) | collective-permute-done | bytes 458784 | tf_op jit(solution)/shard_map/ppermute | solution.py:8
  28.1 1.4 convolution_convert_fusion
  29.5 2.5 pad_maximum_fusion
  32.0 5.1 %all-to-all-start = ((bf16[8,40,7296]{2,1,0:T(8,128)(2,1)}), bf16[8,40,7296]{2,1,0:T(8,128)(2,1)}, u32[]{:S(2)}, u32[]{:S(2)}) async-start(bf16[8,40,7296]{2,1,0:T(8,128)(2,1)} %bitcast.79), calls=%async_computation | async-start | bytes 9338880 | tf_op jit(solution)/shard_map/all_to_all | solution.py:123
  37.0 2.7 collective-permute-start.3
  39.7 0.6 fusion.74
  41.0 82.2 %collective-permute-done.3 = bf16[1,1792,3,128]{3,1,2,0:T(8,128)(2,1)} collective-permute-done((bf16[1,1792,3,128]{3,1,2,0:T(8,128)(2,1)S(1)}, bf16[1,1792,3,128]{3,1,2,0:T(8,128)(2,1)}, u32[]{:S(2)}, u32[]{:S(2)}) %collective-permute-start.3) | collective-permute-done | bytes 1376288 | tf_op jit(solution)/shard_map/ppermute | solution.py:8
  123.2 1.5 broadcast_select_fusion.2
  124.8 3.6 %collective-permute-start.8 = (bf16[1,1792,3,128]{3,1,2,0:T(8,128)(2,1)}, bf16[1,1792,3,128]{3,1,2,0:T(8,128)(2,1)}, u32[]{:S(2)}, u32[]{:S(2)}) collective-permute-start(bf16[1,1792,3,128]{3,1,2,0:T(8,128)(2,1)} %param.14), channel_id=1, source_target_pairs={{0,8},{1,9},{2,10},{3,11},{4,12},{5,13},{6,14},{7,15},{8,0},{9,1},... | collective-permute-start | bytes 4128776 | tf_op jit(solution)/shard_map/ppermute | solution.py:8
  128.7 1.3 slice_bitcast_fusion
  130.0 1.0 convert_reduce_fusion.1
  131.0 2.4 fusion.16
  133.4 2.4 fusion.27
  135.9 2.4 multiply_convert_fusion.5
  138.3 2.5 fusion.21
  141.0 3.6 %fusion.1 = bf16[3584,1,128]{2,0,1:T(8,128)(2,1)} fusion(bf16[320,128]{1,0:T(8,128)(2,1)S(1)} %get-tuple-element.52, bf16[320,7296]{1,0:T(8,128)(2,1)} %bitcast.5), kind=kOutput, calls=%fused_computation.6 | convolution fusion | flops 294060032 | bytes 3293184 | tf_op jit(solution)/shard_map/dot_general | solution.py:173
  144.6 0.8 convolution_convert_fusion.1
  145.4 1.6 pad_maximum_fusion.2
  147.0 8.5 %all-to-all-start.1 = ((bf16[8,40,3712]{2,1,0:T(8,128)(2,1)}), bf16[8,40,3712]{2,1,0:T(8,128)(2,1)}, u32[]{:S(2)}, u32[]{:S(2)}) async-start(bf16[8,40,3712]{2,1,0:T(8,128)(2,1)} %bitcast.10), calls=%async_computation.1 | async-start | bytes 4751360 | tf_op jit(solution)/shard_map/all_to_all | solution.py:123
  155.4 2.6 fusion
  158.0 2.8 %fusion.2 = bf16[3584,1,128]{2,0,1:T(8,128)(2,1)S(1)} fusion(bf16[320,128]{1,0:T(8,128)(2,1)S(1)} %get-tuple-element.51, f32[320]{0:T(512)S(1)} %convert_reduce_fusion.1, bf16[320,7296]{1,0:T(8,128)(2,1)} %bitcast.5), kind=kOutput, calls=%fused_computation.7 | convolution fusion | flops 297500672 | bytes 3294464 | tf_op jit(solution)/shard_map/dot_general | solution.py:174
  160.9 0.3 pad_maximum_fusion.1
  161.2 1.2 broadcast_select_fusion
  162.6 0.4 select_reduce_fusion
  163.0 55.7 %collective-permute-done.8 = bf16[1,1792,3,128]{3,1,2,0:T(8,128)(2,1)} collective-permute-done((bf16[1,1792,3,128]{3,1,2,0:T(8,128)(2,1)}, bf16[1,1792,3,128]{3,1,2,0:T(8,128)(2,1)}, u32[]{:S(2)}, u32[]{:S(2)}) %collective-permute-start.8) | collective-permute-done | bytes 1376288 | tf_op jit(solution)/shard_map/ppermute | solution.py:8
  218.7 4.2 %fusion.3 = (bf16[1,1792,3,128]{3,1,2,0:T(8,128)(2,1)}, bf16[1792,3,128]{2,0,1:T(8,128)(2,1)S(1)}) fusion(bf16[1792,3,128]{2,0,1:T(8,128)(2,1)} %collective-permute-done.6, bf16[1,1792,3,128]{3,1,2,0:T(8,128)(2,1)} %collective-permute-done.8, bf16[1,1792,3,128]{3,1,2,0:T(8,128)(2,1)} %param.14, pred[]{:T(512)S(6)} %eq.184, ...), kind=kLoop, calls=%fused_computation.13 | loop fusion | flops 8257536 | bytes 9633794 | tf_op jit(solution)/shard_map/convert_element_type | solution.py:193
  222.9 25.1 %collective-permute-done.7 = bf16[1,1792,3,128]{3,1,2,0:T(8,128)(2,1)} collective-permute-done((bf16[1,1792,3,128]{3,1,2,0:T(8,128)(2,1)}, bf16[1,1792,3,128]{3,1,2,0:T(8,128)(2,1)}, u32[]{:S(2)}, u32[]{:S(2)}) %collective-permute-start.7) | collective-permute-done | bytes 1376288 | tf_op jit(solution)/shard_map/ppermute | solution.py:8
  247.9 3.7 %fusion.4 = bf16[1,1792,3,128]{3,1,2,0:T(8,128)(2,1)} fusion(bf16[1792,3,128]{2,0,1:T(8,128)(2,1)} %collective-permute-done.6, bf16[1792,3,128]{2,0,1:T(8,128)(2,1)S(1)} %get-tuple-element.41, bf16[1,1792,3,128]{3,1,2,0:T(8,128)(2,1)} %collective-permute-done.7, bf16[1,1792,3,128]{3,1,2,0:T(8,128)(2,1)} %param.13, pred[]{:T(512)S(6)} %eq.184), kind=kLoop, calls=%fused_computation.15 | loop fusion | flops 6193152 | bytes 6881281 | tf_op jit(solution)/shard_map/convert_element_type | solution.py:192
  251.6 1.1 convert_reduce_fusion
  252.8 3.1 %fusion.5 = f32[64,3584]{1,0:T(8,128)S(1)} fusion(f32[320,64]{0,1:T(8,128)S(1)} %select_reduce_fusion, bf16[320,3712]{1,0:T(8,128)(2,1)} %bitcast.11), kind=kOutput, calls=%fused_computation.19 | convolution fusion | flops 880803840 | bytes 3293184 | tf_op jit(solution)/shard_map/dot_general | solution.py:203
  255.9 0.2 select_reduce_fusion.1
  256.3 3.2 %multiply_bitcast_fusion = f32[1,1792,3,128]{3,1,2,0:T(8,128)} fusion(bf16[1792,3,128]{2,0,1:T(8,128)(2,1)} %collective-permute-done.6, bf16[1792,3,128]{2,0,1:T(8,128)(2,1)S(1)} %copy-done.1), kind=kLoop, calls=%fused_computation.17 | loop fusion | flops 2752512 | bytes 5505024 | tf_op jit(solution)/shard_map/broadcast_in_dim | solution.py:189
  259.7 10.2 %collective-permute-done.5 = bf16[32,3712]{1,0:T(8,128)(2,1)S(1)} collective-permute-done((bf16[32,3712]{1,0:T(8,128)(2,1)S(1)}, bf16[32,3712]{1,0:T(8,128)(2,1)S(1)}, u32[]{:S(2)}, u32[]{:S(2)}) %collective-permute-start.5) | collective-permute-done | bytes 237600 | tf_op jit(solution)/shard_map/ppermute | solution.py:8
  269.8 0.7 copy.69
  270.5 0.7 fusion.31
  (79 shorter events, 3.5 us)
Async XLA Ops:
  0.6 13.9 %collective-permute-start.1 = (f32[32,8]{0,1:T(8,128)}, f32[32,8]{0,1:T(8,128)S(1)}, u32[]{:S(2)}, u32[]{:S(2)}) collective-permute-start(f32[32,8]{0,1:T(8,128)} %param.11), channel_id=1, source_target_pairs={{0,8},{1,9},{2,10},{3,11},{4,12},{5,13},{6,14},{7,15},{8,0},{9,1},... | collective-permute-start | bytes 3080 | tf_op jit(solution)/shard_map/ppermute | solution.py:8
  3.3 7.8 %collective-permute-start = (s32[32,8]{0,1:T(8,128)}, s32[32,8]{0,1:T(8,128)S(1)}, u32[]{:S(2)}, u32[]{:S(2)}) collective-permute-start(s32[32,8]{0,1:T(8,128)} %param.10), channel_id=1, source_target_pairs={{0,8},{1,9},{2,10},{3,11},{4,12},{5,13},{6,14},{7,15},{8,0},{9,1},... | collective-permute-start | bytes 3080 | tf_op jit(solution)/shard_map/ppermute | solution.py:8
  5.5 22.6 %collective-permute-start.2 = (bf16[32,7168]{1,0:T(8,128)(2,1)S(1)}, bf16[32,7168]{1,0:T(8,128)(2,1)S(1)}, u32[]{:S(2)}, u32[]{:S(2)}) collective-permute-start(bf16[32,7168]{1,0:T(8,128)(2,1)S(1)} %constant_dynamic-update-slice_fusion.1), channel_id=1, source_target_pairs={{0,8},{1,9},{2,10},{3,11},{4,12},{5,13},{6,14},{7,15},{8,0},{9,1},... | collective-permute-start | bytes 1376264 | tf_op jit(solution)/shard_map/ppermute | solution.py:8
  32.0 5.1 %copy-start.3 = (bf16[1,1792,3,128]{3,1,2,0:T(8,128)(2,1)S(1)}, bf16[1,1792,3,128]{3,1,2,0:T(8,128)(2,1)}, u32[]{:S(2)}) copy-start(bf16[1,1792,3,128]{3,1,2,0:T(8,128)(2,1)} %param.12) | copy-start | bytes 4128772
  32.0 7.8 %copy-start.8 = (s32[8]{0:T(128)S(1)}, s32[8]{0:T(128)}, u32[]{:S(2)}) copy-start(s32[8]{0:T(128)} %param.15) | copy-start | bytes 100
  32.0 98.1 %all-to-all-start = ((bf16[8,40,7296]{2,1,0:T(8,128)(2,1)}), bf16[8,40,7296]{2,1,0:T(8,128)(2,1)}, u32[]{:S(2)}, u32[]{:S(2)}) async-start(bf16[8,40,7296]{2,1,0:T(8,128)(2,1)} %bitcast.79), calls=%async_computation | async-start | bytes 9338880 | tf_op jit(solution)/shard_map/all_to_all | solution.py:123
  37.0 86.1 %collective-permute-start.3 = (bf16[1,1792,3,128]{3,1,2,0:T(8,128)(2,1)S(1)}, bf16[1,1792,3,128]{3,1,2,0:T(8,128)(2,1)}, u32[]{:S(2)}, u32[]{:S(2)}) collective-permute-start(bf16[1,1792,3,128]{3,1,2,0:T(8,128)(2,1)S(1)} %copy-done.3), channel_id=1, source_target_pairs={{0,8},{1,9},{2,10},{3,11},{4,12},{5,13},{6,14},{7,15},{8,0},{9,1},... | collective-permute-start | bytes 4128776 | tf_op jit(solution)/shard_map/ppermute | solution.py:8
  124.7 3.8 %copy-start.2 = (bf16[1,1792,3,128]{3,1,2,0:T(8,128)(2,1)}, bf16[1,1792,3,128]{3,1,2,0:T(8,128)(2,1)S(1)}, u32[]{:S(2)}) copy-start(bf16[1,1792,3,128]{3,1,2,0:T(8,128)(2,1)S(1)} %broadcast_select_fusion.2) | copy-start | bytes 4128772
  124.7 3.6 %collective-permute-start.4 = (bf16[1,1792,3,128]{3,1,2,0:T(8,128)(2,1)S(1)}, bf16[1,1792,3,128]{3,1,2,0:T(8,128)(2,1)S(1)}, u32[]{:S(2)}, u32[]{:S(2)}) collective-permute-start(bf16[1,1792,3,128]{3,1,2,0:T(8,128)(2,1)S(1)} %broadcast_select_fusion.2), channel_id=1, source_target_pairs={{0,16},{16,0},{1,17},{17,1},{2,18},{18,2},{3,19},{19,3},{4,20},{20... | collective-permute-start | bytes 4128776 | tf_op jit(solution)/shard_map/ppermute | solution.py:143
  124.8 93.9 %collective-permute-start.8 = (bf16[1,1792,3,128]{3,1,2,0:T(8,128)(2,1)}, bf16[1,1792,3,128]{3,1,2,0:T(8,128)(2,1)}, u32[]{:S(2)}, u32[]{:S(2)}) collective-permute-start(bf16[1,1792,3,128]{3,1,2,0:T(8,128)(2,1)} %param.14), channel_id=1, source_target_pairs={{0,8},{1,9},{2,10},{3,11},{4,12},{5,13},{6,14},{7,15},{8,0},{9,1},... | collective-permute-start | bytes 4128776 | tf_op jit(solution)/shard_map/ppermute | solution.py:8
  140.8 3.8 %copy-start.4 = (bf16[3584,128]{1,0:T(8,128)(2,1)S(1)}, bf16[3584,128]{1,0:T(8,128)(2,1)}, u32[]{:S(2)}) copy-start(bf16[3584,128]{1,0:T(8,128)(2,1)} %get-tuple-element.46) | copy-start | bytes 2752516
  140.8 3.8 %copy-start.5 = (bf16[3584,128]{1,0:T(8,128)(2,1)S(1)}, bf16[3584,128]{1,0:T(8,128)(2,1)}, u32[]{:S(2)}) copy-start(bf16[3584,128]{1,0:T(8,128)(2,1)} %get-tuple-element.47) | copy-start | bytes 2752516
  147.0 104.7 %all-to-all-start.1 = ((bf16[8,40,3712]{2,1,0:T(8,128)(2,1)}), bf16[8,40,3712]{2,1,0:T(8,128)(2,1)}, u32[]{:S(2)}, u32[]{:S(2)}) async-start(bf16[8,40,3712]{2,1,0:T(8,128)(2,1)} %bitcast.10), calls=%async_computation.1 | async-start | bytes 4751360 | tf_op jit(solution)/shard_map/all_to_all | solution.py:123
  158.0 2.8 %copy-start.6 = (bf16[3584,1,128]{2,0,1:T(8,128)(2,1)S(1)}, bf16[3584,1,128]{2,0,1:T(8,128)(2,1)}, u32[]{:S(2)}) copy-start(bf16[3584,1,128]{2,0,1:T(8,128)(2,1)} %fusion.1) | copy-start | bytes 2752516
  161.2 1.2 copy-start.7
  162.4 56.3 %collective-permute-start.6 = (bf16[1792,3,128]{2,0,1:T(8,128)(2,1)}, bf16[1792,3,128]{2,0,1:T(8,128)(2,1)}, u32[]{:S(2)}, u32[]{:S(2)}) collective-permute-start(bf16[1792,3,128]{2,0,1:T(8,128)(2,1)} %broadcast_select_fusion), channel_id=1, source_target_pairs={{0,16},{16,0},{1,17},{17,1},{2,18},{18,2},{3,19},{19,3},{4,20},{20... | collective-permute-start | bytes 4128776 | tf_op jit(solution)/shard_map/ppermute | solution.py:183
  162.4 85.5 %collective-permute-start.7 = (bf16[1,1792,3,128]{3,1,2,0:T(8,128)(2,1)}, bf16[1,1792,3,128]{3,1,2,0:T(8,128)(2,1)}, u32[]{:S(2)}, u32[]{:S(2)}) collective-permute-start(bf16[1,1792,3,128]{3,1,2,0:T(8,128)(2,1)} %param.13), channel_id=1, source_target_pairs={{0,8},{1,9},{2,10},{3,11},{4,12},{5,13},{6,14},{7,15},{8,0},{9,1},... | collective-permute-start | bytes 4128776 | tf_op jit(solution)/shard_map/ppermute | solution.py:8
  222.9 25.1 %copy-start = (bf16[1792,3,128]{2,0,1:T(8,128)(2,1)}, bf16[1792,3,128]{2,0,1:T(8,128)(2,1)S(1)}, u32[]{:S(2)}) copy-start(bf16[1792,3,128]{2,0,1:T(8,128)(2,1)S(1)} %get-tuple-element.41) | copy-start | bytes 4128772
  251.6 4.7 %copy-start.1 = (bf16[1792,3,128]{2,0,1:T(8,128)(2,1)S(1)}, bf16[1792,3,128]{2,0,1:T(8,128)(2,1)}, u32[]{:S(2)}) copy-start(bf16[1792,3,128]{2,0,1:T(8,128)(2,1)} %copy-done) | copy-start | bytes 4128772
  256.3 13.6 %collective-permute-start.5 = (bf16[32,3712]{1,0:T(8,128)(2,1)S(1)}, bf16[32,3712]{1,0:T(8,128)(2,1)S(1)}, u32[]{:S(2)}, u32[]{:S(2)}) collective-permute-start(bf16[32,3712]{1,0:T(8,128)(2,1)S(1)} %concatenate.118), channel_id=1, source_target_pairs={{0,8},{1,9},{2,10},{3,11},{4,12},{5,13},{6,14},{7,15},{8,0},{9,1},... | collective-permute-start | bytes 712712 | tf_op jit(solution)/shard_map/ppermute | solution.py:8

commit v20 on v8

--- a/solution.py
+++ b/solution.py
@@ -89,9 +89,12 @@
     two_stage = half_axis <= 8
     if two_stage:
         packed = jnp.concatenate([tokens, out_grad], axis=1)
-        p_packed, p_ids, p_gate, their_weights = from_partner(
-            (packed, expert_ids, gate_probs, weights), "expert", swap_bit
-        )
+        small = jnp.concatenate([expert_ids.astype(jnp.float32), gate_probs], axis=1)
+        p_packed, p_small, their_weights = from_partner(
+            (packed, small, weights), "expert", swap_bit
+        )
+        p_ids = p_small[:, :route_count].astype(jnp.int32)
+        p_gate = p_small[:, route_count:]
         both = jnp.concatenate([packed, p_packed], axis=0)
         ids2 = jnp.concatenate([flat_ids, p_ids.reshape(-1)])
         gate2 = jnp.concatenate([flat_gate, p_gate.reshape(-1)])

time: 271 us -> 272 us (level)
  waiting for transfers between devices: 183 us -> 189 us
  starting transfers between devices: 28.5 us -> 23 us
    ppermute x8 -> x7, waiting for transfers between devices: 183 us -> 189 us  [from_partner(): lax.ppermute(value, axis, [(i, i ^ 1 << bit) for i in range(lax.axis_size...]
    ppermute x8 -> x7, starting transfers between devices: 14.9 us -> 10.1 us  [from_partner(): lax.ppermute(value, axis, [(i, i ^ 1 << bit) for i in range(lax.axis_size...]
  transfers between devices with their start and end apart: 12 -> 11, of which waited for: 5 -> 5; matrix products, arithmetic and copies ran while one was open for 18% -> 17% of each run, Pallas kernels for 0% -> 0%
where the time goes in v20:
time: 272 us; the launch traced here: 270 us
  waiting for transfers between devices  189 us (69%)
  other arithmetic  26.6 us (10%)
  matrix products  24 us (9%)
  starting transfers between devices  23 us (8%)
  local copies, waits for them, and re-layouts  6.59 us (2%)
    ppermute x7, waiting for transfers between devices, from_partner(): lax.ppermute(value, axis, [(i, i ^ 1 << bit) for i in range(lax.axis_size...  189 us
    all_to_all x2, starting transfers between devices, spread(): lax.all_to_all(parts, 'expert', 0, 0, tiled=True, axis_index_groups=halves)  12.8 us
    ppermute x7, starting transfers between devices, from_partner(): lax.ppermute(value, axis, [(i, i ^ 1 << bit) for i in range(lax.axis_size...  10.1 us
  transfers between devices with their start and end apart: 11, of which 5 were waited for; matrix products, arithmetic and copies ran while one was open for 17% of the time, Pallas kernels for 0%

profile of v20, /device:TPU:6, one launch (start us, length us, event | category | flops | bytes accessed | tf_op | source)
XLA Modules:
  0.0 270.4 jit_solution(17077112532469983507)
XLA Ops:
  0.6 0.7 convert_element_type.109
  1.3 0.7 pad_maximum_fusion.3
  2.0 2.6 collective-permute-start
  4.6 1.0 constant_dynamic-update-slice_fusion.2
  5.6 1.0 constant_dynamic-update-slice_fusion.1
  6.5 0.4 collective-permute-start.1
  6.9 0.8 copy.41
  7.9 0.6 reduce-window.14
  8.9 0.7 convert.28
  10.2 0.6 reduce-window.16
  11.1 0.7 select_reduce_fusion.3
  12.6 0.2 select_reduce_fusion.2
  12.8 0.4 fusion.29
  13.3 16.0 %collective-permute-done.1 = bf16[32,7168]{1,0:T(8,128)(2,1)S(1)} collective-permute-done((bf16[32,7168]{1,0:T(8,128)(2,1)S(1)}, bf16[32,7168]{1,0:T(8,128)(2,1)S(1)}, u32[]{:S(2)}, u32[]{:S(2)}) %collective-permute-start.1) | collective-permute-done | bytes 458784 | tf_op jit(solution)/shard_map/ppermute | solution.py:8
  29.3 1.4 convolution_convert_fusion
  30.7 2.5 pad_maximum_fusion
  33.1 5.1 %all-to-all-start = ((bf16[8,40,7296]{2,1,0:T(8,128)(2,1)}), bf16[8,40,7296]{2,1,0:T(8,128)(2,1)}, u32[]{:S(2)}, u32[]{:S(2)}) async-start(bf16[8,40,7296]{2,1,0:T(8,128)(2,1)} %bitcast.79), calls=%async_computation | async-start | bytes 9338880 | tf_op jit(solution)/shard_map/all_to_all | solution.py:126
  38.2 0.5 collective-permute-start.2
  38.7 0.6 fusion.68
  40.0 84.2 %collective-permute-done.2 = bf16[1,1792,3,128]{3,1,2,0:T(8,128)(2,1)} collective-permute-done((bf16[1,1792,3,128]{3,1,2,0:T(8,128)(2,1)S(1)}, bf16[1,1792,3,128]{3,1,2,0:T(8,128)(2,1)}, u32[]{:S(2)}, u32[]{:S(2)}) %collective-permute-start.2) | collective-permute-done | bytes 1376288 | tf_op jit(solution)/shard_map/ppermute | solution.py:8
  124.5 3.6 %collective-permute-start.8 = (bf16[1,1792,3,128]{3,1,2,0:T(8,128)(2,1)}, bf16[1,1792,3,128]{3,1,2,0:T(8,128)(2,1)}, u32[]{:S(2)}, u32[]{:S(2)}) collective-permute-start(bf16[1,1792,3,128]{3,1,2,0:T(8,128)(2,1)} %param.14), channel_id=1, source_target_pairs={{0,8},{1,9},{2,10},{3,11},{4,12},{5,13},{6,14},{7,15},{8,0},{9,1},... | collective-permute-start | bytes 4128776 | tf_op jit(solution)/shard_map/ppermute | solution.py:8
  128.4 1.3 slice_bitcast_fusion
  129.8 1.0 convert_reduce_fusion.1
  130.8 2.4 fusion.16
  133.2 2.4 fusion.27
  135.6 2.4 multiply_convert_fusion.5
  138.1 2.5 fusion.21
  140.7 3.6 %fusion.1 = bf16[3584,1,128]{2,0,1:T(8,128)(2,1)} fusion(bf16[320,128]{1,0:T(8,128)(2,1)S(1)} %get-tuple-element.38, bf16[320,7296]{1,0:T(8,128)(2,1)} %bitcast.5), kind=kOutput, calls=%fused_computation.6 | convolution fusion | flops 294060032 | bytes 3293184 | tf_op jit(solution)/shard_map/dot_general | solution.py:176
  144.3 0.8 convolution_convert_fusion.1
  145.1 1.6 pad_maximum_fusion.2
  146.7 7.7 %all-to-all-start.1 = ((bf16[8,40,3712]{2,1,0:T(8,128)(2,1)}), bf16[8,40,3712]{2,1,0:T(8,128)(2,1)}, u32[]{:S(2)}, u32[]{:S(2)}) async-start(bf16[8,40,3712]{2,1,0:T(8,128)(2,1)} %bitcast.10), calls=%async_computation.1 | async-start | bytes 4751360 | tf_op jit(solution)/shard_map/all_to_all | solution.py:126
  154.4 2.6 fusion
  157.0 2.8 %fusion.2 = bf16[3584,1,128]{2,0,1:T(8,128)(2,1)S(1)} fusion(bf16[320,128]{1,0:T(8,128)(2,1)S(1)} %get-tuple-element.37, f32[320]{0:T(512)S(1)} %convert_reduce_fusion.1, bf16[320,7296]{1,0:T(8,128)(2,1)} %bitcast.5), kind=kOutput, calls=%fused_computation.7 | convolution fusion | flops 297500672 | bytes 3294464 | tf_op jit(solution)/shard_map/dot_general | solution.py:177
  159.9 0.3 pad_maximum_fusion.1
  160.2 1.2 broadcast_select_fusion
  161.6 0.4 select_reduce_fusion
  162.0 56.4 %collective-permute-done.8 = bf16[1,1792,3,128]{3,1,2,0:T(8,128)(2,1)} collective-permute-done((bf16[1,1792,3,128]{3,1,2,0:T(8,128)(2,1)}, bf16[1,1792,3,128]{3,1,2,0:T(8,128)(2,1)}, u32[]{:S(2)}, u32[]{:S(2)}) %collective-permute-start.8) | collective-permute-done | bytes 1376288 | tf_op jit(solution)/shard_map/ppermute | solution.py:8
  218.4 4.2 %fusion.3 = (bf16[1,1792,3,128]{3,1,2,0:T(8,128)(2,1)}, bf16[1792,3,128]{2,0,1:T(8,128)(2,1)S(1)}) fusion(bf16[1792,3,128]{2,0,1:T(8,128)(2,1)} %collective-permute-done.6, bf16[1,1792,3,128]{3,1,2,0:T(8,128)(2,1)} %collective-permute-done.8, bf16[1,1792,3,128]{3,1,2,0:T(8,128)(2,1)} %param.14, pred[]{:T(512)S(6)} %eq.180, ...), kind=kLoop, calls=%fused_computation.13 | loop fusion | flops 8257536 | bytes 9633794 | tf_op jit(solution)/shard_map/convert_element_type | solution.py:196
  222.6 25.1 %collective-permute-done.7 = bf16[1,1792,3,128]{3,1,2,0:T(8,128)(2,1)} collective-permute-done((bf16[1,1792,3,128]{3,1,2,0:T(8,128)(2,1)}, bf16[1,1792,3,128]{3,1,2,0:T(8,128)(2,1)}, u32[]{:S(2)}, u32[]{:S(2)}) %collective-permute-start.7) | collective-permute-done | bytes 1376288 | tf_op jit(solution)/shard_map/ppermute | solution.py:8
  247.6 3.7 %fusion.4 = bf16[1,1792,3,128]{3,1,2,0:T(8,128)(2,1)} fusion(bf16[1792,3,128]{2,0,1:T(8,128)(2,1)} %collective-permute-done.6, bf16[1792,3,128]{2,0,1:T(8,128)(2,1)S(1)} %get-tuple-element.29, bf16[1,1792,3,128]{3,1,2,0:T(8,128)(2,1)} %collective-permute-done.7, bf16[1,1792,3,128]{3,1,2,0:T(8,128)(2,1)} %param.13, pred[]{:T(512)S(6)} %eq.180), kind=kLoop, calls=%fused_computation.15 | loop fusion | flops 6193152 | bytes 6881281 | tf_op jit(solution)/shard_map/convert_element_type | solution.py:195
  251.4 1.1 convert_reduce_fusion
  252.5 3.1 %fusion.5 = f32[64,3584]{1,0:T(8,128)S(1)} fusion(f32[320,64]{0,1:T(8,128)S(1)} %select_reduce_fusion, bf16[320,3712]{1,0:T(8,128)(2,1)} %bitcast.11), kind=kOutput, calls=%fused_computation.19 | convolution fusion | flops 880803840 | bytes 3293184 | tf_op jit(solution)/shard_map/dot_general | solution.py:206
  255.7 0.2 select_reduce_fusion.1
  255.9 3.0 %collective-permute-start.5 = (bf16[256]{0:T(256)(128)(2,1)S(1)}, bf16[256]{0:T(256)(128)(2,1)S(1)}, u32[]{:S(2)}, u32[]{:S(2)}) collective-permute-start(bf16[256]{0:T(256)(128)(2,1)S(1)} %slice.85), channel_id=1, source_target_pairs={{0,8},{1,9},{2,10},{3,11},{4,12},{5,13},{6,14},{7,15},{8,0},{9,1},... | collective-permute-start | bytes 1544 | tf_op jit(solution)/shard_map/ppermute | solution.py:8
  258.8 3.2 %multiply_bitcast_fusion = f32[1,1792,3,128]{3,1,2,0:T(8,128)} fusion(bf16[1792,3,128]{2,0,1:T(8,128)(2,1)} %collective-permute-done.6, bf16[1792,3,128]{2,0,1:T(8,128)(2,1)S(1)} %copy-done.1), kind=kLoop, calls=%fused_computation.17 | loop fusion | flops 2752512 | bytes 5505024 | tf_op jit(solution)/shard_map/broadcast_in_dim | solution.py:192
  262.1 6.8 %collective-permute-done.5 = bf16[256]{0:T(256)(128)(2,1)S(1)} collective-permute-done((bf16[256]{0:T(256)(128)(2,1)S(1)}, bf16[256]{0:T(256)(128)(2,1)S(1)}, u32[]{:S(2)}, u32[]{:S(2)}) %collective-permute-start.5) | collective-permute-done | bytes 544 | tf_op jit(solution)/shard_map/ppermute | solution.py:8
  269.0 0.7 copy.52
  269.7 0.7 fusion.31
  (76 shorter events, 3.3 us)
Async XLA Ops:
  2.0 7.8 %collective-permute-start = (f32[32,16]{0,1:T(8,128)S(1)}, f32[32,16]{0,1:T(8,128)S(1)}, u32[]{:S(2)}, u32[]{:S(2)}) collective-permute-start(f32[32,16]{0,1:T(8,128)S(1)} %pad_maximum_fusion.3), channel_id=1, source_target_pairs={{0,8},{1,9},{2,10},{3,11},{4,12},{5,13},{6,14},{7,15},{8,0},{9,1},... | collective-permute-start | bytes 6152 | tf_op jit(solution)/shard_map/ppermute | solution.py:8
  6.5 22.8 %collective-permute-start.1 = (bf16[32,7168]{1,0:T(8,128)(2,1)S(1)}, bf16[32,7168]{1,0:T(8,128)(2,1)S(1)}, u32[]{:S(2)}, u32[]{:S(2)}) collective-permute-start(bf16[32,7168]{1,0:T(8,128)(2,1)S(1)} %constant_dynamic-update-slice_fusion.1), channel_id=1, source_target_pairs={{0,8},{1,9},{2,10},{3,11},{4,12},{5,13},{6,14},{7,15},{8,0},{9,1},... | collective-permute-start | bytes 1376264 | tf_op jit(solution)/shard_map/ppermute | solution.py:8
  33.1 5.1 %copy-start.3 = (bf16[1,1792,3,128]{3,1,2,0:T(8,128)(2,1)S(1)}, bf16[1,1792,3,128]{3,1,2,0:T(8,128)(2,1)}, u32[]{:S(2)}) copy-start(bf16[1,1792,3,128]{3,1,2,0:T(8,128)(2,1)} %param.12) | copy-start | bytes 4128772
  33.1 5.6 %copy-start.8 = (s32[8]{0:T(128)S(1)}, s32[8]{0:T(128)}, u32[]{:S(2)}) copy-start(s32[8]{0:T(128)} %param.15) | copy-start | bytes 100
  33.1 96.6 %all-to-all-start = ((bf16[8,40,7296]{2,1,0:T(8,128)(2,1)}), bf16[8,40,7296]{2,1,0:T(8,128)(2,1)}, u32[]{:S(2)}, u32[]{:S(2)}) async-start(bf16[8,40,7296]{2,1,0:T(8,128)(2,1)} %bitcast.79), calls=%async_computation | async-start | bytes 9338880 | tf_op jit(solution)/shard_map/all_to_all | solution.py:126
  38.2 86.0 %collective-permute-start.2 = (bf16[1,1792,3,128]{3,1,2,0:T(8,128)(2,1)S(1)}, bf16[1,1792,3,128]{3,1,2,0:T(8,128)(2,1)}, u32[]{:S(2)}, u32[]{:S(2)}) collective-permute-start(bf16[1,1792,3,128]{3,1,2,0:T(8,128)(2,1)S(1)} %copy-done.3), channel_id=1, source_target_pairs={{0,8},{1,9},{2,10},{3,11},{4,12},{5,13},{6,14},{7,15},{8,0},{9,1},... | collective-permute-start | bytes 4128776 | tf_op jit(solution)/shard_map/ppermute | solution.py:8
  124.4 3.8 %copy-start.2 = (bf16[1,1792,3,128]{3,1,2,0:T(8,128)(2,1)}, bf16[1,1792,3,128]{3,1,2,0:T(8,128)(2,1)S(1)}, u32[]{:S(2)}) copy-start(bf16[1,1792,3,128]{3,1,2,0:T(8,128)(2,1)S(1)} %broadcast_select_fusion.2) | copy-start | bytes 4128772
  124.4 3.6 %collective-permute-start.3 = (bf16[1,1792,3,128]{3,1,2,0:T(8,128)(2,1)S(1)}, bf16[1,1792,3,128]{3,1,2,0:T(8,128)(2,1)S(1)}, u32[]{:S(2)}, u32[]{:S(2)}) collective-permute-start(bf16[1,1792,3,128]{3,1,2,0:T(8,128)(2,1)S(1)} %broadcast_select_fusion.2), channel_id=1, source_target_pairs={{0,16},{16,0},{1,17},{17,1},{2,18},{18,2},{3,19},{19,3},{4,20},{20... | collective-permute-start | bytes 4128776 | tf_op jit(solution)/shard_map/ppermute | solution.py:146
  124.5 93.9 %collective-permute-start.8 = (bf16[1,1792,3,128]{3,1,2,0:T(8,128)(2,1)}, bf16[1,1792,3,128]{3,1,2,0:T(8,128)(2,1)}, u32[]{:S(2)}, u32[]{:S(2)}) collective-permute-start(bf16[1,1792,3,128]{3,1,2,0:T(8,128)(2,1)} %param.14), channel_id=1, source_target_pairs={{0,8},{1,9},{2,10},{3,11},{4,12},{5,13},{6,14},{7,15},{8,0},{9,1},... | collective-permute-start | bytes 4128776 | tf_op jit(solution)/shard_map/ppermute | solution.py:8
  140.6 3.8 %copy-start.4 = (bf16[3584,128]{1,0:T(8,128)(2,1)S(1)}, bf16[3584,128]{1,0:T(8,128)(2,1)}, u32[]{:S(2)}) copy-start(bf16[3584,128]{1,0:T(8,128)(2,1)} %get-tuple-element.32) | copy-start | bytes 2752516
  140.6 3.8 %copy-start.5 = (bf16[3584,128]{1,0:T(8,128)(2,1)S(1)}, bf16[3584,128]{1,0:T(8,128)(2,1)}, u32[]{:S(2)}) copy-start(bf16[3584,128]{1,0:T(8,128)(2,1)} %get-tuple-element.33) | copy-start | bytes 2752516
  146.7 104.7 %all-to-all-start.1 = ((bf16[8,40,3712]{2,1,0:T(8,128)(2,1)}), bf16[8,40,3712]{2,1,0:T(8,128)(2,1)}, u32[]{:S(2)}, u32[]{:S(2)}) async-start(bf16[8,40,3712]{2,1,0:T(8,128)(2,1)} %bitcast.10), calls=%async_computation.1 | async-start | bytes 4751360 | tf_op jit(solution)/shard_map/all_to_all | solution.py:126
  157.0 2.8 %copy-start.6 = (bf16[3584,1,128]{2,0,1:T(8,128)(2,1)S(1)}, bf16[3584,1,128]{2,0,1:T(8,128)(2,1)}, u32[]{:S(2)}) copy-start(bf16[3584,1,128]{2,0,1:T(8,128)(2,1)} %fusion.1) | copy-start | bytes 2752516
  160.2 1.2 copy-start.7
  161.4 57.0 %collective-permute-start.6 = (bf16[1792,3,128]{2,0,1:T(8,128)(2,1)}, bf16[1792,3,128]{2,0,1:T(8,128)(2,1)}, u32[]{:S(2)}, u32[]{:S(2)}) collective-permute-start(bf16[1792,3,128]{2,0,1:T(8,128)(2,1)} %broadcast_select_fusion), channel_id=1, source_target_pairs={{0,16},{16,0},{1,17},{17,1},{2,18},{18,2},{3,19},{19,3},{4,20},{20... | collective-permute-start | bytes 4128776 | tf_op jit(solution)/shard_map/ppermute | solution.py:186
  161.4 86.2 %collective-permute-start.7 = (bf16[1,1792,3,128]{3,1,2,0:T(8,128)(2,1)}, bf16[1,1792,3,128]{3,1,2,0:T(8,128)(2,1)}, u32[]{:S(2)}, u32[]{:S(2)}) collective-permute-start(bf16[1,1792,3,128]{3,1,2,0:T(8,128)(2,1)} %param.13), channel_id=1, source_target_pairs={{0,8},{1,9},{2,10},{3,11},{4,12},{5,13},{6,14},{7,15},{8,0},{9,1},... | collective-permute-start | bytes 4128776 | tf_op jit(solution)/shard_map/ppermute | solution.py:8
  222.6 25.1 %copy-start = (bf16[1792,3,128]{2,0,1:T(8,128)(2,1)}, bf16[1792,3,128]{2,0,1:T(8,128)(2,1)S(1)}, u32[]{:S(2)}) copy-start(bf16[1792,3,128]{2,0,1:T(8,128)(2,1)S(1)} %get-tuple-element.29) | copy-start | bytes 4128772
  251.4 7.5 %copy-start.1 = (bf16[1792,3,128]{2,0,1:T(8,128)(2,1)S(1)}, bf16[1792,3,128]{2,0,1:T(8,128)(2,1)}, u32[]{:S(2)}) copy-start(bf16[1792,3,128]{2,0,1:T(8,128)(2,1)} %copy-done) | copy-start | bytes 4128772
  255.6 14.1 %collective-permute-start.4 = (bf16[32,3584]{1,0:T(8,128)(2,1)S(1)}, bf16[32,3584]{1,0:T(8,128)(2,1)S(1)}, u32[]{:S(2)}, u32[]{:S(2)}) collective-permute-start(bf16[32,3584]{1,0:T(8,128)(2,1)S(1)} %slice.148), channel_id=1, source_target_pairs={{0,8},{1,9},{2,10},{3,11},{4,12},{5,13},{6,14},{7,15},{8,0},{9,1},... | collective-permute-start | bytes 688136 | tf_op jit(solution)/shard_map/ppermute | solution.py:8
  255.9 13.0 %collective-permute-start.5 = (bf16[256]{0:T(256)(128)(2,1)S(1)}, bf16[256]{0:T(256)(128)(2,1)S(1)}, u32[]{:S(2)}, u32[]{:S(2)}) collective-permute-start(bf16[256]{0:T(256)(128)(2,1)S(1)} %slice.85), channel_id=1, source_target_pairs={{0,8},{1,9},{2,10},{3,11},{4,12},{5,13},{6,14},{7,15},{8,0},{9,1},... | collective-permute-start | bytes 1544 | tf_op jit(solution)/shard_map/ppermute | solution.py:8

commit v21 on v19

--- a/solution.py
+++ b/solution.py
@@ -89,9 +89,12 @@
     two_stage = half_axis <= 8
     if two_stage:
         packed = jnp.concatenate([tokens, out_grad], axis=1)
-        p_packed, p_ids, p_gate, their_weights = from_partner(
-            (packed, expert_ids, gate_probs, weights), "expert", swap_bit
-        )
+        small = jnp.concatenate([expert_ids.astype(jnp.float32), gate_probs], axis=1)
+        p_packed, p_small, their_weights = from_partner(
+            (packed, small, weights), "expert", swap_bit
+        )
+        p_ids = p_small[:, :route_count].astype(jnp.int32)
+        p_gate = p_small[:, route_count:]
         both = jnp.concatenate([packed, p_packed], axis=0)
         ids2 = jnp.concatenate([flat_ids, p_ids.reshape(-1)])
         gate2 = jnp.concatenate([flat_gate, p_gate.reshape(-1)])

time: 271 us -> 273 us (level)
  starting transfers between devices: 25.5 us -> 20 us
  waiting for transfers between devices: 186 us -> 191 us
    ppermute x7 -> x6, waiting for transfers between devices: 186 us -> 191 us  [from_partner(): lax.ppermute(value, axis, [(i, i ^ 1 << bit) for i in range(lax.axis_size...]
    ppermute x7 -> x6, starting transfers between devices: 11.9 us -> 8.41 us  [from_partner(): lax.ppermute(value, axis, [(i, i ^ 1 << bit) for i in range(lax.axis_size...]
  transfers between devices with their start and end apart: 11 -> 10, of which waited for: 5 -> 5; matrix products, arithmetic and copies ran while one was open for 18% -> 18% of each run, Pallas kernels for 0% -> 0%
where the time goes in v21:
time: 273 us; the launch traced here: 272 us
  waiting for transfers between devices  191 us (70%)
  other arithmetic  28.7 us (11%)
  matrix products  24 us (9%)
  starting transfers between devices  20 us (7%)
  local copies, waits for them, and re-layouts  6.85 us (3%)
    ppermute x6, waiting for transfers between devices, from_partner(): lax.ppermute(value, axis, [(i, i ^ 1 << bit) for i in range(lax.axis_size...  191 us
    all_to_all x2, starting transfers between devices, spread(): lax.all_to_all(parts, 'expert', 0, 0, tiled=True, axis_index_groups=halves)  11.5 us
    ppermute x6, starting transfers between devices, from_partner(): lax.ppermute(value, axis, [(i, i ^ 1 << bit) for i in range(lax.axis_size...  8.41 us
  transfers between devices with their start and end apart: 10, of which 5 were waited for; matrix products, arithmetic and copies ran while one was open for 18% of the time, Pallas kernels for 0%

profile of v21, /device:TPU:6, one launch (start us, length us, event | category | flops | bytes accessed | tf_op | source)
XLA Modules:
  0.0 271.7 jit_solution(4657928737955335188)
XLA Ops:
  0.6 0.7 convert_element_type.110
  1.3 0.7 pad_maximum_fusion.3
  2.0 2.6 collective-permute-start
  4.6 1.0 constant_dynamic-update-slice_fusion.2
  5.6 1.0 constant_dynamic-update-slice_fusion.1
  6.5 0.4 collective-permute-start.1
  6.9 0.8 copy.57
  7.9 0.6 reduce-window.14
  8.9 0.7 convert.33
  10.2 0.8 pad_add_fusion
  11.0 0.6 reduce-window.16
  11.9 0.7 select_reduce_fusion.3
  13.6 0.4 fusion.29
  14.1 15.2 %collective-permute-done.1 = bf16[32,7168]{1,0:T(8,128)(2,1)S(1)} collective-permute-done((bf16[32,7168]{1,0:T(8,128)(2,1)S(1)}, bf16[32,7168]{1,0:T(8,128)(2,1)S(1)}, u32[]{:S(2)}, u32[]{:S(2)}) %collective-permute-start.1) | collective-permute-done | bytes 458784 | tf_op jit(solution)/shard_map/ppermute | solution.py:8
  29.3 1.4 convolution_convert_fusion
  30.7 2.5 pad_maximum_fusion
  33.1 5.1 %all-to-all-start = ((bf16[8,40,7296]{2,1,0:T(8,128)(2,1)}), bf16[8,40,7296]{2,1,0:T(8,128)(2,1)}, u32[]{:S(2)}, u32[]{:S(2)}) async-start(bf16[8,40,7296]{2,1,0:T(8,128)(2,1)} %bitcast.79), calls=%async_computation | async-start | bytes 9338880 | tf_op jit(solution)/shard_map/all_to_all | solution.py:126
  38.2 0.5 collective-permute-start.2
  38.7 0.6 fusion.74
  40.0 84.2 %collective-permute-done.2 = bf16[1,1792,3,128]{3,1,2,0:T(8,128)(2,1)} collective-permute-done((bf16[1,1792,3,128]{3,1,2,0:T(8,128)(2,1)S(1)}, bf16[1,1792,3,128]{3,1,2,0:T(8,128)(2,1)}, u32[]{:S(2)}, u32[]{:S(2)}) %collective-permute-start.2) | collective-permute-done | bytes 1376288 | tf_op jit(solution)/shard_map/ppermute | solution.py:8
  124.2 1.5 broadcast_select_fusion.2
  125.8 3.6 %collective-permute-start.7 = (bf16[1,1792,3,128]{3,1,2,0:T(8,128)(2,1)}, bf16[1,1792,3,128]{3,1,2,0:T(8,128)(2,1)}, u32[]{:S(2)}, u32[]{:S(2)}) collective-permute-start(bf16[1,1792,3,128]{3,1,2,0:T(8,128)(2,1)} %param.14), channel_id=1, source_target_pairs={{0,8},{1,9},{2,10},{3,11},{4,12},{5,13},{6,14},{7,15},{8,0},{9,1},... | collective-permute-start | bytes 4128776 | tf_op jit(solution)/shard_map/ppermute | solution.py:8
  129.7 1.3 slice_bitcast_fusion
  131.1 1.0 convert_reduce_fusion.1
  132.1 2.4 fusion.16
  134.5 2.4 fusion.27
  137.0 2.4 multiply_convert_fusion.5
  139.4 2.5 fusion.21
  142.0 3.6 %fusion.1 = bf16[3584,1,128]{2,0,1:T(8,128)(2,1)} fusion(bf16[320,128]{1,0:T(8,128)(2,1)S(1)} %get-tuple-element.52, bf16[320,7296]{1,0:T(8,128)(2,1)} %bitcast.5), kind=kOutput, calls=%fused_computation.6 | convolution fusion | flops 294060032 | bytes 3293184 | tf_op jit(solution)/shard_map/dot_general | solution.py:176
  145.7 0.8 convolution_convert_fusion.1
  146.5 1.6 pad_maximum_fusion.2
  148.0 6.4 %all-to-all-start.1 = ((bf16[8,40,3712]{2,1,0:T(8,128)(2,1)}), bf16[8,40,3712]{2,1,0:T(8,128)(2,1)}, u32[]{:S(2)}, u32[]{:S(2)}) async-start(bf16[8,40,3712]{2,1,0:T(8,128)(2,1)} %bitcast.10), calls=%async_computation.1 | async-start | bytes 4751360 | tf_op jit(solution)/shard_map/all_to_all | solution.py:126
  154.4 2.6 fusion
  157.0 2.8 %fusion.2 = bf16[3584,1,128]{2,0,1:T(8,128)(2,1)S(1)} fusion(bf16[320,128]{1,0:T(8,128)(2,1)S(1)} %get-tuple-element.51, f32[320]{0:T(512)S(1)} %convert_reduce_fusion.1, bf16[320,7296]{1,0:T(8,128)(2,1)} %bitcast.5), kind=kOutput, calls=%fused_computation.7 | convolution fusion | flops 297500672 | bytes 3294464 | tf_op jit(solution)/shard_map/dot_general | solution.py:177
  159.9 0.3 pad_maximum_fusion.1
  160.2 1.2 broadcast_select_fusion
  161.4 1.3 collective-permute-start.6
  162.9 0.4 select_reduce_fusion
  163.3 56.4 %collective-permute-done.7 = bf16[1,1792,3,128]{3,1,2,0:T(8,128)(2,1)} collective-permute-done((bf16[1,1792,3,128]{3,1,2,0:T(8,128)(2,1)}, bf16[1,1792,3,128]{3,1,2,0:T(8,128)(2,1)}, u32[]{:S(2)}, u32[]{:S(2)}) %collective-permute-start.7) | collective-permute-done | bytes 1376288 | tf_op jit(solution)/shard_map/ppermute | solution.py:8
  219.7 4.2 %fusion.3 = (bf16[1,1792,3,128]{3,1,2,0:T(8,128)(2,1)}, bf16[1792,3,128]{2,0,1:T(8,128)(2,1)S(1)}) fusion(bf16[1792,3,128]{2,0,1:T(8,128)(2,1)} %collective-permute-done.5, bf16[1,1792,3,128]{3,1,2,0:T(8,128)(2,1)} %collective-permute-done.7, bf16[1,1792,3,128]{3,1,2,0:T(8,128)(2,1)} %param.14, pred[]{:T(512)S(6)} %eq.184, ...), kind=kLoop, calls=%fused_computation.13 | loop fusion | flops 8257536 | bytes 9633794 | tf_op jit(solution)/shard_map/convert_element_type | solution.py:196
  223.9 25.1 %collective-permute-done.6 = bf16[1,1792,3,128]{3,1,2,0:T(8,128)(2,1)} collective-permute-done((bf16[1,1792,3,128]{3,1,2,0:T(8,128)(2,1)}, bf16[1,1792,3,128]{3,1,2,0:T(8,128)(2,1)}, u32[]{:S(2)}, u32[]{:S(2)}) %collective-permute-start.6) | collective-permute-done | bytes 1376288 | tf_op jit(solution)/shard_map/ppermute | solution.py:8
  249.0 3.7 %fusion.4 = bf16[1,1792,3,128]{3,1,2,0:T(8,128)(2,1)} fusion(bf16[1792,3,128]{2,0,1:T(8,128)(2,1)} %collective-permute-done.5, bf16[1792,3,128]{2,0,1:T(8,128)(2,1)S(1)} %get-tuple-element.41, bf16[1,1792,3,128]{3,1,2,0:T(8,128)(2,1)} %collective-permute-done.6, bf16[1,1792,3,128]{3,1,2,0:T(8,128)(2,1)} %param.13, pred[]{:T(512)S(6)} %eq.184), kind=kLoop, calls=%fused_computation.15 | loop fusion | flops 6193152 | bytes 6881281 | tf_op jit(solution)/shard_map/convert_element_type | solution.py:195
  252.7 1.1 convert_reduce_fusion
  253.8 3.1 %fusion.5 = f32[64,3584]{1,0:T(8,128)S(1)} fusion(f32[320,64]{0,1:T(8,128)S(1)} %select_reduce_fusion, bf16[320,3712]{1,0:T(8,128)(2,1)} %bitcast.11), kind=kOutput, calls=%fused_computation.19 | convolution fusion | flops 880803840 | bytes 3293184 | tf_op jit(solution)/shard_map/dot_general | solution.py:206
  257.4 3.2 %multiply_bitcast_fusion = f32[1,1792,3,128]{3,1,2,0:T(8,128)} fusion(bf16[1792,3,128]{2,0,1:T(8,128)(2,1)} %collective-permute-done.5, bf16[1792,3,128]{2,0,1:T(8,128)(2,1)S(1)} %copy-done.1), kind=kLoop, calls=%fused_computation.17 | loop fusion | flops 2752512 | bytes 5505024 | tf_op jit(solution)/shard_map/broadcast_in_dim | solution.py:192
  260.7 9.6 %collective-permute-done.4 = bf16[32,3712]{1,0:T(8,128)(2,1)S(1)} collective-permute-done((bf16[32,3712]{1,0:T(8,128)(2,1)S(1)}, bf16[32,3712]{1,0:T(8,128)(2,1)S(1)}, u32[]{:S(2)}, u32[]{:S(2)}) %collective-permute-start.4) | collective-permute-done | bytes 237600 | tf_op jit(solution)/shard_map/ppermute | solution.py:8
  270.4 0.7 copy.70
  271.0 0.7 fusion.31
  (80 shorter events, 3.9 us)
Async XLA Ops:
  2.0 7.8 %collective-permute-start = (f32[32,16]{0,1:T(8,128)S(1)}, f32[32,16]{0,1:T(8,128)S(1)}, u32[]{:S(2)}, u32[]{:S(2)}) collective-permute-start(f32[32,16]{0,1:T(8,128)S(1)} %pad_maximum_fusion.3), channel_id=1, source_target_pairs={{0,8},{1,9},{2,10},{3,11},{4,12},{5,13},{6,14},{7,15},{8,0},{9,1},... | collective-permute-start | bytes 6152 | tf_op jit(solution)/shard_map/ppermute | solution.py:8
  6.5 22.8 %collective-permute-start.1 = (bf16[32,7168]{1,0:T(8,128)(2,1)S(1)}, bf16[32,7168]{1,0:T(8,128)(2,1)S(1)}, u32[]{:S(2)}, u32[]{:S(2)}) collective-permute-start(bf16[32,7168]{1,0:T(8,128)(2,1)S(1)} %constant_dynamic-update-slice_fusion.1), channel_id=1, source_target_pairs={{0,8},{1,9},{2,10},{3,11},{4,12},{5,13},{6,14},{7,15},{8,0},{9,1},... | collective-permute-start | bytes 1376264 | tf_op jit(solution)/shard_map/ppermute | solution.py:8
  33.1 5.1 %copy-start.3 = (bf16[1,1792,3,128]{3,1,2,0:T(8,128)(2,1)S(1)}, bf16[1,1792,3,128]{3,1,2,0:T(8,128)(2,1)}, u32[]{:S(2)}) copy-start(bf16[1,1792,3,128]{3,1,2,0:T(8,128)(2,1)} %param.12) | copy-start | bytes 4128772
  33.1 5.6 %copy-start.8 = (s32[8]{0:T(128)S(1)}, s32[8]{0:T(128)}, u32[]{:S(2)}) copy-start(s32[8]{0:T(128)} %param.15) | copy-start | bytes 100
  33.1 98.0 %all-to-all-start = ((bf16[8,40,7296]{2,1,0:T(8,128)(2,1)}), bf16[8,40,7296]{2,1,0:T(8,128)(2,1)}, u32[]{:S(2)}, u32[]{:S(2)}) async-start(bf16[8,40,7296]{2,1,0:T(8,128)(2,1)} %bitcast.79), calls=%async_computation | async-start | bytes 9338880 | tf_op jit(solution)/shard_map/all_to_all | solution.py:126
  38.2 86.0 %collective-permute-start.2 = (bf16[1,1792,3,128]{3,1,2,0:T(8,128)(2,1)S(1)}, bf16[1,1792,3,128]{3,1,2,0:T(8,128)(2,1)}, u32[]{:S(2)}, u32[]{:S(2)}) collective-permute-start(bf16[1,1792,3,128]{3,1,2,0:T(8,128)(2,1)S(1)} %copy-done.3), channel_id=1, source_target_pairs={{0,8},{1,9},{2,10},{3,11},{4,12},{5,13},{6,14},{7,15},{8,0},{9,1},... | collective-permute-start | bytes 4128776 | tf_op jit(solution)/shard_map/ppermute | solution.py:8
  125.7 3.8 %copy-start.2 = (bf16[1,1792,3,128]{3,1,2,0:T(8,128)(2,1)}, bf16[1,1792,3,128]{3,1,2,0:T(8,128)(2,1)S(1)}, u32[]{:S(2)}) copy-start(bf16[1,1792,3,128]{3,1,2,0:T(8,128)(2,1)S(1)} %broadcast_select_fusion.2) | copy-start | bytes 4128772
  125.7 3.6 %collective-permute-start.3 = (bf16[1,1792,3,128]{3,1,2,0:T(8,128)(2,1)S(1)}, bf16[1,1792,3,128]{3,1,2,0:T(8,128)(2,1)S(1)}, u32[]{:S(2)}, u32[]{:S(2)}) collective-permute-start(bf16[1,1792,3,128]{3,1,2,0:T(8,128)(2,1)S(1)} %broadcast_select_fusion.2), channel_id=1, source_target_pairs={{0,16},{16,0},{1,17},{17,1},{2,18},{18,2},{3,19},{19,3},{4,20},{20... | collective-permute-start | bytes 4128776 | tf_op jit(solution)/shard_map/ppermute | solution.py:146
  125.8 93.9 %collective-permute-start.7 = (bf16[1,1792,3,128]{3,1,2,0:T(8,128)(2,1)}, bf16[1,1792,3,128]{3,1,2,0:T(8,128)(2,1)}, u32[]{:S(2)}, u32[]{:S(2)}) collective-permute-start(bf16[1,1792,3,128]{3,1,2,0:T(8,128)(2,1)} %param.14), channel_id=1, source_target_pairs={{0,8},{1,9},{2,10},{3,11},{4,12},{5,13},{6,14},{7,15},{8,0},{9,1},... | collective-permute-start | bytes 4128776 | tf_op jit(solution)/shard_map/ppermute | solution.py:8
  141.9 3.8 %copy-start.4 = (bf16[3584,128]{1,0:T(8,128)(2,1)S(1)}, bf16[3584,128]{1,0:T(8,128)(2,1)}, u32[]{:S(2)}) copy-start(bf16[3584,128]{1,0:T(8,128)(2,1)} %get-tuple-element.46) | copy-start | bytes 2752516
  141.9 3.8 %copy-start.5 = (bf16[3584,128]{1,0:T(8,128)(2,1)S(1)}, bf16[3584,128]{1,0:T(8,128)(2,1)}, u32[]{:S(2)}) copy-start(bf16[3584,128]{1,0:T(8,128)(2,1)} %get-tuple-element.47) | copy-start | bytes 2752516
  148.0 104.7 %all-to-all-start.1 = ((bf16[8,40,3712]{2,1,0:T(8,128)(2,1)}), bf16[8,40,3712]{2,1,0:T(8,128)(2,1)}, u32[]{:S(2)}, u32[]{:S(2)}) async-start(bf16[8,40,3712]{2,1,0:T(8,128)(2,1)} %bitcast.10), calls=%async_computation.1 | async-start | bytes 4751360 | tf_op jit(solution)/shard_map/all_to_all | solution.py:126
  157.0 2.8 %copy-start.6 = (bf16[3584,1,128]{2,0,1:T(8,128)(2,1)S(1)}, bf16[3584,1,128]{2,0,1:T(8,128)(2,1)}, u32[]{:S(2)}) copy-start(bf16[3584,1,128]{2,0,1:T(8,128)(2,1)} %fusion.1) | copy-start | bytes 2752516
  160.2 2.6 copy-start.7
  161.4 58.3 %collective-permute-start.5 = (bf16[1792,3,128]{2,0,1:T(8,128)(2,1)}, bf16[1792,3,128]{2,0,1:T(8,128)(2,1)}, u32[]{:S(2)}, u32[]{:S(2)}) collective-permute-start(bf16[1792,3,128]{2,0,1:T(8,128)(2,1)} %broadcast_select_fusion), channel_id=1, source_target_pairs={{0,16},{16,0},{1,17},{17,1},{2,18},{18,2},{3,19},{19,3},{4,20},{20... | collective-permute-start | bytes 4128776 | tf_op jit(solution)/shard_map/ppermute | solution.py:186
  161.4 87.6 %collective-permute-start.6 = (bf16[1,1792,3,128]{3,1,2,0:T(8,128)(2,1)}, bf16[1,1792,3,128]{3,1,2,0:T(8,128)(2,1)}, u32[]{:S(2)}, u32[]{:S(2)}) collective-permute-start(bf16[1,1792,3,128]{3,1,2,0:T(8,128)(2,1)} %param.13), channel_id=1, source_target_pairs={{0,8},{1,9},{2,10},{3,11},{4,12},{5,13},{6,14},{7,15},{8,0},{9,1},... | collective-permute-start | bytes 4128776 | tf_op jit(solution)/shard_map/ppermute | solution.py:8
  223.9 25.1 %copy-start = (bf16[1792,3,128]{2,0,1:T(8,128)(2,1)}, bf16[1792,3,128]{2,0,1:T(8,128)(2,1)S(1)}, u32[]{:S(2)}) copy-start(bf16[1792,3,128]{2,0,1:T(8,128)(2,1)S(1)} %get-tuple-element.41) | copy-start | bytes 4128772
  252.7 4.7 %copy-start.1 = (bf16[1792,3,128]{2,0,1:T(8,128)(2,1)S(1)}, bf16[1792,3,128]{2,0,1:T(8,128)(2,1)}, u32[]{:S(2)}) copy-start(bf16[1792,3,128]{2,0,1:T(8,128)(2,1)} %copy-done) | copy-start | bytes 4128772
  257.3 13.0 %collective-permute-start.4 = (bf16[32,3712]{1,0:T(8,128)(2,1)S(1)}, bf16[32,3712]{1,0:T(8,128)(2,1)S(1)}, u32[]{:S(2)}, u32[]{:S(2)}) collective-permute-start(bf16[32,3712]{1,0:T(8,128)(2,1)S(1)} %concatenate.122), channel_id=1, source_target_pairs={{0,8},{1,9},{2,10},{3,11},{4,12},{5,13},{6,14},{7,15},{8,0},{9,1},... | collective-permute-start | bytes 712712 | tf_op jit(solution)/shard_map/ppermute | solution.py:8
